TPU v7x, 32 devices: a whole 2x2x4 slice. The times are simulated.
32 devices in a mesh: rows: 8 (over z, x), cols: 4 (over y, core).
Axes of the slice: x: 2, y: 2, z: 4, core: 2. Of those that a mesh axis runs over, the one named last changes fastest.
Arguments:
- probes: float32 [64, 128, 512], P(None, 'rows', 'cols'), may hold values from -6 to 6
- observed: float32 [128, 512], P('rows', 'cols'), may hold values from -1.8 to 1.8
- kappa_sq: float32 [128, 512], P('rows', 'cols'), may hold values from 0.01 to 1
- variance_weight: float32 [128, 512], P('rows', 'cols'), may hold values from 0.25 to 10
Outputs:
- grad_kappa: float32 [128, 512], P('rows', 'cols')
- grad_weight: float32 [128, 512], P('rows', 'cols')
All inputs are finite; a program needn't handle non-finite values.
Results may differ from a plain program's by a relative error of at most 0.0001.
Values sent between devices are 32-bit elements; how exact they have to be, the bound alone decides.
No kernel may reach another device: no remote copies, remote signals or barrier semaphores. Data moves between devices by JAX's collectives and lax.ppermute only.
A program may use at most 64 MiB of HBM per device.

v0:
```python
import jax
import jax.numpy as jnp
from jax import lax
from jax.sharding import PartitionSpec as P

ITERS = 3


def extended(cells, sides, width):
    for axis, dim in sides:
        count = lax.axis_size(axis)
        ends = count - 1
        head = lax.slice_in_dim(cells, 0, width, axis=dim)
        tail = lax.slice_in_dim(cells, cells.shape[dim] - width, cells.shape[dim], axis=dim)
        cells = jnp.concatenate(
            [
                lax.ppermute(tail, axis, [(i, (i + 1) % count) for i in range(ends)]),
                cells,
                lax.ppermute(head, axis, [((i + 1) % count, i) for i in range(ends)]),
            ],
            axis=dim,
        )
    return cells


def stencil(padded, kappa_sq):
    centre = padded[..., 1:-1, 1:-1]
    edge_sum = (
        padded[..., :-2, 1:-1]
        + padded[..., 2:, 1:-1]
        + padded[..., 1:-1, :-2]
        + padded[..., 1:-1, 2:]
    )
    corners = (
        padded[..., :-2, :-2] + padded[..., :-2, 2:] + padded[..., 2:, :-2] + padded[..., 2:, 2:]
    )
    return (kappa_sq + 20.0 / 6.0) * centre - (4.0 * edge_sum + corners) / 6.0


def with_rim(field):
    return extended(field, (("rows", 1), ("cols", 2)), 1)


def inner_sum(first_field, second_field):
    return jnp.sum(first_field * second_field, axis=(1, 2))


def sectioned_sum(local_terms):
    col_total = lax.psum(local_terms, "cols")
    return lax.psum(col_total, "rows")


def on_device(probes, observed, kappa_sq, variance_weight):
    residual = probes
    solution = jnp.zeros_like(probes)
    direction = probes
    stiff_probe = None
    norm_now = sectioned_sum(inner_sum(residual, residual))
    for iteration in range(ITERS):
        stiffness = stencil(with_rim(direction), kappa_sq)
        applied = stencil(with_rim(variance_weight * stiffness), kappa_sq)
        stiffness, applied = (stiffness, applied)
        if iteration == 0:
            stiff_probe = stiffness
        step_len = norm_now / sectioned_sum(inner_sum(direction, applied))
        solution = solution + step_len[:, None, None] * direction
        residual = residual - step_len[:, None, None] * applied
        if iteration + 1 < ITERS:
            norm_next = sectioned_sum(inner_sum(residual, residual))
            direction = residual + (norm_next / norm_now)[:, None, None] * direction
            norm_now = norm_next
    stacked = jnp.concatenate([solution, observed[None]], axis=0)
    stiff_all = stencil(with_rim(stacked), kappa_sq)
    stiff_solution = stiff_all[:-1]
    stiff_obs = stiff_all[-1]
    probe_count = probes.shape[0]
    weight_total = jnp.sum(stiff_solution * stiff_probe, axis=0)
    kappa_total = jnp.sum(solution * stiff_probe + stiff_solution * probes, axis=0)
    grad_weight = 0.5 * weight_total / probe_count - 0.5 * stiff_obs * stiff_obs
    grad_kappa = (
        0.5 * variance_weight * (kappa_total / probe_count) - observed * variance_weight * stiff_obs
    )
    return (grad_kappa, grad_weight)


def solution(mesh):
    placed = (P(None, "rows", "cols"), P("rows", "cols"), P("rows", "cols"), P("rows", "cols"))
    return jax.shard_map(
        on_device,
        mesh=mesh,
        in_specs=placed,
        out_specs=(P("rows", "cols"), P("rows", "cols")),
        check_vma=False,
    )
```

profile of v0, /device:TPU:0, one launch (start us, length us, event | category | flops | bytes accessed | tf_op | source)
XLA Modules:
  0.0 278.7 jit_solution(426669800941834101)
XLA Ops:
  1.7 4.9 %collective-permute-start = (f32[64,1,128]{2,1,0:T(1,128)S(1)}, f32[64,1,128]{2,1,0:T(1,128)S(1)}, u32[]{:S(2)}, u32[]{:S(2)}) collective-permute-start(f32[64,1,128]{2,1,0:T(1,128)S(1)} %get-tuple-element.59), channel_id=1, source_target_pairs={{0,4},{4,8},{8,12},{12,16},{16,20},{20,24},{24,28},{1,5},{5,9},{9,... | collective-permute-start | bytes 98312 | tf_op jit(solution)/shard_map/ppermute | solution.py:17
  8.2 4.2 %collective-permute-done.1 = f32[64,1,128]{2,1,0:T(1,128)S(1)} collective-permute-done((f32[64,1,128]{2,1,0:T(1,128)S(1)}, f32[64,1,128]{2,1,0:T(1,128)S(1)}, u32[]{:S(2)}, u32[]{:S(2)}) %collective-permute-start.1) | collective-permute-done | bytes 32800 | tf_op jit(solution)/shard_map/ppermute | solution.py:19
  15.7 3.0 %collective-permute-start.2 = (f32[64,18,1]{0,2,1:T(1,128)S(1)}, f32[64,18,1]{0,2,1:T(1,128)S(1)}, u32[]{:S(2)}, u32[]{:S(2)}) collective-permute-start(f32[64,18,1]{0,2,1:T(1,128)S(1)} %copy.17), channel_id=1, source_target_pairs={{0,1},{1,2},{2,3},{4,5},{5,6},{6,7},{8,9},{9,10},{10,11},{12,13},{... | collective-permute-start | bytes 13832 | tf_op jit(solution)/shard_map/ppermute | solution.py:17
  22.6 4.4 %collective-permute-start.4 = (f32[64,1,128]{2,1,0:T(1,128)S(1)}, f32[64,1,128]{2,1,0:T(1,128)S(1)}, u32[]{:S(2)}, u32[]{:S(2)}) collective-permute-start(f32[64,1,128]{2,1,0:T(1,128)S(1)} %get-tuple-element.57), channel_id=1, source_target_pairs={{0,4},{4,8},{8,12},{12,16},{16,20},{20,24},{24,28},{1,5},{5,9},{9,... | collective-permute-start | bytes 98312 | tf_op jit(solution)/shard_map/ppermute | solution.py:17
  28.6 4.4 %collective-permute-done.5 = f32[64,1,128]{2,1,0:T(1,128)S(1)} collective-permute-done((f32[64,1,128]{2,1,0:T(1,128)S(1)}, f32[64,1,128]{2,1,0:T(1,128)S(1)}, u32[]{:S(2)}, u32[]{:S(2)}) %collective-permute-start.5) | collective-permute-done | bytes 32800 | tf_op jit(solution)/shard_map/ppermute | solution.py:19
  37.4 4.1 %collective-permute-done.7 = f32[64,18,1]{0,2,1:T(1,128)S(1)} collective-permute-done((f32[64,18,1]{0,2,1:T(1,128)S(1)}, f32[64,18,1]{0,2,1:T(1,128)S(1)}, u32[]{:S(2)}, u32[]{:S(2)}) %collective-permute-start.7) | collective-permute-done | bytes 4640 | tf_op jit(solution)/shard_map/ppermute | solution.py:19
  44.8 8.1 %all-reduce.1 = (f32[64]{0:T(128)S(1)}, f32[64]{0:T(128)S(1)}) all-reduce(f32[64]{0:T(128)S(1)} %get-tuple-element.5, f32[64]{0:T(128)S(1)} %get-tuple-element.4), channel_id=1, replica_groups=mesh['rows'=8,'cols'=4] {'cols'}, use_global_device_ids=true, to_apply=%region_1.0 | all-reduce | flops 128 | bytes 1024 | tf_op jit(solution)/shard_map/psum | solution.py:49
  52.9 18.8 %all-reduce = (f32[64]{0:T(128)S(1)}, f32[64]{0:T(128)S(1)}) all-reduce(f32[64]{0:T(128)S(1)} %get-tuple-element.8, f32[64]{0:T(128)S(1)} %get-tuple-element.9), channel_id=1, replica_groups=mesh['rows'=8,'cols'=4] {'rows'}, use_global_device_ids=true, to_apply=%region_2.0 | all-reduce | flops 128 | bytes 1024 | tf_op jit(solution)/shard_map/psum | solution.py:50
  72.7 5.6 %psum.88 = f32[64]{0:T(128)S(1)} all-reduce(f32[64]{0:T(128)S(1)} %get-tuple-element.12), channel_id=1, replica_groups=mesh['rows'=8,'cols'=4] {'cols'}, use_global_device_ids=true, to_apply=%region_7.0 | all-reduce | flops 64 | bytes 512 | tf_op jit(solution)/shard_map/psum | solution.py:49
  78.3 17.4 %psum.89 = f32[64]{0:T(128)S(1)} all-reduce(f32[64]{0:T(128)S(1)} %psum.88), channel_id=1, replica_groups=mesh['rows'=8,'cols'=4] {'rows'}, use_global_device_ids=true, to_apply=%region_8.0 | all-reduce | flops 64 | bytes 512 | tf_op jit(solution)/shard_map/psum | solution.py:50
  95.9 3.6 %collective-permute-start.8 = (f32[64,1,128]{2,1,0:T(1,128)S(1)}, f32[64,1,128]{2,1,0:T(1,128)S(1)}, u32[]{:S(2)}, u32[]{:S(2)}) collective-permute-start(f32[64,1,128]{2,1,0:T(1,128)S(1)} %get-tuple-element.55), channel_id=1, source_target_pairs={{0,4},{4,8},{8,12},{12,16},{16,20},{20,24},{24,28},{1,5},{5,9},{9,... | collective-permute-start | bytes 98312 | tf_op jit(solution)/shard_map/ppermute | solution.py:17
  101.1 4.2 %collective-permute-done.9 = f32[64,1,128]{2,1,0:T(1,128)S(1)} collective-permute-done((f32[64,1,128]{2,1,0:T(1,128)S(1)}, f32[64,1,128]{2,1,0:T(1,128)S(1)}, u32[]{:S(2)}, u32[]{:S(2)}) %collective-permute-start.9) | collective-permute-done | bytes 32800 | tf_op jit(solution)/shard_map/ppermute | solution.py:19
  109.2 3.4 %collective-permute-done.11 = f32[64,18,1]{0,2,1:T(1,128)S(1)} collective-permute-done((f32[64,18,1]{0,2,1:T(1,128)S(1)}, f32[64,18,1]{0,2,1:T(1,128)S(1)}, u32[]{:S(2)}, u32[]{:S(2)}) %collective-permute-start.11) | collective-permute-done | bytes 4640 | tf_op jit(solution)/shard_map/ppermute | solution.py:19
  114.5 2.8 %collective-permute-start.12 = (f32[64,1,128]{2,1,0:T(1,128)S(1)}, f32[64,1,128]{2,1,0:T(1,128)S(1)}, u32[]{:S(2)}, u32[]{:S(2)}) collective-permute-start(f32[64,1,128]{2,1,0:T(1,128)S(1)} %get-tuple-element.53), channel_id=1, source_target_pairs={{0,4},{4,8},{8,12},{12,16},{16,20},{20,24},{24,28},{1,5},{5,9},{9,... | collective-permute-start | bytes 98312 | tf_op jit(solution)/shard_map/ppermute | solution.py:17
  118.9 4.2 %collective-permute-done.13 = f32[64,1,128]{2,1,0:T(1,128)S(1)} collective-permute-done((f32[64,1,128]{2,1,0:T(1,128)S(1)}, f32[64,1,128]{2,1,0:T(1,128)S(1)}, u32[]{:S(2)}, u32[]{:S(2)}) %collective-permute-start.13) | collective-permute-done | bytes 32800 | tf_op jit(solution)/shard_map/ppermute | solution.py:19
  125.7 2.9 %collective-permute-start.14 = (f32[64,18,1]{0,2,1:T(1,128)S(1)}, f32[64,18,1]{0,2,1:T(1,128)S(1)}, u32[]{:S(2)}, u32[]{:S(2)}) collective-permute-start(f32[64,18,1]{0,2,1:T(1,128)S(1)} %copy.29), channel_id=1, source_target_pairs={{0,1},{1,2},{2,3},{4,5},{5,6},{6,7},{8,9},{9,10},{10,11},{12,13},{... | collective-permute-start | bytes 13832 | tf_op jit(solution)/shard_map/ppermute | solution.py:17
  137.3 8.0 %psum.90 = f32[64]{0:T(128)S(1)} all-reduce(f32[64]{0:T(128)S(1)} %get-tuple-element.10), channel_id=1, replica_groups=mesh['rows'=8,'cols'=4] {'cols'}, use_global_device_ids=true, to_apply=%region_10.0 | all-reduce | flops 64 | bytes 512 | tf_op jit(solution)/shard_map/psum | solution.py:49
  145.3 18.0 %psum.91 = f32[64]{0:T(128)S(1)} all-reduce(f32[64]{0:T(128)S(1)} %psum.90), channel_id=1, replica_groups=mesh['rows'=8,'cols'=4] {'rows'}, use_global_device_ids=true, to_apply=%region_11.0 | all-reduce | flops 64 | bytes 512 | tf_op jit(solution)/shard_map/psum | solution.py:50
  164.3 5.6 %psum.92 = f32[64]{0:T(128)S(1)} all-reduce(f32[64]{0:T(128)S(1)} %multiply_reduce_fusion.1), channel_id=1, replica_groups=mesh['rows'=8,'cols'=4] {'cols'}, use_global_device_ids=true, to_apply=%region_13.0 | all-reduce | flops 64 | bytes 512 | tf_op jit(solution)/shard_map/psum | solution.py:49
  170.0 18.2 %psum.93 = f32[64]{0:T(128)S(1)} all-reduce(f32[64]{0:T(128)S(1)} %psum.92), channel_id=1, replica_groups=mesh['rows'=8,'cols'=4] {'rows'}, use_global_device_ids=true, to_apply=%region_14.0 | all-reduce | flops 64 | bytes 512 | tf_op jit(solution)/shard_map/psum | solution.py:50
  188.5 2.9 %collective-permute-start.16 = (f32[64,1,128]{2,1,0:T(1,128)S(1)}, f32[64,1,128]{2,1,0:T(1,128)S(1)}, u32[]{:S(2)}, u32[]{:S(2)}) collective-permute-start(f32[64,1,128]{2,1,0:T(1,128)S(1)} %get-tuple-element.51), channel_id=1, source_target_pairs={{0,4},{4,8},{8,12},{12,16},{16,20},{20,24},{24,28},{1,5},{5,9},{9,... | collective-permute-start | bytes 98312 | tf_op jit(solution)/shard_map/ppermute | solution.py:17
  192.9 4.2 %collective-permute-done.17 = f32[64,1,128]{2,1,0:T(1,128)S(1)} collective-permute-done((f32[64,1,128]{2,1,0:T(1,128)S(1)}, f32[64,1,128]{2,1,0:T(1,128)S(1)}, u32[]{:S(2)}, u32[]{:S(2)}) %collective-permute-start.17) | collective-permute-done | bytes 32800 | tf_op jit(solution)/shard_map/ppermute | solution.py:19
  203.0 3.4 %collective-permute-done.19 = f32[64,18,1]{0,2,1:T(1,128)S(1)} collective-permute-done((f32[64,18,1]{0,2,1:T(1,128)S(1)}, f32[64,18,1]{0,2,1:T(1,128)S(1)}, u32[]{:S(2)}, u32[]{:S(2)}) %collective-permute-start.19) | collective-permute-done | bytes 4640 | tf_op jit(solution)/shard_map/ppermute | solution.py:19
  210.2 2.8 %collective-permute-start.20 = (f32[64,1,128]{2,1,0:T(1,128)S(1)}, f32[64,1,128]{2,1,0:T(1,128)S(1)}, u32[]{:S(2)}, u32[]{:S(2)}) collective-permute-start(f32[64,1,128]{2,1,0:T(1,128)S(1)} %get-tuple-element.49), channel_id=1, source_target_pairs={{0,4},{4,8},{8,12},{12,16},{16,20},{20,24},{24,28},{1,5},{5,9},{9,... | collective-permute-start | bytes 98312 | tf_op jit(solution)/shard_map/ppermute | solution.py:17
  214.6 4.2 %collective-permute-done.21 = f32[64,1,128]{2,1,0:T(1,128)S(1)} collective-permute-done((f32[64,1,128]{2,1,0:T(1,128)S(1)}, f32[64,1,128]{2,1,0:T(1,128)S(1)}, u32[]{:S(2)}, u32[]{:S(2)}) %collective-permute-start.21) | collective-permute-done | bytes 32800 | tf_op jit(solution)/shard_map/ppermute | solution.py:19
  221.5 2.9 %collective-permute-start.22 = (f32[64,18,1]{0,2,1:T(1,128)S(1)}, f32[64,18,1]{0,2,1:T(1,128)S(1)}, u32[]{:S(2)}, u32[]{:S(2)}) collective-permute-start(f32[64,18,1]{0,2,1:T(1,128)S(1)} %copy.37), channel_id=1, source_target_pairs={{0,1},{1,2},{2,3},{4,5},{5,6},{6,7},{8,9},{9,10},{10,11},{12,13},{... | collective-permute-start | bytes 13832 | tf_op jit(solution)/shard_map/ppermute | solution.py:17
  226.3 2.4 collective-permute-done.23
  233.1 8.1 %psum.94 = f32[64]{0:T(128)S(1)} all-reduce(f32[64]{0:T(128)S(1)} %fusion.10), channel_id=1, replica_groups=mesh['rows'=8,'cols'=4] {'cols'}, use_global_device_ids=true, to_apply=%region_16.0 | all-reduce | flops 64 | bytes 512 | tf_op jit(solution)/shard_map/psum | solution.py:49
  241.1 18.0 %psum.95 = f32[64]{0:T(128)S(1)} all-reduce(f32[64]{0:T(128)S(1)} %psum.94), channel_id=1, replica_groups=mesh['rows'=8,'cols'=4] {'rows'}, use_global_device_ids=true, to_apply=%region_17.0 | all-reduce | flops 64 | bytes 512 | tf_op jit(solution)/shard_map/psum | solution.py:50
  259.5 3.0 %collective-permute-start.24 = (f32[65,1,128]{2,1,0:T(1,128)S(1)}, f32[65,1,128]{2,1,0:T(1,128)S(1)}, u32[]{:S(2)}, u32[]{:S(2)}) collective-permute-start(f32[65,1,128]{2,1,0:T(1,128)S(1)} %get-tuple-element.47), channel_id=1, source_target_pairs={{0,4},{4,8},{8,12},{12,16},{16,20},{20,24},{24,28},{1,5},{5,9},{9,... | collective-permute-start | bytes 99848 | tf_op jit(solution)/shard_map/ppermute | solution.py:17
  264.1 4.2 %collective-permute-done.25 = f32[65,1,128]{2,1,0:T(1,128)S(1)} collective-permute-done((f32[65,1,128]{2,1,0:T(1,128)S(1)}, f32[65,1,128]{2,1,0:T(1,128)S(1)}, u32[]{:S(2)}, u32[]{:S(2)}) %collective-permute-start.25) | collective-permute-done | bytes 33312 | tf_op jit(solution)/shard_map/ppermute | solution.py:19
  272.3 3.2 %collective-permute-done.27 = f32[65,18,1]{0,2,1:T(1,128)S(1)} collective-permute-done((f32[65,18,1]{0,2,1:T(1,128)S(1)}, f32[65,18,1]{0,2,1:T(1,128)S(1)}, u32[]{:S(2)}, u32[]{:S(2)}) %collective-permute-start.27) | collective-permute-done | bytes 4712 | tf_op jit(solution)/shard_map/ppermute | solution.py:19
  (120 shorter events, 72.1 us)
Async XLA Ops:
  1.7 6.5 %collective-permute-start = (f32[64,1,128]{2,1,0:T(1,128)S(1)}, f32[64,1,128]{2,1,0:T(1,128)S(1)}, u32[]{:S(2)}, u32[]{:S(2)}) collective-permute-start(f32[64,1,128]{2,1,0:T(1,128)S(1)} %get-tuple-element.59), channel_id=1, source_target_pairs={{0,4},{4,8},{8,12},{12,16},{16,20},{20,24},{24,28},{1,5},{5,9},{9,... | collective-permute-start | bytes 98312 | tf_op jit(solution)/shard_map/ppermute | solution.py:17
  6.6 5.8 %collective-permute-start.1 = (f32[64,1,128]{2,1,0:T(1,128)S(1)}, f32[64,1,128]{2,1,0:T(1,128)S(1)}, u32[]{:S(2)}, u32[]{:S(2)}) collective-permute-start(f32[64,1,128]{2,1,0:T(1,128)S(1)} %get-tuple-element.60), channel_id=1, source_target_pairs={{4,0},{8,4},{12,8},{16,12},{20,16},{24,20},{28,24},{5,1},{9,5},{13... | collective-permute-start | bytes 98312 | tf_op jit(solution)/shard_map/ppermute | solution.py:19
  13.8 4.9 %copy-start.4 = (f32[16,128]{1,0:T(8,128)S(1)}, f32[16,128]{1,0:T(8,128)}, u32[]{:S(2)}) copy-start(f32[16,128]{1,0:T(8,128)} %param.6) | copy-start | bytes 24580
  13.8 6.4 %copy-start = (f32[64,16,128]{2,1,0:T(8,128)S(1)}, f32[64,16,128]{2,1,0:T(8,128)}, u32[]{:S(2)}) copy-start(f32[64,16,128]{2,1,0:T(8,128)} %param.4) | copy-start | bytes 1572868
  14.4 5.5 %collective-permute-start.3 = (f32[64,18,1]{0,2,1:T(1,128)S(1)}, f32[64,18,1]{0,2,1:T(1,128)S(1)}, u32[]{:S(2)}, u32[]{:S(2)}) collective-permute-start(f32[64,18,1]{0,2,1:T(1,128)S(1)} %copy.19), channel_id=1, source_target_pairs={{1,0},{2,1},{3,2},{5,4},{6,5},{7,6},{9,8},{10,9},{11,10},{13,12},{... | collective-permute-start | bytes 13832 | tf_op jit(solution)/shard_map/ppermute | solution.py:19
  15.7 3.9 %collective-permute-start.2 = (f32[64,18,1]{0,2,1:T(1,128)S(1)}, f32[64,18,1]{0,2,1:T(1,128)S(1)}, u32[]{:S(2)}, u32[]{:S(2)}) collective-permute-start(f32[64,18,1]{0,2,1:T(1,128)S(1)} %copy.17), channel_id=1, source_target_pairs={{0,1},{1,2},{2,3},{4,5},{5,6},{6,7},{8,9},{9,10},{10,11},{12,13},{... | collective-permute-start | bytes 13832 | tf_op jit(solution)/shard_map/ppermute | solution.py:17
  22.6 6.0 %collective-permute-start.4 = (f32[64,1,128]{2,1,0:T(1,128)S(1)}, f32[64,1,128]{2,1,0:T(1,128)S(1)}, u32[]{:S(2)}, u32[]{:S(2)}) collective-permute-start(f32[64,1,128]{2,1,0:T(1,128)S(1)} %get-tuple-element.57), channel_id=1, source_target_pairs={{0,4},{4,8},{8,12},{12,16},{16,20},{20,24},{24,28},{1,5},{5,9},{9,... | collective-permute-start | bytes 98312 | tf_op jit(solution)/shard_map/ppermute | solution.py:17
  27.0 6.0 %collective-permute-start.5 = (f32[64,1,128]{2,1,0:T(1,128)S(1)}, f32[64,1,128]{2,1,0:T(1,128)S(1)}, u32[]{:S(2)}, u32[]{:S(2)}) collective-permute-start(f32[64,1,128]{2,1,0:T(1,128)S(1)} %get-tuple-element.58), channel_id=1, source_target_pairs={{4,0},{8,4},{12,8},{16,12},{20,16},{24,20},{28,24},{5,1},{9,5},{13... | collective-permute-start | bytes 98312 | tf_op jit(solution)/shard_map/ppermute | solution.py:19
  33.6 3.4 %collective-permute-start.6 = (f32[64,18,1]{0,2,1:T(1,128)S(1)}, f32[64,18,1]{0,2,1:T(1,128)S(1)}, u32[]{:S(2)}, u32[]{:S(2)}) collective-permute-start(f32[64,18,1]{0,2,1:T(1,128)S(1)} %copy.21), channel_id=1, source_target_pairs={{0,1},{1,2},{2,3},{4,5},{5,6},{6,7},{8,9},{9,10},{10,11},{12,13},{... | collective-permute-start | bytes 13832 | tf_op jit(solution)/shard_map/ppermute | solution.py:17
  35.8 5.8 %collective-permute-start.7 = (f32[64,18,1]{0,2,1:T(1,128)S(1)}, f32[64,18,1]{0,2,1:T(1,128)S(1)}, u32[]{:S(2)}, u32[]{:S(2)}) collective-permute-start(f32[64,18,1]{0,2,1:T(1,128)S(1)} %copy.23), channel_id=1, source_target_pairs={{1,0},{2,1},{3,2},{5,4},{6,5},{7,6},{9,8},{10,9},{11,10},{13,12},{... | collective-permute-start | bytes 13832 | tf_op jit(solution)/shard_map/ppermute | solution.py:19
  95.9 5.2 %collective-permute-start.8 = (f32[64,1,128]{2,1,0:T(1,128)S(1)}, f32[64,1,128]{2,1,0:T(1,128)S(1)}, u32[]{:S(2)}, u32[]{:S(2)}) collective-permute-start(f32[64,1,128]{2,1,0:T(1,128)S(1)} %get-tuple-element.55), channel_id=1, source_target_pairs={{0,4},{4,8},{8,12},{12,16},{16,20},{20,24},{24,28},{1,5},{5,9},{9,... | collective-permute-start | bytes 98312 | tf_op jit(solution)/shard_map/ppermute | solution.py:17
  99.5 5.8 %collective-permute-start.9 = (f32[64,1,128]{2,1,0:T(1,128)S(1)}, f32[64,1,128]{2,1,0:T(1,128)S(1)}, u32[]{:S(2)}, u32[]{:S(2)}) collective-permute-start(f32[64,1,128]{2,1,0:T(1,128)S(1)} %get-tuple-element.56), channel_id=1, source_target_pairs={{4,0},{8,4},{12,8},{16,12},{20,16},{24,20},{28,24},{5,1},{9,5},{13... | collective-permute-start | bytes 98312 | tf_op jit(solution)/shard_map/ppermute | solution.py:19
  106.0 2.8 %collective-permute-start.10 = (f32[64,18,1]{0,2,1:T(1,128)S(1)}, f32[64,18,1]{0,2,1:T(1,128)S(1)}, u32[]{:S(2)}, u32[]{:S(2)}) collective-permute-start(f32[64,18,1]{0,2,1:T(1,128)S(1)} %copy.25), channel_id=1, source_target_pairs={{0,1},{1,2},{2,3},{4,5},{5,6},{6,7},{8,9},{9,10},{10,11},{12,13},{... | collective-permute-start | bytes 13832 | tf_op jit(solution)/shard_map/ppermute | solution.py:17
  107.5 5.0 %collective-permute-start.11 = (f32[64,18,1]{0,2,1:T(1,128)S(1)}, f32[64,18,1]{0,2,1:T(1,128)S(1)}, u32[]{:S(2)}, u32[]{:S(2)}) collective-permute-start(f32[64,18,1]{0,2,1:T(1,128)S(1)} %copy.27), channel_id=1, source_target_pairs={{1,0},{2,1},{3,2},{5,4},{6,5},{7,6},{9,8},{10,9},{11,10},{13,12},{... | collective-permute-start | bytes 13832 | tf_op jit(solution)/shard_map/ppermute | solution.py:19
  114.5 4.4 %collective-permute-start.12 = (f32[64,1,128]{2,1,0:T(1,128)S(1)}, f32[64,1,128]{2,1,0:T(1,128)S(1)}, u32[]{:S(2)}, u32[]{:S(2)}) collective-permute-start(f32[64,1,128]{2,1,0:T(1,128)S(1)} %get-tuple-element.53), channel_id=1, source_target_pairs={{0,4},{4,8},{8,12},{12,16},{16,20},{20,24},{24,28},{1,5},{5,9},{9,... | collective-permute-start | bytes 98312 | tf_op jit(solution)/shard_map/ppermute | solution.py:17
  117.3 5.8 %collective-permute-start.13 = (f32[64,1,128]{2,1,0:T(1,128)S(1)}, f32[64,1,128]{2,1,0:T(1,128)S(1)}, u32[]{:S(2)}, u32[]{:S(2)}) collective-permute-start(f32[64,1,128]{2,1,0:T(1,128)S(1)} %get-tuple-element.54), channel_id=1, source_target_pairs={{4,0},{8,4},{12,8},{16,12},{20,16},{24,20},{28,24},{5,1},{9,5},{13... | collective-permute-start | bytes 98312 | tf_op jit(solution)/shard_map/ppermute | solution.py:19
  125.7 4.6 %collective-permute-start.14 = (f32[64,18,1]{0,2,1:T(1,128)S(1)}, f32[64,18,1]{0,2,1:T(1,128)S(1)}, u32[]{:S(2)}, u32[]{:S(2)}) collective-permute-start(f32[64,18,1]{0,2,1:T(1,128)S(1)} %copy.29), channel_id=1, source_target_pairs={{0,1},{1,2},{2,3},{4,5},{5,6},{6,7},{8,9},{9,10},{10,11},{12,13},{... | collective-permute-start | bytes 13832 | tf_op jit(solution)/shard_map/ppermute | solution.py:17
  128.9 4.0 %collective-permute-start.15 = (f32[64,18,1]{0,2,1:T(1,128)S(1)}, f32[64,18,1]{0,2,1:T(1,128)S(1)}, u32[]{:S(2)}, u32[]{:S(2)}) collective-permute-start(f32[64,18,1]{0,2,1:T(1,128)S(1)} %copy.31), channel_id=1, source_target_pairs={{1,0},{2,1},{3,2},{5,4},{6,5},{7,6},{9,8},{10,9},{11,10},{13,12},{... | collective-permute-start | bytes 13832 | tf_op jit(solution)/shard_map/ppermute | solution.py:19
  188.5 4.4 %collective-permute-start.16 = (f32[64,1,128]{2,1,0:T(1,128)S(1)}, f32[64,1,128]{2,1,0:T(1,128)S(1)}, u32[]{:S(2)}, u32[]{:S(2)}) collective-permute-start(f32[64,1,128]{2,1,0:T(1,128)S(1)} %get-tuple-element.51), channel_id=1, source_target_pairs={{0,4},{4,8},{8,12},{12,16},{16,20},{20,24},{24,28},{1,5},{5,9},{9,... | collective-permute-start | bytes 98312 | tf_op jit(solution)/shard_map/ppermute | solution.py:17
  191.3 5.8 %collective-permute-start.17 = (f32[64,1,128]{2,1,0:T(1,128)S(1)}, f32[64,1,128]{2,1,0:T(1,128)S(1)}, u32[]{:S(2)}, u32[]{:S(2)}) collective-permute-start(f32[64,1,128]{2,1,0:T(1,128)S(1)} %get-tuple-element.52), channel_id=1, source_target_pairs={{4,0},{8,4},{12,8},{16,12},{20,16},{24,20},{28,24},{5,1},{9,5},{13... | collective-permute-start | bytes 98312 | tf_op jit(solution)/shard_map/ppermute | solution.py:19
  199.8 2.8 %collective-permute-start.18 = (f32[64,18,1]{0,2,1:T(1,128)S(1)}, f32[64,18,1]{0,2,1:T(1,128)S(1)}, u32[]{:S(2)}, u32[]{:S(2)}) collective-permute-start(f32[64,18,1]{0,2,1:T(1,128)S(1)} %copy.33), channel_id=1, source_target_pairs={{0,1},{1,2},{2,3},{4,5},{5,6},{6,7},{8,9},{9,10},{10,11},{12,13},{... | collective-permute-start | bytes 13832 | tf_op jit(solution)/shard_map/ppermute | solution.py:17
  201.3 5.0 %collective-permute-start.19 = (f32[64,18,1]{0,2,1:T(1,128)S(1)}, f32[64,18,1]{0,2,1:T(1,128)S(1)}, u32[]{:S(2)}, u32[]{:S(2)}) collective-permute-start(f32[64,18,1]{0,2,1:T(1,128)S(1)} %copy.35), channel_id=1, source_target_pairs={{1,0},{2,1},{3,2},{5,4},{6,5},{7,6},{9,8},{10,9},{11,10},{13,12},{... | collective-permute-start | bytes 13832 | tf_op jit(solution)/shard_map/ppermute | solution.py:19
  210.2 4.4 %collective-permute-start.20 = (f32[64,1,128]{2,1,0:T(1,128)S(1)}, f32[64,1,128]{2,1,0:T(1,128)S(1)}, u32[]{:S(2)}, u32[]{:S(2)}) collective-permute-start(f32[64,1,128]{2,1,0:T(1,128)S(1)} %get-tuple-element.49), channel_id=1, source_target_pairs={{0,4},{4,8},{8,12},{12,16},{16,20},{20,24},{24,28},{1,5},{5,9},{9,... | collective-permute-start | bytes 98312 | tf_op jit(solution)/shard_map/ppermute | solution.py:17
  213.1 5.8 %collective-permute-start.21 = (f32[64,1,128]{2,1,0:T(1,128)S(1)}, f32[64,1,128]{2,1,0:T(1,128)S(1)}, u32[]{:S(2)}, u32[]{:S(2)}) collective-permute-start(f32[64,1,128]{2,1,0:T(1,128)S(1)} %get-tuple-element.50), channel_id=1, source_target_pairs={{4,0},{8,4},{12,8},{16,12},{20,16},{24,20},{28,24},{5,1},{9,5},{13... | collective-permute-start | bytes 98312 | tf_op jit(solution)/shard_map/ppermute | solution.py:19
  221.5 4.4 %collective-permute-start.22 = (f32[64,18,1]{0,2,1:T(1,128)S(1)}, f32[64,18,1]{0,2,1:T(1,128)S(1)}, u32[]{:S(2)}, u32[]{:S(2)}) collective-permute-start(f32[64,18,1]{0,2,1:T(1,128)S(1)} %copy.37), channel_id=1, source_target_pairs={{0,1},{1,2},{2,3},{4,5},{5,6},{6,7},{8,9},{9,10},{10,11},{12,13},{... | collective-permute-start | bytes 13832 | tf_op jit(solution)/shard_map/ppermute | solution.py:17
  224.7 4.0 %collective-permute-start.23 = (f32[64,18,1]{0,2,1:T(1,128)S(1)}, f32[64,18,1]{0,2,1:T(1,128)S(1)}, u32[]{:S(2)}, u32[]{:S(2)}) collective-permute-start(f32[64,18,1]{0,2,1:T(1,128)S(1)} %copy.39), channel_id=1, source_target_pairs={{1,0},{2,1},{3,2},{5,4},{6,5},{7,6},{9,8},{10,9},{11,10},{13,12},{... | collective-permute-start | bytes 13832 | tf_op jit(solution)/shard_map/ppermute | solution.py:19
  233.1 26.4 %copy-start.2 = (f32[16,128]{1,0:T(8,128)S(1)}, f32[16,128]{1,0:T(8,128)}, u32[]{:S(2)}) copy-start(f32[16,128]{1,0:T(8,128)} %param.5) | copy-start | bytes 24580
  259.5 4.6 %collective-permute-start.24 = (f32[65,1,128]{2,1,0:T(1,128)S(1)}, f32[65,1,128]{2,1,0:T(1,128)S(1)}, u32[]{:S(2)}, u32[]{:S(2)}) collective-permute-start(f32[65,1,128]{2,1,0:T(1,128)S(1)} %get-tuple-element.47), channel_id=1, source_target_pairs={{0,4},{4,8},{8,12},{12,16},{16,20},{20,24},{24,28},{1,5},{5,9},{9,... | collective-permute-start | bytes 99848 | tf_op jit(solution)/shard_map/ppermute | solution.py:17
  262.5 5.8 %collective-permute-start.25 = (f32[65,1,128]{2,1,0:T(1,128)S(1)}, f32[65,1,128]{2,1,0:T(1,128)S(1)}, u32[]{:S(2)}, u32[]{:S(2)}) collective-permute-start(f32[65,1,128]{2,1,0:T(1,128)S(1)} %get-tuple-element.48), channel_id=1, source_target_pairs={{4,0},{8,4},{12,8},{16,12},{20,16},{24,20},{28,24},{5,1},{9,5},{13... | collective-permute-start | bytes 99848 | tf_op jit(solution)/shard_map/ppermute | solution.py:19
  269.0 2.9 %collective-permute-start.26 = (f32[65,18,1]{0,2,1:T(1,128)S(1)}, f32[65,18,1]{0,2,1:T(1,128)S(1)}, u32[]{:S(2)}, u32[]{:S(2)}) collective-permute-start(f32[65,18,1]{0,2,1:T(1,128)S(1)} %copy.41), channel_id=1, source_target_pairs={{0,1},{1,2},{2,3},{4,5},{5,6},{6,7},{8,9},{9,10},{10,11},{12,13},{... | collective-permute-start | bytes 14048 | tf_op jit(solution)/shard_map/ppermute | solution.py:17
  270.6 5.0 %collective-permute-start.27 = (f32[65,18,1]{0,2,1:T(1,128)S(1)}, f32[65,18,1]{0,2,1:T(1,128)S(1)}, u32[]{:S(2)}, u32[]{:S(2)}) collective-permute-start(f32[65,18,1]{0,2,1:T(1,128)S(1)} %copy.43), channel_id=1, source_target_pairs={{1,0},{2,1},{3,2},{5,4},{6,5},{7,6},{9,8},{10,9},{11,10},{13,12},{... | collective-permute-start | bytes 14048 | tf_op jit(solution)/shard_map/ppermute | solution.py:19
  276.9 1.0 copy-start.1
  (1 other events, 0.9 us)
where the time goes:
time: 282 us; the launch traced here: 279 us
  blocking collectives  126 us (45%)
  starting transfers between devices  57.2 us (20%)
  waiting for transfers between devices  51.2 us (18%)
  other arithmetic  22.3 us (8%)
  local copies, waits for them, and re-layouts  20.8 us (7%)
    psum x5, blocking collectives, sectioned_sum(): return lax.psum(col_total, 'rows')  90.5 us
    ppermute x14, waiting for transfers between devices, extended(): lax.ppermute(head, axis, [((i + 1) % count, i) for i in range(ends)])  48.4 us
    ppermute x14, starting transfers between devices, extended(): lax.ppermute(tail, axis, [(i, (i + 1) % count) for i in range(ends)])  38.9 us
    psum x5, blocking collectives, sectioned_sum(): col_total = lax.psum(local_terms, 'cols')  35.5 us
    ppermute x14, starting transfers between devices, extended(): lax.ppermute(head, axis, [((i + 1) % count, i) for i in range(ends)])  18.3 us
    concatenate x14, other arithmetic, extended(): jnp.concatenate([lax.ppermute(tail, axis, [(i, (i + 1) % count) for i in...  11.3 us
    slice x20, local copies, waits for them, and re-layouts, extended(): lax.slice_in_dim(cells, cells.shape[dim] - width, cells.shape[dim], axis=...  11 us
    reduce_sum x5, other arithmetic, inner_sum(): return jnp.sum(first_field * second_field, axis=(1, 2))  6.3 us
  transfers between devices with their start and end apart: 28, of which 21 were waited for; matrix products, arithmetic and copies ran while one was open for 1% of the time, Pallas kernels for 0%

commit v1 on v0

--- a/solution.py
+++ b/solution.py
@@ -4,6 +4,7 @@
 from jax.sharding import PartitionSpec as P
 
 ITERS = 3
+HALO = 2 * ITERS
 
 
 def extended(cells, sides, width):
@@ -37,43 +38,78 @@
     return (kappa_sq + 20.0 / 6.0) * centre - (4.0 * edge_sum + corners) / 6.0
 
 
-def with_rim(field):
-    return extended(field, (("rows", 1), ("cols", 2)), 1)
+def stiffen(field, kappa_sq):
+    pads = ((0, 0),) * (field.ndim - 2) + ((1, 1), (1, 1))
+    return stencil(jnp.pad(field, pads), kappa_sq)
 
 
-def inner_sum(first_field, second_field):
-    return jnp.sum(first_field * second_field, axis=(1, 2))
+def all_sum(terms):
+    for axis in ("cols", "rows"):
+        count = lax.axis_size(axis)
+        if count & (count - 1):
+            terms = lax.psum(terms, axis)
+            continue
+        hop = 1
+        while hop < count:
+            terms = terms + lax.ppermute(terms, axis, [(i, i ^ hop) for i in range(count)])
+            hop *= 2
+    return terms
 
 
-def sectioned_sum(local_terms):
-    col_total = lax.psum(local_terms, "cols")
-    return lax.psum(col_total, "rows")
+def inside_mask(rows, cols):
+    row_at = lax.axis_index("rows") * rows - HALO + lax.iota(jnp.int32, rows + 2 * HALO)
+    col_at = lax.axis_index("cols") * cols - HALO + lax.iota(jnp.int32, cols + 2 * HALO)
+    row_in = (row_at >= 0) & (row_at < rows * lax.axis_size("rows"))
+    col_in = (col_at >= 0) & (col_at < cols * lax.axis_size("cols"))
+    return (row_in[:, None] & col_in[None, :]).astype(jnp.float32)
 
 
 def on_device(probes, observed, kappa_sq, variance_weight):
-    residual = probes
-    solution = jnp.zeros_like(probes)
-    direction = probes
-    stiff_probe = None
-    norm_now = sectioned_sum(inner_sum(residual, residual))
+    probe_count, rows, cols = probes.shape
+    stacked = jnp.concatenate(
+        [probes, observed[None], kappa_sq[None], variance_weight[None]], axis=0
+    )
+    ext = extended(stacked, (("rows", 1), ("cols", 2)), HALO)
+    probe_ext = ext[:probe_count]
+    observed_ext = ext[probe_count]
+    kappa_ext = ext[probe_count + 1]
+    weight_ext = ext[probe_count + 2]
+    mask = inside_mask(rows, cols)
+
+    def inner(field):
+        return field[..., HALO : HALO + rows, HALO : HALO + cols]
+
+    def dot(first, second):
+        return jnp.sum(inner(first) * inner(second), axis=(-2, -1))
+
+    def apply_q(direction):
+        stiffness = stiffen(direction, kappa_ext)
+        applied = mask * stiffen(weight_ext * stiffness, kappa_ext)
+        return stiffness, applied
+
+    residual = probe_ext
+    direction = probe_ext
+    solution = None
+    stiff_probe, applied = apply_q(direction)
+    first = all_sum(jnp.stack([dot(residual, residual), dot(direction, applied)]))
+    norm_now = first[0]
+    curvature = first[1]
     for iteration in range(ITERS):
-        stiffness = stencil(with_rim(direction), kappa_sq)
-        applied = stencil(with_rim(variance_weight * stiffness), kappa_sq)
-        stiffness, applied = (stiffness, applied)
-        if iteration == 0:
-            stiff_probe = stiffness
-        step_len = norm_now / sectioned_sum(inner_sum(direction, applied))
-        solution = solution + step_len[:, None, None] * direction
-        residual = residual - step_len[:, None, None] * applied
+        if iteration > 0:
+            _, applied = apply_q(direction)
+            curvature = all_sum(dot(direction, applied))
+        step_len = (norm_now / curvature)[:, None, None]
+        solution = step_len * direction if solution is None else solution + step_len * direction
         if iteration + 1 < ITERS:
-            norm_next = sectioned_sum(inner_sum(residual, residual))
+            residual = residual - step_len * applied
+            norm_next = all_sum(dot(residual, residual))
             direction = residual + (norm_next / norm_now)[:, None, None] * direction
             norm_now = norm_next
-    stacked = jnp.concatenate([solution, observed[None]], axis=0)
-    stiff_all = stencil(with_rim(stacked), kappa_sq)
-    stiff_solution = stiff_all[:-1]
-    stiff_obs = stiff_all[-1]
-    probe_count = probes.shape[0]
+
+    stiff_solution = inner(stiffen(solution, kappa_ext))
+    stiff_obs = inner(stiffen(observed_ext, kappa_ext))
+    stiff_probe = inner(stiff_probe)
+    solution = inner(solution)
     weight_total = jnp.sum(stiff_solution * stiff_probe, axis=0)
     kappa_total = jnp.sum(solution * stiff_probe + stiff_solution * probes, axis=0)
     grad_weight = 0.5 * weight_total / probe_count - 0.5 * stiff_obs * stiff_obs

time: 282 us -> 174 us (0.62); the launches traced: 279 us -> 174 us
  blocking collectives: 126 us -> 0 us
  other arithmetic: 22.3 us -> 62.3 us
  local copies, waits for them, and re-layouts: 20.8 us -> 4.41 us
    psum x10 -> x0, blocking collectives: 126 us -> none  [the longest x5 90.5 us: sectioned_sum(): return lax.psum(col_total, 'rows')]
    ppermute x0 -> x25, starting transfers between devices: none -> 44.2 us  [all_sum(): lax.ppermute(terms, axis, [(i, i ^ hop) for i in range(count)])]
    ppermute x14 -> x2, waiting for transfers between devices: 48.4 us -> 4.58 us  [extended(): lax.ppermute(head, axis, [((i + 1) % count, i) for i in range(ends)])]
    ppermute x0 -> x25, waiting for transfers between devices: none -> 40 us  [all_sum(): lax.ppermute(terms, axis, [(i, i ^ hop) for i in range(count)])]
    ppermute x14 -> x2, starting transfers between devices: 38.9 us -> 8.54 us  [extended(): lax.ppermute(tail, axis, [(i, (i + 1) % count) for i in range(ends)])]
    mul x3 -> x5, other arithmetic: 2.59 us -> 20.6 us  [apply_q(): applied = mask * stiffen(weight_ext * stiffness, kappa_ext)]
    ppermute x14 -> x2, starting transfers between devices: 18.3 us -> 2.58 us  [extended(): lax.ppermute(head, axis, [((i + 1) % count, i) for i in range(ends)])]
    add x2 -> x25, other arithmetic: 0.28 us -> 13.7 us  [the longest x3 13 us: stencil(): padded[..., :-2, 1:-1] + padded[..., 2:, 1:-1] + padded[..., 1:-1, :-2]]
  transfers between devices with their start and end apart: 28 -> 29, of which waited for: 21 -> 27; matrix products, arithmetic and copies ran while one was open for 1% -> 1% of each run, Pallas kernels for 0% -> 0%
where the time goes in v1:
time: 174 us
  other arithmetic  62.3 us (36%)
  starting transfers between devices  55.4 us (32%)
  waiting for transfers between devices  50.6 us (29%)
  local copies, waits for them, and re-layouts  4.41 us (3%)
    ppermute x25, starting transfers between devices, all_sum(): lax.ppermute(terms, axis, [(i, i ^ hop) for i in range(count)])  44.2 us
    ppermute x25, waiting for transfers between devices, all_sum(): lax.ppermute(terms, axis, [(i, i ^ hop) for i in range(count)])  40 us
    mul x5, other arithmetic, apply_q(): applied = mask * stiffen(weight_ext * stiffness, kappa_ext)  20.6 us
    add x3, other arithmetic, stencil(): padded[..., :-2, 1:-1] + padded[..., 2:, 1:-1] + padded[..., 1:-1, :-2]  13 us
    reduce_sum x5, other arithmetic, dot(): return jnp.sum(inner(first) * inner(second), axis=(-2, -1))  10.1 us
    ppermute x2, starting transfers between devices, extended(): lax.ppermute(tail, axis, [(i, (i + 1) % count) for i in range(ends)])  8.54 us
    sub x2, other arithmetic, on_device(): residual = residual - step_len * applied  8.4 us
    ppermute x2, waiting for transfers between devices, extended(): lax.ppermute(tail, axis, [(i, (i + 1) % count) for i in range(ends)])  6.03 us
  transfers between devices with their start and end apart: 29, of which 27 were waited for; matrix products, arithmetic and copies ran while one was open for 1% of the time, Pallas kernels for 0%

profile of v1, /device:TPU:0, one launch (start us, length us, event | category | flops | bytes accessed | tf_op | source)
XLA Modules:
  0.0 173.7 jit_solution(8411867241380863355)
XLA Ops:
  3.2 5.5 %collective-permute-start = (f32[67,6,128]{2,1,0:T(8,128)S(1)}, f32[67,6,128]{2,1,0:T(8,128)S(1)}, u32[]{:S(2)}, u32[]{:S(2)}) collective-permute-start(f32[67,6,128]{2,1,0:T(8,128)S(1)} %get-tuple-element.33), channel_id=1, source_target_pairs={{0,4},{4,8},{8,12},{12,16},{16,20},{20,24},{24,28},{1,5},{5,9},{9,... | collective-permute-start | bytes 617480 | tf_op jit(solution)/shard_map/ppermute | solution.py:18
  8.8 4.6 %collective-permute-done.1 = f32[67,6,128]{2,1,0:T(8,128)S(1)} collective-permute-done((f32[67,6,128]{2,1,0:T(8,128)S(1)}, f32[67,6,128]{2,1,0:T(8,128)S(1)}, u32[]{:S(2)}, u32[]{:S(2)}) %collective-permute-start.1) | collective-permute-done | bytes 205856 | tf_op jit(solution)/shard_map/ppermute | solution.py:20
  13.3 6.0 %collective-permute-done = f32[67,6,128]{2,1,0:T(8,128)S(1)} collective-permute-done((f32[67,6,128]{2,1,0:T(8,128)S(1)}, f32[67,6,128]{2,1,0:T(8,128)S(1)}, u32[]{:S(2)}, u32[]{:S(2)}) %collective-permute-start) | collective-permute-done | bytes 205856 | tf_op jit(solution)/shard_map/ppermute | solution.py:18
  22.7 3.0 %collective-permute-start.2 = (f32[67,28,6]{0,1,2:T(8,128)S(1)}, f32[67,28,6]{0,1,2:T(8,128)S(1)}, u32[]{:S(2)}, u32[]{:S(2)}) collective-permute-start(f32[67,28,6]{0,1,2:T(8,128)S(1)} %copy.19), channel_id=1, source_target_pairs={{0,1},{1,2},{2,3},{4,5},{5,6},{6,7},{8,9},{9,10},{10,11},{12,13},{... | collective-permute-start | bytes 135080 | tf_op jit(solution)/shard_map/ppermute | solution.py:18
  29.5 4.2 %broadcast_multiply_fusion = (f32[64,28,140]{2,1,0:T(8,128)S(1)}, f32[64,28,140]{2,1,0:T(8,128)S(1)}) fusion(f32[28,140]{1,0:T(8,128)S(1)} %get-tuple-element.17, f32[64,28,140]{2,1,0:T(8,128)S(1)} %slice.362, f32[28,140]{1,0:T(8,128)S(1)} %get-tuple-element.18), kind=kLoop, calls=%fused_computation.24 | loop fusion | flops 3010560 | bytes 3041920 | tf_op jit(solution)/shard_map/mul | solution.py:87
  33.7 4.0 %subtract_multiply_fusion.3 = f32[64,28,140]{2,1,0:T(8,128)S(1)} fusion(f32[64,28,140]{2,1,0:T(8,128)S(1)} %get-tuple-element.14, f32[28,140]{1,0:T(8,128)S(1)} %get-tuple-element.18, f32[28,140]{1,0:T(8,128)S(1)} %and_convert_fusion), kind=kLoop, calls=%fused_computation.12 | loop fusion | flops 3010560 | bytes 2038400 | tf_op jit(solution)/shard_map/mul | solution.py:87
  42.1 2.7 %collective-permute-start.5 = (f32[2,64]{1,0:T(2,128)S(1)}, f32[2,64]{1,0:T(2,128)S(1)}, u32[]{:S(2)}, u32[]{:S(2)}) collective-permute-start(f32[2,64]{1,0:T(2,128)S(1)} %fusion.21), channel_id=1, source_target_pairs={{0,2},{1,3},{2,0},{3,1},{4,6},{5,7},{6,4},{7,5},{8,10},{9,11},{10,... | collective-permute-start | bytes 1544 | tf_op jit(solution)/shard_map/ppermute | solution.py:54
  46.4 2.6 %collective-permute-start.6 = (f32[2,64]{1,0:T(2,128)S(1)}, f32[2,64]{1,0:T(2,128)S(1)}, u32[]{:S(2)}, u32[]{:S(2)}) collective-permute-start(f32[2,64]{1,0:T(2,128)S(1)} %fusion.26), channel_id=1, source_target_pairs={{0,4},{4,0},{8,12},{12,8},{16,20},{20,16},{24,28},{28,24},{1,5},{5... | collective-permute-start | bytes 1544 | tf_op jit(solution)/shard_map/ppermute | solution.py:54
  52.1 2.0 %collective-permute-done.7 = f32[2,64]{1,0:T(2,128)S(1)} collective-permute-done((f32[2,64]{1,0:T(2,128)S(1)}, f32[2,64]{1,0:T(2,128)S(1)}, u32[]{:S(2)}, u32[]{:S(2)}) %collective-permute-start.7) | collective-permute-done | bytes 544 | tf_op jit(solution)/shard_map/ppermute | solution.py:54
  54.1 2.6 %collective-permute-start.8 = (f32[2,64]{1,0:T(2,128)S(1)}, f32[2,64]{1,0:T(2,128)S(1)}, u32[]{:S(2)}, u32[]{:S(2)}) collective-permute-start(f32[2,64]{1,0:T(2,128)S(1)} %add.330), channel_id=1, source_target_pairs={{0,16},{4,20},{8,24},{12,28},{16,0},{20,4},{24,8},{28,12},{1,17},{... | collective-permute-start | bytes 1544 | tf_op jit(solution)/shard_map/ppermute | solution.py:54
  58.6 4.2 %multiply_subtract_fusion.1 = f32[64,28,140]{2,1,0:T(8,128)S(1)} fusion(f32[64]{0:T(128)S(1)} %bitcast_divide_fusion, f32[67,28,140]{2,1,0:T(8,128)S(1)} %pad_maximum_fusion, f32[64,28,140]{2,1,0:T(8,128)S(1)} %get-tuple-element.14, f32[28,140]{1,0:T(8,128)S(1)} %get-tuple-element.18, f32[28,140]{1,0:T(8,128)S(1)} %and_convert_fusion), kind=kLoop, calls=%fused_computation.11 | loop fusion | flops 3512320 | bytes 3042176 | tf_op jit(solution)/shard_map/sub | solution.py:104
  65.0 2.0 %collective-permute-start.10 = (f32[64]{0:T(128)S(1)}, f32[64]{0:T(128)S(1)}, u32[]{:S(2)}, u32[]{:S(2)}) collective-permute-start(f32[64]{0:T(128)S(1)} %add.332), channel_id=1, source_target_pairs={{0,2},{1,3},{2,0},{3,1},{4,6},{5,7},{6,4},{7,5},{8,10},{9,11},{10,... | collective-permute-start | bytes 776 | tf_op jit(solution)/shard_map/ppermute | solution.py:54
  68.6 2.0 %collective-permute-start.11 = (f32[64]{0:T(128)S(1)}, f32[64]{0:T(128)S(1)}, u32[]{:S(2)}, u32[]{:S(2)}) collective-permute-start(f32[64]{0:T(128)S(1)} %add.333), channel_id=1, source_target_pairs={{0,4},{4,0},{8,12},{12,8},{16,20},{20,16},{24,28},{28,24},{1,5},{5... | collective-permute-start | bytes 776 | tf_op jit(solution)/shard_map/ppermute | solution.py:54
  73.7 2.0 %collective-permute-done.12 = f32[64]{0:T(128)S(1)} collective-permute-done((f32[64]{0:T(128)S(1)}, f32[64]{0:T(128)S(1)}, u32[]{:S(2)}, u32[]{:S(2)}) %collective-permute-start.12) | collective-permute-done | bytes 288 | tf_op jit(solution)/shard_map/ppermute | solution.py:54
  75.7 2.6 %collective-permute-start.13 = (f32[64]{0:T(128)S(1)}, f32[64]{0:T(128)S(1)}, u32[]{:S(2)}, u32[]{:S(2)}) collective-permute-start(f32[64]{0:T(128)S(1)} %add.335), channel_id=1, source_target_pairs={{0,16},{4,20},{8,24},{12,28},{16,0},{20,4},{24,8},{28,12},{1,17},{... | collective-permute-start | bytes 776 | tf_op jit(solution)/shard_map/ppermute | solution.py:54
  80.5 4.0 %subtract_multiply_fusion.2 = f32[64,28,140]{2,1,0:T(8,128)S(1)} fusion(f32[64,28,140]{2,1,0:T(8,128)S(1)} %multiply_add_fusion.2, f32[28,140]{1,0:T(8,128)S(1)} %get-tuple-element.17, f32[28,140]{1,0:T(8,128)S(1)} %get-tuple-element.18), kind=kLoop, calls=%fused_computation.9 | loop fusion | flops 3010560 | bytes 2038400 | tf_op jit(solution)/shard_map/mul | solution.py:87
  84.5 4.3 %subtract_multiply_fusion.1 = f32[64,28,140]{2,1,0:T(8,128)S(1)} fusion(f32[64,28,140]{2,1,0:T(8,128)S(1)} %subtract_multiply_fusion.2, f32[28,140]{1,0:T(8,128)S(1)} %get-tuple-element.18, f32[28,140]{1,0:T(8,128)S(1)} %and_convert_fusion), kind=kLoop, calls=%fused_computation.8 | loop fusion | flops 3010560 | bytes 2038400 | tf_op jit(solution)/shard_map/mul | solution.py:87
  91.1 2.0 %collective-permute-start.15 = (f32[64]{0:T(128)S(1)}, f32[64]{0:T(128)S(1)}, u32[]{:S(2)}, u32[]{:S(2)}) collective-permute-start(f32[64]{0:T(128)S(1)} %add.352), channel_id=1, source_target_pairs={{0,2},{1,3},{2,0},{3,1},{4,6},{5,7},{6,4},{7,5},{8,10},{9,11},{10,... | collective-permute-start | bytes 776 | tf_op jit(solution)/shard_map/ppermute | solution.py:54
  94.7 2.0 %collective-permute-start.16 = (f32[64]{0:T(128)S(1)}, f32[64]{0:T(128)S(1)}, u32[]{:S(2)}, u32[]{:S(2)}) collective-permute-start(f32[64]{0:T(128)S(1)} %add.353), channel_id=1, source_target_pairs={{0,4},{4,0},{8,12},{12,8},{16,20},{20,16},{24,28},{28,24},{1,5},{5... | collective-permute-start | bytes 776 | tf_op jit(solution)/shard_map/ppermute | solution.py:54
  101.8 2.6 %collective-permute-start.18 = (f32[64]{0:T(128)S(1)}, f32[64]{0:T(128)S(1)}, u32[]{:S(2)}, u32[]{:S(2)}) collective-permute-start(f32[64]{0:T(128)S(1)} %add.355), channel_id=1, source_target_pairs={{0,16},{4,20},{8,24},{12,28},{16,0},{20,4},{24,8},{28,12},{1,17},{... | collective-permute-start | bytes 776 | tf_op jit(solution)/shard_map/ppermute | solution.py:54
  106.3 4.2 %multiply_subtract_fusion = f32[64,28,140]{2,1,0:T(8,128)S(1)} fusion(f32[64,28,140]{2,1,0:T(8,128)S(1)} %multiply_subtract_fusion.1, f32[64]{0:T(128)S(1)} %add_divide_fusion.1, f32[64,28,140]{2,1,0:T(8,128)S(1)} %subtract_multiply_fusion.2, f32[28,140]{1,0:T(8,128)S(1)} %get-tuple-element.18, f32[28,140]{1,0:T(8,128)S(1)} %and_convert_fusion), kind=kLoop, calls=%fused_computation.7 | loop fusion | flops 3512320 | bytes 3042176 | tf_op jit(solution)/shard_map/sub | solution.py:104
  112.8 2.0 %collective-permute-start.20 = (f32[64]{0:T(128)S(1)}, f32[64]{0:T(128)S(1)}, u32[]{:S(2)}, u32[]{:S(2)}) collective-permute-start(f32[64]{0:T(128)S(1)} %add.358), channel_id=1, source_target_pairs={{0,2},{1,3},{2,0},{3,1},{4,6},{5,7},{6,4},{7,5},{8,10},{9,11},{10,... | collective-permute-start | bytes 776 | tf_op jit(solution)/shard_map/ppermute | solution.py:54
  116.3 2.0 %collective-permute-start.21 = (f32[64]{0:T(128)S(1)}, f32[64]{0:T(128)S(1)}, u32[]{:S(2)}, u32[]{:S(2)}) collective-permute-start(f32[64]{0:T(128)S(1)} %add.359), channel_id=1, source_target_pairs={{0,4},{4,0},{8,12},{12,8},{16,20},{20,16},{24,28},{28,24},{1,5},{5... | collective-permute-start | bytes 776 | tf_op jit(solution)/shard_map/ppermute | solution.py:54
  123.5 2.6 %collective-permute-start.23 = (f32[64]{0:T(128)S(1)}, f32[64]{0:T(128)S(1)}, u32[]{:S(2)}, u32[]{:S(2)}) collective-permute-start(f32[64]{0:T(128)S(1)} %add.361), channel_id=1, source_target_pairs={{0,16},{4,20},{8,24},{12,28},{16,0},{20,4},{24,8},{28,12},{1,17},{... | collective-permute-start | bytes 776 | tf_op jit(solution)/shard_map/ppermute | solution.py:54
  128.3 4.0 %subtract_multiply_fusion = f32[64,28,140]{2,1,0:T(8,128)S(1)} fusion(f32[64,28,140]{2,1,0:T(8,128)S(1)} %multiply_add_fusion.1, f32[28,140]{1,0:T(8,128)S(1)} %get-tuple-element.17, f32[28,140]{1,0:T(8,128)S(1)} %get-tuple-element.18), kind=kLoop, calls=%fused_computation.5 | loop fusion | flops 3010560 | bytes 2038400 | tf_op jit(solution)/shard_map/mul | solution.py:87
  132.4 6.2 %slice_add_fusion.2 = (f32[64,28,140]{2,1,0:T(8,128)}, f32[64,28,140]{2,1,0:T(8,128)}, f32[64,28,140]{2,1,0:T(8,128)}, f32[64,28,140]{2,1,0:T(8,128)}, f32[64,28,140]{2,1,0:T(8,128)}) fusion(f32[64,28,140]{2,1,0:T(8,128)S(1)} %subtract_multiply_fusion), kind=kLoop, calls=%fused_computation.4 | loop fusion | flops 752640 | bytes 6021120 | tf_op jit(solution)/shard_map/add | solution.py:30
  138.6 5.2 %fusion.7 = f32[64]{0:T(128)S(1)} fusion(f32[64,28,140]{2,1,0:T(8,128)S(1)} %subtract_multiply_fusion, f32[64,28,140]{2,1,0:T(8,128)} %get-tuple-element.29, f32[64,28,140]{2,1,0:T(8,128)} %get-tuple-element.27, f32[64,28,140]{2,1,0:T(8,128)} %get-tuple-element.30, f32[64,28,140]{2,1,0:T(8,128)} %get-tuple-element.28, f32[64,28,140]{2,1,0:T(8,128)} %get-tuple-element.26, ...), kind=kLoop, calls=%fused_computation.39 | loop fusion | flops 1441728 | bytes 3686656 | tf_op jit(solution)/shard_map/reduce_sum | solution.py:83
  145.0 2.0 %collective-permute-start.25 = (f32[64]{0:T(128)S(1)}, f32[64]{0:T(128)S(1)}, u32[]{:S(2)}, u32[]{:S(2)}) collective-permute-start(f32[64]{0:T(128)S(1)} %add.378), channel_id=1, source_target_pairs={{0,2},{1,3},{2,0},{3,1},{4,6},{5,7},{6,4},{7,5},{8,10},{9,11},{10,... | collective-permute-start | bytes 776 | tf_op jit(solution)/shard_map/ppermute | solution.py:54
  148.6 2.0 %collective-permute-start.26 = (f32[64]{0:T(128)S(1)}, f32[64]{0:T(128)S(1)}, u32[]{:S(2)}, u32[]{:S(2)}) collective-permute-start(f32[64]{0:T(128)S(1)} %add.379), channel_id=1, source_target_pairs={{0,4},{4,0},{8,12},{12,8},{16,20},{20,16},{24,28},{28,24},{1,5},{5... | collective-permute-start | bytes 776 | tf_op jit(solution)/shard_map/ppermute | solution.py:54
  155.8 2.6 %collective-permute-start.28 = (f32[64]{0:T(128)S(1)}, f32[64]{0:T(128)S(1)}, u32[]{:S(2)}, u32[]{:S(2)}) collective-permute-start(f32[64]{0:T(128)S(1)} %add.381), channel_id=1, source_target_pairs={{0,16},{4,20},{8,24},{12,28},{16,0},{20,4},{24,8},{28,12},{1,17},{... | collective-permute-start | bytes 776 | tf_op jit(solution)/shard_map/ppermute | solution.py:54
  160.9 6.6 %slice_add_fusion = (f32[64,28,140]{2,1,0:T(8,128)S(1)}, f32[64,28,140]{2,1,0:T(8,128)S(1)}, f32[64,28,140]{2,1,0:T(8,128)}, f32[64,28,140]{2,1,0:T(8,128)}, f32...) fusion(f32[64,28,140]{2,1,0:T(8,128)S(1)} %multiply_add_fusion), kind=kLoop, calls=%fused_computation.1 | loop fusion | flops 250880 | bytes 8028160 | tf_op jit(solution)/shard_map/add | solution.py:30
  167.6 4.8 %multiply_reduce_fusion = (f32[16,128]{1,0:T(8,128)S(1)}, f32[16,128]{1,0:T(8,128)S(1)}) fusion(f32[64,28,140]{2,1,0:T(8,128)S(1)} %get-tuple-element.15, f32[64,16,128]{2,1,0:T(8,128)S(1)} %copy-done, f32[64,28,140]{2,1,0:T(8,128)S(1)} %multiply_add_fusion, f32[64,28,140]{2,1,0:T(8,128)} %get-tuple-element.25, f32[64,28,140]{2,1,0:T(8,128)} %get-tuple-element.24, ...), kind=kLoop, calls=%fused_computation.54 | loop fusion | flops 2093056 | bytes 5267456 | tf_op jit(solution)/shard_map/reduce_sum | solution.py:113
  (98 shorter events, 63.3 us)
Async XLA Ops:
  0.6 18.8 %copy-start.1 = (f32[16,128]{1,0:T(8,128)S(1)}, f32[16,128]{1,0:T(8,128)}, u32[]{:S(2)}) copy-start(f32[16,128]{1,0:T(8,128)} %param.7) | copy-start | bytes 24580
  0.6 18.7 %copy-start.3 = (f32[16,128]{1,0:T(8,128)S(1)}, f32[16,128]{1,0:T(8,128)}, u32[]{:S(2)}) copy-start(f32[16,128]{1,0:T(8,128)} %param.6) | copy-start | bytes 24580
  0.7 18.7 %copy-start.2 = (f32[16,128]{1,0:T(8,128)S(1)}, f32[16,128]{1,0:T(8,128)}, u32[]{:S(2)}) copy-start(f32[16,128]{1,0:T(8,128)} %param.5) | copy-start | bytes 24580
  1.9 11.4 %collective-permute-start.1 = (f32[67,6,128]{2,1,0:T(8,128)S(1)}, f32[67,6,128]{2,1,0:T(8,128)S(1)}, u32[]{:S(2)}, u32[]{:S(2)}) collective-permute-start(f32[67,6,128]{2,1,0:T(8,128)S(1)} %get-tuple-element.34), channel_id=1, source_target_pairs={{4,0},{8,4},{12,8},{16,12},{20,16},{24,20},{28,24},{5,1},{9,5},{13... | collective-permute-start | bytes 617480 | tf_op jit(solution)/shard_map/ppermute | solution.py:20
  3.2 16.2 %collective-permute-start = (f32[67,6,128]{2,1,0:T(8,128)S(1)}, f32[67,6,128]{2,1,0:T(8,128)S(1)}, u32[]{:S(2)}, u32[]{:S(2)}) collective-permute-start(f32[67,6,128]{2,1,0:T(8,128)S(1)} %get-tuple-element.33), channel_id=1, source_target_pairs={{0,4},{4,8},{8,12},{12,16},{16,20},{20,24},{24,28},{1,5},{5,9},{9,... | collective-permute-start | bytes 617480 | tf_op jit(solution)/shard_map/ppermute | solution.py:18
  20.7 5.1 %collective-permute-start.3 = (f32[67,28,6]{0,1,2:T(8,128)S(1)}, f32[67,28,6]{0,1,2:T(8,128)S(1)}, u32[]{:S(2)}, u32[]{:S(2)}) collective-permute-start(f32[67,28,6]{0,1,2:T(8,128)S(1)} %copy.20), channel_id=1, source_target_pairs={{1,0},{2,1},{3,2},{5,4},{6,5},{7,6},{9,8},{10,9},{11,10},{13,12},{... | collective-permute-start | bytes 135080 | tf_op jit(solution)/shard_map/ppermute | solution.py:20
  22.7 4.2 %collective-permute-start.2 = (f32[67,28,6]{0,1,2:T(8,128)S(1)}, f32[67,28,6]{0,1,2:T(8,128)S(1)}, u32[]{:S(2)}, u32[]{:S(2)}) collective-permute-start(f32[67,28,6]{0,1,2:T(8,128)S(1)} %copy.19), channel_id=1, source_target_pairs={{0,1},{1,2},{2,3},{4,5},{5,6},{6,7},{8,9},{9,10},{10,11},{12,13},{... | collective-permute-start | bytes 135080 | tf_op jit(solution)/shard_map/ppermute | solution.py:18
  39.5 2.6 %collective-permute-start.4 = (f32[2,64]{1,0:T(2,128)S(1)}, f32[2,64]{1,0:T(2,128)S(1)}, u32[]{:S(2)}, u32[]{:S(2)}) collective-permute-start(f32[2,64]{1,0:T(2,128)S(1)} %pad_maximum_fusion.3), channel_id=1, source_target_pairs={{0,1},{1,0},{2,3},{3,2},{4,5},{5,4},{6,7},{7,6},{8,9},{9,8},{10,11... | collective-permute-start | bytes 1544 | tf_op jit(solution)/shard_map/ppermute | solution.py:54
  42.1 4.2 %collective-permute-start.5 = (f32[2,64]{1,0:T(2,128)S(1)}, f32[2,64]{1,0:T(2,128)S(1)}, u32[]{:S(2)}, u32[]{:S(2)}) collective-permute-start(f32[2,64]{1,0:T(2,128)S(1)} %fusion.21), channel_id=1, source_target_pairs={{0,2},{1,3},{2,0},{3,1},{4,6},{5,7},{6,4},{7,5},{8,10},{9,11},{10,... | collective-permute-start | bytes 1544 | tf_op jit(solution)/shard_map/ppermute | solution.py:54
  46.4 4.1 %collective-permute-start.6 = (f32[2,64]{1,0:T(2,128)S(1)}, f32[2,64]{1,0:T(2,128)S(1)}, u32[]{:S(2)}, u32[]{:S(2)}) collective-permute-start(f32[2,64]{1,0:T(2,128)S(1)} %fusion.26), channel_id=1, source_target_pairs={{0,4},{4,0},{8,12},{12,8},{16,20},{20,16},{24,28},{28,24},{1,5},{5... | collective-permute-start | bytes 1544 | tf_op jit(solution)/shard_map/ppermute | solution.py:54
  50.5 3.6 %collective-permute-start.7 = (f32[2,64]{1,0:T(2,128)S(1)}, f32[2,64]{1,0:T(2,128)S(1)}, u32[]{:S(2)}, u32[]{:S(2)}) collective-permute-start(f32[2,64]{1,0:T(2,128)S(1)} %add.329), channel_id=1, source_target_pairs={{0,8},{4,12},{8,0},{12,4},{16,24},{20,28},{24,16},{28,20},{1,9},{5... | collective-permute-start | bytes 1544 | tf_op jit(solution)/shard_map/ppermute | solution.py:54
  54.1 4.5 %collective-permute-start.8 = (f32[2,64]{1,0:T(2,128)S(1)}, f32[2,64]{1,0:T(2,128)S(1)}, u32[]{:S(2)}, u32[]{:S(2)}) collective-permute-start(f32[2,64]{1,0:T(2,128)S(1)} %add.330), channel_id=1, source_target_pairs={{0,16},{4,20},{8,24},{12,28},{16,0},{20,4},{24,8},{28,12},{1,17},{... | collective-permute-start | bytes 1544 | tf_op jit(solution)/shard_map/ppermute | solution.py:54
  63.8 1.2 collective-permute-start.9
  65.0 3.6 %collective-permute-start.10 = (f32[64]{0:T(128)S(1)}, f32[64]{0:T(128)S(1)}, u32[]{:S(2)}, u32[]{:S(2)}) collective-permute-start(f32[64]{0:T(128)S(1)} %add.332), channel_id=1, source_target_pairs={{0,2},{1,3},{2,0},{3,1},{4,6},{5,7},{6,4},{7,5},{8,10},{9,11},{10,... | collective-permute-start | bytes 776 | tf_op jit(solution)/shard_map/ppermute | solution.py:54
  68.6 3.6 %collective-permute-start.11 = (f32[64]{0:T(128)S(1)}, f32[64]{0:T(128)S(1)}, u32[]{:S(2)}, u32[]{:S(2)}) collective-permute-start(f32[64]{0:T(128)S(1)} %add.333), channel_id=1, source_target_pairs={{0,4},{4,0},{8,12},{12,8},{16,20},{20,16},{24,28},{28,24},{1,5},{5... | collective-permute-start | bytes 776 | tf_op jit(solution)/shard_map/ppermute | solution.py:54
  72.1 3.6 %collective-permute-start.12 = (f32[64]{0:T(128)S(1)}, f32[64]{0:T(128)S(1)}, u32[]{:S(2)}, u32[]{:S(2)}) collective-permute-start(f32[64]{0:T(128)S(1)} %add.334), channel_id=1, source_target_pairs={{0,8},{4,12},{8,0},{12,4},{16,24},{20,28},{24,16},{28,20},{1,9},{5... | collective-permute-start | bytes 776 | tf_op jit(solution)/shard_map/ppermute | solution.py:54
  75.7 4.5 %collective-permute-start.13 = (f32[64]{0:T(128)S(1)}, f32[64]{0:T(128)S(1)}, u32[]{:S(2)}, u32[]{:S(2)}) collective-permute-start(f32[64]{0:T(128)S(1)} %add.335), channel_id=1, source_target_pairs={{0,16},{4,20},{8,24},{12,28},{16,0},{20,4},{24,8},{28,12},{1,17},{... | collective-permute-start | bytes 776 | tf_op jit(solution)/shard_map/ppermute | solution.py:54
  89.9 1.2 collective-permute-start.14
  91.1 3.6 %collective-permute-start.15 = (f32[64]{0:T(128)S(1)}, f32[64]{0:T(128)S(1)}, u32[]{:S(2)}, u32[]{:S(2)}) collective-permute-start(f32[64]{0:T(128)S(1)} %add.352), channel_id=1, source_target_pairs={{0,2},{1,3},{2,0},{3,1},{4,6},{5,7},{6,4},{7,5},{8,10},{9,11},{10,... | collective-permute-start | bytes 776 | tf_op jit(solution)/shard_map/ppermute | solution.py:54
  94.7 3.6 %collective-permute-start.16 = (f32[64]{0:T(128)S(1)}, f32[64]{0:T(128)S(1)}, u32[]{:S(2)}, u32[]{:S(2)}) collective-permute-start(f32[64]{0:T(128)S(1)} %add.353), channel_id=1, source_target_pairs={{0,4},{4,0},{8,12},{12,8},{16,20},{20,16},{24,28},{28,24},{1,5},{5... | collective-permute-start | bytes 776 | tf_op jit(solution)/shard_map/ppermute | solution.py:54
  98.3 3.6 %collective-permute-start.17 = (f32[64]{0:T(128)S(1)}, f32[64]{0:T(128)S(1)}, u32[]{:S(2)}, u32[]{:S(2)}) collective-permute-start(f32[64]{0:T(128)S(1)} %add.354), channel_id=1, source_target_pairs={{0,8},{4,12},{8,0},{12,4},{16,24},{20,28},{24,16},{28,20},{1,9},{5... | collective-permute-start | bytes 776 | tf_op jit(solution)/shard_map/ppermute | solution.py:54
  101.8 4.5 %collective-permute-start.18 = (f32[64]{0:T(128)S(1)}, f32[64]{0:T(128)S(1)}, u32[]{:S(2)}, u32[]{:S(2)}) collective-permute-start(f32[64]{0:T(128)S(1)} %add.355), channel_id=1, source_target_pairs={{0,16},{4,20},{8,24},{12,28},{16,0},{20,4},{24,8},{28,12},{1,17},{... | collective-permute-start | bytes 776 | tf_op jit(solution)/shard_map/ppermute | solution.py:54
  111.5 1.2 collective-permute-start.19
  112.8 3.6 %collective-permute-start.20 = (f32[64]{0:T(128)S(1)}, f32[64]{0:T(128)S(1)}, u32[]{:S(2)}, u32[]{:S(2)}) collective-permute-start(f32[64]{0:T(128)S(1)} %add.358), channel_id=1, source_target_pairs={{0,2},{1,3},{2,0},{3,1},{4,6},{5,7},{6,4},{7,5},{8,10},{9,11},{10,... | collective-permute-start | bytes 776 | tf_op jit(solution)/shard_map/ppermute | solution.py:54
  116.3 3.6 %collective-permute-start.21 = (f32[64]{0:T(128)S(1)}, f32[64]{0:T(128)S(1)}, u32[]{:S(2)}, u32[]{:S(2)}) collective-permute-start(f32[64]{0:T(128)S(1)} %add.359), channel_id=1, source_target_pairs={{0,4},{4,0},{8,12},{12,8},{16,20},{20,16},{24,28},{28,24},{1,5},{5... | collective-permute-start | bytes 776 | tf_op jit(solution)/shard_map/ppermute | solution.py:54
  119.9 3.6 %collective-permute-start.22 = (f32[64]{0:T(128)S(1)}, f32[64]{0:T(128)S(1)}, u32[]{:S(2)}, u32[]{:S(2)}) collective-permute-start(f32[64]{0:T(128)S(1)} %add.360), channel_id=1, source_target_pairs={{0,8},{4,12},{8,0},{12,4},{16,24},{20,28},{24,16},{28,20},{1,9},{5... | collective-permute-start | bytes 776 | tf_op jit(solution)/shard_map/ppermute | solution.py:54
  123.5 4.5 %collective-permute-start.23 = (f32[64]{0:T(128)S(1)}, f32[64]{0:T(128)S(1)}, u32[]{:S(2)}, u32[]{:S(2)}) collective-permute-start(f32[64]{0:T(128)S(1)} %add.361), channel_id=1, source_target_pairs={{0,16},{4,20},{8,24},{12,28},{16,0},{20,4},{24,8},{28,12},{1,17},{... | collective-permute-start | bytes 776 | tf_op jit(solution)/shard_map/ppermute | solution.py:54
  143.8 1.2 collective-permute-start.24
  145.0 3.6 %collective-permute-start.25 = (f32[64]{0:T(128)S(1)}, f32[64]{0:T(128)S(1)}, u32[]{:S(2)}, u32[]{:S(2)}) collective-permute-start(f32[64]{0:T(128)S(1)} %add.378), channel_id=1, source_target_pairs={{0,2},{1,3},{2,0},{3,1},{4,6},{5,7},{6,4},{7,5},{8,10},{9,11},{10,... | collective-permute-start | bytes 776 | tf_op jit(solution)/shard_map/ppermute | solution.py:54
  148.6 3.6 %collective-permute-start.26 = (f32[64]{0:T(128)S(1)}, f32[64]{0:T(128)S(1)}, u32[]{:S(2)}, u32[]{:S(2)}) collective-permute-start(f32[64]{0:T(128)S(1)} %add.379), channel_id=1, source_target_pairs={{0,4},{4,0},{8,12},{12,8},{16,20},{20,16},{24,28},{28,24},{1,5},{5... | collective-permute-start | bytes 776 | tf_op jit(solution)/shard_map/ppermute | solution.py:54
  152.2 3.6 %collective-permute-start.27 = (f32[64]{0:T(128)S(1)}, f32[64]{0:T(128)S(1)}, u32[]{:S(2)}, u32[]{:S(2)}) collective-permute-start(f32[64]{0:T(128)S(1)} %add.380), channel_id=1, source_target_pairs={{0,8},{4,12},{8,0},{12,4},{16,24},{20,28},{24,16},{28,20},{1,9},{5... | collective-permute-start | bytes 776 | tf_op jit(solution)/shard_map/ppermute | solution.py:54
  155.8 4.5 %collective-permute-start.28 = (f32[64]{0:T(128)S(1)}, f32[64]{0:T(128)S(1)}, u32[]{:S(2)}, u32[]{:S(2)}) collective-permute-start(f32[64]{0:T(128)S(1)} %add.381), channel_id=1, source_target_pairs={{0,16},{4,20},{8,24},{12,28},{16,0},{20,4},{24,8},{28,12},{1,17},{... | collective-permute-start | bytes 776 | tf_op jit(solution)/shard_map/ppermute | solution.py:54
  (1 other events, 18.7 us)

commit v2 on v1

v2 whole, which is shorter than its diff:
```python
import functools

import jax
import jax.numpy as jnp
from jax import lax
from jax.experimental import pallas as pl
from jax.experimental.pallas import tpu as pltpu
from jax.sharding import PartitionSpec as P

ITERS = 3
HALO = 2 * ITERS
BLOCK = 8


def extended(cells, sides, width):
    for axis, dim in sides:
        count = lax.axis_size(axis)
        ends = count - 1
        head = lax.slice_in_dim(cells, 0, width, axis=dim)
        tail = lax.slice_in_dim(cells, cells.shape[dim] - width, cells.shape[dim], axis=dim)
        cells = jnp.concatenate(
            [
                lax.ppermute(tail, axis, [(i, (i + 1) % count) for i in range(ends)]),
                cells,
                lax.ppermute(head, axis, [((i + 1) % count, i) for i in range(ends)]),
            ],
            axis=dim,
        )
    return cells


def stencil(padded, kappa_sq):
    centre = padded[..., 1:-1, 1:-1]
    edge_sum = (
        padded[..., :-2, 1:-1]
        + padded[..., 2:, 1:-1]
        + padded[..., 1:-1, :-2]
        + padded[..., 1:-1, 2:]
    )
    corners = (
        padded[..., :-2, :-2] + padded[..., :-2, 2:] + padded[..., 2:, :-2] + padded[..., 2:, 2:]
    )
    return (kappa_sq + 20.0 / 6.0) * centre - (4.0 * edge_sum + corners) / 6.0


def stiffen(field, kappa_sq):
    pads = ((0, 0),) * (field.ndim - 2) + ((1, 1), (1, 1))
    return stencil(jnp.pad(field, pads), kappa_sq)


def all_sum(terms):
    for axis in ("cols", "rows"):
        count = lax.axis_size(axis)
        if count & (count - 1):
            terms = lax.psum(terms, axis)
            continue
        hop = 1
        while hop < count:
            terms = terms + lax.ppermute(terms, axis, [(i, i ^ hop) for i in range(count)])
            hop *= 2
    return terms


def _roll(value, shift, axis):
    return pltpu.roll(value, shift % value.shape[axis], axis)


def _stiffen_slab(value, centre_gain):
    vertical = _roll(value, 1, 0) + _roll(value, -1, 0)
    edge_sum = vertical + _roll(value, 1, 1) + _roll(value, -1, 1)
    corners = _roll(vertical, 1, 1) + _roll(vertical, -1, 1)
    return centre_gain * value - (4.0 * edge_sum + corners) / 6.0


def _lane_sum(value, keep):
    rows = jnp.sum(jnp.where(keep, value, 0.0), axis=0, keepdims=True)
    lanes = value.shape[1]
    total = rows[:, :128]
    for start in range(128, lanes, 128):
        total = total + rows[:, start : start + 128]
    return total


def _first_kernel(z_ref, gain_ref, weight_ref, inside_ref, inner_ref,
                  stiff_ref, applied_ref, zz_ref, za_ref):
    def body(i, carry):
        gain = gain_ref[...]
        z = z_ref[i]
        stiffness = _stiffen_slab(z, gain)
        applied = _stiffen_slab(weight_ref[...] * stiffness, gain)
        applied = jnp.where(inside_ref[...] > 0.5, applied, 0.0)
        stiff_ref[i] = stiffness
        applied_ref[i] = applied
        keep = inner_ref[...] > 0.5
        zz_ref[pl.ds(i, 1), :] = _lane_sum(z * z, keep)
        za_ref[pl.ds(i, 1), :] = _lane_sum(z * applied, keep)
        return carry

    lax.fori_loop(0, BLOCK, body, 0)


def _start_kernel(step_ref, z_ref, applied_ref, inner_ref, solution_ref, residual_ref, rr_ref):
    base = pl.program_id(0) * BLOCK

    def body(i, carry):
        step = step_ref[base + i]
        z = z_ref[i]
        residual = z - step * applied_ref[i]
        solution_ref[i] = step * z
        residual_ref[i] = residual
        rr_ref[pl.ds(i, 1), :] = _lane_sum(residual * residual, inner_ref[...] > 0.5)
        return carry

    lax.fori_loop(0, BLOCK, body, 0)


def _update_kernel(step_ref, solution_ref, direction_ref, residual_ref, applied_ref, inner_ref,
                   solution_out, residual_out, rr_ref):
    base = pl.program_id(0) * BLOCK

    def body(i, carry):
        step = step_ref[base + i]
        residual = residual_ref[i] - step * applied_ref[i]
        solution_out[i] = solution_ref[i] + step * direction_ref[i]
        residual_out[i] = residual
        rr_ref[pl.ds(i, 1), :] = _lane_sum(residual * residual, inner_ref[...] > 0.5)
        return carry

    lax.fori_loop(0, BLOCK, body, 0)


def _direction_kernel(beta_ref, residual_ref, direction_ref, gain_ref, weight_ref, inside_ref,
                      inner_ref, direction_out, applied_out, pa_ref):
    base = pl.program_id(0) * BLOCK

    def body(i, carry):
        beta = beta_ref[base + i]
        direction = residual_ref[i] + beta * direction_ref[i]
        gain = gain_ref[...]
        stiffness = _stiffen_slab(direction, gain)
        applied = _stiffen_slab(weight_ref[...] * stiffness, gain)
        applied = jnp.where(inside_ref[...] > 0.5, applied, 0.0)
        direction_out[i] = direction
        applied_out[i] = applied
        pa_ref[pl.ds(i, 1), :] = _lane_sum(direction * applied, inner_ref[...] > 0.5)
        return carry

    lax.fori_loop(0, BLOCK, body, 0)


def _final_kernel(step_ref, solution_ref, direction_ref, z_ref, stiff_ref, gain_ref,
                  weight_total, kappa_total):
    base = pl.program_id(0) * BLOCK

    @pl.when(pl.program_id(0) == 0)
    def _():
        weight_total[...] = jnp.zeros_like(weight_total)
        kappa_total[...] = jnp.zeros_like(kappa_total)

    def body(i, carry):
        step = step_ref[base + i]
        solution = solution_ref[i] + step * direction_ref[i]
        stiff_solution = _stiffen_slab(solution, gain_ref[...])
        stiff_probe = stiff_ref[i]
        weight_total[...] = weight_total[...] + stiff_solution * stiff_probe
        kappa_total[...] = kappa_total[...] + (solution * stiff_probe + stiff_solution * z_ref[i])
        return carry

    lax.fori_loop(0, BLOCK, body, 0)


def _field_spec(shape, offset=0):
    return pl.BlockSpec((BLOCK,) + shape, lambda g, *_: (g + offset, 0, 0))


def _plane_spec(shape, index=None):
    if index is None:
        return pl.BlockSpec(shape, lambda g, *_: (0, 0))
    return pl.BlockSpec((None,) + shape, lambda g, *_: (index, 0, 0))


def _call(kernel, scalars, inputs, in_specs, out_shapes, out_specs, probes, passes, sequential=False):
    field_bytes = 4 * probes * out_shapes[0].shape[-1] * out_shapes[0].shape[-2]
    grid_spec = pltpu.PrefetchScalarGridSpec(
        num_scalar_prefetch=len(scalars),
        grid=(probes // BLOCK,),
        in_specs=in_specs,
        out_specs=out_specs,
    )
    return pl.pallas_call(
        kernel,
        grid_spec=grid_spec,
        out_shape=out_shapes,
        compiler_params=pltpu.CompilerParams(
            dimension_semantics=("arbitrary" if sequential else "parallel",)
        ),
        cost_estimate=pl.CostEstimate(
            flops=30 * field_bytes // 4, transcendentals=0, bytes_accessed=passes * field_bytes
        ),
    )(*scalars, *inputs)


def on_device(probes, observed, kappa_sq, variance_weight):
    probe_count, rows, cols = probes.shape
    assert probe_count % BLOCK == 0 and rows >= HALO and cols >= HALO
    stacked = jnp.concatenate(
        [probes, observed[None], kappa_sq[None], variance_weight[None]], axis=0
    )
    ext = extended(stacked, (("rows", 1), ("cols", 2)), HALO)
    slab_rows = -(-(rows + 2 * HALO) // 8) * 8
    slab_cols = -(-(cols + 2 * HALO) // 128) * 128
    ext = jnp.pad(
        ext, ((0, 0), (0, slab_rows - ext.shape[1]), (0, slab_cols - ext.shape[2]))
    )
    slab = (slab_rows, slab_cols)
    observed_ext = ext[probe_count]
    gain = ext[probe_count + 1] + 20.0 / 6.0
    weight_ext = ext[probe_count + 2]

    row_at = lax.axis_index("rows") * rows - HALO + lax.iota(jnp.int32, slab_rows)
    col_at = lax.axis_index("cols") * cols - HALO + lax.iota(jnp.int32, slab_cols)
    row_in = (row_at >= 0) & (row_at < rows * lax.axis_size("rows"))
    col_in = (col_at >= 0) & (col_at < cols * lax.axis_size("cols"))
    inside = (row_in[:, None] & col_in[None, :]).astype(jnp.float32)
    row_inner = (lax.iota(jnp.int32, slab_rows) >= HALO) & (lax.iota(jnp.int32, slab_rows) < HALO + rows)
    col_inner = (lax.iota(jnp.int32, slab_cols) >= HALO) & (lax.iota(jnp.int32, slab_cols) < HALO + cols)
    inner = (row_inner[:, None] & col_inner[None, :]).astype(jnp.float32)

    field = jax.ShapeDtypeStruct((probe_count,) + slab, jnp.float32)
    dots = jax.ShapeDtypeStruct((probe_count, 128), jnp.float32)
    dot_spec = pl.BlockSpec((BLOCK, 128), lambda g, *_: (g, 0))
    fspec = _field_spec(slab)
    pspec = _plane_spec(slab)

    def lane_total(partial):
        return jnp.sum(partial, axis=1)

    stiff_probe, applied, zz, za = _call(
        _first_kernel, (), (ext, gain, weight_ext, inside, inner),
        [fspec, pspec, pspec, pspec, pspec],
        (field, field, dots, dots), (fspec, fspec, dot_spec, dot_spec), probe_count, 3,
    )
    first = all_sum(jnp.stack([lane_total(zz), lane_total(za)]))
    norm_now = first[0]
    step_len = norm_now / first[1]
    solution, residual, rr = _call(
        _start_kernel, (step_len,), (ext, applied, inner),
        [fspec, fspec, pspec], (field, field, dots), (fspec, fspec, dot_spec), probe_count, 4,
    )
    direction = ext
    for iteration in range(1, ITERS):
        norm_next = all_sum(lane_total(rr))
        beta = norm_next / norm_now
        norm_now = norm_next
        direction, applied, pa = _call(
            _direction_kernel, (beta,),
            (residual, direction, gain, weight_ext, inside, inner),
            [fspec, fspec, pspec, pspec, pspec, pspec],
            (field, field, dots), (fspec, fspec, dot_spec), probe_count, 4,
        )
        step_len = norm_now / all_sum(lane_total(pa))
        if iteration + 1 < ITERS:
            solution, residual, rr = _call(
                _update_kernel, (step_len,), (solution, direction, residual, applied, inner),
                [fspec, fspec, fspec, fspec, pspec],
                (field, field, dots), (fspec, fspec, dot_spec), probe_count, 6,
            )

    plane = jax.ShapeDtypeStruct(slab, jnp.float32)
    weight_total, kappa_total = _call(
        _final_kernel, (step_len,), (solution, direction, ext, stiff_probe, gain),
        [fspec, fspec, fspec, fspec, pspec],
        (plane, plane), (pspec, pspec), probe_count, 4, sequential=True,
    )

    def inner_of(plane_value):
        return plane_value[HALO : HALO + rows, HALO : HALO + cols]

    weight_total = inner_of(weight_total)
    kappa_total = inner_of(kappa_total)
    stiff_obs = inner_of(stiffen(observed_ext, ext[probe_count + 1]))
    grad_weight = 0.5 * weight_total / probe_count - 0.5 * stiff_obs * stiff_obs
    grad_kappa = (
        0.5 * variance_weight * (kappa_total / probe_count) - observed * variance_weight * stiff_obs
    )
    return (grad_kappa, grad_weight)


def solution(mesh):
    placed = (P(None, "rows", "cols"), P("rows", "cols"), P("rows", "cols"), P("rows", "cols"))
    return jax.shard_map(
        on_device,
        mesh=mesh,
        in_specs=placed,
        out_specs=(P("rows", "cols"), P("rows", "cols")),
        check_vma=False,
    )
```

time: 174 us -> 208 us (1.20)
  Pallas kernels: 0 us -> 77.7 us
  other arithmetic: 62.3 us -> 14.8 us
  waiting for transfers between devices: 50.6 us -> 62.6 us
  starting transfers between devices: 55.4 us -> 44.8 us
    pallas_call x0 -> x6, Pallas kernels: none -> 77.7 us  [_call(): pl.pallas_call(kernel, grid_spec=grid_spec, out_shape=out_shapes, compile...]
    mul x5 -> x0, other arithmetic: 20.6 us -> none  [apply_q(): applied = mask * stiffen(weight_ext * stiffness, kappa_ext)]
    add x3 -> x1, other arithmetic: 13 us -> 0.11 us  [stencil(): padded[..., :-2, 1:-1] + padded[..., 2:, 1:-1] + padded[..., 1:-1, :-2]]
    ppermute x25, waiting for transfers between devices: 40 us -> 50.4 us  [all_sum(): lax.ppermute(terms, axis, [(i, i ^ hop) for i in range(count)])]
    reduce_sum x6, other arithmetic: 14.9 us -> 5.19 us  [lane_total(): return jnp.sum(partial, axis=1)]
    sub x2 -> x0, other arithmetic: 8.4 us -> none  [on_device(): residual = residual - step_len * applied]
    ppermute x25, starting transfers between devices: 44.2 us -> 36 us  [all_sum(): lax.ppermute(terms, axis, [(i, i ^ hop) for i in range(count)])]
    ppermute x2, waiting for transfers between devices: 6.03 us -> 10.3 us  [extended(): lax.ppermute(tail, axis, [(i, (i + 1) % count) for i in range(ends)])]
where the time goes in v2:
time: 208 us; the launch traced here: 206 us
  Pallas kernels  77.7 us (37%)
  waiting for transfers between devices  62.6 us (30%)
  starting transfers between devices  44.8 us (22%)
  other arithmetic  14.8 us (7%)
  local copies, waits for them, and re-layouts  5.64 us (3%)
    pallas_call x6, Pallas kernels, _call(): pl.pallas_call(kernel, grid_spec=grid_spec, out_shape=out_shapes, compile...  77.7 us
    ppermute x25, waiting for transfers between devices, all_sum(): lax.ppermute(terms, axis, [(i, i ^ hop) for i in range(count)])  50.4 us
    ppermute x25, starting transfers between devices, all_sum(): lax.ppermute(terms, axis, [(i, i ^ hop) for i in range(count)])  36 us
    ppermute x2, waiting for transfers between devices, extended(): lax.ppermute(tail, axis, [(i, (i + 1) % count) for i in range(ends)])  10.3 us
    ppermute x2, starting transfers between devices, extended(): lax.ppermute(tail, axis, [(i, (i + 1) % count) for i in range(ends)])  6.18 us
    reduce_sum x6, other arithmetic, lane_total(): return jnp.sum(partial, axis=1)  5.19 us
  transfers between devices with their start and end apart: 29, of which 27 were waited for; matrix products, arithmetic and copies ran while one was open for 1% of the time, Pallas kernels for 0%

profile of v2, /device:TPU:0, one launch (start us, length us, event | category | flops | bytes accessed | tf_op | source)
XLA Modules:
  0.0 206.4 jit_solution(11115748941773514011)
XLA Ops:
  1.9 4.9 %collective-permute-start = (f32[67,6,128]{2,1,0:T(8,128)S(1)}, f32[67,6,128]{2,1,0:T(8,128)S(1)}, u32[]{:S(2)}, u32[]{:S(2)}) collective-permute-start(f32[67,6,128]{2,1,0:T(8,128)S(1)} %get-tuple-element.47), channel_id=1, source_target_pairs={{0,4},{4,8},{8,12},{12,16},{16,20},{20,24},{24,28},{1,5},{5,9},{9,... | collective-permute-start | bytes 617480 | tf_op jit(solution)/shard_map/ppermute | solution.py:23
  8.2 10.3 %collective-permute-done = f32[67,6,128]{2,1,0:T(8,128)S(1)} collective-permute-done((f32[67,6,128]{2,1,0:T(8,128)S(1)}, f32[67,6,128]{2,1,0:T(8,128)S(1)}, u32[]{:S(2)}, u32[]{:S(2)}) %collective-permute-start) | collective-permute-done | bytes 205856 | tf_op jit(solution)/shard_map/ppermute | solution.py:23
  24.9 1.9 collective-permute-done.3
  31.3 16.1 %shard_map.59 = (f32[64,32,256]{2,1,0:T(8,128)}, f32[64,32,256]{2,1,0:T(8,128)}, f32[64,128]{1,0:T(8,128)}, f32[64,128]{1,0:T(8,128)}) custom-call(f32[67,32,256]{2,1,0:T(8,128)} %pad.8.z_ref.direction_ref, f32[32,256]{1,0:T(8,128)} %get-tuple-element.44.gain_ref, f32[32,256]{1,0:T(8,128)} %get-tuple-element.43.weight_ref, ...), custom_call_target="tpu_custom_call" | custom-call | flops 15728640 | bytes 6291456 | tf_op jit(solution)/shard_map/pallas_call | solution.py:190
  49.1 3.3 %collective-permute-start.4 = (f32[2,64]{1,0:T(2,128)S(1)}, f32[2,64]{1,0:T(2,128)S(1)}, u32[]{:S(2)}, u32[]{:S(2)}) collective-permute-start(f32[2,64]{1,0:T(2,128)S(1)} %pad_maximum_fusion.3), channel_id=1, source_target_pairs={{0,1},{1,0},{2,3},{3,2},{4,5},{5,4},{6,7},{7,6},{8,9},{9,8},{10,11... | collective-permute-start | bytes 1544 | tf_op jit(solution)/shard_map/ppermute | solution.py:59
  53.5 3.4 %collective-permute-done.5 = f32[2,64]{1,0:T(2,128)S(1)} collective-permute-done((f32[2,64]{1,0:T(2,128)S(1)}, f32[2,64]{1,0:T(2,128)S(1)}, u32[]{:S(2)}, u32[]{:S(2)}) %collective-permute-start.5) | collective-permute-done | bytes 544 | tf_op jit(solution)/shard_map/ppermute | solution.py:59
  56.9 2.6 %collective-permute-start.6 = (f32[2,64]{1,0:T(2,128)S(1)}, f32[2,64]{1,0:T(2,128)S(1)}, u32[]{:S(2)}, u32[]{:S(2)}) collective-permute-start(f32[2,64]{1,0:T(2,128)S(1)} %fusion.11), channel_id=1, source_target_pairs={{0,4},{4,0},{8,12},{12,8},{16,20},{20,16},{24,28},{28,24},{1,5},{5... | collective-permute-start | bytes 1544 | tf_op jit(solution)/shard_map/ppermute | solution.py:59
  61.0 3.0 %collective-permute-start.7 = (f32[2,64]{1,0:T(2,128)S(1)}, f32[2,64]{1,0:T(2,128)S(1)}, u32[]{:S(2)}, u32[]{:S(2)}) collective-permute-start(f32[2,64]{1,0:T(2,128)S(1)} %add.136), channel_id=1, source_target_pairs={{0,8},{4,12},{8,0},{12,4},{16,24},{20,28},{24,16},{28,20},{1,9},{5... | collective-permute-start | bytes 1544 | tf_op jit(solution)/shard_map/ppermute | solution.py:59
  65.6 3.0 %collective-permute-start.8 = (f32[2,64]{1,0:T(2,128)S(1)}, f32[2,64]{1,0:T(2,128)S(1)}, u32[]{:S(2)}, u32[]{:S(2)}) collective-permute-start(f32[2,64]{1,0:T(2,128)S(1)} %add.137), channel_id=1, source_target_pairs={{0,16},{4,20},{8,24},{12,28},{16,0},{20,4},{24,8},{28,12},{1,17},{... | collective-permute-start | bytes 1544 | tf_op jit(solution)/shard_map/ppermute | solution.py:59
  70.7 7.8 %shard_map.60 = (f32[64,32,256]{2,1,0:T(8,128)}, f32[64,32,256]{2,1,0:T(8,128)}, f32[64,128]{1,0:T(8,128)}) custom-call(f32[64]{0:T(128)} %bitcast_divide_fusion.step_ref, f32[67,32,256]{2,1,0:T(8,128)} %pad.8.z_ref.direction_ref, f32[64,32,256]{2,1,0:T(8,128)} %get-tuple-element.21.applied_ref, f32[32,256]{1,0:T(8,128)} %get-tuple-element.56.inner_ref), custom_call_target="tpu_custom_call" | custom-call | flops 15728640 | bytes 8388608 | tf_op jit(solution)/shard_map/pallas_call | solution.py:190
  80.7 3.4 %collective-permute-done.10 = f32[64]{0:T(128)S(1)} collective-permute-done((f32[64]{0:T(128)S(1)}, f32[64]{0:T(128)S(1)}, u32[]{:S(2)}, u32[]{:S(2)}) %collective-permute-start.10) | collective-permute-done | bytes 288 | tf_op jit(solution)/shard_map/ppermute | solution.py:59
  85.1 2.6 %collective-permute-done.11 = f32[64]{0:T(128)S(1)} collective-permute-done((f32[64]{0:T(128)S(1)}, f32[64]{0:T(128)S(1)}, u32[]{:S(2)}, u32[]{:S(2)}) %collective-permute-start.11) | collective-permute-done | bytes 288 | tf_op jit(solution)/shard_map/ppermute | solution.py:59
  87.7 1.9 collective-permute-start.12
  89.6 1.7 collective-permute-done.12
  91.3 2.9 %collective-permute-start.13 = (f32[64]{0:T(128)S(1)}, f32[64]{0:T(128)S(1)}, u32[]{:S(2)}, u32[]{:S(2)}) collective-permute-start(f32[64]{0:T(128)S(1)} %add.142), channel_id=1, source_target_pairs={{0,16},{4,20},{8,24},{12,28},{16,0},{20,4},{24,8},{28,12},{1,17},{... | collective-permute-start | bytes 776 | tf_op jit(solution)/shard_map/ppermute | solution.py:59
  96.3 17.1 %shard_map.61 = (f32[64,32,256]{2,1,0:T(8,128)}, f32[64,32,256]{2,1,0:T(8,128)}, f32[64,128]{1,0:T(8,128)}) custom-call(f32[64]{0:T(128)} %get-tuple-element.40.beta_ref, f32[64,32,256]{2,1,0:T(8,128)} %get-tuple-element.23.residual_ref, f32[67,32,256]{2,1,0:T(8,128)} %pad.8.z_ref.direction_ref, f32[32,256]{1,0:T(8,128)} %get-tuple-element.44.gain_ref, ...), custom_call_target="tpu_custom_call" | custom-call | flops 15728640 | bytes 8388608 | tf_op jit(solution)/shard_map/pallas_call | solution.py:190
  115.6 3.4 %collective-permute-done.15 = f32[64]{0:T(128)S(1)} collective-permute-done((f32[64]{0:T(128)S(1)}, f32[64]{0:T(128)S(1)}, u32[]{:S(2)}, u32[]{:S(2)}) %collective-permute-start.15) | collective-permute-done | bytes 288 | tf_op jit(solution)/shard_map/ppermute | solution.py:59
  120.0 2.6 %collective-permute-done.16 = f32[64]{0:T(128)S(1)} collective-permute-done((f32[64]{0:T(128)S(1)}, f32[64]{0:T(128)S(1)}, u32[]{:S(2)}, u32[]{:S(2)}) %collective-permute-start.16) | collective-permute-done | bytes 288 | tf_op jit(solution)/shard_map/ppermute | solution.py:59
  122.6 1.9 collective-permute-start.17
  124.5 1.7 collective-permute-done.17
  126.2 2.9 %collective-permute-start.18 = (f32[64]{0:T(128)S(1)}, f32[64]{0:T(128)S(1)}, u32[]{:S(2)}, u32[]{:S(2)}) collective-permute-start(f32[64]{0:T(128)S(1)} %add.147), channel_id=1, source_target_pairs={{0,16},{4,20},{8,24},{12,28},{16,0},{20,4},{24,8},{28,12},{1,17},{... | collective-permute-start | bytes 776 | tf_op jit(solution)/shard_map/ppermute | solution.py:59
  131.2 8.7 %shard_map.62 = (f32[64,32,256]{2,1,0:T(8,128)}, f32[64,32,256]{2,1,0:T(8,128)}, f32[64,128]{1,0:T(8,128)}) custom-call(f32[64]{0:T(128)} %add_divide_fusion.1.step_ref, f32[64,32,256]{2,1,0:T(8,128)} %get-tuple-element.25.solution_ref, f32[64,32,256]{2,1,0:T(8,128)} %get-tuple-element.26.direction_ref, f32[64,32,256]{2,1,0:T(8,128)} %get-tuple-element.23.residual_ref, ...), custom_call_target="tpu_custom_call" | custom-call | flops 15728640 | bytes 12582912 | tf_op jit(solution)/shard_map/pallas_call | solution.py:190
  142.2 3.4 %collective-permute-done.20 = f32[64]{0:T(128)S(1)} collective-permute-done((f32[64]{0:T(128)S(1)}, f32[64]{0:T(128)S(1)}, u32[]{:S(2)}, u32[]{:S(2)}) %collective-permute-start.20) | collective-permute-done | bytes 288 | tf_op jit(solution)/shard_map/ppermute | solution.py:59
  146.5 2.6 %collective-permute-done.21 = f32[64]{0:T(128)S(1)} collective-permute-done((f32[64]{0:T(128)S(1)}, f32[64]{0:T(128)S(1)}, u32[]{:S(2)}, u32[]{:S(2)}) %collective-permute-start.21) | collective-permute-done | bytes 288 | tf_op jit(solution)/shard_map/ppermute | solution.py:59
  149.2 1.9 collective-permute-start.22
  152.7 2.9 %collective-permute-start.23 = (f32[64]{0:T(128)S(1)}, f32[64]{0:T(128)S(1)}, u32[]{:S(2)}, u32[]{:S(2)}) collective-permute-start(f32[64]{0:T(128)S(1)} %add.152), channel_id=1, source_target_pairs={{0,16},{4,20},{8,24},{12,28},{16,0},{20,4},{24,8},{28,12},{1,17},{... | collective-permute-start | bytes 776 | tf_op jit(solution)/shard_map/ppermute | solution.py:59
  157.7 17.1 %shard_map.63 = (f32[64,32,256]{2,1,0:T(8,128)}, f32[64,32,256]{2,1,0:T(8,128)}, f32[64,128]{1,0:T(8,128)}) custom-call(f32[64]{0:T(128)} %get-tuple-element.38.beta_ref, f32[64,32,256]{2,1,0:T(8,128)} %get-tuple-element.29.residual_ref, f32[64,32,256]{2,1,0:T(8,128)} %get-tuple-element.26.direction_ref, f32[32,256]{1,0:T(8,128)} %get-tuple-element.44.gain_ref, ...), custom_call_target="tpu_custom_call" | custom-call | flops 15728640 | bytes 8388608 | tf_op jit(solution)/shard_map/pallas_call | solution.py:190
  177.1 3.4 %collective-permute-done.25 = f32[64]{0:T(128)S(1)} collective-permute-done((f32[64]{0:T(128)S(1)}, f32[64]{0:T(128)S(1)}, u32[]{:S(2)}, u32[]{:S(2)}) %collective-permute-start.25) | collective-permute-done | bytes 288 | tf_op jit(solution)/shard_map/ppermute | solution.py:59
  181.4 2.6 %collective-permute-done.26 = f32[64]{0:T(128)S(1)} collective-permute-done((f32[64]{0:T(128)S(1)}, f32[64]{0:T(128)S(1)}, u32[]{:S(2)}, u32[]{:S(2)}) %collective-permute-start.26) | collective-permute-done | bytes 288 | tf_op jit(solution)/shard_map/ppermute | solution.py:59
  184.1 1.9 collective-permute-start.27
  187.6 2.9 %collective-permute-start.28 = (f32[64]{0:T(128)S(1)}, f32[64]{0:T(128)S(1)}, u32[]{:S(2)}, u32[]{:S(2)}) collective-permute-start(f32[64]{0:T(128)S(1)} %add.157), channel_id=1, source_target_pairs={{0,16},{4,20},{8,24},{12,28},{16,0},{20,4},{24,8},{28,12},{1,17},{... | collective-permute-start | bytes 776 | tf_op jit(solution)/shard_map/ppermute | solution.py:59
  192.6 10.9 %shard_map.64 = (f32[32,256]{1,0:T(8,128)}, f32[32,256]{1,0:T(8,128)}) custom-call(f32[64]{0:T(128)} %add_divide_fusion.step_ref, f32[64,32,256]{2,1,0:T(8,128)} %get-tuple-element.31.solution_ref, f32[64,32,256]{2,1,0:T(8,128)} %get-tuple-element.32.direction_ref, f32[67,32,256]{2,1,0:T(8,128)} %pad.8.z_ref.direction_ref, ...), custom_call_target="tpu_custom_call" | custom-call | flops 15728640 | bytes 8388608 | tf_op jit(solution)/shard_map/pallas_call | solution.py:190
  (92 shorter events, 48.6 us)
Async XLA Ops:
  0.6 17.9 %copy-start.2 = (f32[16,128]{1,0:T(8,128)S(1)}, f32[16,128]{1,0:T(8,128)}, u32[]{:S(2)}) copy-start(f32[16,128]{1,0:T(8,128)} %param.5) | copy-start | bytes 24580
  0.6 17.8 %copy-start.3 = (f32[16,128]{1,0:T(8,128)S(1)}, f32[16,128]{1,0:T(8,128)}, u32[]{:S(2)}) copy-start(f32[16,128]{1,0:T(8,128)} %param.6) | copy-start | bytes 24580
  0.7 17.8 %copy-start.1 = (f32[16,128]{1,0:T(8,128)S(1)}, f32[16,128]{1,0:T(8,128)}, u32[]{:S(2)}) copy-start(f32[16,128]{1,0:T(8,128)} %param.7) | copy-start | bytes 24580
  1.9 16.6 %collective-permute-start = (f32[67,6,128]{2,1,0:T(8,128)S(1)}, f32[67,6,128]{2,1,0:T(8,128)S(1)}, u32[]{:S(2)}, u32[]{:S(2)}) collective-permute-start(f32[67,6,128]{2,1,0:T(8,128)S(1)} %get-tuple-element.47), channel_id=1, source_target_pairs={{0,4},{4,8},{8,12},{12,16},{16,20},{20,24},{24,28},{1,5},{5,9},{9,... | collective-permute-start | bytes 617480 | tf_op jit(solution)/shard_map/ppermute | solution.py:23
  6.8 11.7 %collective-permute-start.1 = (f32[67,6,128]{2,1,0:T(8,128)S(1)}, f32[67,6,128]{2,1,0:T(8,128)S(1)}, u32[]{:S(2)}, u32[]{:S(2)}) collective-permute-start(f32[67,6,128]{2,1,0:T(8,128)S(1)} %get-tuple-element.48), channel_id=1, source_target_pairs={{4,0},{8,4},{12,8},{16,12},{20,16},{24,20},{28,24},{5,1},{9,5},{13... | collective-permute-start | bytes 617480 | tf_op jit(solution)/shard_map/ppermute | solution.py:25
  19.8 4.0 %collective-permute-start.2 = (f32[67,28,6]{0,1,2:T(8,128)S(1)}, f32[67,28,6]{0,1,2:T(8,128)S(1)}, u32[]{:S(2)}, u32[]{:S(2)}) collective-permute-start(f32[67,28,6]{0,1,2:T(8,128)S(1)} %copy.6), channel_id=1, source_target_pairs={{0,1},{1,2},{2,3},{4,5},{5,6},{6,7},{8,9},{9,10},{10,11},{12,13},{... | collective-permute-start | bytes 135080 | tf_op jit(solution)/shard_map/ppermute | solution.py:23
  21.8 4.9 %collective-permute-start.3 = (f32[67,28,6]{0,1,2:T(8,128)S(1)}, f32[67,28,6]{0,1,2:T(8,128)S(1)}, u32[]{:S(2)}, u32[]{:S(2)}) collective-permute-start(f32[67,28,6]{0,1,2:T(8,128)S(1)} %copy.7), channel_id=1, source_target_pairs={{1,0},{2,1},{3,2},{5,4},{6,5},{7,6},{9,8},{10,9},{11,10},{13,12},{... | collective-permute-start | bytes 135080 | tf_op jit(solution)/shard_map/ppermute | solution.py:25
  49.1 4.1 %collective-permute-start.4 = (f32[2,64]{1,0:T(2,128)S(1)}, f32[2,64]{1,0:T(2,128)S(1)}, u32[]{:S(2)}, u32[]{:S(2)}) collective-permute-start(f32[2,64]{1,0:T(2,128)S(1)} %pad_maximum_fusion.3), channel_id=1, source_target_pairs={{0,1},{1,0},{2,3},{3,2},{4,5},{5,4},{6,7},{7,6},{8,9},{9,8},{10,11... | collective-permute-start | bytes 1544 | tf_op jit(solution)/shard_map/ppermute | solution.py:59
  53.3 3.6 %collective-permute-start.5 = (f32[2,64]{1,0:T(2,128)S(1)}, f32[2,64]{1,0:T(2,128)S(1)}, u32[]{:S(2)}, u32[]{:S(2)}) collective-permute-start(f32[2,64]{1,0:T(2,128)S(1)} %fusion.6), channel_id=1, source_target_pairs={{0,2},{1,3},{2,0},{3,1},{4,6},{5,7},{6,4},{7,5},{8,10},{9,11},{10,... | collective-permute-start | bytes 1544 | tf_op jit(solution)/shard_map/ppermute | solution.py:59
  56.9 4.1 %collective-permute-start.6 = (f32[2,64]{1,0:T(2,128)S(1)}, f32[2,64]{1,0:T(2,128)S(1)}, u32[]{:S(2)}, u32[]{:S(2)}) collective-permute-start(f32[2,64]{1,0:T(2,128)S(1)} %fusion.11), channel_id=1, source_target_pairs={{0,4},{4,0},{8,12},{12,8},{16,20},{20,16},{24,28},{28,24},{1,5},{5... | collective-permute-start | bytes 1544 | tf_op jit(solution)/shard_map/ppermute | solution.py:59
  61.0 4.5 %collective-permute-start.7 = (f32[2,64]{1,0:T(2,128)S(1)}, f32[2,64]{1,0:T(2,128)S(1)}, u32[]{:S(2)}, u32[]{:S(2)}) collective-permute-start(f32[2,64]{1,0:T(2,128)S(1)} %add.136), channel_id=1, source_target_pairs={{0,8},{4,12},{8,0},{12,4},{16,24},{20,28},{24,16},{28,20},{1,9},{5... | collective-permute-start | bytes 1544 | tf_op jit(solution)/shard_map/ppermute | solution.py:59
  65.6 4.6 %collective-permute-start.8 = (f32[2,64]{1,0:T(2,128)S(1)}, f32[2,64]{1,0:T(2,128)S(1)}, u32[]{:S(2)}, u32[]{:S(2)}) collective-permute-start(f32[2,64]{1,0:T(2,128)S(1)} %add.137), channel_id=1, source_target_pairs={{0,16},{4,20},{8,24},{12,28},{16,0},{20,4},{24,8},{28,12},{1,17},{... | collective-permute-start | bytes 1544 | tf_op jit(solution)/shard_map/ppermute | solution.py:59
  79.3 1.2 collective-permute-start.9
  80.6 3.6 %collective-permute-start.10 = (f32[64]{0:T(128)S(1)}, f32[64]{0:T(128)S(1)}, u32[]{:S(2)}, u32[]{:S(2)}) collective-permute-start(f32[64]{0:T(128)S(1)} %add.139), channel_id=1, source_target_pairs={{0,2},{1,3},{2,0},{3,1},{4,6},{5,7},{6,4},{7,5},{8,10},{9,11},{10,... | collective-permute-start | bytes 776 | tf_op jit(solution)/shard_map/ppermute | solution.py:59
  84.1 3.6 %collective-permute-start.11 = (f32[64]{0:T(128)S(1)}, f32[64]{0:T(128)S(1)}, u32[]{:S(2)}, u32[]{:S(2)}) collective-permute-start(f32[64]{0:T(128)S(1)} %add.140), channel_id=1, source_target_pairs={{0,4},{4,0},{8,12},{12,8},{16,20},{20,16},{24,28},{28,24},{1,5},{5... | collective-permute-start | bytes 776 | tf_op jit(solution)/shard_map/ppermute | solution.py:59
  87.7 3.6 %collective-permute-start.12 = (f32[64]{0:T(128)S(1)}, f32[64]{0:T(128)S(1)}, u32[]{:S(2)}, u32[]{:S(2)}) collective-permute-start(f32[64]{0:T(128)S(1)} %add.141), channel_id=1, source_target_pairs={{0,8},{4,12},{8,0},{12,4},{16,24},{20,28},{24,16},{28,20},{1,9},{5... | collective-permute-start | bytes 776 | tf_op jit(solution)/shard_map/ppermute | solution.py:59
  91.3 4.5 %collective-permute-start.13 = (f32[64]{0:T(128)S(1)}, f32[64]{0:T(128)S(1)}, u32[]{:S(2)}, u32[]{:S(2)}) collective-permute-start(f32[64]{0:T(128)S(1)} %add.142), channel_id=1, source_target_pairs={{0,16},{4,20},{8,24},{12,28},{16,0},{20,4},{24,8},{28,12},{1,17},{... | collective-permute-start | bytes 776 | tf_op jit(solution)/shard_map/ppermute | solution.py:59
  114.3 1.2 collective-permute-start.14
  115.5 3.6 %collective-permute-start.15 = (f32[64]{0:T(128)S(1)}, f32[64]{0:T(128)S(1)}, u32[]{:S(2)}, u32[]{:S(2)}) collective-permute-start(f32[64]{0:T(128)S(1)} %add.144), channel_id=1, source_target_pairs={{0,2},{1,3},{2,0},{3,1},{4,6},{5,7},{6,4},{7,5},{8,10},{9,11},{10,... | collective-permute-start | bytes 776 | tf_op jit(solution)/shard_map/ppermute | solution.py:59
  119.1 3.6 %collective-permute-start.16 = (f32[64]{0:T(128)S(1)}, f32[64]{0:T(128)S(1)}, u32[]{:S(2)}, u32[]{:S(2)}) collective-permute-start(f32[64]{0:T(128)S(1)} %add.145), channel_id=1, source_target_pairs={{0,4},{4,0},{8,12},{12,8},{16,20},{20,16},{24,28},{28,24},{1,5},{5... | collective-permute-start | bytes 776 | tf_op jit(solution)/shard_map/ppermute | solution.py:59
  122.6 3.6 %collective-permute-start.17 = (f32[64]{0:T(128)S(1)}, f32[64]{0:T(128)S(1)}, u32[]{:S(2)}, u32[]{:S(2)}) collective-permute-start(f32[64]{0:T(128)S(1)} %add.146), channel_id=1, source_target_pairs={{0,8},{4,12},{8,0},{12,4},{16,24},{20,28},{24,16},{28,20},{1,9},{5... | collective-permute-start | bytes 776 | tf_op jit(solution)/shard_map/ppermute | solution.py:59
  126.2 4.5 %collective-permute-start.18 = (f32[64]{0:T(128)S(1)}, f32[64]{0:T(128)S(1)}, u32[]{:S(2)}, u32[]{:S(2)}) collective-permute-start(f32[64]{0:T(128)S(1)} %add.147), channel_id=1, source_target_pairs={{0,16},{4,20},{8,24},{12,28},{16,0},{20,4},{24,8},{28,12},{1,17},{... | collective-permute-start | bytes 776 | tf_op jit(solution)/shard_map/ppermute | solution.py:59
  140.8 1.2 collective-permute-start.19
  142.0 3.6 %collective-permute-start.20 = (f32[64]{0:T(128)S(1)}, f32[64]{0:T(128)S(1)}, u32[]{:S(2)}, u32[]{:S(2)}) collective-permute-start(f32[64]{0:T(128)S(1)} %add.149), channel_id=1, source_target_pairs={{0,2},{1,3},{2,0},{3,1},{4,6},{5,7},{6,4},{7,5},{8,10},{9,11},{10,... | collective-permute-start | bytes 776 | tf_op jit(solution)/shard_map/ppermute | solution.py:59
  145.6 3.6 %collective-permute-start.21 = (f32[64]{0:T(128)S(1)}, f32[64]{0:T(128)S(1)}, u32[]{:S(2)}, u32[]{:S(2)}) collective-permute-start(f32[64]{0:T(128)S(1)} %add.150), channel_id=1, source_target_pairs={{0,4},{4,0},{8,12},{12,8},{16,20},{20,16},{24,28},{28,24},{1,5},{5... | collective-permute-start | bytes 776 | tf_op jit(solution)/shard_map/ppermute | solution.py:59
  149.2 3.6 %collective-permute-start.22 = (f32[64]{0:T(128)S(1)}, f32[64]{0:T(128)S(1)}, u32[]{:S(2)}, u32[]{:S(2)}) collective-permute-start(f32[64]{0:T(128)S(1)} %add.151), channel_id=1, source_target_pairs={{0,8},{4,12},{8,0},{12,4},{16,24},{20,28},{24,16},{28,20},{1,9},{5... | collective-permute-start | bytes 776 | tf_op jit(solution)/shard_map/ppermute | solution.py:59
  152.7 4.5 %collective-permute-start.23 = (f32[64]{0:T(128)S(1)}, f32[64]{0:T(128)S(1)}, u32[]{:S(2)}, u32[]{:S(2)}) collective-permute-start(f32[64]{0:T(128)S(1)} %add.152), channel_id=1, source_target_pairs={{0,16},{4,20},{8,24},{12,28},{16,0},{20,4},{24,8},{28,12},{1,17},{... | collective-permute-start | bytes 776 | tf_op jit(solution)/shard_map/ppermute | solution.py:59
  175.7 1.2 collective-permute-start.24
  176.9 3.6 %collective-permute-start.25 = (f32[64]{0:T(128)S(1)}, f32[64]{0:T(128)S(1)}, u32[]{:S(2)}, u32[]{:S(2)}) collective-permute-start(f32[64]{0:T(128)S(1)} %add.154), channel_id=1, source_target_pairs={{0,2},{1,3},{2,0},{3,1},{4,6},{5,7},{6,4},{7,5},{8,10},{9,11},{10,... | collective-permute-start | bytes 776 | tf_op jit(solution)/shard_map/ppermute | solution.py:59
  180.5 3.6 %collective-permute-start.26 = (f32[64]{0:T(128)S(1)}, f32[64]{0:T(128)S(1)}, u32[]{:S(2)}, u32[]{:S(2)}) collective-permute-start(f32[64]{0:T(128)S(1)} %add.155), channel_id=1, source_target_pairs={{0,4},{4,0},{8,12},{12,8},{16,20},{20,16},{24,28},{28,24},{1,5},{5... | collective-permute-start | bytes 776 | tf_op jit(solution)/shard_map/ppermute | solution.py:59
  184.1 3.6 %collective-permute-start.27 = (f32[64]{0:T(128)S(1)}, f32[64]{0:T(128)S(1)}, u32[]{:S(2)}, u32[]{:S(2)}) collective-permute-start(f32[64]{0:T(128)S(1)} %add.156), channel_id=1, source_target_pairs={{0,8},{4,12},{8,0},{12,4},{16,24},{20,28},{24,16},{28,20},{1,9},{5... | collective-permute-start | bytes 776 | tf_op jit(solution)/shard_map/ppermute | solution.py:59
  187.6 4.5 %collective-permute-start.28 = (f32[64]{0:T(128)S(1)}, f32[64]{0:T(128)S(1)}, u32[]{:S(2)}, u32[]{:S(2)}) collective-permute-start(f32[64]{0:T(128)S(1)} %add.157), channel_id=1, source_target_pairs={{0,16},{4,20},{8,24},{12,28},{16,0},{20,4},{24,8},{28,12},{1,17},{... | collective-permute-start | bytes 776 | tf_op jit(solution)/shard_map/ppermute | solution.py:59
  (1 other events, 17.8 us)

commit v3 on v1

--- a/solution.py
+++ b/solution.py
@@ -56,35 +56,61 @@
     return terms
 
 
-def inside_mask(rows, cols):
-    row_at = lax.axis_index("rows") * rows - HALO + lax.iota(jnp.int32, rows + 2 * HALO)
-    col_at = lax.axis_index("cols") * cols - HALO + lax.iota(jnp.int32, cols + 2 * HALO)
-    row_in = (row_at >= 0) & (row_at < rows * lax.axis_size("rows"))
-    col_in = (col_at >= 0) & (col_at < cols * lax.axis_size("cols"))
-    return (row_in[:, None] & col_in[None, :]).astype(jnp.float32)
+def stiffen_lanes(field, kappa_sq):
+    padded = jnp.pad(field, ((1, 1), (1, 1), (0, 0)))
+    centre = padded[1:-1, 1:-1]
+    edge_sum = padded[:-2, 1:-1] + padded[2:, 1:-1] + padded[1:-1, :-2] + padded[1:-1, 2:]
+    corners = padded[:-2, :-2] + padded[:-2, 2:] + padded[2:, :-2] + padded[2:, 2:]
+    return (kappa_sq + 20.0 / 6.0) * centre - (4.0 * edge_sum + corners) / 6.0
 
 
 def on_device(probes, observed, kappa_sq, variance_weight):
     probe_count, rows, cols = probes.shape
+    assert rows >= HALO and cols % 2 == 0 and cols // 2 >= HALO
+    half = cols // 2
+    width = half + 2 * HALO
     stacked = jnp.concatenate(
         [probes, observed[None], kappa_sq[None], variance_weight[None]], axis=0
     )
     ext = extended(stacked, (("rows", 1), ("cols", 2)), HALO)
-    probe_ext = ext[:probe_count]
-    observed_ext = ext[probe_count]
-    kappa_ext = ext[probe_count + 1]
-    weight_ext = ext[probe_count + 2]
-    mask = inside_mask(rows, cols)
+    halves = [ext[:, :, h * half : h * half + width] for h in range(2)]
+
+    def on_lanes(index):
+        if index is None:
+            return jnp.concatenate([jnp.transpose(h[:probe_count], (1, 2, 0)) for h in halves], axis=2)
+        return jnp.concatenate(
+            [jnp.broadcast_to(h[index][:, :, None], h.shape[1:] + (probe_count,)) for h in halves],
+            axis=2,
+        )
+
+    probe_ext = on_lanes(None)
+    kappa_ext = on_lanes(probe_count + 1)
+    weight_ext = on_lanes(probe_count + 2)
+
+    row_at = lax.axis_index("rows") * rows - HALO + lax.iota(jnp.int32, rows + 2 * HALO)
+    row_in = (row_at >= 0) & (row_at < rows * lax.axis_size("rows"))
+    col_in = []
+    for h in range(2):
+        col_at = lax.axis_index("cols") * cols - HALO + h * half + lax.iota(jnp.int32, width)
+        col_in.append((col_at >= 0) & (col_at < cols * lax.axis_size("cols")))
+    col_in = jnp.concatenate(
+        [jnp.broadcast_to(c[:, None], (width, probe_count)) for c in col_in], axis=1
+    )
+    mask = (row_in[:, None, None] & col_in[None, :, :]).astype(jnp.float32)
 
     def inner(field):
-        return field[..., HALO : HALO + rows, HALO : HALO + cols]
+        return field[HALO : HALO + rows, HALO : HALO + half]
 
     def dot(first, second):
-        return jnp.sum(inner(first) * inner(second), axis=(-2, -1))
+        lanes = jnp.sum(inner(first) * inner(second), axis=(0, 1))
+        return jnp.sum(lanes.reshape(2, probe_count), axis=0)
+
+    def on_lane(scalars):
+        return jnp.tile(scalars, 2)[None, None, :]
 
     def apply_q(direction):
-        stiffness = stiffen(direction, kappa_ext)
-        applied = mask * stiffen(weight_ext * stiffness, kappa_ext)
+        stiffness = stiffen_lanes(direction, kappa_ext)
+        applied = mask * stiffen_lanes(weight_ext * stiffness, kappa_ext)
         return stiffness, applied
 
     residual = probe_ext
@@ -98,20 +124,26 @@
         if iteration > 0:
             _, applied = apply_q(direction)
             curvature = all_sum(dot(direction, applied))
-        step_len = (norm_now / curvature)[:, None, None]
+        step_len = on_lane(norm_now / curvature)
         solution = step_len * direction if solution is None else solution + step_len * direction
         if iteration + 1 < ITERS:
             residual = residual - step_len * applied
             norm_next = all_sum(dot(residual, residual))
-            direction = residual + (norm_next / norm_now)[:, None, None] * direction
+            direction = residual + on_lane(norm_next / norm_now) * direction
             norm_now = norm_next
 
-    stiff_solution = inner(stiffen(solution, kappa_ext))
-    stiff_obs = inner(stiffen(observed_ext, kappa_ext))
+    stiff_solution = inner(stiffen_lanes(solution, kappa_ext))
     stiff_probe = inner(stiff_probe)
     solution = inner(solution)
-    weight_total = jnp.sum(stiff_solution * stiff_probe, axis=0)
-    kappa_total = jnp.sum(solution * stiff_probe + stiff_solution * probes, axis=0)
+    probe_in = inner(probe_ext)
+
+    def probe_total(terms):
+        per_half = jnp.sum(terms.reshape(rows, half, 2, probe_count), axis=3)
+        return jnp.transpose(per_half, (0, 2, 1)).reshape(rows, cols)
+
+    weight_total = probe_total(stiff_solution * stiff_probe)
+    kappa_total = probe_total(solution * stiff_probe + stiff_solution * probe_in)
+    stiff_obs = stiffen(ext[probe_count], ext[probe_count + 1])[HALO : HALO + rows, HALO : HALO + cols]
     grad_weight = 0.5 * weight_total / probe_count - 0.5 * stiff_obs * stiff_obs
     grad_kappa = (
         0.5 * variance_weight * (kappa_total / probe_count) - observed * variance_weight * stiff_obs

time: 174 us -> 219 us (1.26); the launches traced: 174 us -> 216 us
  other arithmetic: 62.3 us -> 97.2 us
  local copies, waits for them, and re-layouts: 4.41 us -> 13.5 us
    sub x2, other arithmetic: 8.4 us -> 26 us  [on_device(): residual = residual - step_len * applied]
    add x2 -> x5, other arithmetic: 0.64 us -> 14.1 us  [the longest x2 9.19 us: stiffen_lanes(): padded[:-2, 1:-1] + padded[2:, 1:-1] + padded[1:-1, :-2] + padded[1:-1, 2:]]
    add x3 -> x1, other arithmetic: 13 us -> 0.11 us  [stencil(): padded[..., :-2, 1:-1] + padded[..., 2:, 1:-1] + padded[..., 1:-1, :-2]]
    concatenate x2 -> x3, other arithmetic: 1.39 us -> 7 us  [extended(): jnp.concatenate([lax.ppermute(tail, axis, [(i, (i + 1) % count) for i in...]
    ppermute x2, waiting for transfers between devices: 6.03 us -> 11.2 us  [extended(): lax.ppermute(tail, axis, [(i, (i + 1) % count) for i in range(ends)])]
    reduce_sum x6 -> x12, other arithmetic: 14.9 us -> 19.8 us  [the longest x5 14.2 us: dot(): lanes = jnp.sum(inner(first) * inner(second), axis=(0, 1))]
    ppermute x2, waiting for transfers between devices: 4.58 us -> 0.01 us  [extended(): lax.ppermute(head, axis, [((i + 1) % count, i) for i in range(ends)])]
    unnamed x8 -> x52, local copies, waits for them, and re-layouts: 0.02 us -> 4.46 us
  transfers between devices with their start and end apart: 29 -> 29, of which waited for: 27 -> 26; matrix products, arithmetic and copies ran while one was open for 1% -> 2% of each run, Pallas kernels for 0% -> 0%
where the time goes in v3:
time: 219 us; the launch traced here: 216 us
  other arithmetic  97.2 us (44%)
  starting transfers between devices  54.6 us (25%)
  waiting for transfers between devices  49 us (22%)
  local copies, waits for them, and re-layouts  13.5 us (6%)
    ppermute x25, starting transfers between devices, all_sum(): lax.ppermute(terms, axis, [(i, i ^ hop) for i in range(count)])  44.1 us
    ppermute x25, waiting for transfers between devices, all_sum(): lax.ppermute(terms, axis, [(i, i ^ hop) for i in range(count)])  37.8 us
    sub x2, other arithmetic, on_device(): residual = residual - step_len * applied  26 us
    mul x5, other arithmetic, apply_q(): applied = mask * stiffen_lanes(weight_ext * stiffness, kappa_ext)  23.1 us
    reduce_sum x5, other arithmetic, dot(): lanes = jnp.sum(inner(first) * inner(second), axis=(0, 1))  14.2 us
    ppermute x2, waiting for transfers between devices, extended(): lax.ppermute(tail, axis, [(i, (i + 1) % count) for i in range(ends)])  11.2 us
    add x2, other arithmetic, stiffen_lanes(): padded[:-2, 1:-1] + padded[2:, 1:-1] + padded[1:-1, :-2] + padded[1:-1, 2:]  9.19 us
    ppermute x2, starting transfers between devices, extended(): lax.ppermute(tail, axis, [(i, (i + 1) % count) for i in range(ends)])  7.92 us
  transfers between devices with their start and end apart: 29, of which 26 were waited for; matrix products, arithmetic and copies ran while one was open for 2% of the time, Pallas kernels for 0%

profile of v3, /device:TPU:0, one launch (start us, length us, event | category | flops | bytes accessed | tf_op | source)
XLA Modules:
  0.0 215.8 jit_solution(2971295408678621874)
XLA Ops:
  1.9 4.9 %collective-permute-start = (f32[67,6,128]{2,1,0:T(8,128)S(1)}, f32[67,6,128]{2,1,0:T(8,128)S(1)}, u32[]{:S(2)}, u32[]{:S(2)}) collective-permute-start(f32[67,6,128]{2,1,0:T(8,128)S(1)} %get-tuple-element.39), channel_id=1, source_target_pairs={{0,4},{4,8},{8,12},{12,16},{16,20},{20,24},{24,28},{1,5},{5,9},{9,... | collective-permute-start | bytes 617480 | tf_op jit(solution)/shard_map/ppermute | solution.py:18
  8.2 10.3 %collective-permute-done = f32[67,6,128]{2,1,0:T(8,128)S(1)} collective-permute-done((f32[67,6,128]{2,1,0:T(8,128)S(1)}, f32[67,6,128]{2,1,0:T(8,128)S(1)}, u32[]{:S(2)}, u32[]{:S(2)}) %collective-permute-start) | collective-permute-done | bytes 205856 | tf_op jit(solution)/shard_map/ppermute | solution.py:18
  24.0 3.0 %collective-permute-start.2 = (f32[67,28,6]{0,1,2:T(8,128)S(1)}, f32[67,28,6]{0,1,2:T(8,128)S(1)}, u32[]{:S(2)}, u32[]{:S(2)}) collective-permute-start(f32[67,28,6]{0,1,2:T(8,128)S(1)} %copy.19), channel_id=1, source_target_pairs={{0,1},{1,2},{2,3},{4,5},{5,6},{6,7},{8,9},{9,10},{10,11},{12,13},{... | collective-permute-start | bytes 135080 | tf_op jit(solution)/shard_map/ppermute | solution.py:18
  31.0 4.1 %maximum_maximum_fusion = (f32[67,28,134]{2,1,0:T(8,128)S(1)}, f32[67,28,134]{2,1,0:T(8,128)S(1)}) fusion(f32[67,6,128]{2,1,0:T(8,128)S(1)} %collective-permute-done.1, f32[1,16,128]{2,1,0:T(8,128)S(1)} %bitcast.35, f32[1,16,128]{2,1,0:T(8,128)S(1)} %bitcast.47, f32[1,16,128]{2,1,0:T(8,128)S(1)} %bitcast.41, f32[64,16,128]{2,1,0:T(8,128)S(1)} %copy-done.7, ...), kind=kLoop, calls=%fused_computation.3 | loop fusion | flops 3016608 | bytes 3061632 | tf_op jit(solution)/shard_map/concatenate | solution.py:16
  37.7 5.8 %fusion.14 = (f32[28,76,128]{1,0,2:T(8,128)S(1)}, f32[28,76,128]{1,0,2:T(8,128)}, f32[28,76,128]{1,0,2:T(8,128)}) fusion(f32[28,76,64]{1,0,2:T(8,128)S(1)} %broadcast_in_dim.63, f32[28,76,64]{1,0,2:T(8,128)S(1)} %broadcast_in_dim.61, f32[28,76,128]{1,0,2:T(8,128)S(1)} %pad_maximum_fusion, f32[28,76,64]{1,0,2:T(8,128)S(1)} %broadcast_in_dim.59, ...), kind=kLoop, calls=%fused_computation.22 | loop fusion | flops 4085760 | bytes 6537216 | tf_op jit(solution)/shard_map/mul | solution.py:113
  43.5 4.1 %fusion.7 = f32[28,76,128]{1,0,2:T(8,128)S(1)} fusion(f32[28,76,128]{1,0,2:T(8,128)S(1)} %get-tuple-element.14, f32[28,76,64]{1,0,2:T(8,128)S(1)} %broadcast_in_dim.59, f32[28,76,64]{1,0,2:T(8,128)S(1)} %broadcast_in_dim.57, pred[76,128]{0,1:T(8,128)(4,1)S(1)} %pad_add_fusion, pred[28]{0:T(512)(128)(4,1)S(1)} %compare_and_fusion.2), kind=kLoop, calls=%fused_computation.14 | loop fusion | flops 4085760 | bytes 3278364 | tf_op jit(solution)/shard_map/mul | solution.py:113
  47.6 4.1 %multiply_reduce_fusion = (f32[128]{0:T(128)S(1)}, f32[128]{0:T(128)S(1)}) fusion(f32[28,76,64]{1,0,2:T(8,128)S(1)} %get-tuple-element.48, f32[28,76,64]{1,0,2:T(8,128)S(1)} %get-tuple-element.49, f32[28,76,128]{1,0,2:T(8,128)S(1)} %fusion.7), kind=kLoop, calls=%fused_computation.130 | loop fusion | flops 786176 | bytes 1614848 | tf_op jit(solution)/shard_map/reduce_sum | solution.py:105
  54.7 2.7 %collective-permute-start.5 = (f32[2,64]{1,0:T(2,128)S(1)}, f32[2,64]{1,0:T(2,128)S(1)}, u32[]{:S(2)}, u32[]{:S(2)}) collective-permute-start(f32[2,64]{1,0:T(2,128)S(1)} %fusion.63), channel_id=1, source_target_pairs={{0,2},{1,3},{2,0},{3,1},{4,6},{5,7},{6,4},{7,5},{8,10},{9,11},{10,... | collective-permute-start | bytes 1544 | tf_op jit(solution)/shard_map/ppermute | solution.py:54
  58.9 2.6 %collective-permute-start.6 = (f32[2,64]{1,0:T(2,128)S(1)}, f32[2,64]{1,0:T(2,128)S(1)}, u32[]{:S(2)}, u32[]{:S(2)}) collective-permute-start(f32[2,64]{1,0:T(2,128)S(1)} %fusion.69), channel_id=1, source_target_pairs={{0,4},{4,0},{8,12},{12,8},{16,20},{20,16},{24,28},{28,24},{1,5},{5... | collective-permute-start | bytes 1544 | tf_op jit(solution)/shard_map/ppermute | solution.py:54
  63.0 3.1 %collective-permute-start.7 = (f32[2,64]{1,0:T(2,128)S(1)}, f32[2,64]{1,0:T(2,128)S(1)}, u32[]{:S(2)}, u32[]{:S(2)}) collective-permute-start(f32[2,64]{1,0:T(2,128)S(1)} %add.353), channel_id=1, source_target_pairs={{0,8},{4,12},{8,0},{12,4},{16,24},{20,28},{24,16},{28,20},{1,9},{5... | collective-permute-start | bytes 1544 | tf_op jit(solution)/shard_map/ppermute | solution.py:54
  67.7 3.0 %collective-permute-start.8 = (f32[2,64]{1,0:T(2,128)S(1)}, f32[2,64]{1,0:T(2,128)S(1)}, u32[]{:S(2)}, u32[]{:S(2)}) collective-permute-start(f32[2,64]{1,0:T(2,128)S(1)} %add.354), channel_id=1, source_target_pairs={{0,16},{4,20},{8,24},{12,28},{16,0},{20,4},{24,8},{28,12},{1,17},{... | collective-permute-start | bytes 1544 | tf_op jit(solution)/shard_map/ppermute | solution.py:54
  72.4 13.1 %multiply_subtract_fusion.1 = f32[28,76,128]{1,0,2:T(8,128)S(1)} fusion(f32[128]{0:T(128)S(1)} %mul.195, f32[28,76,64]{1,0,2:T(8,128)S(1)} %get-tuple-element.48, f32[28,76,64]{1,0,2:T(8,128)} %copy-done, f32[28,76,128]{1,0,2:T(8,128)} %copy-done.5, f32[28,76,64]{1,0,2:T(8,128)S(1)} %broadcast_in_dim.59, f32[28,76,64]{1,0,2:T(8,128)S(1)} %broadcast_in_dim.57, ...), kind=kLoop, calls=%fused_computation.63 | loop fusion | flops 4902912 | bytes 4368412 | tf_op jit(solution)/shard_map/sub | solution.py:130
  94.6 2.7 %collective-permute-done.11 = f32[64]{0:T(128)S(1)} collective-permute-done((f32[64]{0:T(128)S(1)}, f32[64]{0:T(128)S(1)}, u32[]{:S(2)}, u32[]{:S(2)}) %collective-permute-start.11) | collective-permute-done | bytes 288 | tf_op jit(solution)/shard_map/ppermute | solution.py:54
  101.0 2.9 %collective-permute-start.13 = (f32[64]{0:T(128)S(1)}, f32[64]{0:T(128)S(1)}, u32[]{:S(2)}, u32[]{:S(2)}) collective-permute-start(f32[64]{0:T(128)S(1)} %add.359), channel_id=1, source_target_pairs={{0,16},{4,20},{8,24},{12,28},{16,0},{20,4},{24,8},{28,12},{1,17},{... | collective-permute-start | bytes 776 | tf_op jit(solution)/shard_map/ppermute | solution.py:54
  105.5 2.3 %multiply_add_fusion.2 = f32[28,76,128]{1,0,2:T(8,128)S(1)} fusion(f32[28,76,128]{1,0,2:T(8,128)} %copy-done.4, f32[128]{0:T(128)S(1)} %mul.200, f32[28,76,64]{1,0,2:T(8,128)S(1)} %get-tuple-element.48, f32[28,76,64]{1,0,2:T(8,128)} %copy-done), kind=kLoop, calls=%fused_computation.62 | loop fusion | flops 817152 | bytes 3269120 | tf_op jit(solution)/shard_map/add | solution.py:132
  108.0 4.3 %fusion.9 = f32[28,76,128]{1,0,2:T(8,128)S(1)} fusion(f32[28,76,128]{1,0,2:T(8,128)S(1)} %multiply_add_fusion.2, f32[28,76,64]{1,0,2:T(8,128)S(1)} %broadcast_in_dim.59, f32[28,76,64]{1,0,2:T(8,128)S(1)} %broadcast_in_dim.57, f32[28,76,64]{1,0,2:T(8,128)S(1)} %copy-done.12, f32[28,76,64]{1,0,2:T(8,128)S(1)} %copy-done.15), kind=kLoop, calls=%fused_computation.16 | loop fusion | flops 4085760 | bytes 4358144 | tf_op jit(solution)/shard_map/mul | solution.py:113
  112.4 4.2 %fusion.11 = f32[28,76,128]{1,0,2:T(8,128)S(1)} fusion(f32[28,76,128]{1,0,2:T(8,128)S(1)} %fusion.9, f32[28,76,64]{1,0,2:T(8,128)S(1)} %broadcast_in_dim.59, f32[28,76,64]{1,0,2:T(8,128)S(1)} %broadcast_in_dim.57, pred[76,128]{0,1:T(8,128)(4,1)S(1)} %pad_add_fusion, pred[28]{0:T(512)(128)(4,1)S(1)} %compare_and_fusion.2), kind=kLoop, calls=%fused_computation.18 | loop fusion | flops 4085760 | bytes 3278364 | tf_op jit(solution)/shard_map/mul | solution.py:113
  116.6 2.1 fusion.53
  124.4 2.7 %collective-permute-done.16 = f32[64]{0:T(128)S(1)} collective-permute-done((f32[64]{0:T(128)S(1)}, f32[64]{0:T(128)S(1)}, u32[]{:S(2)}, u32[]{:S(2)}) %collective-permute-start.16) | collective-permute-done | bytes 288 | tf_op jit(solution)/shard_map/ppermute | solution.py:54
  130.7 2.9 %collective-permute-start.18 = (f32[64]{0:T(128)S(1)}, f32[64]{0:T(128)S(1)}, u32[]{:S(2)}, u32[]{:S(2)}) collective-permute-start(f32[64]{0:T(128)S(1)} %add.379), channel_id=1, source_target_pairs={{0,16},{4,20},{8,24},{12,28},{16,0},{20,4},{24,8},{28,12},{1,17},{... | collective-permute-start | bytes 776 | tf_op jit(solution)/shard_map/ppermute | solution.py:54
  135.3 12.9 %multiply_subtract_fusion = f32[28,76,128]{1,0,2:T(8,128)S(1)} fusion(f32[28,76,128]{1,0,2:T(8,128)} %copy-done.4, f32[128]{0:T(128)S(1)} %mul.210, f32[28,76,128]{1,0,2:T(8,128)} %copy-done.6, f32[28,76,64]{1,0,2:T(8,128)S(1)} %broadcast_in_dim.59, f32[28,76,64]{1,0,2:T(8,128)S(1)} %broadcast_in_dim.57, pred[76,128]{0,1:T(8,128)(4,1)S(1)} %pad_add_fusion, ...), kind=kLoop, calls=%fused_computation.39 | loop fusion | flops 4630528 | bytes 4368412 | tf_op jit(solution)/shard_map/sub | solution.py:130
  157.4 2.7 %collective-permute-done.21 = f32[64]{0:T(128)S(1)} collective-permute-done((f32[64]{0:T(128)S(1)}, f32[64]{0:T(128)S(1)}, u32[]{:S(2)}, u32[]{:S(2)}) %collective-permute-start.21) | collective-permute-done | bytes 288 | tf_op jit(solution)/shard_map/ppermute | solution.py:54
  163.7 2.9 %collective-permute-start.23 = (f32[64]{0:T(128)S(1)}, f32[64]{0:T(128)S(1)}, u32[]{:S(2)}, u32[]{:S(2)}) collective-permute-start(f32[64]{0:T(128)S(1)} %add.385), channel_id=1, source_target_pairs={{0,16},{4,20},{8,24},{12,28},{16,0},{20,4},{24,8},{28,12},{1,17},{... | collective-permute-start | bytes 776 | tf_op jit(solution)/shard_map/ppermute | solution.py:54
  168.2 2.6 %multiply_add_fusion.1 = f32[28,76,128]{1,0,2:T(8,128)S(1)} fusion(f32[28,76,128]{1,0,2:T(8,128)} %copy-done.3, f32[28,76,128]{1,0,2:T(8,128)} %copy-done.2, f32[128]{0:T(128)S(1)} %mul.215), kind=kLoop, calls=%fused_computation.38 | loop fusion | flops 544768 | bytes 3269120 | tf_op jit(solution)/shard_map/add | solution.py:132
  171.1 4.7 %fusion.13 = f32[28,76,128]{1,0,2:T(8,128)S(1)} fusion(f32[28,76,128]{1,0,2:T(8,128)S(1)} %multiply_add_fusion.1, f32[28,76,64]{1,0,2:T(8,128)S(1)} %broadcast_in_dim.59, f32[28,76,64]{1,0,2:T(8,128)S(1)} %broadcast_in_dim.57, f32[28,76,64]{1,0,2:T(8,128)S(1)} %copy-done.13, f32[28,76,64]{1,0,2:T(8,128)S(1)} %copy-done.16), kind=kLoop, calls=%fused_computation.20 | loop fusion | flops 4085760 | bytes 4358144 | tf_op jit(solution)/shard_map/mul | solution.py:113
  175.8 3.6 %slice_add_fusion.2 = (f32[28,76,128]{1,0,2:T(8,128)S(1)}, f32[28,76,128]{1,0,2:T(8,128)S(1)}, f32[28,76,128]{1,0,2:T(8,128)S(1)}, f32[28,76,128]{1,0,2:T(8,128)S(1)}, f32[28,76,128]{1,0,2:T(8,128)S(1)}) fusion(f32[28,76,128]{1,0,2:T(8,128)S(1)} %fusion.13), kind=kLoop, calls=%fused_computation.26 | loop fusion | flops 817152 | bytes 6537216 | tf_op jit(solution)/shard_map/add | solution.py:62
  179.5 3.9 %fusion.48 = f32[128]{0:T(128)S(1)} fusion(f32[28,76,128]{1,0,2:T(8,128)S(1)} %fusion.13, f32[28,76,128]{1,0,2:T(8,128)S(1)} %get-tuple-element.33, f32[28,76,128]{1,0,2:T(8,128)S(1)} %get-tuple-element.31, f32[28,76,128]{1,0,2:T(8,128)S(1)} %get-tuple-element.34, f32[28,76,128]{1,0,2:T(8,128)S(1)} %get-tuple-element.32, ...), kind=kLoop, calls=%fused_computation.110 | loop fusion | flops 1441664 | bytes 4325888 | tf_op jit(solution)/shard_map/reduce_sum | solution.py:105
  189.1 2.8 %pad_maximum_fusion.2 = f32[67,28,140]{2,1,0:T(8,128)S(1)} fusion(f32[67,28,6]{2,1,0:T(8,128)} %copy.22, f32[67,6,128]{2,1,0:T(8,128)S(1)} %copy-done.20, f32[1,16,128]{2,1,0:T(8,128)S(1)} %bitcast.38, f32[1,16,128]{2,1,0:T(8,128)S(1)} %bitcast.50, f32[1,16,128]{2,1,0:T(8,128)S(1)} %bitcast.44, f32[64,16,128]{2,1,0:T(8,128)S(1)} %copy-done.8, ...), kind=kLoop, calls=%fused_computation.5 | loop fusion | flops 1838480 | bytes 2101120 | tf_op jit(solution)/shard_map/concatenate | solution.py:16
  195.5 2.8 %collective-permute-start.28 = (f32[64]{0:T(128)S(1)}, f32[64]{0:T(128)S(1)}, u32[]{:S(2)}, u32[]{:S(2)}) collective-permute-start(f32[64]{0:T(128)S(1)} %add.405), channel_id=1, source_target_pairs={{0,16},{4,20},{8,24},{12,28},{16,0},{20,4},{24,8},{28,12},{1,17},{... | collective-permute-start | bytes 776 | tf_op jit(solution)/shard_map/ppermute | solution.py:54
  200.1 2.8 %multiply_add_fusion = f32[28,76,128]{1,0,2:T(8,128)S(1)} fusion(f32[28,76,128]{1,0,2:T(8,128)} %copy-done.2, f32[128]{0:T(128)S(1)} %mul.225, f32[128]{0:T(128)S(1)} %mul.210, f32[128]{0:T(128)S(1)} %mul.195, f32[28,76,128]{1,0,2:T(8,128)} %copy-done.3, f32[128]{0:T(128)S(1)} %mul.215, f32[28,76,64]{1,0,2:T(8,128)S(1)} %get-tuple-element.48, ...), kind=kLoop, calls=%fused_computation.24 | loop fusion | flops 2179072 | bytes 4360192 | tf_op jit(solution)/shard_map/add | solution.py:128
  202.9 5.6 %slice_add_fusion = (f32[28,76,128]{1,0,2:T(8,128)S(1)}, f32[28,76,128]{1,0,2:T(8,128)S(1)}, f32[28,76,128]{1,0,2:T(8,128)S(1)}, f32[28,76,128]{1,0,2:T(8,128)S(...) fusion(f32[28,76,128]{1,0,2:T(8,128)S(1)} %multiply_add_fusion), kind=kLoop, calls=%fused_computation.23 | loop fusion | flops 272384 | bytes 8716288 | tf_op jit(solution)/shard_map/add | solution.py:62
  208.5 5.5 %bitcast_reduce_fusion = (f32[16,64,2]{1,0,2:T(8,128)S(1)}, f32[16,64,2]{1,0,2:T(8,128)S(1)}) fusion(f32[28,76,128]{1,0,2:T(8,128)S(1)} %copy-done.21, f32[28,76,64]{1,0,2:T(8,128)S(1)} %get-tuple-element.48, f32[28,76,64]{1,0,2:T(8,128)S(1)} %copy-done.1, f32[28,76,128]{1,0,2:T(8,128)S(1)} %multiply_add_fusion, f32[28,76,128]{1,0,2:T(8,128)} %get-tuple-element.28, ...), kind=kLoop, calls=%fused_computation.127 | loop fusion | flops 2224128 | bytes 6348800 | tf_op jit(solution)/shard_map/reduce_sum | solution.py:141
  (180 shorter events, 76.4 us)
Async XLA Ops:
  0.6 17.8 %copy-start.7 = (f32[64,16,128]{2,1,0:T(8,128)S(1)}, f32[64,16,128]{2,1,0:T(8,128)}, u32[]{:S(2)}) copy-start(f32[64,16,128]{2,1,0:T(8,128)} %param.4) | copy-start | bytes 1572868
  0.6 17.8 %copy-start.23 = (f32[16,128]{1,0:T(8,128)S(1)}, f32[16,128]{1,0:T(8,128)}, u32[]{:S(2)}) copy-start(f32[16,128]{1,0:T(8,128)} %param.7) | copy-start | bytes 24580
  0.7 17.8 %copy-start.24 = (f32[16,128]{1,0:T(8,128)S(1)}, f32[16,128]{1,0:T(8,128)}, u32[]{:S(2)}) copy-start(f32[16,128]{1,0:T(8,128)} %param.5) | copy-start | bytes 24580
  1.9 16.6 %collective-permute-start = (f32[67,6,128]{2,1,0:T(8,128)S(1)}, f32[67,6,128]{2,1,0:T(8,128)S(1)}, u32[]{:S(2)}, u32[]{:S(2)}) collective-permute-start(f32[67,6,128]{2,1,0:T(8,128)S(1)} %get-tuple-element.39), channel_id=1, source_target_pairs={{0,4},{4,8},{8,12},{12,16},{16,20},{20,24},{24,28},{1,5},{5,9},{9,... | collective-permute-start | bytes 617480 | tf_op jit(solution)/shard_map/ppermute | solution.py:18
  6.8 11.7 %collective-permute-start.1 = (f32[67,6,128]{2,1,0:T(8,128)S(1)}, f32[67,6,128]{2,1,0:T(8,128)S(1)}, u32[]{:S(2)}, u32[]{:S(2)}) collective-permute-start(f32[67,6,128]{2,1,0:T(8,128)S(1)} %get-tuple-element.40), channel_id=1, source_target_pairs={{4,0},{8,4},{12,8},{16,12},{20,16},{24,20},{28,24},{5,1},{9,5},{13... | collective-permute-start | bytes 617480 | tf_op jit(solution)/shard_map/ppermute | solution.py:20
  22.7 6.3 %collective-permute-start.3 = (f32[67,28,6]{0,1,2:T(8,128)S(1)}, f32[67,28,6]{0,1,2:T(8,128)S(1)}, u32[]{:S(2)}, u32[]{:S(2)}) collective-permute-start(f32[67,28,6]{0,1,2:T(8,128)S(1)} %copy.21), channel_id=1, source_target_pairs={{1,0},{2,1},{3,2},{5,4},{6,5},{7,6},{9,8},{10,9},{11,10},{13,12},{... | collective-permute-start | bytes 135080 | tf_op jit(solution)/shard_map/ppermute | solution.py:20
  24.0 4.0 %collective-permute-start.2 = (f32[67,28,6]{0,1,2:T(8,128)S(1)}, f32[67,28,6]{0,1,2:T(8,128)S(1)}, u32[]{:S(2)}, u32[]{:S(2)}) collective-permute-start(f32[67,28,6]{0,1,2:T(8,128)S(1)} %copy.19), channel_id=1, source_target_pairs={{0,1},{1,2},{2,3},{4,5},{5,6},{6,7},{8,9},{9,10},{10,11},{12,13},{... | collective-permute-start | bytes 135080 | tf_op jit(solution)/shard_map/ppermute | solution.py:18
  51.9 2.7 %collective-permute-start.4 = (f32[2,64]{1,0:T(2,128)S(1)}, f32[2,64]{1,0:T(2,128)S(1)}, u32[]{:S(2)}, u32[]{:S(2)}) collective-permute-start(f32[2,64]{1,0:T(2,128)S(1)} %pad_maximum_fusion.6), channel_id=1, source_target_pairs={{0,1},{1,0},{2,3},{3,2},{4,5},{5,4},{6,7},{7,6},{8,9},{9,8},{10,11... | collective-permute-start | bytes 1544 | tf_op jit(solution)/shard_map/ppermute | solution.py:54
  54.7 4.2 %collective-permute-start.5 = (f32[2,64]{1,0:T(2,128)S(1)}, f32[2,64]{1,0:T(2,128)S(1)}, u32[]{:S(2)}, u32[]{:S(2)}) collective-permute-start(f32[2,64]{1,0:T(2,128)S(1)} %fusion.63), channel_id=1, source_target_pairs={{0,2},{1,3},{2,0},{3,1},{4,6},{5,7},{6,4},{7,5},{8,10},{9,11},{10,... | collective-permute-start | bytes 1544 | tf_op jit(solution)/shard_map/ppermute | solution.py:54
  58.9 4.1 %collective-permute-start.6 = (f32[2,64]{1,0:T(2,128)S(1)}, f32[2,64]{1,0:T(2,128)S(1)}, u32[]{:S(2)}, u32[]{:S(2)}) collective-permute-start(f32[2,64]{1,0:T(2,128)S(1)} %fusion.69), channel_id=1, source_target_pairs={{0,4},{4,0},{8,12},{12,8},{16,20},{20,16},{24,28},{28,24},{1,5},{5... | collective-permute-start | bytes 1544 | tf_op jit(solution)/shard_map/ppermute | solution.py:54
  63.0 4.7 %collective-permute-start.7 = (f32[2,64]{1,0:T(2,128)S(1)}, f32[2,64]{1,0:T(2,128)S(1)}, u32[]{:S(2)}, u32[]{:S(2)}) collective-permute-start(f32[2,64]{1,0:T(2,128)S(1)} %add.353), channel_id=1, source_target_pairs={{0,8},{4,12},{8,0},{12,4},{16,24},{20,28},{24,16},{28,20},{1,9},{5... | collective-permute-start | bytes 1544 | tf_op jit(solution)/shard_map/ppermute | solution.py:54
  67.7 4.6 %collective-permute-start.8 = (f32[2,64]{1,0:T(2,128)S(1)}, f32[2,64]{1,0:T(2,128)S(1)}, u32[]{:S(2)}, u32[]{:S(2)}) collective-permute-start(f32[2,64]{1,0:T(2,128)S(1)} %add.354), channel_id=1, source_target_pairs={{0,16},{4,20},{8,24},{12,28},{16,0},{20,4},{24,8},{28,12},{1,17},{... | collective-permute-start | bytes 1544 | tf_op jit(solution)/shard_map/ppermute | solution.py:54
  89.0 1.2 collective-permute-start.9
  90.3 3.6 %collective-permute-start.10 = (f32[64]{0:T(128)S(1)}, f32[64]{0:T(128)S(1)}, u32[]{:S(2)}, u32[]{:S(2)}) collective-permute-start(f32[64]{0:T(128)S(1)} %add.356), channel_id=1, source_target_pairs={{0,2},{1,3},{2,0},{3,1},{4,6},{5,7},{6,4},{7,5},{8,10},{9,11},{10,... | collective-permute-start | bytes 776 | tf_op jit(solution)/shard_map/ppermute | solution.py:54
  93.8 3.6 %collective-permute-start.11 = (f32[64]{0:T(128)S(1)}, f32[64]{0:T(128)S(1)}, u32[]{:S(2)}, u32[]{:S(2)}) collective-permute-start(f32[64]{0:T(128)S(1)} %add.357), channel_id=1, source_target_pairs={{0,4},{4,0},{8,12},{12,8},{16,20},{20,16},{24,28},{28,24},{1,5},{5... | collective-permute-start | bytes 776 | tf_op jit(solution)/shard_map/ppermute | solution.py:54
  97.4 3.6 %collective-permute-start.12 = (f32[64]{0:T(128)S(1)}, f32[64]{0:T(128)S(1)}, u32[]{:S(2)}, u32[]{:S(2)}) collective-permute-start(f32[64]{0:T(128)S(1)} %add.358), channel_id=1, source_target_pairs={{0,8},{4,12},{8,0},{12,4},{16,24},{20,28},{24,16},{28,20},{1,9},{5... | collective-permute-start | bytes 776 | tf_op jit(solution)/shard_map/ppermute | solution.py:54
  101.0 4.5 %collective-permute-start.13 = (f32[64]{0:T(128)S(1)}, f32[64]{0:T(128)S(1)}, u32[]{:S(2)}, u32[]{:S(2)}) collective-permute-start(f32[64]{0:T(128)S(1)} %add.359), channel_id=1, source_target_pairs={{0,16},{4,20},{8,24},{12,28},{16,0},{20,4},{24,8},{28,12},{1,17},{... | collective-permute-start | bytes 776 | tf_op jit(solution)/shard_map/ppermute | solution.py:54
  118.8 1.2 collective-permute-start.14
  120.0 3.6 %collective-permute-start.15 = (f32[64]{0:T(128)S(1)}, f32[64]{0:T(128)S(1)}, u32[]{:S(2)}, u32[]{:S(2)}) collective-permute-start(f32[64]{0:T(128)S(1)} %add.376), channel_id=1, source_target_pairs={{0,2},{1,3},{2,0},{3,1},{4,6},{5,7},{6,4},{7,5},{8,10},{9,11},{10,... | collective-permute-start | bytes 776 | tf_op jit(solution)/shard_map/ppermute | solution.py:54
  123.6 3.6 %collective-permute-start.16 = (f32[64]{0:T(128)S(1)}, f32[64]{0:T(128)S(1)}, u32[]{:S(2)}, u32[]{:S(2)}) collective-permute-start(f32[64]{0:T(128)S(1)} %add.377), channel_id=1, source_target_pairs={{0,4},{4,0},{8,12},{12,8},{16,20},{20,16},{24,28},{28,24},{1,5},{5... | collective-permute-start | bytes 776 | tf_op jit(solution)/shard_map/ppermute | solution.py:54
  127.1 3.6 %collective-permute-start.17 = (f32[64]{0:T(128)S(1)}, f32[64]{0:T(128)S(1)}, u32[]{:S(2)}, u32[]{:S(2)}) collective-permute-start(f32[64]{0:T(128)S(1)} %add.378), channel_id=1, source_target_pairs={{0,8},{4,12},{8,0},{12,4},{16,24},{20,28},{24,16},{28,20},{1,9},{5... | collective-permute-start | bytes 776 | tf_op jit(solution)/shard_map/ppermute | solution.py:54
  130.7 4.5 %collective-permute-start.18 = (f32[64]{0:T(128)S(1)}, f32[64]{0:T(128)S(1)}, u32[]{:S(2)}, u32[]{:S(2)}) collective-permute-start(f32[64]{0:T(128)S(1)} %add.379), channel_id=1, source_target_pairs={{0,16},{4,20},{8,24},{12,28},{16,0},{20,4},{24,8},{28,12},{1,17},{... | collective-permute-start | bytes 776 | tf_op jit(solution)/shard_map/ppermute | solution.py:54
  151.7 1.2 collective-permute-start.19
  153.0 3.6 %collective-permute-start.20 = (f32[64]{0:T(128)S(1)}, f32[64]{0:T(128)S(1)}, u32[]{:S(2)}, u32[]{:S(2)}) collective-permute-start(f32[64]{0:T(128)S(1)} %add.382), channel_id=1, source_target_pairs={{0,2},{1,3},{2,0},{3,1},{4,6},{5,7},{6,4},{7,5},{8,10},{9,11},{10,... | collective-permute-start | bytes 776 | tf_op jit(solution)/shard_map/ppermute | solution.py:54
  156.5 3.6 %collective-permute-start.21 = (f32[64]{0:T(128)S(1)}, f32[64]{0:T(128)S(1)}, u32[]{:S(2)}, u32[]{:S(2)}) collective-permute-start(f32[64]{0:T(128)S(1)} %add.383), channel_id=1, source_target_pairs={{0,4},{4,0},{8,12},{12,8},{16,20},{20,16},{24,28},{28,24},{1,5},{5... | collective-permute-start | bytes 776 | tf_op jit(solution)/shard_map/ppermute | solution.py:54
  160.1 3.6 %collective-permute-start.22 = (f32[64]{0:T(128)S(1)}, f32[64]{0:T(128)S(1)}, u32[]{:S(2)}, u32[]{:S(2)}) collective-permute-start(f32[64]{0:T(128)S(1)} %add.384), channel_id=1, source_target_pairs={{0,8},{4,12},{8,0},{12,4},{16,24},{20,28},{24,16},{28,20},{1,9},{5... | collective-permute-start | bytes 776 | tf_op jit(solution)/shard_map/ppermute | solution.py:54
  163.7 4.5 %collective-permute-start.23 = (f32[64]{0:T(128)S(1)}, f32[64]{0:T(128)S(1)}, u32[]{:S(2)}, u32[]{:S(2)}) collective-permute-start(f32[64]{0:T(128)S(1)} %add.385), channel_id=1, source_target_pairs={{0,16},{4,20},{8,24},{12,28},{16,0},{20,4},{24,8},{28,12},{1,17},{... | collective-permute-start | bytes 776 | tf_op jit(solution)/shard_map/ppermute | solution.py:54
  183.5 1.2 collective-permute-start.24
  184.7 3.6 %collective-permute-start.25 = (f32[64]{0:T(128)S(1)}, f32[64]{0:T(128)S(1)}, u32[]{:S(2)}, u32[]{:S(2)}) collective-permute-start(f32[64]{0:T(128)S(1)} %add.402), channel_id=1, source_target_pairs={{0,2},{1,3},{2,0},{3,1},{4,6},{5,7},{6,4},{7,5},{8,10},{9,11},{10,... | collective-permute-start | bytes 776 | tf_op jit(solution)/shard_map/ppermute | solution.py:54
  188.3 3.6 %collective-permute-start.26 = (f32[64]{0:T(128)S(1)}, f32[64]{0:T(128)S(1)}, u32[]{:S(2)}, u32[]{:S(2)}) collective-permute-start(f32[64]{0:T(128)S(1)} %add.403), channel_id=1, source_target_pairs={{0,4},{4,0},{8,12},{12,8},{16,20},{20,16},{24,28},{28,24},{1,5},{5... | collective-permute-start | bytes 776 | tf_op jit(solution)/shard_map/ppermute | solution.py:54
  191.9 3.6 %collective-permute-start.27 = (f32[64]{0:T(128)S(1)}, f32[64]{0:T(128)S(1)}, u32[]{:S(2)}, u32[]{:S(2)}) collective-permute-start(f32[64]{0:T(128)S(1)} %add.404), channel_id=1, source_target_pairs={{0,8},{4,12},{8,0},{12,4},{16,24},{20,28},{24,16},{28,20},{1,9},{5... | collective-permute-start | bytes 776 | tf_op jit(solution)/shard_map/ppermute | solution.py:54
  195.5 4.5 %collective-permute-start.28 = (f32[64]{0:T(128)S(1)}, f32[64]{0:T(128)S(1)}, u32[]{:S(2)}, u32[]{:S(2)}) collective-permute-start(f32[64]{0:T(128)S(1)} %add.405), channel_id=1, source_target_pairs={{0,16},{4,20},{8,24},{12,28},{16,0},{20,4},{24,8},{28,12},{1,17},{... | collective-permute-start | bytes 776 | tf_op jit(solution)/shard_map/ppermute | solution.py:54
  (23 other events, 146.5 us)

commit v4 on v1

v4 whole, which is shorter than its diff:
```python
import jax
import jax.numpy as jnp
from jax import lax
from jax.experimental import pallas as pl
from jax.experimental.pallas import tpu as pltpu
from jax.sharding import PartitionSpec as P

ITERS = 3
HALO = 2 * ITERS


def extended(cells, sides, width):
    for axis, dim in sides:
        count = lax.axis_size(axis)
        ends = count - 1
        head = lax.slice_in_dim(cells, 0, width, axis=dim)
        tail = lax.slice_in_dim(cells, cells.shape[dim] - width, cells.shape[dim], axis=dim)
        cells = jnp.concatenate(
            [
                lax.ppermute(tail, axis, [(i, (i + 1) % count) for i in range(ends)]),
                cells,
                lax.ppermute(head, axis, [((i + 1) % count, i) for i in range(ends)]),
            ],
            axis=dim,
        )
    return cells


def stencil(padded, kappa_sq):
    centre = padded[..., 1:-1, 1:-1]
    edge_sum = (
        padded[..., :-2, 1:-1]
        + padded[..., 2:, 1:-1]
        + padded[..., 1:-1, :-2]
        + padded[..., 1:-1, 2:]
    )
    corners = (
        padded[..., :-2, :-2] + padded[..., :-2, 2:] + padded[..., 2:, :-2] + padded[..., 2:, 2:]
    )
    return (kappa_sq + 20.0 / 6.0) * centre - (4.0 * edge_sum + corners) / 6.0


def stiffen(field, kappa_sq):
    pads = ((0, 0),) * (field.ndim - 2) + ((1, 1), (1, 1))
    return stencil(jnp.pad(field, pads), kappa_sq)


def all_sum(terms):
    for axis in ("cols", "rows"):
        count = lax.axis_size(axis)
        if count & (count - 1):
            terms = lax.psum(terms, axis)
            continue
        hop = 1
        while hop < count:
            terms = terms + lax.ppermute(terms, axis, [(i, i ^ hop) for i in range(count)])
            hop *= 2
    return terms


def _stiffen_row(ref, r, gain):
    mid = ref[r]
    vertical = ref[r - 1] + ref[r + 1]
    n = mid.shape[0]
    edge_sum = vertical + pltpu.roll(mid, 1, 0) + pltpu.roll(mid, n - 1, 0)
    corners = pltpu.roll(vertical, 1, 0) + pltpu.roll(vertical, n - 1, 0)
    return gain * mid - (4.0 * edge_sum + corners) * (1.0 / 6.0)


def _row_sum(value, keep):
    return jnp.sum(jnp.where(keep, value, 0.0), axis=0, keepdims=True)


class _Plan:
    def __init__(self, slab_rows, first_inner, inner_rows):
        self.slab_rows = slab_rows
        self.first_inner = first_inner
        self.inner_rows = inner_rows

    def inner_row(self, r):
        return (r >= self.first_inner) & (r < self.first_inner + self.inner_rows)


def _zero_edges(ref):
    ref[0] = jnp.zeros(ref.shape[1:], ref.dtype)
    ref[ref.shape[0] - 1] = jnp.zeros(ref.shape[1:], ref.dtype)


def _apply_q(plan, source, gain_ref, weight_ref, inside_ref, row_ref, inner_ref, stiff_ref,
             applied_ref, dot_source):
    last = plan.slab_rows - 1
    _zero_edges(stiff_ref)
    _zero_edges(applied_ref)

    def first_pass(r, carry):
        stiff_ref[r] = weight_ref[r] * _stiffen_row(source, r, gain_ref[r])
        return carry

    lax.fori_loop(1, last, first_pass, 0)

    def second_pass(r, totals):
        applied = _stiffen_row(stiff_ref, r, gain_ref[r])
        keep = (inside_ref[...] > 0.5) & (row_ref[r] > 0.5)
        applied = jnp.where(keep, applied, 0.0)
        applied_ref[r] = applied
        inner = (inner_ref[...] > 0.5) & plan.inner_row(r)
        return totals + _row_sum(dot_source[r] * applied, inner)

    return lax.fori_loop(1, last, second_pass, jnp.zeros((1, source.shape[2]), jnp.float32))


def _first_kernel(plan, z_ref, gain_ref, weight_ref, inside_ref, row_ref, inner_ref,
                  stiff_out, applied_out, dots_out, scratch):
    last = plan.slab_rows - 1
    _zero_edges(stiff_out)

    def probe_pass(r, totals):
        stiff_out[r] = _stiffen_row(z_ref, r, gain_ref[r])
        z = z_ref[r]
        inner = (inner_ref[...] > 0.5) & plan.inner_row(r)
        return totals + _row_sum(z * z, inner)

    zz = lax.fori_loop(1, last, probe_pass, jnp.zeros((1, z_ref.shape[2]), jnp.float32))
    _zero_edges(scratch)

    def weigh(r, carry):
        scratch[r] = weight_ref[r] * stiff_out[r]
        return carry

    lax.fori_loop(1, last, weigh, 0)

    def second_pass(r, totals):
        applied = _stiffen_row(scratch, r, gain_ref[r])
        keep = (inside_ref[...] > 0.5) & (row_ref[r] > 0.5)
        applied = jnp.where(keep, applied, 0.0)
        applied_out[r] = applied
        inner = (inner_ref[...] > 0.5) & plan.inner_row(r)
        return totals + _row_sum(z_ref[r] * applied, inner)

    _zero_edges(applied_out)
    za = lax.fori_loop(1, last, second_pass, jnp.zeros((1, z_ref.shape[2]), jnp.float32))
    dots_out[0:1, :] = zz
    dots_out[1:2, :] = za


def _start_kernel(plan, step_ref, z_ref, applied_ref, inner_ref, solution_out, residual_out, rr_out):
    step = step_ref[...]

    def body(r, totals):
        z = z_ref[r]
        residual = z - step * applied_ref[r]
        solution_out[r] = step * z
        residual_out[r] = residual
        inner = (inner_ref[...] > 0.5) & plan.inner_row(r)
        return totals + _row_sum(residual * residual, inner)

    rr_out[...] = lax.fori_loop(0, plan.slab_rows, body, jnp.zeros((1, z_ref.shape[2]), jnp.float32))


def _update_kernel(plan, step_ref, solution_ref, direction_ref, residual_ref, applied_ref, inner_ref,
                   solution_out, residual_out, rr_out):
    step = step_ref[...]

    def body(r, totals):
        residual = residual_ref[r] - step * applied_ref[r]
        solution_out[r] = solution_ref[r] + step * direction_ref[r]
        residual_out[r] = residual
        inner = (inner_ref[...] > 0.5) & plan.inner_row(r)
        return totals + _row_sum(residual * residual, inner)

    rr_out[...] = lax.fori_loop(
        0, plan.slab_rows, body, jnp.zeros((1, residual_ref.shape[2]), jnp.float32)
    )


def _direction_kernel(plan, beta_ref, residual_ref, direction_ref, gain_ref, weight_ref, inside_ref,
                      row_ref, inner_ref, direction_out, applied_out, pa_out, scratch):
    beta = beta_ref[...]

    def new_direction(r, carry):
        direction_out[r] = residual_ref[r] + beta * direction_ref[r]
        return carry

    lax.fori_loop(0, plan.slab_rows, new_direction, 0)
    pa_out[...] = _apply_q(plan, direction_out, gain_ref, weight_ref, inside_ref, row_ref, inner_ref,
                           scratch, applied_out, direction_out)


def _final_kernel(plan, step_ref, solution_ref, direction_ref, z_ref, stiff_ref, gain_ref,
                  weight_out, kappa_out, scratch):
    step = step_ref[...]
    last = plan.slab_rows - 1

    def new_solution(r, carry):
        scratch[r] = solution_ref[r] + step * direction_ref[r]
        return carry

    lax.fori_loop(0, plan.slab_rows, new_solution, 0)
    _zero_edges(weight_out)
    _zero_edges(kappa_out)

    def body(r, carry):
        stiff_solution = _stiffen_row(scratch, r, gain_ref[r])
        stiff_probe = stiff_ref[r]
        weight_out[r] = stiff_solution * stiff_probe
        kappa_out[r] = scratch[r] * stiff_probe + stiff_solution * z_ref[r]
        return carry

    lax.fori_loop(1, last, body, 0)


def _vmem():
    return pl.BlockSpec(memory_space=pltpu.VMEM)


def _call(kernel, plan, inputs, out_shapes, scratch=0, smem=()):
    field = out_shapes[0]
    nbytes = 4 * field.shape[0] * field.shape[1] * field.shape[2]
    in_specs = [
        pl.BlockSpec(memory_space=pltpu.SMEM) if i in smem else _vmem() for i in range(len(inputs))
    ]
    return pl.pallas_call(
        lambda *refs: kernel(plan, *refs),
        out_shape=out_shapes,
        in_specs=in_specs,
        out_specs=tuple(_vmem() for _ in out_shapes),
        scratch_shapes=[pltpu.VMEM(field.shape, jnp.float32)] * scratch,
        cost_estimate=pl.CostEstimate(
            flops=40 * nbytes // 4,
            transcendentals=0,
            bytes_accessed=(len(inputs) + len(out_shapes)) * nbytes,
        ),
    )(*inputs)


def on_device(probes, observed, kappa_sq, variance_weight):
    probe_count, rows, cols = probes.shape
    assert rows >= HALO and cols % 2 == 0 and cols // 2 >= HALO
    half = cols // 2
    width = half + 2 * HALO
    sublanes = -(-width // 8) * 8
    slab_rows = rows + 2 * HALO
    lanes = 2 * probe_count
    stacked = jnp.concatenate(
        [probes, observed[None], kappa_sq[None], variance_weight[None]], axis=0
    )
    ext = extended(stacked, (("rows", 1), ("cols", 2)), HALO)
    halves = [
        jnp.pad(ext[:, :, h * half : h * half + width], ((0, 0), (0, 0), (0, sublanes - width)))
        for h in range(2)
    ]

    def plane_on_lanes(index):
        return jnp.concatenate(
            [jnp.broadcast_to(h[index][:, :, None], h.shape[1:] + (probe_count,)) for h in halves],
            axis=2,
        )

    z = jnp.concatenate([jnp.transpose(h[:probe_count], (1, 2, 0)) for h in halves], axis=2)
    gain = plane_on_lanes(probe_count + 1) + 20.0 / 6.0
    weight = plane_on_lanes(probe_count + 2)

    row_at = lax.axis_index("rows") * rows - HALO + lax.iota(jnp.int32, slab_rows)
    row_in = ((row_at >= 0) & (row_at < rows * lax.axis_size("rows"))).astype(jnp.float32)
    col_in = []
    col_inner = []
    for h in range(2):
        at = lax.iota(jnp.int32, sublanes)
        col_at = lax.axis_index("cols") * cols - HALO + h * half + at
        col_in.append((col_at >= 0) & (col_at < cols * lax.axis_size("cols")) & (at < width))
        col_inner.append((at >= HALO) & (at < HALO + half))

    def on_lanes_of(columns):
        return jnp.concatenate(
            [jnp.broadcast_to(c[:, None], (sublanes, probe_count)) for c in columns], axis=1
        ).astype(jnp.float32)

    inside = on_lanes_of(col_in)
    inner = on_lanes_of(col_inner)
    plan = _Plan(slab_rows, HALO, rows)

    field = jax.ShapeDtypeStruct((slab_rows, sublanes, lanes), jnp.float32)
    lane_row = jax.ShapeDtypeStruct((1, lanes), jnp.float32)

    def per_probe(lane_totals):
        return jnp.sum(lane_totals.reshape(lane_totals.shape[:-1] + (2, probe_count)), axis=-2)

    def on_lane(scalars):
        return jnp.tile(scalars, 2)[None, :]

    stiff_probe, applied, first = _call(
        _first_kernel, plan, (z, gain, weight, inside, row_in, inner),
        (field, field, jax.ShapeDtypeStruct((2, lanes), jnp.float32)), scratch=1, smem=(4,),
    )
    first = all_sum(per_probe(first))
    norm_now = first[0]
    step_len = norm_now / first[1]
    solution, residual, rr = _call(
        _start_kernel, plan, (on_lane(step_len), z, applied, inner), (field, field, lane_row)
    )
    direction = z
    for iteration in range(1, ITERS):
        norm_next = all_sum(per_probe(rr[0]))
        beta = norm_next / norm_now
        norm_now = norm_next
        direction, applied, pa = _call(
            _direction_kernel, plan,
            (on_lane(beta), residual, direction, gain, weight, inside, row_in, inner),
            (field, field, lane_row), scratch=1, smem=(6,),
        )
        step_len = norm_now / all_sum(per_probe(pa[0]))
        if iteration + 1 < ITERS:
            solution, residual, rr = _call(
                _update_kernel, plan,
                (on_lane(step_len), solution, direction, residual, applied, inner),
                (field, field, lane_row),
            )

    weight_terms, kappa_terms = _call(
        _final_kernel, plan, (on_lane(step_len), solution, direction, z, stiff_probe, gain),
        (field, field), scratch=1,
    )

    def probe_total(terms):
        terms = terms[HALO : HALO + rows, HALO : HALO + half]
        per_half = jnp.sum(terms.reshape(rows, half, 2, probe_count), axis=3)
        return jnp.transpose(per_half, (0, 2, 1)).reshape(rows, cols)

    weight_total = probe_total(weight_terms)
    kappa_total = probe_total(kappa_terms)
    stiff_obs = stiffen(ext[probe_count], ext[probe_count + 1])[HALO : HALO + rows, HALO : HALO + cols]
    grad_weight = 0.5 * weight_total / probe_count - 0.5 * stiff_obs * stiff_obs
    grad_kappa = (
        0.5 * variance_weight * (kappa_total / probe_count) - observed * variance_weight * stiff_obs
    )
    return (grad_kappa, grad_weight)


def solution(mesh):
    placed = (P(None, "rows", "cols"), P("rows", "cols"), P("rows", "cols"), P("rows", "cols"))
    return jax.shard_map(
        on_device,
        mesh=mesh,
        in_specs=placed,
        out_specs=(P("rows", "cols"), P("rows", "cols")),
        check_vma=False,
    )
```

time: 174 us -> 212 us (1.22)
  Pallas kernels: 0 us -> 32 us
  local copies, waits for them, and re-layouts: 4.41 us -> 28.8 us
  other arithmetic: 62.3 us -> 40.8 us
  waiting for transfers between devices: 50.6 us -> 65.1 us
  starting transfers between devices: 55.4 us -> 43.6 us
    pallas_call x0 -> x6, Pallas kernels: none -> 32 us  [_call(): pl.pallas_call(lambda *refs: kernel(plan, *refs), out_shape=out_shapes, i...]
    mul x5 -> x0, other arithmetic: 20.6 us -> none  [apply_q(): applied = mask * stiffen(weight_ext * stiffness, kappa_ext)]
    another operation x0 -> x14, local copies, waits for them, and re-layouts: none -> 13.1 us  [the longest x10 8.04 us: on_lane(): return jnp.tile(scalars, 2)[None, :]]
    add x3 -> x1, other arithmetic: 13 us -> 0.11 us  [stencil(): padded[..., :-2, 1:-1] + padded[..., 2:, 1:-1] + padded[..., 1:-1, :-2]]
    ppermute x25, starting transfers between devices: 44.2 us -> 34.9 us  [all_sum(): lax.ppermute(terms, axis, [(i, i ^ hop) for i in range(count)])]
    sub x2 -> x0, other arithmetic: 8.4 us -> none  [on_device(): residual = residual - step_len * applied]
    ppermute x25, waiting for transfers between devices: 40 us -> 48.4 us  [all_sum(): lax.ppermute(terms, axis, [(i, i ^ hop) for i in range(count)])]
    ppermute x2, waiting for transfers between devices: 6.03 us -> 13.6 us  [extended(): lax.ppermute(tail, axis, [(i, (i + 1) % count) for i in range(ends)])]
  transfers between devices with their start and end apart: 29 -> 29, of which waited for: 27 -> 26; matrix products, arithmetic and copies ran while one was open for 1% -> 4% of each run, Pallas kernels for 0% -> 0%
where the time goes in v4:
time: 212 us; the launch traced here: 211 us
  waiting for transfers between devices  65.1 us (31%)
  starting transfers between devices  43.6 us (21%)
  other arithmetic  40.8 us (19%)
  Pallas kernels  32 us (15%)
  local copies, waits for them, and re-layouts  28.8 us (14%)
    ppermute x25, waiting for transfers between devices, all_sum(): lax.ppermute(terms, axis, [(i, i ^ hop) for i in range(count)])  48.4 us
    ppermute x25, starting transfers between devices, all_sum(): lax.ppermute(terms, axis, [(i, i ^ hop) for i in range(count)])  34.9 us
    pallas_call x6, Pallas kernels, _call(): pl.pallas_call(lambda *refs: kernel(plan, *refs), out_shape=out_shapes, i...  32 us
    ppermute x2, waiting for transfers between devices, extended(): lax.ppermute(tail, axis, [(i, (i + 1) % count) for i in range(ends)])  13.6 us
    another operation x10, local copies, waits for them, and re-layouts, on_lane(): return jnp.tile(scalars, 2)[None, :]  8.04 us
    pallas_call x4, other arithmetic, _call(): pl.pallas_call(lambda *refs: kernel(plan, *refs), out_shape=out_shapes, i...  7.32 us
    ppermute x2, starting transfers between devices, extended(): lax.ppermute(tail, axis, [(i, (i + 1) % count) for i in range(ends)])  6.18 us
    reduce_sum x5, other arithmetic, per_probe(): jnp.sum(lane_totals.reshape(lane_totals.shape[:-1] + (2, probe_count)), a...  6.14 us
  transfers between devices with their start and end apart: 29, of which 26 were waited for; matrix products, arithmetic and copies ran while one was open for 4% of the time, Pallas kernels for 0%

profile of v4, /device:TPU:0, one launch (start us, length us, event | category | flops | bytes accessed | tf_op | source)
XLA Modules:
  0.0 211.3 jit_solution(16642813434175970861)
XLA Ops:
  4.2 2.7 %pad_maximum_fusion.12 = (f32[67,6,128]{0,2,1:T(8,128)}, f32[67,6,128]{0,2,1:T(8,128)}) fusion(f32[1,16,128]{0,2,1:T(8,128)S(1)} %copy.23, f32[1,16,128]{0,2,1:T(8,128)S(1)} %copy.22, f32[1,16,128]{0,2,1:T(8,128)} %copy.21, f32[64,16,128]{0,2,1:T(8,128)S(1)} %copy.20), kind=kLoop, calls=%fused_computation.36 | loop fusion | flops 308736 | bytes 960512 | tf_op jit(solution)/shard_map/slice | solution.py:17
  6.9 4.9 %collective-permute-start = (f32[67,6,128]{0,2,1:T(8,128)}, f32[67,6,128]{0,2,1:T(8,128)S(1)}, u32[]{:S(2)}, u32[]{:S(2)}) collective-permute-start(f32[67,6,128]{0,2,1:T(8,128)} %get-tuple-element.50), channel_id=1, source_target_pairs={{0,4},{4,8},{8,12},{12,16},{16,20},{20,24},{24,28},{1,5},{5,9},{9,... | collective-permute-start | bytes 617480 | tf_op jit(solution)/shard_map/ppermute | solution.py:20
  15.2 13.6 %collective-permute-done = f32[67,6,128]{0,2,1:T(8,128)S(1)} collective-permute-done((f32[67,6,128]{0,2,1:T(8,128)}, f32[67,6,128]{0,2,1:T(8,128)S(1)}, u32[]{:S(2)}, u32[]{:S(2)}) %collective-permute-start) | collective-permute-done | bytes 205856 | tf_op jit(solution)/shard_map/ppermute | solution.py:20
  33.1 3.1 %collective-permute-done.3 = f32[67,28,6]{0,2,1:T(8,128)S(1)} collective-permute-done((f32[67,28,6]{0,2,1:T(8,128)S(1)}, f32[67,28,6]{0,2,1:T(8,128)S(1)}, u32[]{:S(2)}, u32[]{:S(2)}) %collective-permute-start.3) | collective-permute-done | bytes 45056 | tf_op jit(solution)/shard_map/ppermute | solution.py:22
  36.2 2.2 %fusion.8 = (f32[67,28,80]{0,2,1:T(8,128)S(1)}, f32[67,28,80]{0,2,1:T(8,128)S(1)}) fusion(f32[67,28,6]{0,2,1:T(8,128)S(1)} %collective-permute-done.2, f32[67,6,128]{0,2,1:T(8,128)} %collective-permute-done.1, f32[67,6,128]{0,2,1:T(8,128)S(1)} %collective-permute-done, f32[1,16,128]{0,2,1:T(8,128)S(1)} %copy.23, f32[1,16,128]{0,2,1:T(8,128)S(1)} %copy.22, ...), kind=kLoop, calls=%fused_computation.22 | loop fusion | flops 3151680 | bytes 2251280 | tf_op jit(solution)/shard_map/jit(_pad)/pad | solution.py:249
  38.4 3.2 %slice_reduce_fusion.1 = (f32[28,80]{1,0:T(8,128)S(1)}, f32[28,80]{1,0:T(8,128)S(1)}, f32[28,80]{1,0:T(8,128)S(1)}, f32[28,80]{1,0:T(8,128)S(1)}) fusion(f32[67,28,80]{0,2,1:T(8,128)S(1)} %get-tuple-element.47, f32[67,28,80]{0,2,1:T(8,128)S(1)} %get-tuple-element.46), kind=kLoop, calls=%fused_computation.4 | loop fusion | bytes 71680 | tf_op jit(solution)/shard_map/slice | solution.py:255
  47.3 6.1 %shard_map.59 = (f32[28,80,128]{2,1,0:T(8,128)}, f32[28,80,128]{2,1,0:T(8,128)}, f32[2,128]{1,0:T(2,128)}) custom-call(f32[28,80,128]{2,1,0:T(8,128)} %pad_maximum_fusion.7.refs_0_.refs_1_.refs_2_.refs_3_, f32[28,80,128]{2,1,0:T(8,128)} %maximum_add_fusion.refs_1_.refs_3_.refs_5_, f32[28,80,128]{2,1,0:T(8,128)} %pad_maximum_fusion.8.refs_2_.refs_4_, ...), custom_call_target="tpu_custom_call" | custom-call | flops 11468800 | bytes 10321920 | tf_op jit(solution)/shard_map/pallas_call | solution.py:222
  56.1 3.4 %collective-permute-start.4 = (f32[2,64]{1,0:T(2,128)}, f32[2,64]{1,0:T(2,128)S(1)}, u32[]{:S(2)}, u32[]{:S(2)}) collective-permute-start(f32[2,64]{1,0:T(2,128)} %reduce_sum.63), channel_id=1, source_target_pairs={{0,1},{1,0},{2,3},{3,2},{4,5},{5,4},{6,7},{7,6},{8,9},{9,8},{10,11... | collective-permute-start | bytes 1544 | tf_op jit(solution)/shard_map/ppermute | solution.py:56
  61.3 3.5 %collective-permute-done.5 = f32[2,64]{1,0:T(2,128)S(1)} collective-permute-done((f32[2,64]{1,0:T(2,128)S(1)}, f32[2,64]{1,0:T(2,128)S(1)}, u32[]{:S(2)}, u32[]{:S(2)}) %collective-permute-start.5) | collective-permute-done | bytes 544 | tf_op jit(solution)/shard_map/ppermute | solution.py:56
  64.8 2.4 %collective-permute-start.6 = (f32[2,64]{1,0:T(2,128)S(1)}, f32[2,64]{1,0:T(2,128)S(1)}, u32[]{:S(2)}, u32[]{:S(2)}) collective-permute-start(f32[2,64]{1,0:T(2,128)S(1)} %add.158), channel_id=1, source_target_pairs={{0,4},{4,0},{8,12},{12,8},{16,20},{20,16},{24,28},{28,24},{1,5},{5... | collective-permute-start | bytes 1544 | tf_op jit(solution)/shard_map/ppermute | solution.py:56
  68.7 3.1 %collective-permute-start.7 = (f32[2,64]{1,0:T(2,128)S(1)}, f32[2,64]{1,0:T(2,128)S(1)}, u32[]{:S(2)}, u32[]{:S(2)}) collective-permute-start(f32[2,64]{1,0:T(2,128)S(1)} %add.159), channel_id=1, source_target_pairs={{0,8},{4,12},{8,0},{12,4},{16,24},{20,28},{24,16},{28,20},{1,9},{5... | collective-permute-start | bytes 1544 | tf_op jit(solution)/shard_map/ppermute | solution.py:56
  73.4 3.0 %collective-permute-start.8 = (f32[2,64]{1,0:T(2,128)S(1)}, f32[2,64]{1,0:T(2,128)S(1)}, u32[]{:S(2)}, u32[]{:S(2)}) collective-permute-start(f32[2,64]{1,0:T(2,128)S(1)} %add.160), channel_id=1, source_target_pairs={{0,16},{4,20},{8,24},{12,28},{16,0},{20,4},{24,8},{28,12},{1,17},{... | collective-permute-start | bytes 1544 | tf_op jit(solution)/shard_map/ppermute | solution.py:56
  80.4 3.8 %shard_map.60 = (f32[28,80,128]{2,1,0:T(8,128)}, f32[28,80,128]{2,1,0:T(8,128)}, f32[1,128]{1,0:T(1,128)}) custom-call(f32[1,128]{1,0:T(1,128)} %broadcast_in_dim_tile.15.refs_0_, f32[28,80,128]{2,1,0:T(8,128)} %pad_maximum_fusion.7.refs_0_.refs_1_.refs_2_.refs_3_, f32[28,80,128]{2,1,0:T(8,128)} %get-tuple-element.19.refs_2_, ...), custom_call_target="tpu_custom_call" | custom-call | flops 11468800 | bytes 8028160 | tf_op jit(solution)/shard_map/pallas_call | solution.py:222
  91.1 3.4 %collective-permute-done.10 = f32[64]{0:T(128)S(1)} collective-permute-done((f32[64]{0:T(128)S(1)}, f32[64]{0:T(128)S(1)}, u32[]{:S(2)}, u32[]{:S(2)}) %collective-permute-start.10) | collective-permute-done | bytes 288 | tf_op jit(solution)/shard_map/ppermute | solution.py:56
  95.4 2.7 %collective-permute-done.11 = f32[64]{0:T(128)S(1)} collective-permute-done((f32[64]{0:T(128)S(1)}, f32[64]{0:T(128)S(1)}, u32[]{:S(2)}, u32[]{:S(2)}) %collective-permute-start.11) | collective-permute-done | bytes 288 | tf_op jit(solution)/shard_map/ppermute | solution.py:56
  98.1 1.9 collective-permute-start.12
  101.7 2.9 %collective-permute-start.13 = (f32[64]{0:T(128)S(1)}, f32[64]{0:T(128)S(1)}, u32[]{:S(2)}, u32[]{:S(2)}) collective-permute-start(f32[64]{0:T(128)S(1)} %add.165), channel_id=1, source_target_pairs={{0,16},{4,20},{8,24},{12,28},{16,0},{20,4},{24,8},{28,12},{1,17},{... | collective-permute-start | bytes 776 | tf_op jit(solution)/shard_map/ppermute | solution.py:56
  109.2 6.2 %shard_map.61 = (f32[28,80,128]{2,1,0:T(8,128)}, f32[28,80,128]{2,1,0:T(8,128)}, f32[1,128]{1,0:T(1,128)}) custom-call(f32[1,128]{1,0:T(1,128)} %broadcast_in_dim_tile.16.refs_0_, f32[28,80,128]{2,1,0:T(8,128)} %get-tuple-element.21.refs_1_.refs_3_, f32[28,80,128]{2,1,0:T(8,128)} %pad_maximum_fusion.7.refs_0_.refs_1_.refs_2_.refs_3_, ...), custom_call_target="tpu_custom_call" | custom-call | flops 11468800 | bytes 12615680 | tf_op jit(solution)/shard_map/pallas_call | solution.py:222
  121.8 3.4 %collective-permute-done.15 = f32[64]{0:T(128)S(1)} collective-permute-done((f32[64]{0:T(128)S(1)}, f32[64]{0:T(128)S(1)}, u32[]{:S(2)}, u32[]{:S(2)}) %collective-permute-start.15) | collective-permute-done | bytes 288 | tf_op jit(solution)/shard_map/ppermute | solution.py:56
  126.1 2.7 %collective-permute-done.16 = f32[64]{0:T(128)S(1)} collective-permute-done((f32[64]{0:T(128)S(1)}, f32[64]{0:T(128)S(1)}, u32[]{:S(2)}, u32[]{:S(2)}) %collective-permute-start.16) | collective-permute-done | bytes 288 | tf_op jit(solution)/shard_map/ppermute | solution.py:56
  132.4 2.9 %collective-permute-start.18 = (f32[64]{0:T(128)S(1)}, f32[64]{0:T(128)S(1)}, u32[]{:S(2)}, u32[]{:S(2)}) collective-permute-start(f32[64]{0:T(128)S(1)} %add.170), channel_id=1, source_target_pairs={{0,16},{4,20},{8,24},{12,28},{16,0},{20,4},{24,8},{28,12},{1,17},{... | collective-permute-start | bytes 776 | tf_op jit(solution)/shard_map/ppermute | solution.py:56
  139.5 4.5 %shard_map.62 = (f32[28,80,128]{2,1,0:T(8,128)}, f32[28,80,128]{2,1,0:T(8,128)}, f32[1,128]{1,0:T(1,128)}) custom-call(f32[1,128]{1,0:T(1,128)} %broadcast_in_dim_tile.17.refs_0_, f32[28,80,128]{2,1,0:T(8,128)} %get-tuple-element.23.refs_1_, f32[28,80,128]{2,1,0:T(8,128)} %get-tuple-element.24.refs_2_, f32[28,80,128]{2,1,0:T(8,128)} %get-tuple-element.21.refs_1_.refs_3_, ...), custom_call_target="tpu_custom_call" | custom-call | flops 11468800 | bytes 10321920 | tf_op jit(solution)/shard_map/pallas_call | solution.py:222
  150.3 3.4 %collective-permute-done.20 = f32[64]{0:T(128)S(1)} collective-permute-done((f32[64]{0:T(128)S(1)}, f32[64]{0:T(128)S(1)}, u32[]{:S(2)}, u32[]{:S(2)}) %collective-permute-start.20) | collective-permute-done | bytes 288 | tf_op jit(solution)/shard_map/ppermute | solution.py:56
  154.6 2.7 %collective-permute-done.21 = f32[64]{0:T(128)S(1)} collective-permute-done((f32[64]{0:T(128)S(1)}, f32[64]{0:T(128)S(1)}, u32[]{:S(2)}, u32[]{:S(2)}) %collective-permute-start.21) | collective-permute-done | bytes 288 | tf_op jit(solution)/shard_map/ppermute | solution.py:56
  160.9 2.9 %collective-permute-start.23 = (f32[64]{0:T(128)S(1)}, f32[64]{0:T(128)S(1)}, u32[]{:S(2)}, u32[]{:S(2)}) collective-permute-start(f32[64]{0:T(128)S(1)} %add.175), channel_id=1, source_target_pairs={{0,16},{4,20},{8,24},{12,28},{16,0},{20,4},{24,8},{28,12},{1,17},{... | collective-permute-start | bytes 776 | tf_op jit(solution)/shard_map/ppermute | solution.py:56
  168.4 6.2 %shard_map.63 = (f32[28,80,128]{2,1,0:T(8,128)}, f32[28,80,128]{2,1,0:T(8,128)}, f32[1,128]{1,0:T(1,128)}) custom-call(f32[1,128]{1,0:T(1,128)} %broadcast_in_dim_tile.18.refs_0_, f32[28,80,128]{2,1,0:T(8,128)} %get-tuple-element.27.refs_1_, f32[28,80,128]{2,1,0:T(8,128)} %get-tuple-element.24.refs_2_, ...), custom_call_target="tpu_custom_call" | custom-call | flops 11468800 | bytes 12615680 | tf_op jit(solution)/shard_map/pallas_call | solution.py:222
  181.1 3.4 %collective-permute-done.25 = f32[64]{0:T(128)S(1)} collective-permute-done((f32[64]{0:T(128)S(1)}, f32[64]{0:T(128)S(1)}, u32[]{:S(2)}, u32[]{:S(2)}) %collective-permute-start.25) | collective-permute-done | bytes 288 | tf_op jit(solution)/shard_map/ppermute | solution.py:56
  185.4 2.4 %pad_maximum_fusion = f32[67,28,140]{0,2,1:T(8,128)S(1)} fusion(f32[67,28,6]{0,2,1:T(8,128)} %copy-done.2, f32[67,6,128]{0,2,1:T(8,128)} %collective-permute-done.1, f32[1,16,128]{0,2,1:T(8,128)S(1)} %copy.23, f32[1,16,128]{0,2,1:T(8,128)S(1)} %copy.22, f32[1,16,128]{0,2,1:T(8,128)} %copy.21, f32[64,16,128]{0,2,1:T(8,128)S(1)} %copy.20, ...), kind=kLoop, calls=%fused_computation.3 | loop fusion | flops 1838480 | bytes 2101120 | tf_op jit(solution)/shard_map/concatenate | solution.py:18
  188.2 1.9 collective-permute-start.27
  190.1 3.0 %fusion = (f32[28,140]{1,0:T(8,128)S(1)}, f32[28,140]{1,0:T(8,128)S(1)}) fusion(f32[67,28,140]{0,2,1:T(8,128)S(1)} %pad_maximum_fusion), kind=kLoop, calls=%fused_computation.2 | loop fusion | flops 3920 | bytes 62720 | tf_op jit(solution)/shard_map/add | solution.py:40
  193.2 2.7 %collective-permute-start.28 = (f32[64]{0:T(128)S(1)}, f32[64]{0:T(128)S(1)}, u32[]{:S(2)}, u32[]{:S(2)}) collective-permute-start(f32[64]{0:T(128)S(1)} %add.180), channel_id=1, source_target_pairs={{0,16},{4,20},{8,24},{12,28},{16,0},{20,4},{24,8},{28,12},{1,17},{... | collective-permute-start | bytes 776 | tf_op jit(solution)/shard_map/ppermute | solution.py:56
  198.3 5.2 %shard_map.64 = (f32[28,80,128]{2,1,0:T(8,128)}, f32[28,80,128]{2,1,0:T(8,128)}) custom-call(f32[1,128]{1,0:T(1,128)} %broadcast_in_dim_tile.19.refs_0_, f32[28,80,128]{2,1,0:T(8,128)} %get-tuple-element.29.refs_1_, f32[28,80,128]{2,1,0:T(8,128)} %get-tuple-element.30.refs_2_, f32[28,80,128]{2,1,0:T(8,128)} %pad_maximum_fusion.7.refs_0_.refs_1_.refs_2_.refs_3_, ...), custom_call_target="tpu_custom_call" | custom-call | flops 11468800 | bytes 9175040 | tf_op jit(solution)/shard_map/pallas_call | solution.py:222
  (142 shorter events, 90.7 us)
Async XLA Ops:
  6.9 22.0 %collective-permute-start = (f32[67,6,128]{0,2,1:T(8,128)}, f32[67,6,128]{0,2,1:T(8,128)S(1)}, u32[]{:S(2)}, u32[]{:S(2)}) collective-permute-start(f32[67,6,128]{0,2,1:T(8,128)} %get-tuple-element.50), channel_id=1, source_target_pairs={{0,4},{4,8},{8,12},{12,16},{16,20},{20,24},{24,28},{1,5},{5,9},{9,... | collective-permute-start | bytes 617480 | tf_op jit(solution)/shard_map/ppermute | solution.py:20
  11.8 17.1 %collective-permute-start.1 = (f32[67,6,128]{0,2,1:T(8,128)}, f32[67,6,128]{0,2,1:T(8,128)}, u32[]{:S(2)}, u32[]{:S(2)}) collective-permute-start(f32[67,6,128]{0,2,1:T(8,128)} %get-tuple-element.51), channel_id=1, source_target_pairs={{4,0},{8,4},{12,8},{16,12},{20,16},{24,20},{28,24},{5,1},{9,5},{13... | collective-permute-start | bytes 617480 | tf_op jit(solution)/shard_map/ppermute | solution.py:22
  15.2 21.0 %copy-start = (f32[1,16,128]{0,2,1:T(8,128)S(1)}, f32[1,16,128]{0,2,1:T(8,128)}, u32[]{:S(2)}) copy-start(f32[1,16,128]{0,2,1:T(8,128)} %copy.21) | copy-start | bytes 24580
  15.2 21.0 %copy-start.8 = (pred[80]{0:T(512)(128)(4,1)S(1)}, pred[80]{0:T(512)(128)(4,1)}, u32[]{:S(2)}) copy-start(pred[80]{0:T(512)(128)(4,1)} %constant.21.clone.1) | copy-start | bytes 244
  29.9 3.1 %collective-permute-start.2 = (f32[67,28,6]{0,2,1:T(8,128)S(1)}, f32[67,28,6]{0,2,1:T(8,128)S(1)}, u32[]{:S(2)}, u32[]{:S(2)}) collective-permute-start(f32[67,28,6]{0,2,1:T(8,128)S(1)} %get-tuple-element.48), channel_id=1, source_target_pairs={{0,1},{1,2},{2,3},{4,5},{5,6},{6,7},{8,9},{9,10},{10,11},{12,13},{... | collective-permute-start | bytes 135080 | tf_op jit(solution)/shard_map/ppermute | solution.py:20
  31.2 5.0 %collective-permute-start.3 = (f32[67,28,6]{0,2,1:T(8,128)S(1)}, f32[67,28,6]{0,2,1:T(8,128)S(1)}, u32[]{:S(2)}, u32[]{:S(2)}) collective-permute-start(f32[67,28,6]{0,2,1:T(8,128)S(1)} %get-tuple-element.49), channel_id=1, source_target_pairs={{1,0},{2,1},{3,2},{5,4},{6,5},{7,6},{9,8},{10,9},{11,10},{13,12},{... | collective-permute-start | bytes 135080 | tf_op jit(solution)/shard_map/ppermute | solution.py:22
  56.1 4.4 %collective-permute-start.4 = (f32[2,64]{1,0:T(2,128)}, f32[2,64]{1,0:T(2,128)S(1)}, u32[]{:S(2)}, u32[]{:S(2)}) collective-permute-start(f32[2,64]{1,0:T(2,128)} %reduce_sum.63), channel_id=1, source_target_pairs={{0,1},{1,0},{2,3},{3,2},{4,5},{5,4},{6,7},{7,6},{8,9},{9,8},{10,11... | collective-permute-start | bytes 1544 | tf_op jit(solution)/shard_map/ppermute | solution.py:56
  61.2 3.6 %collective-permute-start.5 = (f32[2,64]{1,0:T(2,128)S(1)}, f32[2,64]{1,0:T(2,128)S(1)}, u32[]{:S(2)}, u32[]{:S(2)}) collective-permute-start(f32[2,64]{1,0:T(2,128)S(1)} %add.157), channel_id=1, source_target_pairs={{0,2},{1,3},{2,0},{3,1},{4,6},{5,7},{6,4},{7,5},{8,10},{9,11},{10,... | collective-permute-start | bytes 1544 | tf_op jit(solution)/shard_map/ppermute | solution.py:56
  64.8 3.9 %collective-permute-start.6 = (f32[2,64]{1,0:T(2,128)S(1)}, f32[2,64]{1,0:T(2,128)S(1)}, u32[]{:S(2)}, u32[]{:S(2)}) collective-permute-start(f32[2,64]{1,0:T(2,128)S(1)} %add.158), channel_id=1, source_target_pairs={{0,4},{4,0},{8,12},{12,8},{16,20},{20,16},{24,28},{28,24},{1,5},{5... | collective-permute-start | bytes 1544 | tf_op jit(solution)/shard_map/ppermute | solution.py:56
  68.7 4.7 %collective-permute-start.7 = (f32[2,64]{1,0:T(2,128)S(1)}, f32[2,64]{1,0:T(2,128)S(1)}, u32[]{:S(2)}, u32[]{:S(2)}) collective-permute-start(f32[2,64]{1,0:T(2,128)S(1)} %add.159), channel_id=1, source_target_pairs={{0,8},{4,12},{8,0},{12,4},{16,24},{20,28},{24,16},{28,20},{1,9},{5... | collective-permute-start | bytes 1544 | tf_op jit(solution)/shard_map/ppermute | solution.py:56
  73.4 4.6 %collective-permute-start.8 = (f32[2,64]{1,0:T(2,128)S(1)}, f32[2,64]{1,0:T(2,128)S(1)}, u32[]{:S(2)}, u32[]{:S(2)}) collective-permute-start(f32[2,64]{1,0:T(2,128)S(1)} %add.160), channel_id=1, source_target_pairs={{0,16},{4,20},{8,24},{12,28},{16,0},{20,4},{24,8},{28,12},{1,17},{... | collective-permute-start | bytes 1544 | tf_op jit(solution)/shard_map/ppermute | solution.py:56
  89.0 1.4 collective-permute-start.9
  91.0 3.6 %collective-permute-start.10 = (f32[64]{0:T(128)S(1)}, f32[64]{0:T(128)S(1)}, u32[]{:S(2)}, u32[]{:S(2)}) collective-permute-start(f32[64]{0:T(128)S(1)} %add.162), channel_id=1, source_target_pairs={{0,2},{1,3},{2,0},{3,1},{4,6},{5,7},{6,4},{7,5},{8,10},{9,11},{10,... | collective-permute-start | bytes 776 | tf_op jit(solution)/shard_map/ppermute | solution.py:56
  94.6 3.6 %collective-permute-start.11 = (f32[64]{0:T(128)S(1)}, f32[64]{0:T(128)S(1)}, u32[]{:S(2)}, u32[]{:S(2)}) collective-permute-start(f32[64]{0:T(128)S(1)} %add.163), channel_id=1, source_target_pairs={{0,4},{4,0},{8,12},{12,8},{16,20},{20,16},{24,28},{28,24},{1,5},{5... | collective-permute-start | bytes 776 | tf_op jit(solution)/shard_map/ppermute | solution.py:56
  98.1 3.6 %collective-permute-start.12 = (f32[64]{0:T(128)S(1)}, f32[64]{0:T(128)S(1)}, u32[]{:S(2)}, u32[]{:S(2)}) collective-permute-start(f32[64]{0:T(128)S(1)} %add.164), channel_id=1, source_target_pairs={{0,8},{4,12},{8,0},{12,4},{16,24},{20,28},{24,16},{28,20},{1,9},{5... | collective-permute-start | bytes 776 | tf_op jit(solution)/shard_map/ppermute | solution.py:56
  101.7 4.5 %collective-permute-start.13 = (f32[64]{0:T(128)S(1)}, f32[64]{0:T(128)S(1)}, u32[]{:S(2)}, u32[]{:S(2)}) collective-permute-start(f32[64]{0:T(128)S(1)} %add.165), channel_id=1, source_target_pairs={{0,16},{4,20},{8,24},{12,28},{16,0},{20,4},{24,8},{28,12},{1,17},{... | collective-permute-start | bytes 776 | tf_op jit(solution)/shard_map/ppermute | solution.py:56
  119.7 1.4 collective-permute-start.14
  121.7 3.6 %collective-permute-start.15 = (f32[64]{0:T(128)S(1)}, f32[64]{0:T(128)S(1)}, u32[]{:S(2)}, u32[]{:S(2)}) collective-permute-start(f32[64]{0:T(128)S(1)} %add.167), channel_id=1, source_target_pairs={{0,2},{1,3},{2,0},{3,1},{4,6},{5,7},{6,4},{7,5},{8,10},{9,11},{10,... | collective-permute-start | bytes 776 | tf_op jit(solution)/shard_map/ppermute | solution.py:56
  125.3 3.6 %collective-permute-start.16 = (f32[64]{0:T(128)S(1)}, f32[64]{0:T(128)S(1)}, u32[]{:S(2)}, u32[]{:S(2)}) collective-permute-start(f32[64]{0:T(128)S(1)} %add.168), channel_id=1, source_target_pairs={{0,4},{4,0},{8,12},{12,8},{16,20},{20,16},{24,28},{28,24},{1,5},{5... | collective-permute-start | bytes 776 | tf_op jit(solution)/shard_map/ppermute | solution.py:56
  128.8 3.6 %collective-permute-start.17 = (f32[64]{0:T(128)S(1)}, f32[64]{0:T(128)S(1)}, u32[]{:S(2)}, u32[]{:S(2)}) collective-permute-start(f32[64]{0:T(128)S(1)} %add.169), channel_id=1, source_target_pairs={{0,8},{4,12},{8,0},{12,4},{16,24},{20,28},{24,16},{28,20},{1,9},{5... | collective-permute-start | bytes 776 | tf_op jit(solution)/shard_map/ppermute | solution.py:56
  132.4 4.5 %collective-permute-start.18 = (f32[64]{0:T(128)S(1)}, f32[64]{0:T(128)S(1)}, u32[]{:S(2)}, u32[]{:S(2)}) collective-permute-start(f32[64]{0:T(128)S(1)} %add.170), channel_id=1, source_target_pairs={{0,16},{4,20},{8,24},{12,28},{16,0},{20,4},{24,8},{28,12},{1,17},{... | collective-permute-start | bytes 776 | tf_op jit(solution)/shard_map/ppermute | solution.py:56
  148.2 1.4 collective-permute-start.19
  150.2 3.6 %collective-permute-start.20 = (f32[64]{0:T(128)S(1)}, f32[64]{0:T(128)S(1)}, u32[]{:S(2)}, u32[]{:S(2)}) collective-permute-start(f32[64]{0:T(128)S(1)} %add.172), channel_id=1, source_target_pairs={{0,2},{1,3},{2,0},{3,1},{4,6},{5,7},{6,4},{7,5},{8,10},{9,11},{10,... | collective-permute-start | bytes 776 | tf_op jit(solution)/shard_map/ppermute | solution.py:56
  153.8 3.6 %collective-permute-start.21 = (f32[64]{0:T(128)S(1)}, f32[64]{0:T(128)S(1)}, u32[]{:S(2)}, u32[]{:S(2)}) collective-permute-start(f32[64]{0:T(128)S(1)} %add.173), channel_id=1, source_target_pairs={{0,4},{4,0},{8,12},{12,8},{16,20},{20,16},{24,28},{28,24},{1,5},{5... | collective-permute-start | bytes 776 | tf_op jit(solution)/shard_map/ppermute | solution.py:56
  157.4 3.6 %collective-permute-start.22 = (f32[64]{0:T(128)S(1)}, f32[64]{0:T(128)S(1)}, u32[]{:S(2)}, u32[]{:S(2)}) collective-permute-start(f32[64]{0:T(128)S(1)} %add.174), channel_id=1, source_target_pairs={{0,8},{4,12},{8,0},{12,4},{16,24},{20,28},{24,16},{28,20},{1,9},{5... | collective-permute-start | bytes 776 | tf_op jit(solution)/shard_map/ppermute | solution.py:56
  160.9 4.5 %collective-permute-start.23 = (f32[64]{0:T(128)S(1)}, f32[64]{0:T(128)S(1)}, u32[]{:S(2)}, u32[]{:S(2)}) collective-permute-start(f32[64]{0:T(128)S(1)} %add.175), channel_id=1, source_target_pairs={{0,16},{4,20},{8,24},{12,28},{16,0},{20,4},{24,8},{28,12},{1,17},{... | collective-permute-start | bytes 776 | tf_op jit(solution)/shard_map/ppermute | solution.py:56
  179.0 1.4 collective-permute-start.24
  181.0 3.6 %collective-permute-start.25 = (f32[64]{0:T(128)S(1)}, f32[64]{0:T(128)S(1)}, u32[]{:S(2)}, u32[]{:S(2)}) collective-permute-start(f32[64]{0:T(128)S(1)} %add.177), channel_id=1, source_target_pairs={{0,2},{1,3},{2,0},{3,1},{4,6},{5,7},{6,4},{7,5},{8,10},{9,11},{10,... | collective-permute-start | bytes 776 | tf_op jit(solution)/shard_map/ppermute | solution.py:56
  184.6 3.6 %collective-permute-start.26 = (f32[64]{0:T(128)S(1)}, f32[64]{0:T(128)S(1)}, u32[]{:S(2)}, u32[]{:S(2)}) collective-permute-start(f32[64]{0:T(128)S(1)} %add.178), channel_id=1, source_target_pairs={{0,4},{4,0},{8,12},{12,8},{16,20},{20,16},{24,28},{28,24},{1,5},{5... | collective-permute-start | bytes 776 | tf_op jit(solution)/shard_map/ppermute | solution.py:56
  188.2 9.5 %copy-start.7 = (f32[64]{0:T(128)S(1)}, f32[64]{0:T(128)}, u32[]{:S(2)}) copy-start(f32[64]{0:T(128)} %get-tuple-element.43) | copy-start | bytes 772
  188.2 5.0 %collective-permute-start.27 = (f32[64]{0:T(128)S(1)}, f32[64]{0:T(128)S(1)}, u32[]{:S(2)}, u32[]{:S(2)}) collective-permute-start(f32[64]{0:T(128)S(1)} %add.179), channel_id=1, source_target_pairs={{0,8},{4,12},{8,0},{12,4},{16,24},{20,28},{24,16},{28,20},{1,9},{5... | collective-permute-start | bytes 776 | tf_op jit(solution)/shard_map/ppermute | solution.py:56
  193.2 4.5 %collective-permute-start.28 = (f32[64]{0:T(128)S(1)}, f32[64]{0:T(128)S(1)}, u32[]{:S(2)}, u32[]{:S(2)}) collective-permute-start(f32[64]{0:T(128)S(1)} %add.180), channel_id=1, source_target_pairs={{0,16},{4,20},{8,24},{12,28},{16,0},{20,4},{24,8},{28,12},{1,17},{... | collective-permute-start | bytes 776 | tf_op jit(solution)/shard_map/ppermute | solution.py:56
  (6 other events, 12.1 us)

commit v5 on v4

--- a/solution.py
+++ b/solution.py
@@ -67,6 +67,15 @@
     return gain * mid - (4.0 * edge_sum + corners) * (1.0 / 6.0)
 
 
+def _total(ref, row):
+    value = ref[row : row + 1, :]
+    return value + pltpu.roll(value, value.shape[1] // 2, 1)
+
+
+def _ratio(num_ref, num_row, den_ref, den_row):
+    return _total(num_ref, num_row) / _total(den_ref, den_row)
+
+
 def _row_sum(value, keep):
     return jnp.sum(jnp.where(keep, value, 0.0), axis=0, keepdims=True)
 
@@ -143,8 +152,8 @@
     dots_out[1:2, :] = za
 
 
-def _start_kernel(plan, step_ref, z_ref, applied_ref, inner_ref, solution_out, residual_out, rr_out):
-    step = step_ref[...]
+def _start_kernel(plan, first_ref, z_ref, applied_ref, inner_ref, solution_out, residual_out, rr_out):
+    step = _ratio(first_ref, 0, first_ref, 1)
 
     def body(r, totals):
         z = z_ref[r]
@@ -157,9 +166,9 @@
     rr_out[...] = lax.fori_loop(0, plan.slab_rows, body, jnp.zeros((1, z_ref.shape[2]), jnp.float32))
 
 
-def _update_kernel(plan, step_ref, solution_ref, direction_ref, residual_ref, applied_ref, inner_ref,
-                   solution_out, residual_out, rr_out):
-    step = step_ref[...]
+def _update_kernel(plan, norm_ref, curvature_ref, solution_ref, direction_ref, residual_ref,
+                   applied_ref, inner_ref, solution_out, residual_out, rr_out):
+    step = _ratio(norm_ref, 0, curvature_ref, 0)
 
     def body(r, totals):
         residual = residual_ref[r] - step * applied_ref[r]
@@ -173,9 +182,9 @@
     )
 
 
-def _direction_kernel(plan, beta_ref, residual_ref, direction_ref, gain_ref, weight_ref, inside_ref,
-                      row_ref, inner_ref, direction_out, applied_out, pa_out, scratch):
-    beta = beta_ref[...]
+def _direction_kernel(plan, next_ref, now_ref, residual_ref, direction_ref, gain_ref, weight_ref,
+                      inside_ref, row_ref, inner_ref, direction_out, applied_out, pa_out, scratch):
+    beta = _ratio(next_ref, 0, now_ref, 0)
 
     def new_direction(r, carry):
         direction_out[r] = residual_ref[r] + beta * direction_ref[r]
@@ -186,9 +195,9 @@
                            scratch, applied_out, direction_out)
 
 
-def _final_kernel(plan, step_ref, solution_ref, direction_ref, z_ref, stiff_ref, gain_ref,
-                  weight_out, kappa_out, scratch):
-    step = step_ref[...]
+def _final_kernel(plan, norm_ref, curvature_ref, solution_ref, direction_ref, z_ref, stiff_ref,
+                  gain_ref, weight_out, kappa_out, scratch):
+    step = _ratio(norm_ref, 0, curvature_ref, 0)
     last = plan.slab_rows - 1
 
     def new_solution(r, carry):
@@ -282,42 +291,34 @@
     field = jax.ShapeDtypeStruct((slab_rows, sublanes, lanes), jnp.float32)
     lane_row = jax.ShapeDtypeStruct((1, lanes), jnp.float32)
 
-    def per_probe(lane_totals):
-        return jnp.sum(lane_totals.reshape(lane_totals.shape[:-1] + (2, probe_count)), axis=-2)
-
-    def on_lane(scalars):
-        return jnp.tile(scalars, 2)[None, :]
-
     stiff_probe, applied, first = _call(
         _first_kernel, plan, (z, gain, weight, inside, row_in, inner),
         (field, field, jax.ShapeDtypeStruct((2, lanes), jnp.float32)), scratch=1, smem=(4,),
     )
-    first = all_sum(per_probe(first))
-    norm_now = first[0]
-    step_len = norm_now / first[1]
+    first = all_sum(first)
     solution, residual, rr = _call(
-        _start_kernel, plan, (on_lane(step_len), z, applied, inner), (field, field, lane_row)
+        _start_kernel, plan, (first, z, applied, inner), (field, field, lane_row)
     )
     direction = z
+    norm_now = first
     for iteration in range(1, ITERS):
-        norm_next = all_sum(per_probe(rr[0]))
-        beta = norm_next / norm_now
-        norm_now = norm_next
+        norm_next = all_sum(rr)
         direction, applied, pa = _call(
             _direction_kernel, plan,
-            (on_lane(beta), residual, direction, gain, weight, inside, row_in, inner),
-            (field, field, lane_row), scratch=1, smem=(6,),
+            (norm_next, norm_now, residual, direction, gain, weight, inside, row_in, inner),
+            (field, field, lane_row), scratch=1, smem=(7,),
         )
-        step_len = norm_now / all_sum(per_probe(pa[0]))
+        norm_now = norm_next
+        curvature = all_sum(pa)
         if iteration + 1 < ITERS:
             solution, residual, rr = _call(
                 _update_kernel, plan,
-                (on_lane(step_len), solution, direction, residual, applied, inner),
+                (norm_now, curvature, solution, direction, residual, applied, inner),
                 (field, field, lane_row),
             )
 
     weight_terms, kappa_terms = _call(
-        _final_kernel, plan, (on_lane(step_len), solution, direction, z, stiff_probe, gain),
+        _final_kernel, plan, (norm_now, curvature, solution, direction, z, stiff_probe, gain),
         (field, field), scratch=1,
     )
 

time: 212 us -> 182 us (0.86)
  local copies, waits for them, and re-layouts: 28.8 us -> 13.2 us
  other arithmetic: 40.8 us -> 27 us
    another operation x14 -> x0, local copies, waits for them, and re-layouts: 13.1 us -> none  [the longest x10 8.04 us: on_lane(): return jnp.tile(scalars, 2)[None, :]]
    pallas_call x4 -> x0, other arithmetic: 7.32 us -> none  [_call(): pl.pallas_call(lambda *refs: kernel(plan, *refs), out_shape=out_shapes, i...]
    reduce_sum x5 -> x0, other arithmetic: 6.14 us -> none  [per_probe(): jnp.sum(lane_totals.reshape(lane_totals.shape[:-1] + (2, probe_count)), a...]
    div x4 -> x0, other arithmetic: 3.02 us -> none  [the longest x2 2.36 us: on_device(): beta = norm_next / norm_now]
    add x21 -> x25, other arithmetic: 3.2 us -> 5.92 us  [all_sum(): terms + lax.ppermute(terms, axis, [(i, i ^ hop) for i in range(count)])]
  transfers between devices with their start and end apart: 29 -> 29, of which waited for: 26 -> 26; matrix products, arithmetic and copies ran while one was open for 4% -> 5% of each run, Pallas kernels for 0% -> 0%
where the time goes in v5:
time: 182 us
  waiting for transfers between devices  64.8 us (36%)
  starting transfers between devices  43.6 us (24%)
  Pallas kernels  32.2 us (18%)
  other arithmetic  27 us (15%)
  local copies, waits for them, and re-layouts  13.2 us (7%)
    ppermute x25, waiting for transfers between devices, all_sum(): lax.ppermute(terms, axis, [(i, i ^ hop) for i in range(count)])  48.1 us
    ppermute x25, starting transfers between devices, all_sum(): lax.ppermute(terms, axis, [(i, i ^ hop) for i in range(count)])  34.9 us
    pallas_call x6, Pallas kernels, _call(): pl.pallas_call(lambda *refs: kernel(plan, *refs), out_shape=out_shapes, i...  32.2 us
    ppermute x2, waiting for transfers between devices, extended(): lax.ppermute(tail, axis, [(i, (i + 1) % count) for i in range(ends)])  13.6 us
    ppermute x2, starting transfers between devices, extended(): lax.ppermute(tail, axis, [(i, (i + 1) % count) for i in range(ends)])  6.18 us
    add x25, other arithmetic, all_sum(): terms + lax.ppermute(terms, axis, [(i, i ^ hop) for i in range(count)])  5.92 us
    slice x2, other arithmetic, extended(): lax.slice_in_dim(cells, cells.shape[dim] - width, cells.shape[dim], axis=...  3.75 us
  transfers between devices with their start and end apart: 29, of which 26 were waited for; matrix products, arithmetic and copies ran while one was open for 5% of the time, Pallas kernels for 0%

profile of v5, /device:TPU:0, one launch (start us, length us, event | category | flops | bytes accessed | tf_op | source)
XLA Modules:
  0.0 181.8 jit_solution(5007270895427143453)
XLA Ops:
  4.2 2.7 %pad_maximum_fusion.12 = (f32[67,6,128]{0,2,1:T(8,128)}, f32[67,6,128]{0,2,1:T(8,128)}) fusion(f32[1,16,128]{0,2,1:T(8,128)S(1)} %copy.23, f32[1,16,128]{0,2,1:T(8,128)S(1)} %copy.22, f32[1,16,128]{0,2,1:T(8,128)} %copy.21, f32[64,16,128]{0,2,1:T(8,128)S(1)} %copy.20), kind=kLoop, calls=%fused_computation.36 | loop fusion | flops 308736 | bytes 960512 | tf_op jit(solution)/shard_map/slice | solution.py:17
  6.9 4.9 %collective-permute-start = (f32[67,6,128]{0,2,1:T(8,128)}, f32[67,6,128]{0,2,1:T(8,128)S(1)}, u32[]{:S(2)}, u32[]{:S(2)}) collective-permute-start(f32[67,6,128]{0,2,1:T(8,128)} %get-tuple-element.46), channel_id=1, source_target_pairs={{0,4},{4,8},{8,12},{12,16},{16,20},{20,24},{24,28},{1,5},{5,9},{9,... | collective-permute-start | bytes 617480 | tf_op jit(solution)/shard_map/ppermute | solution.py:20
  15.2 13.6 %collective-permute-done = f32[67,6,128]{0,2,1:T(8,128)S(1)} collective-permute-done((f32[67,6,128]{0,2,1:T(8,128)}, f32[67,6,128]{0,2,1:T(8,128)S(1)}, u32[]{:S(2)}, u32[]{:S(2)}) %collective-permute-start) | collective-permute-done | bytes 205856 | tf_op jit(solution)/shard_map/ppermute | solution.py:20
  33.1 3.1 %collective-permute-done.3 = f32[67,28,6]{0,2,1:T(8,128)S(1)} collective-permute-done((f32[67,28,6]{0,2,1:T(8,128)S(1)}, f32[67,28,6]{0,2,1:T(8,128)S(1)}, u32[]{:S(2)}, u32[]{:S(2)}) %collective-permute-start.3) | collective-permute-done | bytes 45056 | tf_op jit(solution)/shard_map/ppermute | solution.py:22
  36.2 2.2 %fusion.8 = (f32[67,28,80]{0,2,1:T(8,128)S(1)}, f32[67,28,80]{0,2,1:T(8,128)S(1)}) fusion(f32[67,28,6]{0,2,1:T(8,128)S(1)} %collective-permute-done.2, f32[67,6,128]{0,2,1:T(8,128)} %collective-permute-done.1, f32[67,6,128]{0,2,1:T(8,128)S(1)} %collective-permute-done, f32[1,16,128]{0,2,1:T(8,128)S(1)} %copy.23, f32[1,16,128]{0,2,1:T(8,128)S(1)} %copy.22, ...), kind=kLoop, calls=%fused_computation.22 | loop fusion | flops 3151680 | bytes 2251280 | tf_op jit(solution)/shard_map/jit(_pad)/pad | solution.py:258
  38.4 3.2 %slice_reduce_fusion.1 = (f32[28,80]{1,0:T(8,128)S(1)}, f32[28,80]{1,0:T(8,128)S(1)}, f32[28,80]{1,0:T(8,128)S(1)}, f32[28,80]{1,0:T(8,128)S(1)}) fusion(f32[67,28,80]{0,2,1:T(8,128)S(1)} %get-tuple-element.43, f32[67,28,80]{0,2,1:T(8,128)S(1)} %get-tuple-element.42), kind=kLoop, calls=%fused_computation.4 | loop fusion | bytes 71680 | tf_op jit(solution)/shard_map/slice | solution.py:264
  47.3 6.1 %shard_map.59 = (f32[28,80,128]{2,1,0:T(8,128)}, f32[28,80,128]{2,1,0:T(8,128)}, f32[2,128]{1,0:T(2,128)}) custom-call(f32[28,80,128]{2,1,0:T(8,128)} %pad_maximum_fusion.7.refs_0_.refs_1_.refs_3_.refs_4_, f32[28,80,128]{2,1,0:T(8,128)} %maximum_add_fusion.refs_1_.refs_4_.refs_6_, f32[28,80,128]{2,1,0:T(8,128)} %pad_maximum_fusion.8.refs_2_.refs_5_, ...), custom_call_target="tpu_custom_call" | custom-call | flops 11468800 | bytes 10321920 | tf_op jit(solution)/shard_map/pallas_call | solution.py:231
  53.4 3.4 %collective-permute-start.4 = (f32[2,128]{1,0:T(2,128)}, f32[2,128]{1,0:T(2,128)S(1)}, u32[]{:S(2)}, u32[]{:S(2)}) collective-permute-start(f32[2,128]{1,0:T(2,128)} %get-tuple-element.18), channel_id=1, source_target_pairs={{0,1},{1,0},{2,3},{3,2},{4,5},{5,4},{6,7},{7,6},{8,9},{9,8},{10,11... | collective-permute-start | bytes 3080 | tf_op jit(solution)/shard_map/ppermute | solution.py:56
  58.7 3.5 %collective-permute-done.5 = f32[2,128]{1,0:T(2,128)S(1)} collective-permute-done((f32[2,128]{1,0:T(2,128)S(1)}, f32[2,128]{1,0:T(2,128)S(1)}, u32[]{:S(2)}, u32[]{:S(2)}) %collective-permute-start.5) | collective-permute-done | bytes 1056 | tf_op jit(solution)/shard_map/ppermute | solution.py:56
  62.1 2.4 %collective-permute-start.6 = (f32[2,128]{1,0:T(2,128)S(1)}, f32[2,128]{1,0:T(2,128)S(1)}, u32[]{:S(2)}, u32[]{:S(2)}) collective-permute-start(f32[2,128]{1,0:T(2,128)S(1)} %add.158), channel_id=1, source_target_pairs={{0,4},{4,0},{8,12},{12,8},{16,20},{20,16},{24,28},{28,24},{1,5},{5... | collective-permute-start | bytes 3080 | tf_op jit(solution)/shard_map/ppermute | solution.py:56
  66.0 3.1 %collective-permute-start.7 = (f32[2,128]{1,0:T(2,128)S(1)}, f32[2,128]{1,0:T(2,128)S(1)}, u32[]{:S(2)}, u32[]{:S(2)}) collective-permute-start(f32[2,128]{1,0:T(2,128)S(1)} %add.159), channel_id=1, source_target_pairs={{0,8},{4,12},{8,0},{12,4},{16,24},{20,28},{24,16},{28,20},{1,9},{5... | collective-permute-start | bytes 3080 | tf_op jit(solution)/shard_map/ppermute | solution.py:56
  70.7 3.0 %collective-permute-start.8 = (f32[2,128]{1,0:T(2,128)S(1)}, f32[2,128]{1,0:T(2,128)S(1)}, u32[]{:S(2)}, u32[]{:S(2)}) collective-permute-start(f32[2,128]{1,0:T(2,128)S(1)} %add.160), channel_id=1, source_target_pairs={{0,16},{4,20},{8,24},{12,28},{16,0},{20,4},{24,8},{28,12},{1,17},{... | collective-permute-start | bytes 3080 | tf_op jit(solution)/shard_map/ppermute | solution.py:56
  75.9 3.8 %shard_map.60 = (f32[28,80,128]{2,1,0:T(8,128)}, f32[28,80,128]{2,1,0:T(8,128)}, f32[1,128]{1,0:T(1,128)}) custom-call(f32[2,128]{1,0:T(2,128)} %add.161.refs_0_.refs_1_, f32[28,80,128]{2,1,0:T(8,128)} %pad_maximum_fusion.7.refs_0_.refs_1_.refs_3_.refs_4_, f32[28,80,128]{2,1,0:T(8,128)} %get-tuple-element.19.refs_2_, ...), custom_call_target="tpu_custom_call" | custom-call | flops 11468800 | bytes 8028160 | tf_op jit(solution)/shard_map/pallas_call | solution.py:231
  81.8 3.4 %collective-permute-done.10 = f32[1,128]{1,0:T(1,128)S(1)} collective-permute-done((f32[1,128]{1,0:T(1,128)S(1)}, f32[1,128]{1,0:T(1,128)S(1)}, u32[]{:S(2)}, u32[]{:S(2)}) %collective-permute-start.10) | collective-permute-done | bytes 544 | tf_op jit(solution)/shard_map/ppermute | solution.py:56
  86.0 2.7 %collective-permute-done.11 = f32[1,128]{1,0:T(1,128)S(1)} collective-permute-done((f32[1,128]{1,0:T(1,128)S(1)}, f32[1,128]{1,0:T(1,128)S(1)}, u32[]{:S(2)}, u32[]{:S(2)}) %collective-permute-start.11) | collective-permute-done | bytes 544 | tf_op jit(solution)/shard_map/ppermute | solution.py:56
  88.8 1.9 %collective-permute-start.12 = (f32[1,128]{1,0:T(1,128)S(1)}, f32[1,128]{1,0:T(1,128)S(1)}, u32[]{:S(2)}, u32[]{:S(2)}) collective-permute-start(f32[1,128]{1,0:T(1,128)S(1)} %add.164), channel_id=1, source_target_pairs={{0,8},{4,12},{8,0},{12,4},{16,24},{20,28},{24,16},{28,20},{1,9},{5... | collective-permute-start | bytes 1544 | tf_op jit(solution)/shard_map/ppermute | solution.py:56
  92.4 2.9 %collective-permute-start.13 = (f32[1,128]{1,0:T(1,128)S(1)}, f32[1,128]{1,0:T(1,128)S(1)}, u32[]{:S(2)}, u32[]{:S(2)}) collective-permute-start(f32[1,128]{1,0:T(1,128)S(1)} %add.165), channel_id=1, source_target_pairs={{0,16},{4,20},{8,24},{12,28},{16,0},{20,4},{24,8},{28,12},{1,17},{... | collective-permute-start | bytes 1544 | tf_op jit(solution)/shard_map/ppermute | solution.py:56
  97.3 6.2 %shard_map.61 = (f32[28,80,128]{2,1,0:T(8,128)}, f32[28,80,128]{2,1,0:T(8,128)}, f32[1,128]{1,0:T(1,128)}) custom-call(f32[1,128]{1,0:T(1,128)} %add.166.refs_0_.refs_1_, f32[2,128]{1,0:T(2,128)} %add.161.refs_0_.refs_1_, f32[28,80,128]{2,1,0:T(8,128)} %get-tuple-element.21.refs_2_.refs_4_, f32[28,80,128]{2,1,0:T(8,128)} %pad_maximum_fusion.7.refs_0_.refs_1_.refs_3_.refs_4_, ...), custom_call_target="tpu_custom_call" | custom-call | flops 11468800 | bytes 13762560 | tf_op jit(solution)/shard_map/pallas_call | solution.py:231
  105.6 3.4 %collective-permute-done.15 = f32[1,128]{1,0:T(1,128)S(1)} collective-permute-done((f32[1,128]{1,0:T(1,128)S(1)}, f32[1,128]{1,0:T(1,128)S(1)}, u32[]{:S(2)}, u32[]{:S(2)}) %collective-permute-start.15) | collective-permute-done | bytes 544 | tf_op jit(solution)/shard_map/ppermute | solution.py:56
  109.8 2.7 %collective-permute-done.16 = f32[1,128]{1,0:T(1,128)S(1)} collective-permute-done((f32[1,128]{1,0:T(1,128)S(1)}, f32[1,128]{1,0:T(1,128)S(1)}, u32[]{:S(2)}, u32[]{:S(2)}) %collective-permute-start.16) | collective-permute-done | bytes 544 | tf_op jit(solution)/shard_map/ppermute | solution.py:56
  112.6 1.9 %collective-permute-start.17 = (f32[1,128]{1,0:T(1,128)S(1)}, f32[1,128]{1,0:T(1,128)S(1)}, u32[]{:S(2)}, u32[]{:S(2)}) collective-permute-start(f32[1,128]{1,0:T(1,128)S(1)} %add.169), channel_id=1, source_target_pairs={{0,8},{4,12},{8,0},{12,4},{16,24},{20,28},{24,16},{28,20},{1,9},{5... | collective-permute-start | bytes 1544 | tf_op jit(solution)/shard_map/ppermute | solution.py:56
  116.2 2.9 %collective-permute-start.18 = (f32[1,128]{1,0:T(1,128)S(1)}, f32[1,128]{1,0:T(1,128)S(1)}, u32[]{:S(2)}, u32[]{:S(2)}) collective-permute-start(f32[1,128]{1,0:T(1,128)S(1)} %add.170), channel_id=1, source_target_pairs={{0,16},{4,20},{8,24},{12,28},{16,0},{20,4},{24,8},{28,12},{1,17},{... | collective-permute-start | bytes 1544 | tf_op jit(solution)/shard_map/ppermute | solution.py:56
  121.1 4.6 %shard_map.62 = (f32[28,80,128]{2,1,0:T(8,128)}, f32[28,80,128]{2,1,0:T(8,128)}, f32[1,128]{1,0:T(1,128)}) custom-call(f32[1,128]{1,0:T(1,128)} %add.166.refs_0_.refs_1_, f32[1,128]{1,0:T(1,128)} %add.171.refs_1_, f32[28,80,128]{2,1,0:T(8,128)} %get-tuple-element.23.refs_2_, f32[28,80,128]{2,1,0:T(8,128)} %get-tuple-element.24.refs_3_, ...), custom_call_target="tpu_custom_call" | custom-call | flops 11468800 | bytes 11468800 | tf_op jit(solution)/shard_map/pallas_call | solution.py:231
  127.8 3.4 %collective-permute-done.20 = f32[1,128]{1,0:T(1,128)S(1)} collective-permute-done((f32[1,128]{1,0:T(1,128)S(1)}, f32[1,128]{1,0:T(1,128)S(1)}, u32[]{:S(2)}, u32[]{:S(2)}) %collective-permute-start.20) | collective-permute-done | bytes 544 | tf_op jit(solution)/shard_map/ppermute | solution.py:56
  132.1 2.7 %collective-permute-done.21 = f32[1,128]{1,0:T(1,128)S(1)} collective-permute-done((f32[1,128]{1,0:T(1,128)S(1)}, f32[1,128]{1,0:T(1,128)S(1)}, u32[]{:S(2)}, u32[]{:S(2)}) %collective-permute-start.21) | collective-permute-done | bytes 544 | tf_op jit(solution)/shard_map/ppermute | solution.py:56
  138.4 2.9 %collective-permute-start.23 = (f32[1,128]{1,0:T(1,128)S(1)}, f32[1,128]{1,0:T(1,128)S(1)}, u32[]{:S(2)}, u32[]{:S(2)}) collective-permute-start(f32[1,128]{1,0:T(1,128)S(1)} %add.175), channel_id=1, source_target_pairs={{0,16},{4,20},{8,24},{12,28},{16,0},{20,4},{24,8},{28,12},{1,17},{... | collective-permute-start | bytes 1544 | tf_op jit(solution)/shard_map/ppermute | solution.py:56
  143.4 6.2 %shard_map.63 = (f32[28,80,128]{2,1,0:T(8,128)}, f32[28,80,128]{2,1,0:T(8,128)}, f32[1,128]{1,0:T(1,128)}) custom-call(f32[1,128]{1,0:T(1,128)} %add.176.refs_0_, f32[1,128]{1,0:T(1,128)} %add.166.refs_0_.refs_1_, f32[28,80,128]{2,1,0:T(8,128)} %get-tuple-element.27.refs_2_, f32[28,80,128]{2,1,0:T(8,128)} %get-tuple-element.24.refs_3_, ...), custom_call_target="tpu_custom_call" | custom-call | flops 11468800 | bytes 13762560 | tf_op jit(solution)/shard_map/pallas_call | solution.py:231
  151.7 3.4 %collective-permute-done.25 = f32[1,128]{1,0:T(1,128)S(1)} collective-permute-done((f32[1,128]{1,0:T(1,128)S(1)}, f32[1,128]{1,0:T(1,128)S(1)}, u32[]{:S(2)}, u32[]{:S(2)}) %collective-permute-start.25) | collective-permute-done | bytes 544 | tf_op jit(solution)/shard_map/ppermute | solution.py:56
  156.0 2.4 %pad_maximum_fusion = f32[67,28,140]{0,2,1:T(8,128)S(1)} fusion(f32[67,28,6]{0,2,1:T(8,128)} %copy-done.2, f32[67,6,128]{0,2,1:T(8,128)} %collective-permute-done.1, f32[1,16,128]{0,2,1:T(8,128)S(1)} %copy.23, f32[1,16,128]{0,2,1:T(8,128)S(1)} %copy.22, f32[1,16,128]{0,2,1:T(8,128)} %copy.21, f32[64,16,128]{0,2,1:T(8,128)S(1)} %copy.20, ...), kind=kLoop, calls=%fused_computation.3 | loop fusion | flops 1838480 | bytes 2101120 | tf_op jit(solution)/shard_map/concatenate | solution.py:18
  160.6 3.0 %fusion = (f32[28,140]{1,0:T(8,128)S(1)}, f32[28,140]{1,0:T(8,128)S(1)}) fusion(f32[67,28,140]{0,2,1:T(8,128)S(1)} %pad_maximum_fusion), kind=kLoop, calls=%fused_computation.2 | loop fusion | flops 3920 | bytes 62720 | tf_op jit(solution)/shard_map/add | solution.py:40
  163.7 2.7 %collective-permute-start.28 = (f32[1,128]{1,0:T(1,128)S(1)}, f32[1,128]{1,0:T(1,128)S(1)}, u32[]{:S(2)}, u32[]{:S(2)}) collective-permute-start(f32[1,128]{1,0:T(1,128)S(1)} %add.180), channel_id=1, source_target_pairs={{0,16},{4,20},{8,24},{12,28},{16,0},{20,4},{24,8},{28,12},{1,17},{... | collective-permute-start | bytes 1544 | tf_op jit(solution)/shard_map/ppermute | solution.py:56
  168.7 5.3 %shard_map.64 = (f32[28,80,128]{2,1,0:T(8,128)}, f32[28,80,128]{2,1,0:T(8,128)}) custom-call(f32[1,128]{1,0:T(1,128)} %add.176.refs_0_, f32[1,128]{1,0:T(1,128)} %add.181.refs_1_, f32[28,80,128]{2,1,0:T(8,128)} %get-tuple-element.29.refs_2_, f32[28,80,128]{2,1,0:T(8,128)} %get-tuple-element.30.refs_3_, ...), custom_call_target="tpu_custom_call" | custom-call | flops 11468800 | bytes 10321920 | tf_op jit(solution)/shard_map/pallas_call | solution.py:231
  (112 shorter events, 61.0 us)
Async XLA Ops:
  6.9 22.0 %collective-permute-start = (f32[67,6,128]{0,2,1:T(8,128)}, f32[67,6,128]{0,2,1:T(8,128)S(1)}, u32[]{:S(2)}, u32[]{:S(2)}) collective-permute-start(f32[67,6,128]{0,2,1:T(8,128)} %get-tuple-element.46), channel_id=1, source_target_pairs={{0,4},{4,8},{8,12},{12,16},{16,20},{20,24},{24,28},{1,5},{5,9},{9,... | collective-permute-start | bytes 617480 | tf_op jit(solution)/shard_map/ppermute | solution.py:20
  11.8 17.1 %collective-permute-start.1 = (f32[67,6,128]{0,2,1:T(8,128)}, f32[67,6,128]{0,2,1:T(8,128)}, u32[]{:S(2)}, u32[]{:S(2)}) collective-permute-start(f32[67,6,128]{0,2,1:T(8,128)} %get-tuple-element.47), channel_id=1, source_target_pairs={{4,0},{8,4},{12,8},{16,12},{20,16},{24,20},{28,24},{5,1},{9,5},{13... | collective-permute-start | bytes 617480 | tf_op jit(solution)/shard_map/ppermute | solution.py:22
  15.2 21.0 %copy-start = (f32[1,16,128]{0,2,1:T(8,128)S(1)}, f32[1,16,128]{0,2,1:T(8,128)}, u32[]{:S(2)}) copy-start(f32[1,16,128]{0,2,1:T(8,128)} %copy.21) | copy-start | bytes 24580
  15.2 21.0 %copy-start.6 = (pred[80]{0:T(512)(128)(4,1)S(1)}, pred[80]{0:T(512)(128)(4,1)}, u32[]{:S(2)}) copy-start(pred[80]{0:T(512)(128)(4,1)} %constant.21.clone.1) | copy-start | bytes 244
  29.9 3.1 %collective-permute-start.2 = (f32[67,28,6]{0,2,1:T(8,128)S(1)}, f32[67,28,6]{0,2,1:T(8,128)S(1)}, u32[]{:S(2)}, u32[]{:S(2)}) collective-permute-start(f32[67,28,6]{0,2,1:T(8,128)S(1)} %get-tuple-element.44), channel_id=1, source_target_pairs={{0,1},{1,2},{2,3},{4,5},{5,6},{6,7},{8,9},{9,10},{10,11},{12,13},{... | collective-permute-start | bytes 135080 | tf_op jit(solution)/shard_map/ppermute | solution.py:20
  31.2 5.0 %collective-permute-start.3 = (f32[67,28,6]{0,2,1:T(8,128)S(1)}, f32[67,28,6]{0,2,1:T(8,128)S(1)}, u32[]{:S(2)}, u32[]{:S(2)}) collective-permute-start(f32[67,28,6]{0,2,1:T(8,128)S(1)} %get-tuple-element.45), channel_id=1, source_target_pairs={{1,0},{2,1},{3,2},{5,4},{6,5},{7,6},{9,8},{10,9},{11,10},{13,12},{... | collective-permute-start | bytes 135080 | tf_op jit(solution)/shard_map/ppermute | solution.py:22
  33.1 5.3 %copy-start.1 = (f32[67,28,6]{0,2,1:T(8,128)}, f32[67,28,6]{0,2,1:T(8,128)S(1)}, u32[]{:S(2)}) copy-start(f32[67,28,6]{0,2,1:T(8,128)S(1)} %collective-permute-done.2) | copy-start | bytes 135076
  53.4 4.4 %collective-permute-start.4 = (f32[2,128]{1,0:T(2,128)}, f32[2,128]{1,0:T(2,128)S(1)}, u32[]{:S(2)}, u32[]{:S(2)}) collective-permute-start(f32[2,128]{1,0:T(2,128)} %get-tuple-element.18), channel_id=1, source_target_pairs={{0,1},{1,0},{2,3},{3,2},{4,5},{5,4},{6,7},{7,6},{8,9},{9,8},{10,11... | collective-permute-start | bytes 3080 | tf_op jit(solution)/shard_map/ppermute | solution.py:56
  58.5 3.6 %collective-permute-start.5 = (f32[2,128]{1,0:T(2,128)S(1)}, f32[2,128]{1,0:T(2,128)S(1)}, u32[]{:S(2)}, u32[]{:S(2)}) collective-permute-start(f32[2,128]{1,0:T(2,128)S(1)} %add.157), channel_id=1, source_target_pairs={{0,2},{1,3},{2,0},{3,1},{4,6},{5,7},{6,4},{7,5},{8,10},{9,11},{10,... | collective-permute-start | bytes 3080 | tf_op jit(solution)/shard_map/ppermute | solution.py:56
  62.1 3.9 %collective-permute-start.6 = (f32[2,128]{1,0:T(2,128)S(1)}, f32[2,128]{1,0:T(2,128)S(1)}, u32[]{:S(2)}, u32[]{:S(2)}) collective-permute-start(f32[2,128]{1,0:T(2,128)S(1)} %add.158), channel_id=1, source_target_pairs={{0,4},{4,0},{8,12},{12,8},{16,20},{20,16},{24,28},{28,24},{1,5},{5... | collective-permute-start | bytes 3080 | tf_op jit(solution)/shard_map/ppermute | solution.py:56
  66.0 4.7 %collective-permute-start.7 = (f32[2,128]{1,0:T(2,128)S(1)}, f32[2,128]{1,0:T(2,128)S(1)}, u32[]{:S(2)}, u32[]{:S(2)}) collective-permute-start(f32[2,128]{1,0:T(2,128)S(1)} %add.159), channel_id=1, source_target_pairs={{0,8},{4,12},{8,0},{12,4},{16,24},{20,28},{24,16},{28,20},{1,9},{5... | collective-permute-start | bytes 3080 | tf_op jit(solution)/shard_map/ppermute | solution.py:56
  70.7 4.6 %collective-permute-start.8 = (f32[2,128]{1,0:T(2,128)S(1)}, f32[2,128]{1,0:T(2,128)S(1)}, u32[]{:S(2)}, u32[]{:S(2)}) collective-permute-start(f32[2,128]{1,0:T(2,128)S(1)} %add.160), channel_id=1, source_target_pairs={{0,16},{4,20},{8,24},{12,28},{16,0},{20,4},{24,8},{28,12},{1,17},{... | collective-permute-start | bytes 3080 | tf_op jit(solution)/shard_map/ppermute | solution.py:56
  79.6 1.4 collective-permute-start.9
  81.6 3.6 %collective-permute-start.10 = (f32[1,128]{1,0:T(1,128)S(1)}, f32[1,128]{1,0:T(1,128)S(1)}, u32[]{:S(2)}, u32[]{:S(2)}) collective-permute-start(f32[1,128]{1,0:T(1,128)S(1)} %add.162), channel_id=1, source_target_pairs={{0,2},{1,3},{2,0},{3,1},{4,6},{5,7},{6,4},{7,5},{8,10},{9,11},{10,... | collective-permute-start | bytes 1544 | tf_op jit(solution)/shard_map/ppermute | solution.py:56
  85.2 3.6 %collective-permute-start.11 = (f32[1,128]{1,0:T(1,128)S(1)}, f32[1,128]{1,0:T(1,128)S(1)}, u32[]{:S(2)}, u32[]{:S(2)}) collective-permute-start(f32[1,128]{1,0:T(1,128)S(1)} %add.163), channel_id=1, source_target_pairs={{0,4},{4,0},{8,12},{12,8},{16,20},{20,16},{24,28},{28,24},{1,5},{5... | collective-permute-start | bytes 1544 | tf_op jit(solution)/shard_map/ppermute | solution.py:56
  88.8 3.6 %collective-permute-start.12 = (f32[1,128]{1,0:T(1,128)S(1)}, f32[1,128]{1,0:T(1,128)S(1)}, u32[]{:S(2)}, u32[]{:S(2)}) collective-permute-start(f32[1,128]{1,0:T(1,128)S(1)} %add.164), channel_id=1, source_target_pairs={{0,8},{4,12},{8,0},{12,4},{16,24},{20,28},{24,16},{28,20},{1,9},{5... | collective-permute-start | bytes 1544 | tf_op jit(solution)/shard_map/ppermute | solution.py:56
  92.4 4.5 %collective-permute-start.13 = (f32[1,128]{1,0:T(1,128)S(1)}, f32[1,128]{1,0:T(1,128)S(1)}, u32[]{:S(2)}, u32[]{:S(2)}) collective-permute-start(f32[1,128]{1,0:T(1,128)S(1)} %add.165), channel_id=1, source_target_pairs={{0,16},{4,20},{8,24},{12,28},{16,0},{20,4},{24,8},{28,12},{1,17},{... | collective-permute-start | bytes 1544 | tf_op jit(solution)/shard_map/ppermute | solution.py:56
  103.5 1.2 collective-permute-start.14
  105.4 3.6 %collective-permute-start.15 = (f32[1,128]{1,0:T(1,128)S(1)}, f32[1,128]{1,0:T(1,128)S(1)}, u32[]{:S(2)}, u32[]{:S(2)}) collective-permute-start(f32[1,128]{1,0:T(1,128)S(1)} %add.167), channel_id=1, source_target_pairs={{0,2},{1,3},{2,0},{3,1},{4,6},{5,7},{6,4},{7,5},{8,10},{9,11},{10,... | collective-permute-start | bytes 1544 | tf_op jit(solution)/shard_map/ppermute | solution.py:56
  109.0 3.6 %collective-permute-start.16 = (f32[1,128]{1,0:T(1,128)S(1)}, f32[1,128]{1,0:T(1,128)S(1)}, u32[]{:S(2)}, u32[]{:S(2)}) collective-permute-start(f32[1,128]{1,0:T(1,128)S(1)} %add.168), channel_id=1, source_target_pairs={{0,4},{4,0},{8,12},{12,8},{16,20},{20,16},{24,28},{28,24},{1,5},{5... | collective-permute-start | bytes 1544 | tf_op jit(solution)/shard_map/ppermute | solution.py:56
  112.6 3.6 %collective-permute-start.17 = (f32[1,128]{1,0:T(1,128)S(1)}, f32[1,128]{1,0:T(1,128)S(1)}, u32[]{:S(2)}, u32[]{:S(2)}) collective-permute-start(f32[1,128]{1,0:T(1,128)S(1)} %add.169), channel_id=1, source_target_pairs={{0,8},{4,12},{8,0},{12,4},{16,24},{20,28},{24,16},{28,20},{1,9},{5... | collective-permute-start | bytes 1544 | tf_op jit(solution)/shard_map/ppermute | solution.py:56
  116.2 4.5 %collective-permute-start.18 = (f32[1,128]{1,0:T(1,128)S(1)}, f32[1,128]{1,0:T(1,128)S(1)}, u32[]{:S(2)}, u32[]{:S(2)}) collective-permute-start(f32[1,128]{1,0:T(1,128)S(1)} %add.170), channel_id=1, source_target_pairs={{0,16},{4,20},{8,24},{12,28},{16,0},{20,4},{24,8},{28,12},{1,17},{... | collective-permute-start | bytes 1544 | tf_op jit(solution)/shard_map/ppermute | solution.py:56
  125.8 1.2 collective-permute-start.19
  127.7 3.6 %collective-permute-start.20 = (f32[1,128]{1,0:T(1,128)S(1)}, f32[1,128]{1,0:T(1,128)S(1)}, u32[]{:S(2)}, u32[]{:S(2)}) collective-permute-start(f32[1,128]{1,0:T(1,128)S(1)} %add.172), channel_id=1, source_target_pairs={{0,2},{1,3},{2,0},{3,1},{4,6},{5,7},{6,4},{7,5},{8,10},{9,11},{10,... | collective-permute-start | bytes 1544 | tf_op jit(solution)/shard_map/ppermute | solution.py:56
  131.2 3.6 %collective-permute-start.21 = (f32[1,128]{1,0:T(1,128)S(1)}, f32[1,128]{1,0:T(1,128)S(1)}, u32[]{:S(2)}, u32[]{:S(2)}) collective-permute-start(f32[1,128]{1,0:T(1,128)S(1)} %add.173), channel_id=1, source_target_pairs={{0,4},{4,0},{8,12},{12,8},{16,20},{20,16},{24,28},{28,24},{1,5},{5... | collective-permute-start | bytes 1544 | tf_op jit(solution)/shard_map/ppermute | solution.py:56
  134.8 3.6 %collective-permute-start.22 = (f32[1,128]{1,0:T(1,128)S(1)}, f32[1,128]{1,0:T(1,128)S(1)}, u32[]{:S(2)}, u32[]{:S(2)}) collective-permute-start(f32[1,128]{1,0:T(1,128)S(1)} %add.174), channel_id=1, source_target_pairs={{0,8},{4,12},{8,0},{12,4},{16,24},{20,28},{24,16},{28,20},{1,9},{5... | collective-permute-start | bytes 1544 | tf_op jit(solution)/shard_map/ppermute | solution.py:56
  138.4 4.5 %collective-permute-start.23 = (f32[1,128]{1,0:T(1,128)S(1)}, f32[1,128]{1,0:T(1,128)S(1)}, u32[]{:S(2)}, u32[]{:S(2)}) collective-permute-start(f32[1,128]{1,0:T(1,128)S(1)} %add.175), channel_id=1, source_target_pairs={{0,16},{4,20},{8,24},{12,28},{16,0},{20,4},{24,8},{28,12},{1,17},{... | collective-permute-start | bytes 1544 | tf_op jit(solution)/shard_map/ppermute | solution.py:56
  149.6 1.4 collective-permute-start.24
  151.6 3.6 %collective-permute-start.25 = (f32[1,128]{1,0:T(1,128)S(1)}, f32[1,128]{1,0:T(1,128)S(1)}, u32[]{:S(2)}, u32[]{:S(2)}) collective-permute-start(f32[1,128]{1,0:T(1,128)S(1)} %add.177), channel_id=1, source_target_pairs={{0,2},{1,3},{2,0},{3,1},{4,6},{5,7},{6,4},{7,5},{8,10},{9,11},{10,... | collective-permute-start | bytes 1544 | tf_op jit(solution)/shard_map/ppermute | solution.py:56
  155.1 3.6 %collective-permute-start.26 = (f32[1,128]{1,0:T(1,128)S(1)}, f32[1,128]{1,0:T(1,128)S(1)}, u32[]{:S(2)}, u32[]{:S(2)}) collective-permute-start(f32[1,128]{1,0:T(1,128)S(1)} %add.178), channel_id=1, source_target_pairs={{0,4},{4,0},{8,12},{12,8},{16,20},{20,16},{24,28},{28,24},{1,5},{5... | collective-permute-start | bytes 1544 | tf_op jit(solution)/shard_map/ppermute | solution.py:56
  158.7 5.0 %collective-permute-start.27 = (f32[1,128]{1,0:T(1,128)S(1)}, f32[1,128]{1,0:T(1,128)S(1)}, u32[]{:S(2)}, u32[]{:S(2)}) collective-permute-start(f32[1,128]{1,0:T(1,128)S(1)} %add.179), channel_id=1, source_target_pairs={{0,8},{4,12},{8,0},{12,4},{16,24},{20,28},{24,16},{28,20},{1,9},{5... | collective-permute-start | bytes 1544 | tf_op jit(solution)/shard_map/ppermute | solution.py:56
  163.7 4.5 %collective-permute-start.28 = (f32[1,128]{1,0:T(1,128)S(1)}, f32[1,128]{1,0:T(1,128)S(1)}, u32[]{:S(2)}, u32[]{:S(2)}) collective-permute-start(f32[1,128]{1,0:T(1,128)S(1)} %add.180), channel_id=1, source_target_pairs={{0,16},{4,20},{8,24},{12,28},{16,0},{20,4},{24,8},{28,12},{1,17},{... | collective-permute-start | bytes 1544 | tf_op jit(solution)/shard_map/ppermute | solution.py:56
  (4 other events, 6.2 us)

commit v6 on v5

--- a/solution.py
+++ b/solution.py
@@ -81,7 +81,8 @@
 
 
 class _Plan:
-    def __init__(self, slab_rows, first_inner, inner_rows):
+    def __init__(self, slab_rows, first_inner, inner_rows, half):
+        self.half = half
         self.slab_rows = slab_rows
         self.first_inner = first_inner
         self.inner_rows = inner_rows
@@ -118,38 +119,70 @@
     return lax.fori_loop(1, last, second_pass, jnp.zeros((1, source.shape[2]), jnp.float32))
 
 
-def _first_kernel(plan, z_ref, gain_ref, weight_ref, inside_ref, row_ref, inner_ref,
-                  stiff_out, applied_out, dots_out, scratch):
+def _spread(value, lane):
+    return jnp.broadcast_to(value[:, lane : lane + 1], value.shape)
+
+
+def _plane_row(value, diagonal):
+    return jnp.sum(jnp.where(diagonal, value, 0.0), axis=0, keepdims=True)
+
+
+def _first_kernel(plan, ext_ref, inside_ref, row_ref, inner_ref, diagonal_ref,
+                  z_out, gain_out, weight_out, stiff_out, applied_out, dots_out, stiff_obs_out,
+                  observed_scr, scratch):
     last = plan.slab_rows - 1
+    sublanes = z_out.shape[1]
+    lanes = z_out.shape[2]
+    probes = lanes // 2
+
+    def relayout(r, carry):
+        cells = ext_ref[r]
+        left = cells[0:sublanes]
+        right = cells[plan.half : plan.half + sublanes]
+        low = lax.broadcasted_iota(jnp.int32, (sublanes, lanes), 1) < probes
+        z_out[r] = jnp.where(low, left, pltpu.roll(right, probes, 1))
+        observed_scr[r] = jnp.where(low, _spread(left, probes), _spread(right, probes))
+        gain_out[r] = jnp.where(low, _spread(left, probes + 1), _spread(right, probes + 1)) + 20.0 / 6.0
+        weight_out[r] = jnp.where(low, _spread(left, probes + 2), _spread(right, probes + 2))
+        return carry
+
+    lax.fori_loop(0, plan.slab_rows, relayout, 0)
     _zero_edges(stiff_out)
 
     def probe_pass(r, totals):
-        stiff_out[r] = _stiffen_row(z_ref, r, gain_ref[r])
-        z = z_ref[r]
+        stiff_out[r] = _stiffen_row(z_out, r, gain_out[r])
+        z = z_out[r]
         inner = (inner_ref[...] > 0.5) & plan.inner_row(r)
         return totals + _row_sum(z * z, inner)
 
-    zz = lax.fori_loop(1, last, probe_pass, jnp.zeros((1, z_ref.shape[2]), jnp.float32))
+    zz = lax.fori_loop(1, last, probe_pass, jnp.zeros((1, lanes), jnp.float32))
     _zero_edges(scratch)
 
     def weigh(r, carry):
-        scratch[r] = weight_ref[r] * stiff_out[r]
+        scratch[r] = weight_out[r] * stiff_out[r]
         return carry
 
     lax.fori_loop(1, last, weigh, 0)
 
     def second_pass(r, totals):
-        applied = _stiffen_row(scratch, r, gain_ref[r])
+        applied = _stiffen_row(scratch, r, gain_out[r])
         keep = (inside_ref[...] > 0.5) & (row_ref[r] > 0.5)
         applied = jnp.where(keep, applied, 0.0)
         applied_out[r] = applied
         inner = (inner_ref[...] > 0.5) & plan.inner_row(r)
-        return totals + _row_sum(z_ref[r] * applied, inner)
+        return totals + _row_sum(z_out[r] * applied, inner)
 
     _zero_edges(applied_out)
-    za = lax.fori_loop(1, last, second_pass, jnp.zeros((1, z_ref.shape[2]), jnp.float32))
+    za = lax.fori_loop(1, last, second_pass, jnp.zeros((1, lanes), jnp.float32))
     dots_out[0:1, :] = zz
     dots_out[1:2, :] = za
+
+    def observed_pass(r, carry):
+        stiff_obs = _stiffen_row(observed_scr, plan.first_inner + r, gain_out[plan.first_inner + r])
+        stiff_obs_out[pl.ds(r, 1), :] = _plane_row(stiff_obs, diagonal_ref[...] > 0.5)
+        return carry
+
+    lax.fori_loop(0, plan.inner_rows, observed_pass, 0)
 
 
 def _start_kernel(plan, first_ref, z_ref, applied_ref, inner_ref, solution_out, residual_out, rr_out):
@@ -196,34 +229,54 @@
 
 
 def _final_kernel(plan, norm_ref, curvature_ref, solution_ref, direction_ref, z_ref, stiff_ref,
-                  gain_ref, weight_out, kappa_out, scratch):
+                  gain_ref, stiff_obs_ref, observed_ref, weight_ref, diagonal_ref,
+                  grad_kappa_out, grad_weight_out, scratch):
     step = _ratio(norm_ref, 0, curvature_ref, 0)
-    last = plan.slab_rows - 1
+    lanes = z_ref.shape[2]
+    probes = lanes // 2
 
     def new_solution(r, carry):
         scratch[r] = solution_ref[r] + step * direction_ref[r]
         return carry
 
     lax.fori_loop(0, plan.slab_rows, new_solution, 0)
-    _zero_edges(weight_out)
-    _zero_edges(kappa_out)
-
-    def body(r, carry):
+
+    def probe_sum(value, low):
+        first = jnp.sum(jnp.where(low, value, 0.0), axis=1, keepdims=True)
+        second = jnp.sum(jnp.where(low, 0.0, value), axis=1, keepdims=True)
+        return jnp.where(low, first, second)
+
+    def body(i, carry):
+        r = plan.first_inner + i
+        solution = scratch[r]
         stiff_solution = _stiffen_row(scratch, r, gain_ref[r])
         stiff_probe = stiff_ref[r]
-        weight_out[r] = stiff_solution * stiff_probe
-        kappa_out[r] = scratch[r] * stiff_probe + stiff_solution * z_ref[r]
-        return carry
-
-    lax.fori_loop(1, last, body, 0)
+        low = lax.broadcasted_iota(jnp.int32, solution.shape, 1) < probes
+        diagonal = diagonal_ref[...] > 0.5
+        weight_total = _plane_row(probe_sum(stiff_solution * stiff_probe, low), diagonal)
+        kappa_total = _plane_row(
+            probe_sum(solution * stiff_probe + stiff_solution * z_ref[r], low), diagonal
+        )
+        stiff_obs = stiff_obs_ref[pl.ds(i, 1), :]
+        observed = observed_ref[pl.ds(i, 1), :]
+        weight = weight_ref[pl.ds(i, 1), :]
+        grad_weight_out[pl.ds(i, 1), :] = (
+            0.5 * weight_total / probes - 0.5 * stiff_obs * stiff_obs
+        )
+        grad_kappa_out[pl.ds(i, 1), :] = (
+            0.5 * weight * (kappa_total / probes) - observed * weight * stiff_obs
+        )
+        return carry
+
+    lax.fori_loop(0, plan.inner_rows, body, 0)
 
 
 def _vmem():
     return pl.BlockSpec(memory_space=pltpu.VMEM)
 
 
-def _call(kernel, plan, inputs, out_shapes, scratch=0, smem=()):
-    field = out_shapes[0]
+def _call(kernel, plan, inputs, out_shapes, scratch=0, smem=(), field=None):
+    field = out_shapes[0] if field is None else field
     nbytes = 4 * field.shape[0] * field.shape[1] * field.shape[2]
     in_specs = [
         pl.BlockSpec(memory_space=pltpu.SMEM) if i in smem else _vmem() for i in range(len(inputs))
@@ -244,8 +297,8 @@
 
 def on_device(probes, observed, kappa_sq, variance_weight):
     probe_count, rows, cols = probes.shape
-    assert rows >= HALO and cols % 2 == 0 and cols // 2 >= HALO
     half = cols // 2
+    assert rows >= HALO and cols % 2 == 0 and half >= HALO and half == probe_count
     width = half + 2 * HALO
     sublanes = -(-width // 8) * 8
     slab_rows = rows + 2 * HALO
@@ -254,20 +307,10 @@
         [probes, observed[None], kappa_sq[None], variance_weight[None]], axis=0
     )
     ext = extended(stacked, (("rows", 1), ("cols", 2)), HALO)
-    halves = [
-        jnp.pad(ext[:, :, h * half : h * half + width], ((0, 0), (0, 0), (0, sublanes - width)))
-        for h in range(2)
-    ]
-
-    def plane_on_lanes(index):
-        return jnp.concatenate(
-            [jnp.broadcast_to(h[index][:, :, None], h.shape[1:] + (probe_count,)) for h in halves],
-            axis=2,
-        )
-
-    z = jnp.concatenate([jnp.transpose(h[:probe_count], (1, 2, 0)) for h in halves], axis=2)
-    gain = plane_on_lanes(probe_count + 1) + 20.0 / 6.0
-    weight = plane_on_lanes(probe_count + 2)
+    ext = jnp.pad(
+        ext, ((0, lanes - ext.shape[0]), (0, 0), (0, half + sublanes - ext.shape[2]))
+    )
+    ext = jnp.transpose(ext, (1, 2, 0))
 
     row_at = lax.axis_index("rows") * rows - HALO + lax.iota(jnp.int32, slab_rows)
     row_in = ((row_at >= 0) & (row_at < rows * lax.axis_size("rows"))).astype(jnp.float32)
@@ -286,14 +329,18 @@
 
     inside = on_lanes_of(col_in)
     inner = on_lanes_of(col_inner)
-    plan = _Plan(slab_rows, HALO, rows)
+    lane_col = lax.iota(jnp.int32, lanes) % half + HALO
+    diagonal = (lax.iota(jnp.int32, sublanes)[:, None] == lane_col[None, :]).astype(jnp.float32)
+    plan = _Plan(slab_rows, HALO, rows, half)
 
     field = jax.ShapeDtypeStruct((slab_rows, sublanes, lanes), jnp.float32)
     lane_row = jax.ShapeDtypeStruct((1, lanes), jnp.float32)
-
-    stiff_probe, applied, first = _call(
-        _first_kernel, plan, (z, gain, weight, inside, row_in, inner),
-        (field, field, jax.ShapeDtypeStruct((2, lanes), jnp.float32)), scratch=1, smem=(4,),
+    out_plane = jax.ShapeDtypeStruct((rows, cols), jnp.float32)
+
+    z, gain, weight, stiff_probe, applied, first, stiff_obs = _call(
+        _first_kernel, plan, (ext, inside, row_in, inner, diagonal),
+        (field, field, field, field, field, jax.ShapeDtypeStruct((2, lanes), jnp.float32), out_plane),
+        scratch=2, smem=(2,),
     )
     first = all_sum(first)
     solution, residual, rr = _call(
@@ -317,22 +364,11 @@
                 (field, field, lane_row),
             )
 
-    weight_terms, kappa_terms = _call(
-        _final_kernel, plan, (norm_now, curvature, solution, direction, z, stiff_probe, gain),
-        (field, field), scratch=1,
-    )
-
-    def probe_total(terms):
-        terms = terms[HALO : HALO + rows, HALO : HALO + half]
-        per_half = jnp.sum(terms.reshape(rows, half, 2, probe_count), axis=3)
-        return jnp.transpose(per_half, (0, 2, 1)).reshape(rows, cols)
-
-    weight_total = probe_total(weight_terms)
-    kappa_total = probe_total(kappa_terms)
-    stiff_obs = stiffen(ext[probe_count], ext[probe_count + 1])[HALO : HALO + rows, HALO : HALO + cols]
-    grad_weight = 0.5 * weight_total / probe_count - 0.5 * stiff_obs * stiff_obs
-    grad_kappa = (
-        0.5 * variance_weight * (kappa_total / probe_count) - observed * variance_weight * stiff_obs
+    grad_kappa, grad_weight = _call(
+        _final_kernel, plan,
+        (norm_now, curvature, solution, direction, z, stiff_probe, gain, stiff_obs, observed,
+         variance_weight, diagonal),
+        (out_plane, out_plane), scratch=1, field=field,
     )
     return (grad_kappa, grad_weight)
 

time: 182 us -> 172 us (0.945)
  other arithmetic: 27 us -> 13.7 us
  local copies, waits for them, and re-layouts: 13.2 us -> 5.92 us
  Pallas kernels: 32.2 us -> 38.1 us
  waiting for transfers between devices: 64.8 us -> 69.1 us
    pallas_call x6, Pallas kernels: 32.2 us -> 38.1 us  [_call(): pl.pallas_call(lambda *refs: kernel(plan, *refs), out_shape=out_shapes, i...]
    slice x3 -> x0, local copies, waits for them, and re-layouts: 5.4 us -> none  [the longest x1 3.16 us: plane_on_lanes(): h[index][:, :, None]]
    add x3 -> x1, other arithmetic: 4.53 us -> 0.01 us  [on_device(): lane_col = lax.iota(jnp.int32, lanes) % half + HALO]
    ppermute x25, waiting for transfers between devices: 48.1 us -> 51.8 us  [all_sum(): lax.ppermute(terms, axis, [(i, i ^ hop) for i in range(count)])]
    concatenate x2 -> x0, other arithmetic: 2.78 us -> none  [the longest x1 1.4 us: on_device(): jnp.concatenate([jnp.transpose(h[:probe_count], (1, 2, 0)) for h in halve...]
    reduce_sum x2 -> x0, other arithmetic: 2.3 us -> none  [probe_total(): per_half = jnp.sum(terms.reshape(rows, half, 2, probe_count), axis=3)]
    pad x1 -> x0, other arithmetic: 2.18 us -> none  [on_device(): jnp.pad(ext[:, :, h * half:h * half + width], ((0, 0), (0, 0), (0, sublan...]
  transfers between devices with their start and end apart: 29 -> 29, of which waited for: 26 -> 27; matrix products, arithmetic and copies ran while one was open for 5% -> 1% of each run, Pallas kernels for 0% -> 0%
where the time goes in v6:
time: 172 us
  waiting for transfers between devices  69.1 us (40%)
  starting transfers between devices  43.9 us (26%)
  Pallas kernels  38.1 us (22%)
  other arithmetic  13.7 us (8%)
  local copies, waits for them, and re-layouts  5.92 us (3%)
    ppermute x25, waiting for transfers between devices, all_sum(): lax.ppermute(terms, axis, [(i, i ^ hop) for i in range(count)])  51.8 us
    pallas_call x6, Pallas kernels, _call(): pl.pallas_call(lambda *refs: kernel(plan, *refs), out_shape=out_shapes, i...  38.1 us
    ppermute x25, starting transfers between devices, all_sum(): lax.ppermute(terms, axis, [(i, i ^ hop) for i in range(count)])  35.2 us
    ppermute x2, waiting for transfers between devices, extended(): lax.ppermute(tail, axis, [(i, (i + 1) % count) for i in range(ends)])  14.1 us
    ppermute x2, starting transfers between devices, extended(): lax.ppermute(tail, axis, [(i, (i + 1) % count) for i in range(ends)])  6.18 us
    add x25, other arithmetic, all_sum(): terms + lax.ppermute(terms, axis, [(i, i ^ hop) for i in range(count)])  6.05 us
    slice x2, other arithmetic, extended(): lax.slice_in_dim(cells, cells.shape[dim] - width, cells.shape[dim], axis=...  3.75 us
  transfers between devices with their start and end apart: 29, of which 27 were waited for; matrix products, arithmetic and copies ran while one was open for 1% of the time, Pallas kernels for 0%

profile of v6, /device:TPU:0, one launch (start us, length us, event | category | flops | bytes accessed | tf_op | source)
XLA Modules:
  0.0 171.5 jit_solution(5476359622020523431)
XLA Ops:
  4.9 2.7 %pad_maximum_fusion.4 = (f32[67,6,128]{0,2,1:T(8,128)}, f32[67,6,128]{0,2,1:T(8,128)}) fusion(f32[1,16,128]{0,2,1:T(8,128)S(1)} %copy.10, f32[1,16,128]{0,2,1:T(8,128)S(1)} %copy.9, f32[1,16,128]{0,2,1:T(8,128)} %copy.8, f32[64,16,128]{0,2,1:T(8,128)S(1)} %copy.7), kind=kLoop, calls=%fused_computation.5 | loop fusion | flops 308736 | bytes 960512 | tf_op jit(solution)/shard_map/slice | solution.py:17
  7.6 4.9 %collective-permute-start = (f32[67,6,128]{0,2,1:T(8,128)}, f32[67,6,128]{0,2,1:T(8,128)S(1)}, u32[]{:S(2)}, u32[]{:S(2)}) collective-permute-start(f32[67,6,128]{0,2,1:T(8,128)} %get-tuple-element.40), channel_id=1, source_target_pairs={{0,4},{4,8},{8,12},{12,16},{16,20},{20,24},{24,28},{1,5},{5,9},{9,... | collective-permute-start | bytes 617480 | tf_op jit(solution)/shard_map/ppermute | solution.py:20
  15.4 14.1 %collective-permute-done = f32[67,6,128]{0,2,1:T(8,128)S(1)} collective-permute-done((f32[67,6,128]{0,2,1:T(8,128)}, f32[67,6,128]{0,2,1:T(8,128)S(1)}, u32[]{:S(2)}, u32[]{:S(2)}) %collective-permute-start) | collective-permute-done | bytes 205856 | tf_op jit(solution)/shard_map/ppermute | solution.py:20
  33.7 3.1 %collective-permute-done.3 = f32[67,28,6]{0,2,1:T(8,128)S(1)} collective-permute-done((f32[67,28,6]{0,2,1:T(8,128)S(1)}, f32[67,28,6]{0,2,1:T(8,128)S(1)}, u32[]{:S(2)}, u32[]{:S(2)}) %collective-permute-start.3) | collective-permute-done | bytes 45056 | tf_op jit(solution)/shard_map/ppermute | solution.py:22
  36.9 2.0 %pad_maximum_fusion = f32[67,28,140]{0,2,1:T(8,128)S(1)} fusion(f32[67,28,6]{0,2,1:T(8,128)S(1)} %collective-permute-done.3, f32[67,6,128]{0,2,1:T(8,128)} %collective-permute-done.1, f32[1,16,128]{0,2,1:T(8,128)S(1)} %copy.10, f32[1,16,128]{0,2,1:T(8,128)S(1)} %copy.9, f32[1,16,128]{0,2,1:T(8,128)S(1)} %copy-done, f32[64,16,128]{0,2,1:T(8,128)S(1)} %copy.7, ...), kind=kLoop, calls=%fused_computation | loop fusion | flops 1838480 | bytes 2101120 | tf_op jit(solution)/shard_map/concatenate | solution.py:18
  40.4 11.3 %shard_map.59 = (f32[28,80,128]{2,1,0:T(8,128)}, f32[28,80,128]{2,1,0:T(8,128)}, f32[28,80,128]{2,1,0:T(8,128)}, f32[28,80,128]{2,1,0:T(8,128)}, f32[28,80,128]{...) custom-call(f32[28,144,128]{2,1,0:T(8,128)} %pad_bitcast_fusion.refs_0_, ...), custom_call_target="tpu_custom_call" | custom-call | flops 11468800 | bytes 13762560 | tf_op jit(solution)/shard_map/pallas_call | solution.py:284
  51.7 3.4 %collective-permute-start.4 = (f32[2,128]{1,0:T(2,128)}, f32[2,128]{1,0:T(2,128)S(1)}, u32[]{:S(2)}, u32[]{:S(2)}) collective-permute-start(f32[2,128]{1,0:T(2,128)} %get-tuple-element.20), channel_id=1, source_target_pairs={{0,1},{1,0},{2,3},{3,2},{4,5},{5,4},{6,7},{7,6},{8,9},{9,8},{10,11... | collective-permute-start | bytes 3080 | tf_op jit(solution)/shard_map/ppermute | solution.py:56
  56.9 3.5 %collective-permute-done.5 = f32[2,128]{1,0:T(2,128)S(1)} collective-permute-done((f32[2,128]{1,0:T(2,128)S(1)}, f32[2,128]{1,0:T(2,128)S(1)}, u32[]{:S(2)}, u32[]{:S(2)}) %collective-permute-start.5) | collective-permute-done | bytes 1056 | tf_op jit(solution)/shard_map/ppermute | solution.py:56
  60.4 2.4 %collective-permute-start.6 = (f32[2,128]{1,0:T(2,128)S(1)}, f32[2,128]{1,0:T(2,128)S(1)}, u32[]{:S(2)}, u32[]{:S(2)}) collective-permute-start(f32[2,128]{1,0:T(2,128)S(1)} %add.145), channel_id=1, source_target_pairs={{0,4},{4,0},{8,12},{12,8},{16,20},{20,16},{24,28},{28,24},{1,5},{5... | collective-permute-start | bytes 3080 | tf_op jit(solution)/shard_map/ppermute | solution.py:56
  64.3 3.1 %collective-permute-start.7 = (f32[2,128]{1,0:T(2,128)S(1)}, f32[2,128]{1,0:T(2,128)S(1)}, u32[]{:S(2)}, u32[]{:S(2)}) collective-permute-start(f32[2,128]{1,0:T(2,128)S(1)} %add.146), channel_id=1, source_target_pairs={{0,8},{4,12},{8,0},{12,4},{16,24},{20,28},{24,16},{28,20},{1,9},{5... | collective-permute-start | bytes 3080 | tf_op jit(solution)/shard_map/ppermute | solution.py:56
  68.9 3.0 %collective-permute-start.8 = (f32[2,128]{1,0:T(2,128)S(1)}, f32[2,128]{1,0:T(2,128)S(1)}, u32[]{:S(2)}, u32[]{:S(2)}) collective-permute-start(f32[2,128]{1,0:T(2,128)S(1)} %add.147), channel_id=1, source_target_pairs={{0,16},{4,20},{8,24},{12,28},{16,0},{20,4},{24,8},{28,12},{1,17},{... | collective-permute-start | bytes 3080 | tf_op jit(solution)/shard_map/ppermute | solution.py:56
  74.1 3.9 %shard_map.60 = (f32[28,80,128]{2,1,0:T(8,128)}, f32[28,80,128]{2,1,0:T(8,128)}, f32[1,128]{1,0:T(1,128)}) custom-call(f32[2,128]{1,0:T(2,128)} %add.148.refs_0_.refs_1_, f32[28,80,128]{2,1,0:T(8,128)} %get-tuple-element.21.refs_1_.refs_3_.refs_4_, f32[28,80,128]{2,1,0:T(8,128)} %get-tuple-element.22.refs_2_, f32[80,128]{1,0:T(8,128)} %get-tuple-element.43.refs_3_.refs_8_.refs_6_), custom_call_target="tpu_custom_call" | custom-call | flops 11468800 | bytes 8028160 | tf_op jit(solution)/shard_map/pallas_call | solution.py:284
  80.1 3.4 %collective-permute-done.10 = f32[1,128]{1,0:T(1,128)S(1)} collective-permute-done((f32[1,128]{1,0:T(1,128)S(1)}, f32[1,128]{1,0:T(1,128)S(1)}, u32[]{:S(2)}, u32[]{:S(2)}) %collective-permute-start.10) | collective-permute-done | bytes 544 | tf_op jit(solution)/shard_map/ppermute | solution.py:56
  84.3 2.7 %collective-permute-done.11 = f32[1,128]{1,0:T(1,128)S(1)} collective-permute-done((f32[1,128]{1,0:T(1,128)S(1)}, f32[1,128]{1,0:T(1,128)S(1)}, u32[]{:S(2)}, u32[]{:S(2)}) %collective-permute-start.11) | collective-permute-done | bytes 544 | tf_op jit(solution)/shard_map/ppermute | solution.py:56
  87.1 1.9 %collective-permute-start.12 = (f32[1,128]{1,0:T(1,128)S(1)}, f32[1,128]{1,0:T(1,128)S(1)}, u32[]{:S(2)}, u32[]{:S(2)}) collective-permute-start(f32[1,128]{1,0:T(1,128)S(1)} %add.151), channel_id=1, source_target_pairs={{0,8},{4,12},{8,0},{12,4},{16,24},{20,28},{24,16},{28,20},{1,9},{5... | collective-permute-start | bytes 1544 | tf_op jit(solution)/shard_map/ppermute | solution.py:56
  90.7 2.9 %collective-permute-start.13 = (f32[1,128]{1,0:T(1,128)S(1)}, f32[1,128]{1,0:T(1,128)S(1)}, u32[]{:S(2)}, u32[]{:S(2)}) collective-permute-start(f32[1,128]{1,0:T(1,128)S(1)} %add.152), channel_id=1, source_target_pairs={{0,16},{4,20},{8,24},{12,28},{16,0},{20,4},{24,8},{28,12},{1,17},{... | collective-permute-start | bytes 1544 | tf_op jit(solution)/shard_map/ppermute | solution.py:56
  95.7 6.2 %shard_map.61 = (f32[28,80,128]{2,1,0:T(8,128)}, f32[28,80,128]{2,1,0:T(8,128)}, f32[1,128]{1,0:T(1,128)}) custom-call(f32[1,128]{1,0:T(1,128)} %add.153.refs_0_.refs_1_, f32[2,128]{1,0:T(2,128)} %add.148.refs_0_.refs_1_, f32[28,80,128]{2,1,0:T(8,128)} %get-tuple-element.24.refs_2_.refs_4_, f32[28,80,128]{2,1,0:T(8,128)} %get-tuple-element.21.refs_1_.refs_3_.refs_4_, ...), custom_call_target="tpu_custom_call" | custom-call | flops 11468800 | bytes 13762560 | tf_op jit(solution)/shard_map/pallas_call | solution.py:284
  103.9 3.4 %collective-permute-done.15 = f32[1,128]{1,0:T(1,128)S(1)} collective-permute-done((f32[1,128]{1,0:T(1,128)S(1)}, f32[1,128]{1,0:T(1,128)S(1)}, u32[]{:S(2)}, u32[]{:S(2)}) %collective-permute-start.15) | collective-permute-done | bytes 544 | tf_op jit(solution)/shard_map/ppermute | solution.py:56
  108.2 2.7 %collective-permute-done.16 = f32[1,128]{1,0:T(1,128)S(1)} collective-permute-done((f32[1,128]{1,0:T(1,128)S(1)}, f32[1,128]{1,0:T(1,128)S(1)}, u32[]{:S(2)}, u32[]{:S(2)}) %collective-permute-start.16) | collective-permute-done | bytes 544 | tf_op jit(solution)/shard_map/ppermute | solution.py:56
  110.9 1.9 %collective-permute-start.17 = (f32[1,128]{1,0:T(1,128)S(1)}, f32[1,128]{1,0:T(1,128)S(1)}, u32[]{:S(2)}, u32[]{:S(2)}) collective-permute-start(f32[1,128]{1,0:T(1,128)S(1)} %add.156), channel_id=1, source_target_pairs={{0,8},{4,12},{8,0},{12,4},{16,24},{20,28},{24,16},{28,20},{1,9},{5... | collective-permute-start | bytes 1544 | tf_op jit(solution)/shard_map/ppermute | solution.py:56
  114.5 2.9 %collective-permute-start.18 = (f32[1,128]{1,0:T(1,128)S(1)}, f32[1,128]{1,0:T(1,128)S(1)}, u32[]{:S(2)}, u32[]{:S(2)}) collective-permute-start(f32[1,128]{1,0:T(1,128)S(1)} %add.157), channel_id=1, source_target_pairs={{0,16},{4,20},{8,24},{12,28},{16,0},{20,4},{24,8},{28,12},{1,17},{... | collective-permute-start | bytes 1544 | tf_op jit(solution)/shard_map/ppermute | solution.py:56
  119.5 4.6 %shard_map.62 = (f32[28,80,128]{2,1,0:T(8,128)}, f32[28,80,128]{2,1,0:T(8,128)}, f32[1,128]{1,0:T(1,128)}) custom-call(f32[1,128]{1,0:T(1,128)} %add.153.refs_0_.refs_1_, f32[1,128]{1,0:T(1,128)} %add.158.refs_1_, f32[28,80,128]{2,1,0:T(8,128)} %get-tuple-element.28.refs_2_, f32[28,80,128]{2,1,0:T(8,128)} %get-tuple-element.29.refs_3_, ...), custom_call_target="tpu_custom_call" | custom-call | flops 11468800 | bytes 11468800 | tf_op jit(solution)/shard_map/pallas_call | solution.py:284
  126.1 3.4 %collective-permute-done.20 = f32[1,128]{1,0:T(1,128)S(1)} collective-permute-done((f32[1,128]{1,0:T(1,128)S(1)}, f32[1,128]{1,0:T(1,128)S(1)}, u32[]{:S(2)}, u32[]{:S(2)}) %collective-permute-start.20) | collective-permute-done | bytes 544 | tf_op jit(solution)/shard_map/ppermute | solution.py:56
  130.4 2.7 %collective-permute-done.21 = f32[1,128]{1,0:T(1,128)S(1)} collective-permute-done((f32[1,128]{1,0:T(1,128)S(1)}, f32[1,128]{1,0:T(1,128)S(1)}, u32[]{:S(2)}, u32[]{:S(2)}) %collective-permute-start.21) | collective-permute-done | bytes 544 | tf_op jit(solution)/shard_map/ppermute | solution.py:56
  133.1 1.9 %collective-permute-start.22 = (f32[1,128]{1,0:T(1,128)S(1)}, f32[1,128]{1,0:T(1,128)S(1)}, u32[]{:S(2)}, u32[]{:S(2)}) collective-permute-start(f32[1,128]{1,0:T(1,128)S(1)} %add.161), channel_id=1, source_target_pairs={{0,8},{4,12},{8,0},{12,4},{16,24},{20,28},{24,16},{28,20},{1,9},{5... | collective-permute-start | bytes 1544 | tf_op jit(solution)/shard_map/ppermute | solution.py:56
  136.7 2.9 %collective-permute-start.23 = (f32[1,128]{1,0:T(1,128)S(1)}, f32[1,128]{1,0:T(1,128)S(1)}, u32[]{:S(2)}, u32[]{:S(2)}) collective-permute-start(f32[1,128]{1,0:T(1,128)S(1)} %add.162), channel_id=1, source_target_pairs={{0,16},{4,20},{8,24},{12,28},{16,0},{20,4},{24,8},{28,12},{1,17},{... | collective-permute-start | bytes 1544 | tf_op jit(solution)/shard_map/ppermute | solution.py:56
  141.8 6.2 %shard_map.63 = (f32[28,80,128]{2,1,0:T(8,128)}, f32[28,80,128]{2,1,0:T(8,128)}, f32[1,128]{1,0:T(1,128)}) custom-call(f32[1,128]{1,0:T(1,128)} %add.163.refs_0_, f32[1,128]{1,0:T(1,128)} %add.153.refs_0_.refs_1_, f32[28,80,128]{2,1,0:T(8,128)} %get-tuple-element.32.refs_2_, f32[28,80,128]{2,1,0:T(8,128)} %get-tuple-element.29.refs_3_, ...), custom_call_target="tpu_custom_call" | custom-call | flops 11468800 | bytes 13762560 | tf_op jit(solution)/shard_map/pallas_call | solution.py:284
  150.1 3.4 %collective-permute-done.25 = f32[1,128]{1,0:T(1,128)S(1)} collective-permute-done((f32[1,128]{1,0:T(1,128)S(1)}, f32[1,128]{1,0:T(1,128)S(1)}, u32[]{:S(2)}, u32[]{:S(2)}) %collective-permute-start.25) | collective-permute-done | bytes 544 | tf_op jit(solution)/shard_map/ppermute | solution.py:56
  154.4 2.7 %collective-permute-done.26 = f32[1,128]{1,0:T(1,128)S(1)} collective-permute-done((f32[1,128]{1,0:T(1,128)S(1)}, f32[1,128]{1,0:T(1,128)S(1)}, u32[]{:S(2)}, u32[]{:S(2)}) %collective-permute-start.26) | collective-permute-done | bytes 544 | tf_op jit(solution)/shard_map/ppermute | solution.py:56
  157.1 1.9 %collective-permute-start.27 = (f32[1,128]{1,0:T(1,128)S(1)}, f32[1,128]{1,0:T(1,128)S(1)}, u32[]{:S(2)}, u32[]{:S(2)}) collective-permute-start(f32[1,128]{1,0:T(1,128)S(1)} %add.166), channel_id=1, source_target_pairs={{0,8},{4,12},{8,0},{12,4},{16,24},{20,28},{24,16},{28,20},{1,9},{5... | collective-permute-start | bytes 1544 | tf_op jit(solution)/shard_map/ppermute | solution.py:56
  160.7 2.9 %collective-permute-start.28 = (f32[1,128]{1,0:T(1,128)S(1)}, f32[1,128]{1,0:T(1,128)S(1)}, u32[]{:S(2)}, u32[]{:S(2)}) collective-permute-start(f32[1,128]{1,0:T(1,128)S(1)} %add.167), channel_id=1, source_target_pairs={{0,16},{4,20},{8,24},{12,28},{16,0},{20,4},{24,8},{28,12},{1,17},{... | collective-permute-start | bytes 1544 | tf_op jit(solution)/shard_map/ppermute | solution.py:56
  165.7 5.9 %shard_map.64 = (f32[16,128]{1,0:T(8,128)}, f32[16,128]{1,0:T(8,128)}) custom-call(f32[1,128]{1,0:T(1,128)} %add.163.refs_0_, f32[1,128]{1,0:T(1,128)} %add.168.refs_1_, f32[28,80,128]{2,1,0:T(8,128)} %get-tuple-element.34.refs_2_, f32[28,80,128]{2,1,0:T(8,128)} %get-tuple-element.35.refs_3_, f32[28,80,128]{2,1,0:T(8,128)} %get-tuple-element.21.refs_1_.refs_3_.refs_4_, ...), custom_call_target="tpu_custom_call" | custom-call | flops 11468800 | bytes 14909440 | tf_op jit(solution)/shard_map/pallas_call | solution.py:284
  (81 shorter events, 46.4 us)
Async XLA Ops:
  0.6 2.5 %copy-start.1 = (f32[16,128]{1,0:T(8,128)S(1)}, f32[16,128]{1,0:T(8,128)}, u32[]{:S(2)}) copy-start(f32[16,128]{1,0:T(8,128)} %refs_9_.1) | copy-start | bytes 24580
  0.6 2.9 %copy-start.2 = (f32[16,128]{1,0:T(8,128)S(1)}, f32[16,128]{1,0:T(8,128)}, u32[]{:S(2)}) copy-start(f32[16,128]{1,0:T(8,128)} %refs_8_.1) | copy-start | bytes 24580
  7.6 22.0 %collective-permute-start = (f32[67,6,128]{0,2,1:T(8,128)}, f32[67,6,128]{0,2,1:T(8,128)S(1)}, u32[]{:S(2)}, u32[]{:S(2)}) collective-permute-start(f32[67,6,128]{0,2,1:T(8,128)} %get-tuple-element.40), channel_id=1, source_target_pairs={{0,4},{4,8},{8,12},{12,16},{16,20},{20,24},{24,28},{1,5},{5,9},{9,... | collective-permute-start | bytes 617480 | tf_op jit(solution)/shard_map/ppermute | solution.py:20
  12.5 17.1 %collective-permute-start.1 = (f32[67,6,128]{0,2,1:T(8,128)}, f32[67,6,128]{0,2,1:T(8,128)}, u32[]{:S(2)}, u32[]{:S(2)}) collective-permute-start(f32[67,6,128]{0,2,1:T(8,128)} %get-tuple-element.41), channel_id=1, source_target_pairs={{4,0},{8,4},{12,8},{16,12},{20,16},{24,20},{28,24},{5,1},{9,5},{13... | collective-permute-start | bytes 617480 | tf_op jit(solution)/shard_map/ppermute | solution.py:22
  15.4 21.5 %copy-start = (f32[1,16,128]{0,2,1:T(8,128)S(1)}, f32[1,16,128]{0,2,1:T(8,128)}, u32[]{:S(2)}) copy-start(f32[1,16,128]{0,2,1:T(8,128)} %copy.8) | copy-start | bytes 24580
  30.6 3.1 %collective-permute-start.2 = (f32[67,28,6]{0,2,1:T(8,128)S(1)}, f32[67,28,6]{0,2,1:T(8,128)S(1)}, u32[]{:S(2)}, u32[]{:S(2)}) collective-permute-start(f32[67,28,6]{0,2,1:T(8,128)S(1)} %get-tuple-element.38), channel_id=1, source_target_pairs={{0,1},{1,2},{2,3},{4,5},{5,6},{6,7},{8,9},{9,10},{10,11},{12,13},{... | collective-permute-start | bytes 135080 | tf_op jit(solution)/shard_map/ppermute | solution.py:20
  31.9 5.0 %collective-permute-start.3 = (f32[67,28,6]{0,2,1:T(8,128)S(1)}, f32[67,28,6]{0,2,1:T(8,128)S(1)}, u32[]{:S(2)}, u32[]{:S(2)}) collective-permute-start(f32[67,28,6]{0,2,1:T(8,128)S(1)} %get-tuple-element.39), channel_id=1, source_target_pairs={{1,0},{2,1},{3,2},{5,4},{6,5},{7,6},{9,8},{10,9},{11,10},{13,12},{... | collective-permute-start | bytes 135080 | tf_op jit(solution)/shard_map/ppermute | solution.py:22
  51.7 4.4 %collective-permute-start.4 = (f32[2,128]{1,0:T(2,128)}, f32[2,128]{1,0:T(2,128)S(1)}, u32[]{:S(2)}, u32[]{:S(2)}) collective-permute-start(f32[2,128]{1,0:T(2,128)} %get-tuple-element.20), channel_id=1, source_target_pairs={{0,1},{1,0},{2,3},{3,2},{4,5},{5,4},{6,7},{7,6},{8,9},{9,8},{10,11... | collective-permute-start | bytes 3080 | tf_op jit(solution)/shard_map/ppermute | solution.py:56
  56.8 3.6 %collective-permute-start.5 = (f32[2,128]{1,0:T(2,128)S(1)}, f32[2,128]{1,0:T(2,128)S(1)}, u32[]{:S(2)}, u32[]{:S(2)}) collective-permute-start(f32[2,128]{1,0:T(2,128)S(1)} %add.144), channel_id=1, source_target_pairs={{0,2},{1,3},{2,0},{3,1},{4,6},{5,7},{6,4},{7,5},{8,10},{9,11},{10,... | collective-permute-start | bytes 3080 | tf_op jit(solution)/shard_map/ppermute | solution.py:56
  60.4 3.9 %collective-permute-start.6 = (f32[2,128]{1,0:T(2,128)S(1)}, f32[2,128]{1,0:T(2,128)S(1)}, u32[]{:S(2)}, u32[]{:S(2)}) collective-permute-start(f32[2,128]{1,0:T(2,128)S(1)} %add.145), channel_id=1, source_target_pairs={{0,4},{4,0},{8,12},{12,8},{16,20},{20,16},{24,28},{28,24},{1,5},{5... | collective-permute-start | bytes 3080 | tf_op jit(solution)/shard_map/ppermute | solution.py:56
  64.3 4.7 %collective-permute-start.7 = (f32[2,128]{1,0:T(2,128)S(1)}, f32[2,128]{1,0:T(2,128)S(1)}, u32[]{:S(2)}, u32[]{:S(2)}) collective-permute-start(f32[2,128]{1,0:T(2,128)S(1)} %add.146), channel_id=1, source_target_pairs={{0,8},{4,12},{8,0},{12,4},{16,24},{20,28},{24,16},{28,20},{1,9},{5... | collective-permute-start | bytes 3080 | tf_op jit(solution)/shard_map/ppermute | solution.py:56
  68.9 4.6 %collective-permute-start.8 = (f32[2,128]{1,0:T(2,128)S(1)}, f32[2,128]{1,0:T(2,128)S(1)}, u32[]{:S(2)}, u32[]{:S(2)}) collective-permute-start(f32[2,128]{1,0:T(2,128)S(1)} %add.147), channel_id=1, source_target_pairs={{0,16},{4,20},{8,24},{12,28},{16,0},{20,4},{24,8},{28,12},{1,17},{... | collective-permute-start | bytes 3080 | tf_op jit(solution)/shard_map/ppermute | solution.py:56
  78.0 1.4 collective-permute-start.9
  79.9 3.6 %collective-permute-start.10 = (f32[1,128]{1,0:T(1,128)S(1)}, f32[1,128]{1,0:T(1,128)S(1)}, u32[]{:S(2)}, u32[]{:S(2)}) collective-permute-start(f32[1,128]{1,0:T(1,128)S(1)} %add.149), channel_id=1, source_target_pairs={{0,2},{1,3},{2,0},{3,1},{4,6},{5,7},{6,4},{7,5},{8,10},{9,11},{10,... | collective-permute-start | bytes 1544 | tf_op jit(solution)/shard_map/ppermute | solution.py:56
  83.5 3.6 %collective-permute-start.11 = (f32[1,128]{1,0:T(1,128)S(1)}, f32[1,128]{1,0:T(1,128)S(1)}, u32[]{:S(2)}, u32[]{:S(2)}) collective-permute-start(f32[1,128]{1,0:T(1,128)S(1)} %add.150), channel_id=1, source_target_pairs={{0,4},{4,0},{8,12},{12,8},{16,20},{20,16},{24,28},{28,24},{1,5},{5... | collective-permute-start | bytes 1544 | tf_op jit(solution)/shard_map/ppermute | solution.py:56
  87.1 3.6 %collective-permute-start.12 = (f32[1,128]{1,0:T(1,128)S(1)}, f32[1,128]{1,0:T(1,128)S(1)}, u32[]{:S(2)}, u32[]{:S(2)}) collective-permute-start(f32[1,128]{1,0:T(1,128)S(1)} %add.151), channel_id=1, source_target_pairs={{0,8},{4,12},{8,0},{12,4},{16,24},{20,28},{24,16},{28,20},{1,9},{5... | collective-permute-start | bytes 1544 | tf_op jit(solution)/shard_map/ppermute | solution.py:56
  90.7 4.5 %collective-permute-start.13 = (f32[1,128]{1,0:T(1,128)S(1)}, f32[1,128]{1,0:T(1,128)S(1)}, u32[]{:S(2)}, u32[]{:S(2)}) collective-permute-start(f32[1,128]{1,0:T(1,128)S(1)} %add.152), channel_id=1, source_target_pairs={{0,16},{4,20},{8,24},{12,28},{16,0},{20,4},{24,8},{28,12},{1,17},{... | collective-permute-start | bytes 1544 | tf_op jit(solution)/shard_map/ppermute | solution.py:56
  101.9 1.2 collective-permute-start.14
  103.8 3.6 %collective-permute-start.15 = (f32[1,128]{1,0:T(1,128)S(1)}, f32[1,128]{1,0:T(1,128)S(1)}, u32[]{:S(2)}, u32[]{:S(2)}) collective-permute-start(f32[1,128]{1,0:T(1,128)S(1)} %add.154), channel_id=1, source_target_pairs={{0,2},{1,3},{2,0},{3,1},{4,6},{5,7},{6,4},{7,5},{8,10},{9,11},{10,... | collective-permute-start | bytes 1544 | tf_op jit(solution)/shard_map/ppermute | solution.py:56
  107.3 3.6 %collective-permute-start.16 = (f32[1,128]{1,0:T(1,128)S(1)}, f32[1,128]{1,0:T(1,128)S(1)}, u32[]{:S(2)}, u32[]{:S(2)}) collective-permute-start(f32[1,128]{1,0:T(1,128)S(1)} %add.155), channel_id=1, source_target_pairs={{0,4},{4,0},{8,12},{12,8},{16,20},{20,16},{24,28},{28,24},{1,5},{5... | collective-permute-start | bytes 1544 | tf_op jit(solution)/shard_map/ppermute | solution.py:56
  110.9 3.6 %collective-permute-start.17 = (f32[1,128]{1,0:T(1,128)S(1)}, f32[1,128]{1,0:T(1,128)S(1)}, u32[]{:S(2)}, u32[]{:S(2)}) collective-permute-start(f32[1,128]{1,0:T(1,128)S(1)} %add.156), channel_id=1, source_target_pairs={{0,8},{4,12},{8,0},{12,4},{16,24},{20,28},{24,16},{28,20},{1,9},{5... | collective-permute-start | bytes 1544 | tf_op jit(solution)/shard_map/ppermute | solution.py:56
  114.5 4.5 %collective-permute-start.18 = (f32[1,128]{1,0:T(1,128)S(1)}, f32[1,128]{1,0:T(1,128)S(1)}, u32[]{:S(2)}, u32[]{:S(2)}) collective-permute-start(f32[1,128]{1,0:T(1,128)S(1)} %add.157), channel_id=1, source_target_pairs={{0,16},{4,20},{8,24},{12,28},{16,0},{20,4},{24,8},{28,12},{1,17},{... | collective-permute-start | bytes 1544 | tf_op jit(solution)/shard_map/ppermute | solution.py:56
  124.1 1.2 collective-permute-start.19
  126.0 3.6 %collective-permute-start.20 = (f32[1,128]{1,0:T(1,128)S(1)}, f32[1,128]{1,0:T(1,128)S(1)}, u32[]{:S(2)}, u32[]{:S(2)}) collective-permute-start(f32[1,128]{1,0:T(1,128)S(1)} %add.159), channel_id=1, source_target_pairs={{0,2},{1,3},{2,0},{3,1},{4,6},{5,7},{6,4},{7,5},{8,10},{9,11},{10,... | collective-permute-start | bytes 1544 | tf_op jit(solution)/shard_map/ppermute | solution.py:56
  129.6 3.6 %collective-permute-start.21 = (f32[1,128]{1,0:T(1,128)S(1)}, f32[1,128]{1,0:T(1,128)S(1)}, u32[]{:S(2)}, u32[]{:S(2)}) collective-permute-start(f32[1,128]{1,0:T(1,128)S(1)} %add.160), channel_id=1, source_target_pairs={{0,4},{4,0},{8,12},{12,8},{16,20},{20,16},{24,28},{28,24},{1,5},{5... | collective-permute-start | bytes 1544 | tf_op jit(solution)/shard_map/ppermute | solution.py:56
  133.1 3.6 %collective-permute-start.22 = (f32[1,128]{1,0:T(1,128)S(1)}, f32[1,128]{1,0:T(1,128)S(1)}, u32[]{:S(2)}, u32[]{:S(2)}) collective-permute-start(f32[1,128]{1,0:T(1,128)S(1)} %add.161), channel_id=1, source_target_pairs={{0,8},{4,12},{8,0},{12,4},{16,24},{20,28},{24,16},{28,20},{1,9},{5... | collective-permute-start | bytes 1544 | tf_op jit(solution)/shard_map/ppermute | solution.py:56
  136.7 4.5 %collective-permute-start.23 = (f32[1,128]{1,0:T(1,128)S(1)}, f32[1,128]{1,0:T(1,128)S(1)}, u32[]{:S(2)}, u32[]{:S(2)}) collective-permute-start(f32[1,128]{1,0:T(1,128)S(1)} %add.162), channel_id=1, source_target_pairs={{0,16},{4,20},{8,24},{12,28},{16,0},{20,4},{24,8},{28,12},{1,17},{... | collective-permute-start | bytes 1544 | tf_op jit(solution)/shard_map/ppermute | solution.py:56
  148.0 1.3 collective-permute-start.24
  150.0 3.6 %collective-permute-start.25 = (f32[1,128]{1,0:T(1,128)S(1)}, f32[1,128]{1,0:T(1,128)S(1)}, u32[]{:S(2)}, u32[]{:S(2)}) collective-permute-start(f32[1,128]{1,0:T(1,128)S(1)} %add.164), channel_id=1, source_target_pairs={{0,2},{1,3},{2,0},{3,1},{4,6},{5,7},{6,4},{7,5},{8,10},{9,11},{10,... | collective-permute-start | bytes 1544 | tf_op jit(solution)/shard_map/ppermute | solution.py:56
  153.5 3.6 %collective-permute-start.26 = (f32[1,128]{1,0:T(1,128)S(1)}, f32[1,128]{1,0:T(1,128)S(1)}, u32[]{:S(2)}, u32[]{:S(2)}) collective-permute-start(f32[1,128]{1,0:T(1,128)S(1)} %add.165), channel_id=1, source_target_pairs={{0,4},{4,0},{8,12},{12,8},{16,20},{20,16},{24,28},{28,24},{1,5},{5... | collective-permute-start | bytes 1544 | tf_op jit(solution)/shard_map/ppermute | solution.py:56
  157.1 3.6 %collective-permute-start.27 = (f32[1,128]{1,0:T(1,128)S(1)}, f32[1,128]{1,0:T(1,128)S(1)}, u32[]{:S(2)}, u32[]{:S(2)}) collective-permute-start(f32[1,128]{1,0:T(1,128)S(1)} %add.166), channel_id=1, source_target_pairs={{0,8},{4,12},{8,0},{12,4},{16,24},{20,28},{24,16},{28,20},{1,9},{5... | collective-permute-start | bytes 1544 | tf_op jit(solution)/shard_map/ppermute | solution.py:56
  160.7 4.5 %collective-permute-start.28 = (f32[1,128]{1,0:T(1,128)S(1)}, f32[1,128]{1,0:T(1,128)S(1)}, u32[]{:S(2)}, u32[]{:S(2)}) collective-permute-start(f32[1,128]{1,0:T(1,128)S(1)} %add.167), channel_id=1, source_target_pairs={{0,16},{4,20},{8,24},{12,28},{16,0},{20,4},{24,8},{28,12},{1,17},{... | collective-permute-start | bytes 1544 | tf_op jit(solution)/shard_map/ppermute | solution.py:56

commit v7 on v6

--- a/solution.py
+++ b/solution.py
@@ -15,13 +15,10 @@
         ends = count - 1
         head = lax.slice_in_dim(cells, 0, width, axis=dim)
         tail = lax.slice_in_dim(cells, cells.shape[dim] - width, cells.shape[dim], axis=dim)
+        below = lax.ppermute(tail.reshape(-1), axis, [(i, (i + 1) % count) for i in range(ends)])
+        above = lax.ppermute(head.reshape(-1), axis, [((i + 1) % count, i) for i in range(ends)])
         cells = jnp.concatenate(
-            [
-                lax.ppermute(tail, axis, [(i, (i + 1) % count) for i in range(ends)]),
-                cells,
-                lax.ppermute(head, axis, [((i + 1) % count, i) for i in range(ends)]),
-            ],
-            axis=dim,
+            [below.reshape(tail.shape), cells, above.reshape(head.shape)], axis=dim
         )
     return cells
 

time: 172 us -> 190 us (1.10)
  local copies, waits for them, and re-layouts: 5.92 us -> 37.8 us
  waiting for transfers between devices: 69.1 us -> 48.1 us
  starting transfers between devices: 43.9 us -> 49.4 us
    reshape x0 -> x12, local copies, waits for them, and re-layouts: none -> 23.5 us  [the longest x4 8.15 us: extended(): above.reshape(head.shape)]
    ppermute x4, waiting for transfers between devices: 17.3 us -> 3.04 us  [the longest x2 3.04 us: extended(): lax.ppermute(head.reshape(-1), axis, [((i + 1) % count, i) for i in range...]
    slice x0 -> x4, local copies, waits for them, and re-layouts: none -> 8.4 us  [the longest x2 4.71 us: extended(): lax.slice_in_dim(cells, cells.shape[dim] - width, cells.shape[dim], axis=...]
    ppermute x25, waiting for transfers between devices: 51.8 us -> 45.1 us  [all_sum(): lax.ppermute(terms, axis, [(i, i ^ hop) for i in range(count)])]
    ppermute x25, starting transfers between devices: 35.2 us -> 39.4 us  [all_sum(): lax.ppermute(terms, axis, [(i, i ^ hop) for i in range(count)])]
  transfers between devices with their start and end apart: 29 -> 29, of which waited for: 27 -> 26; matrix products, arithmetic and copies ran while one was open for 1% -> 9% of each run, Pallas kernels for 0% -> 0%
where the time goes in v7:
time: 190 us; the launch traced here: 189 us
  starting transfers between devices  49.4 us (26%)
  waiting for transfers between devices  48.1 us (25%)
  Pallas kernels  38.2 us (20%)
  local copies, waits for them, and re-layouts  37.8 us (20%)
  other arithmetic  14.6 us (8%)
    ppermute x25, waiting for transfers between devices, all_sum(): lax.ppermute(terms, axis, [(i, i ^ hop) for i in range(count)])  45.1 us
    ppermute x25, starting transfers between devices, all_sum(): lax.ppermute(terms, axis, [(i, i ^ hop) for i in range(count)])  39.4 us
    pallas_call x6, Pallas kernels, _call(): pl.pallas_call(lambda *refs: kernel(plan, *refs), out_shape=out_shapes, i...  38.2 us
    reshape x4, local copies, waits for them, and re-layouts, extended(): above.reshape(head.shape)  8.15 us
    ppermute x2, starting transfers between devices, extended(): lax.ppermute(tail.reshape(-1), axis, [(i, (i + 1) % count) for i in range...  7.44 us
    reshape x4, local copies, waits for them, and re-layouts, extended(): below.reshape(tail.shape)  7.38 us
    add x25, other arithmetic, all_sum(): terms + lax.ppermute(terms, axis, [(i, i ^ hop) for i in range(count)])  5.94 us
    slice x2, local copies, waits for them, and re-layouts, extended(): lax.slice_in_dim(cells, cells.shape[dim] - width, cells.shape[dim], axis=...  4.71 us
  transfers between devices with their start and end apart: 29, of which 26 were waited for; matrix products, arithmetic and copies ran while one was open for 9% of the time, Pallas kernels for 0%

profile of v7, /device:TPU:0, one launch (start us, length us, event | category | flops | bytes accessed | tf_op | source)
XLA Modules:
  0.0 188.9 jit_solution(3793241991343944791)
XLA Ops:
  4.9 2.5 %pad_maximum_fusion.4 = (f32[67,6,128]{0,2,1:T(8,128)}, f32[67,6,128]{0,2,1:T(8,128)S(1)}) fusion(f32[1,16,128]{0,2,1:T(8,128)S(1)} %copy.10, f32[1,16,128]{0,2,1:T(8,128)S(1)} %copy.9, f32[1,16,128]{0,2,1:T(8,128)} %copy.8, f32[64,16,128]{0,2,1:T(8,128)S(1)} %copy.7), kind=kLoop, calls=%fused_computation.5 | loop fusion | flops 308736 | bytes 960512 | tf_op jit(solution)/shard_map/slice | solution.py:17
  11.0 5.5 %collective-permute-start = (f32[51456]{0:T(1024)}, f32[51456]{0:T(1024)}, u32[]{:S(2)}, u32[]{:S(2)}) collective-permute-start(f32[51456]{0:T(1024)} %reshape.65), channel_id=1, source_target_pairs={{0,4},{4,8},{8,12},{12,16},{16,20},{20,24},{24,28},{1,5},{5,9},{9,... | collective-permute-start | bytes 617480 | tf_op jit(solution)/shard_map/ppermute | solution.py:18
  24.9 3.0 %collective-permute-done.1 = f32[51456]{0:T(1024)} collective-permute-done((f32[51456]{0:T(1024)}, f32[51456]{0:T(1024)}, u32[]{:S(2)}, u32[]{:S(2)}) %collective-permute-start.1) | collective-permute-done | bytes 205856 | tf_op jit(solution)/shard_map/ppermute | solution.py:19
  33.3 2.8 %copy.15 = f32[67,28,6]{2,1,0:T(8,128)} copy(f32[67,28,6]{0,2,1:T(8,128)} %get-tuple-element.38) | data formatting | bytes 90048 | tf_op jit(solution)/shard_map/slice | solution.py:17
  36.1 2.3 %reshape.69 = f32[11256]{0:T(1024)} reshape(f32[67,28,6]{2,1,0:T(8,128)} %copy.15) | data formatting | bytes 90048 | tf_op jit(solution)/shard_map/reshape | solution.py:18
  40.3 2.8 %copy.16 = f32[67,28,6]{2,1,0:T(8,128)} copy(f32[67,28,6]{0,2,1:T(8,128)} %get-tuple-element.39) | data formatting | bytes 90048 | tf_op jit(solution)/shard_map/slice | solution.py:16
  43.1 2.3 %reshape.71 = f32[11256]{0:T(1024)} reshape(f32[67,28,6]{2,1,0:T(8,128)} %copy.16) | data formatting | bytes 90048 | tf_op jit(solution)/shard_map/reshape | solution.py:19
  47.2 2.2 %reshape.70 = f32[67,28,6]{2,1,0:T(8,128)} reshape(f32[11256]{0:T(1024)} %collective-permute-done.2) | data formatting | bytes 90048 | tf_op jit(solution)/shard_map/reshape | solution.py:21
  49.4 2.4 %copy.17 = f32[67,28,6]{0,2,1:T(8,128)} copy(f32[67,28,6]{2,1,0:T(8,128)} %reshape.70) | data formatting | bytes 90048 | tf_op jit(solution)/shard_map/reshape | solution.py:21
  51.8 2.2 %reshape.72 = f32[67,28,6]{2,1,0:T(8,128)} reshape(f32[11256]{0:T(1024)} %collective-permute-done.3) | data formatting | bytes 90048 | tf_op jit(solution)/shard_map/reshape | solution.py:21
  54.0 2.4 %copy.18 = f32[67,28,6]{0,2,1:T(8,128)} copy(f32[67,28,6]{2,1,0:T(8,128)} %reshape.72) | data formatting | bytes 90048 | tf_op jit(solution)/shard_map/reshape | solution.py:21
  56.4 2.4 %pad_maximum_fusion = f32[67,28,140]{0,2,1:T(8,128)S(1)} fusion(f32[67,28,6]{0,2,1:T(8,128)} %copy.18, f32[67,6,128]{0,2,1:T(8,128)} %copy.14, f32[1,16,128]{0,2,1:T(8,128)S(1)} %copy.10, f32[1,16,128]{0,2,1:T(8,128)S(1)} %copy.9, f32[1,16,128]{0,2,1:T(8,128)} %copy.8, f32[64,16,128]{0,2,1:T(8,128)S(1)} %copy.7, f32[67,6,128]{0,2,1:T(8,128)S(1)} %copy.13, ...), kind=kLoop, calls=%fused_computation | loop fusion | flops 1838480 | bytes 2101120 | tf_op jit(solution)/shard_map/concatenate | solution.py:20
  60.3 11.3 %shard_map.59 = (f32[28,80,128]{2,1,0:T(8,128)}, f32[28,80,128]{2,1,0:T(8,128)}, f32[28,80,128]{2,1,0:T(8,128)}, f32[28,80,128]{2,1,0:T(8,128)}, f32[28,80,128]{...) custom-call(f32[28,144,128]{2,1,0:T(8,128)} %pad_bitcast_fusion.refs_0_, ...), custom_call_target="tpu_custom_call" | custom-call | flops 11468800 | bytes 13762560 | tf_op jit(solution)/shard_map/pallas_call | solution.py:281
  71.6 2.3 %collective-permute-start.4 = (f32[2,128]{1,0:T(2,128)}, f32[2,128]{1,0:T(2,128)S(1)}, u32[]{:S(2)}, u32[]{:S(2)}) collective-permute-start(f32[2,128]{1,0:T(2,128)} %get-tuple-element.20), channel_id=1, source_target_pairs={{0,1},{1,0},{2,3},{3,2},{4,5},{5,4},{6,7},{7,6},{8,9},{9,8},{10,11... | collective-permute-start | bytes 3080 | tf_op jit(solution)/shard_map/ppermute | solution.py:53
  84.1 2.2 %collective-permute-done.7 = f32[2,128]{1,0:T(2,128)S(1)} collective-permute-done((f32[2,128]{1,0:T(2,128)S(1)}, f32[2,128]{1,0:T(2,128)S(1)}, u32[]{:S(2)}, u32[]{:S(2)}) %collective-permute-start.7) | collective-permute-done | bytes 1056 | tf_op jit(solution)/shard_map/ppermute | solution.py:53
  86.3 2.3 %collective-permute-start.8 = (f32[2,128]{1,0:T(2,128)S(1)}, f32[2,128]{1,0:T(2,128)S(1)}, u32[]{:S(2)}, u32[]{:S(2)}) collective-permute-start(f32[2,128]{1,0:T(2,128)S(1)} %add.147), channel_id=1, source_target_pairs={{0,16},{4,20},{8,24},{12,28},{16,0},{20,4},{24,8},{28,12},{1,17},{... | collective-permute-start | bytes 3080 | tf_op jit(solution)/shard_map/ppermute | solution.py:53
  88.7 2.1 %collective-permute-done.8 = f32[2,128]{1,0:T(2,128)S(1)} collective-permute-done((f32[2,128]{1,0:T(2,128)S(1)}, f32[2,128]{1,0:T(2,128)S(1)}, u32[]{:S(2)}, u32[]{:S(2)}) %collective-permute-start.8) | collective-permute-done | bytes 1056 | tf_op jit(solution)/shard_map/ppermute | solution.py:53
  91.4 3.9 %shard_map.60 = (f32[28,80,128]{2,1,0:T(8,128)}, f32[28,80,128]{2,1,0:T(8,128)}, f32[1,128]{1,0:T(1,128)}) custom-call(f32[2,128]{1,0:T(2,128)} %add.148.refs_0_.refs_1_, f32[28,80,128]{2,1,0:T(8,128)} %get-tuple-element.21.refs_1_.refs_3_.refs_4_, f32[28,80,128]{2,1,0:T(8,128)} %get-tuple-element.22.refs_2_, f32[80,128]{1,0:T(8,128)} %add_convert_fusion.1.refs_3_.refs_8_.refs_6_), custom_call_target="tpu_custom_call" | custom-call | flops 11468800 | bytes 8028160 | tf_op jit(solution)/shard_map/pallas_call | solution.py:281
  105.6 2.2 %collective-permute-done.12 = f32[1,128]{1,0:T(1,128)S(1)} collective-permute-done((f32[1,128]{1,0:T(1,128)S(1)}, f32[1,128]{1,0:T(1,128)S(1)}, u32[]{:S(2)}, u32[]{:S(2)}) %collective-permute-start.12) | collective-permute-done | bytes 544 | tf_op jit(solution)/shard_map/ppermute | solution.py:53
  107.9 2.3 %collective-permute-start.13 = (f32[1,128]{1,0:T(1,128)S(1)}, f32[1,128]{1,0:T(1,128)S(1)}, u32[]{:S(2)}, u32[]{:S(2)}) collective-permute-start(f32[1,128]{1,0:T(1,128)S(1)} %add.152), channel_id=1, source_target_pairs={{0,16},{4,20},{8,24},{12,28},{16,0},{20,4},{24,8},{28,12},{1,17},{... | collective-permute-start | bytes 1544 | tf_op jit(solution)/shard_map/ppermute | solution.py:53
  110.2 2.1 %collective-permute-done.13 = f32[1,128]{1,0:T(1,128)S(1)} collective-permute-done((f32[1,128]{1,0:T(1,128)S(1)}, f32[1,128]{1,0:T(1,128)S(1)}, u32[]{:S(2)}, u32[]{:S(2)}) %collective-permute-start.13) | collective-permute-done | bytes 544 | tf_op jit(solution)/shard_map/ppermute | solution.py:53
  112.8 6.3 %shard_map.61 = (f32[28,80,128]{2,1,0:T(8,128)}, f32[28,80,128]{2,1,0:T(8,128)}, f32[1,128]{1,0:T(1,128)}) custom-call(f32[1,128]{1,0:T(1,128)} %add.153.refs_0_.refs_1_, f32[2,128]{1,0:T(2,128)} %add.148.refs_0_.refs_1_, f32[28,80,128]{2,1,0:T(8,128)} %get-tuple-element.24.refs_2_.refs_4_, f32[28,80,128]{2,1,0:T(8,128)} %get-tuple-element.21.refs_1_.refs_3_.refs_4_, ...), custom_call_target="tpu_custom_call" | custom-call | flops 11468800 | bytes 13762560 | tf_op jit(solution)/shard_map/pallas_call | solution.py:281
  129.6 2.2 %collective-permute-done.17 = f32[1,128]{1,0:T(1,128)S(1)} collective-permute-done((f32[1,128]{1,0:T(1,128)S(1)}, f32[1,128]{1,0:T(1,128)S(1)}, u32[]{:S(2)}, u32[]{:S(2)}) %collective-permute-start.17) | collective-permute-done | bytes 544 | tf_op jit(solution)/shard_map/ppermute | solution.py:53
  131.8 2.3 %collective-permute-start.18 = (f32[1,128]{1,0:T(1,128)S(1)}, f32[1,128]{1,0:T(1,128)S(1)}, u32[]{:S(2)}, u32[]{:S(2)}) collective-permute-start(f32[1,128]{1,0:T(1,128)S(1)} %add.157), channel_id=1, source_target_pairs={{0,16},{4,20},{8,24},{12,28},{16,0},{20,4},{24,8},{28,12},{1,17},{... | collective-permute-start | bytes 1544 | tf_op jit(solution)/shard_map/ppermute | solution.py:53
  134.2 2.1 %collective-permute-done.18 = f32[1,128]{1,0:T(1,128)S(1)} collective-permute-done((f32[1,128]{1,0:T(1,128)S(1)}, f32[1,128]{1,0:T(1,128)S(1)}, u32[]{:S(2)}, u32[]{:S(2)}) %collective-permute-start.18) | collective-permute-done | bytes 544 | tf_op jit(solution)/shard_map/ppermute | solution.py:53
  136.8 4.7 %shard_map.62 = (f32[28,80,128]{2,1,0:T(8,128)}, f32[28,80,128]{2,1,0:T(8,128)}, f32[1,128]{1,0:T(1,128)}) custom-call(f32[1,128]{1,0:T(1,128)} %add.153.refs_0_.refs_1_, f32[1,128]{1,0:T(1,128)} %add.158.refs_1_, f32[28,80,128]{2,1,0:T(8,128)} %get-tuple-element.28.refs_2_, f32[28,80,128]{2,1,0:T(8,128)} %get-tuple-element.29.refs_3_, ...), custom_call_target="tpu_custom_call" | custom-call | flops 11468800 | bytes 11468800 | tf_op jit(solution)/shard_map/pallas_call | solution.py:281
  151.9 2.2 %collective-permute-done.22 = f32[1,128]{1,0:T(1,128)S(1)} collective-permute-done((f32[1,128]{1,0:T(1,128)S(1)}, f32[1,128]{1,0:T(1,128)S(1)}, u32[]{:S(2)}, u32[]{:S(2)}) %collective-permute-start.22) | collective-permute-done | bytes 544 | tf_op jit(solution)/shard_map/ppermute | solution.py:53
  154.2 2.3 %collective-permute-start.23 = (f32[1,128]{1,0:T(1,128)S(1)}, f32[1,128]{1,0:T(1,128)S(1)}, u32[]{:S(2)}, u32[]{:S(2)}) collective-permute-start(f32[1,128]{1,0:T(1,128)S(1)} %add.162), channel_id=1, source_target_pairs={{0,16},{4,20},{8,24},{12,28},{16,0},{20,4},{24,8},{28,12},{1,17},{... | collective-permute-start | bytes 1544 | tf_op jit(solution)/shard_map/ppermute | solution.py:53
  159.2 6.3 %shard_map.63 = (f32[28,80,128]{2,1,0:T(8,128)}, f32[28,80,128]{2,1,0:T(8,128)}, f32[1,128]{1,0:T(1,128)}) custom-call(f32[1,128]{1,0:T(1,128)} %add.163.refs_0_, f32[1,128]{1,0:T(1,128)} %add.153.refs_0_.refs_1_, f32[28,80,128]{2,1,0:T(8,128)} %get-tuple-element.32.refs_2_, f32[28,80,128]{2,1,0:T(8,128)} %get-tuple-element.29.refs_3_, ...), custom_call_target="tpu_custom_call" | custom-call | flops 11468800 | bytes 13762560 | tf_op jit(solution)/shard_map/pallas_call | solution.py:281
  175.9 2.2 %collective-permute-done.27 = f32[1,128]{1,0:T(1,128)S(1)} collective-permute-done((f32[1,128]{1,0:T(1,128)S(1)}, f32[1,128]{1,0:T(1,128)S(1)}, u32[]{:S(2)}, u32[]{:S(2)}) %collective-permute-start.27) | collective-permute-done | bytes 544 | tf_op jit(solution)/shard_map/ppermute | solution.py:53
  178.1 2.3 %collective-permute-start.28 = (f32[1,128]{1,0:T(1,128)S(1)}, f32[1,128]{1,0:T(1,128)S(1)}, u32[]{:S(2)}, u32[]{:S(2)}) collective-permute-start(f32[1,128]{1,0:T(1,128)S(1)} %add.167), channel_id=1, source_target_pairs={{0,16},{4,20},{8,24},{12,28},{16,0},{20,4},{24,8},{28,12},{1,17},{... | collective-permute-start | bytes 1544 | tf_op jit(solution)/shard_map/ppermute | solution.py:53
  183.1 5.9 %shard_map.64 = (f32[16,128]{1,0:T(8,128)}, f32[16,128]{1,0:T(8,128)}) custom-call(f32[1,128]{1,0:T(1,128)} %add.163.refs_0_, f32[1,128]{1,0:T(1,128)} %add.168.refs_1_, f32[28,80,128]{2,1,0:T(8,128)} %get-tuple-element.34.refs_2_, f32[28,80,128]{2,1,0:T(8,128)} %get-tuple-element.35.refs_3_, f32[28,80,128]{2,1,0:T(8,128)} %get-tuple-element.21.refs_1_.refs_3_.refs_4_, ...), custom_call_target="tpu_custom_call" | custom-call | flops 11468800 | bytes 14909440 | tf_op jit(solution)/shard_map/pallas_call | solution.py:281
  (95 shorter events, 85.4 us)
Async XLA Ops:
  0.6 2.5 %copy-start = (f32[16,128]{1,0:T(8,128)S(1)}, f32[16,128]{1,0:T(8,128)}, u32[]{:S(2)}) copy-start(f32[16,128]{1,0:T(8,128)} %refs_9_.1) | copy-start | bytes 24580
  0.6 2.9 %copy-start.1 = (f32[16,128]{1,0:T(8,128)S(1)}, f32[16,128]{1,0:T(8,128)}, u32[]{:S(2)}) copy-start(f32[16,128]{1,0:T(8,128)} %refs_8_.1) | copy-start | bytes 24580
  11.0 11.1 %collective-permute-start = (f32[51456]{0:T(1024)}, f32[51456]{0:T(1024)}, u32[]{:S(2)}, u32[]{:S(2)}) collective-permute-start(f32[51456]{0:T(1024)} %reshape.65), channel_id=1, source_target_pairs={{0,4},{4,8},{8,12},{12,16},{16,20},{20,24},{24,28},{1,5},{5,9},{9,... | collective-permute-start | bytes 617480 | tf_op jit(solution)/shard_map/ppermute | solution.py:18
  19.1 8.8 %collective-permute-start.1 = (f32[51456]{0:T(1024)}, f32[51456]{0:T(1024)}, u32[]{:S(2)}, u32[]{:S(2)}) collective-permute-start(f32[51456]{0:T(1024)} %reshape.67), channel_id=1, source_target_pairs={{4,0},{8,4},{12,8},{16,12},{20,16},{24,20},{28,24},{5,1},{9,5},{13... | collective-permute-start | bytes 617480 | tf_op jit(solution)/shard_map/ppermute | solution.py:19
  38.4 8.8 %collective-permute-start.2 = (f32[11256]{0:T(1024)}, f32[11256]{0:T(1024)}, u32[]{:S(2)}, u32[]{:S(2)}) collective-permute-start(f32[11256]{0:T(1024)} %reshape.69), channel_id=1, source_target_pairs={{0,1},{1,2},{2,3},{4,5},{5,6},{6,7},{8,9},{9,10},{10,11},{12,13},{... | collective-permute-start | bytes 135080 | tf_op jit(solution)/shard_map/ppermute | solution.py:18
  45.4 6.4 %collective-permute-start.3 = (f32[11256]{0:T(1024)}, f32[11256]{0:T(1024)}, u32[]{:S(2)}, u32[]{:S(2)}) collective-permute-start(f32[11256]{0:T(1024)} %reshape.71), channel_id=1, source_target_pairs={{1,0},{2,1},{3,2},{5,4},{6,5},{7,6},{9,8},{10,9},{11,10},{13,12},{... | collective-permute-start | bytes 135080 | tf_op jit(solution)/shard_map/ppermute | solution.py:19
  71.6 3.3 %collective-permute-start.4 = (f32[2,128]{1,0:T(2,128)}, f32[2,128]{1,0:T(2,128)S(1)}, u32[]{:S(2)}, u32[]{:S(2)}) collective-permute-start(f32[2,128]{1,0:T(2,128)} %get-tuple-element.20), channel_id=1, source_target_pairs={{0,1},{1,0},{2,3},{3,2},{4,5},{5,4},{6,7},{7,6},{8,9},{9,8},{10,11... | collective-permute-start | bytes 3080 | tf_op jit(solution)/shard_map/ppermute | solution.py:53
  75.6 3.6 %collective-permute-start.5 = (f32[2,128]{1,0:T(2,128)S(1)}, f32[2,128]{1,0:T(2,128)S(1)}, u32[]{:S(2)}, u32[]{:S(2)}) collective-permute-start(f32[2,128]{1,0:T(2,128)S(1)} %add.144), channel_id=1, source_target_pairs={{0,2},{1,3},{2,0},{3,1},{4,6},{5,7},{6,4},{7,5},{8,10},{9,11},{10,... | collective-permute-start | bytes 3080 | tf_op jit(solution)/shard_map/ppermute | solution.py:53
  79.2 3.6 %collective-permute-start.6 = (f32[2,128]{1,0:T(2,128)S(1)}, f32[2,128]{1,0:T(2,128)S(1)}, u32[]{:S(2)}, u32[]{:S(2)}) collective-permute-start(f32[2,128]{1,0:T(2,128)S(1)} %add.145), channel_id=1, source_target_pairs={{0,4},{4,0},{8,12},{12,8},{16,20},{20,16},{24,28},{28,24},{1,5},{5... | collective-permute-start | bytes 3080 | tf_op jit(solution)/shard_map/ppermute | solution.py:53
  82.8 3.6 %collective-permute-start.7 = (f32[2,128]{1,0:T(2,128)S(1)}, f32[2,128]{1,0:T(2,128)S(1)}, u32[]{:S(2)}, u32[]{:S(2)}) collective-permute-start(f32[2,128]{1,0:T(2,128)S(1)} %add.146), channel_id=1, source_target_pairs={{0,8},{4,12},{8,0},{12,4},{16,24},{20,28},{24,16},{28,20},{1,9},{5... | collective-permute-start | bytes 3080 | tf_op jit(solution)/shard_map/ppermute | solution.py:53
  86.3 4.5 %collective-permute-start.8 = (f32[2,128]{1,0:T(2,128)S(1)}, f32[2,128]{1,0:T(2,128)S(1)}, u32[]{:S(2)}, u32[]{:S(2)}) collective-permute-start(f32[2,128]{1,0:T(2,128)S(1)} %add.147), channel_id=1, source_target_pairs={{0,16},{4,20},{8,24},{12,28},{16,0},{20,4},{24,8},{28,12},{1,17},{... | collective-permute-start | bytes 3080 | tf_op jit(solution)/shard_map/ppermute | solution.py:53
  95.2 1.2 collective-permute-start.9
  97.1 3.6 %collective-permute-start.10 = (f32[1,128]{1,0:T(1,128)S(1)}, f32[1,128]{1,0:T(1,128)S(1)}, u32[]{:S(2)}, u32[]{:S(2)}) collective-permute-start(f32[1,128]{1,0:T(1,128)S(1)} %add.149), channel_id=1, source_target_pairs={{0,2},{1,3},{2,0},{3,1},{4,6},{5,7},{6,4},{7,5},{8,10},{9,11},{10,... | collective-permute-start | bytes 1544 | tf_op jit(solution)/shard_map/ppermute | solution.py:53
  100.7 3.6 %collective-permute-start.11 = (f32[1,128]{1,0:T(1,128)S(1)}, f32[1,128]{1,0:T(1,128)S(1)}, u32[]{:S(2)}, u32[]{:S(2)}) collective-permute-start(f32[1,128]{1,0:T(1,128)S(1)} %add.150), channel_id=1, source_target_pairs={{0,4},{4,0},{8,12},{12,8},{16,20},{20,16},{24,28},{28,24},{1,5},{5... | collective-permute-start | bytes 1544 | tf_op jit(solution)/shard_map/ppermute | solution.py:53
  104.3 3.6 %collective-permute-start.12 = (f32[1,128]{1,0:T(1,128)S(1)}, f32[1,128]{1,0:T(1,128)S(1)}, u32[]{:S(2)}, u32[]{:S(2)}) collective-permute-start(f32[1,128]{1,0:T(1,128)S(1)} %add.151), channel_id=1, source_target_pairs={{0,8},{4,12},{8,0},{12,4},{16,24},{20,28},{24,16},{28,20},{1,9},{5... | collective-permute-start | bytes 1544 | tf_op jit(solution)/shard_map/ppermute | solution.py:53
  107.9 4.5 %collective-permute-start.13 = (f32[1,128]{1,0:T(1,128)S(1)}, f32[1,128]{1,0:T(1,128)S(1)}, u32[]{:S(2)}, u32[]{:S(2)}) collective-permute-start(f32[1,128]{1,0:T(1,128)S(1)} %add.152), channel_id=1, source_target_pairs={{0,16},{4,20},{8,24},{12,28},{16,0},{20,4},{24,8},{28,12},{1,17},{... | collective-permute-start | bytes 1544 | tf_op jit(solution)/shard_map/ppermute | solution.py:53
  119.1 1.4 collective-permute-start.14
  121.1 3.6 %collective-permute-start.15 = (f32[1,128]{1,0:T(1,128)S(1)}, f32[1,128]{1,0:T(1,128)S(1)}, u32[]{:S(2)}, u32[]{:S(2)}) collective-permute-start(f32[1,128]{1,0:T(1,128)S(1)} %add.154), channel_id=1, source_target_pairs={{0,2},{1,3},{2,0},{3,1},{4,6},{5,7},{6,4},{7,5},{8,10},{9,11},{10,... | collective-permute-start | bytes 1544 | tf_op jit(solution)/shard_map/ppermute | solution.py:53
  124.7 3.6 %collective-permute-start.16 = (f32[1,128]{1,0:T(1,128)S(1)}, f32[1,128]{1,0:T(1,128)S(1)}, u32[]{:S(2)}, u32[]{:S(2)}) collective-permute-start(f32[1,128]{1,0:T(1,128)S(1)} %add.155), channel_id=1, source_target_pairs={{0,4},{4,0},{8,12},{12,8},{16,20},{20,16},{24,28},{28,24},{1,5},{5... | collective-permute-start | bytes 1544 | tf_op jit(solution)/shard_map/ppermute | solution.py:53
  128.2 3.6 %collective-permute-start.17 = (f32[1,128]{1,0:T(1,128)S(1)}, f32[1,128]{1,0:T(1,128)S(1)}, u32[]{:S(2)}, u32[]{:S(2)}) collective-permute-start(f32[1,128]{1,0:T(1,128)S(1)} %add.156), channel_id=1, source_target_pairs={{0,8},{4,12},{8,0},{12,4},{16,24},{20,28},{24,16},{28,20},{1,9},{5... | collective-permute-start | bytes 1544 | tf_op jit(solution)/shard_map/ppermute | solution.py:53
  131.8 4.5 %collective-permute-start.18 = (f32[1,128]{1,0:T(1,128)S(1)}, f32[1,128]{1,0:T(1,128)S(1)}, u32[]{:S(2)}, u32[]{:S(2)}) collective-permute-start(f32[1,128]{1,0:T(1,128)S(1)} %add.157), channel_id=1, source_target_pairs={{0,16},{4,20},{8,24},{12,28},{16,0},{20,4},{24,8},{28,12},{1,17},{... | collective-permute-start | bytes 1544 | tf_op jit(solution)/shard_map/ppermute | solution.py:53
  141.4 1.4 collective-permute-start.19
  143.4 3.6 %collective-permute-start.20 = (f32[1,128]{1,0:T(1,128)S(1)}, f32[1,128]{1,0:T(1,128)S(1)}, u32[]{:S(2)}, u32[]{:S(2)}) collective-permute-start(f32[1,128]{1,0:T(1,128)S(1)} %add.159), channel_id=1, source_target_pairs={{0,2},{1,3},{2,0},{3,1},{4,6},{5,7},{6,4},{7,5},{8,10},{9,11},{10,... | collective-permute-start | bytes 1544 | tf_op jit(solution)/shard_map/ppermute | solution.py:53
  147.0 3.6 %collective-permute-start.21 = (f32[1,128]{1,0:T(1,128)S(1)}, f32[1,128]{1,0:T(1,128)S(1)}, u32[]{:S(2)}, u32[]{:S(2)}) collective-permute-start(f32[1,128]{1,0:T(1,128)S(1)} %add.160), channel_id=1, source_target_pairs={{0,4},{4,0},{8,12},{12,8},{16,20},{20,16},{24,28},{28,24},{1,5},{5... | collective-permute-start | bytes 1544 | tf_op jit(solution)/shard_map/ppermute | solution.py:53
  150.6 3.6 %collective-permute-start.22 = (f32[1,128]{1,0:T(1,128)S(1)}, f32[1,128]{1,0:T(1,128)S(1)}, u32[]{:S(2)}, u32[]{:S(2)}) collective-permute-start(f32[1,128]{1,0:T(1,128)S(1)} %add.161), channel_id=1, source_target_pairs={{0,8},{4,12},{8,0},{12,4},{16,24},{20,28},{24,16},{28,20},{1,9},{5... | collective-permute-start | bytes 1544 | tf_op jit(solution)/shard_map/ppermute | solution.py:53
  154.2 4.5 %collective-permute-start.23 = (f32[1,128]{1,0:T(1,128)S(1)}, f32[1,128]{1,0:T(1,128)S(1)}, u32[]{:S(2)}, u32[]{:S(2)}) collective-permute-start(f32[1,128]{1,0:T(1,128)S(1)} %add.162), channel_id=1, source_target_pairs={{0,16},{4,20},{8,24},{12,28},{16,0},{20,4},{24,8},{28,12},{1,17},{... | collective-permute-start | bytes 1544 | tf_op jit(solution)/shard_map/ppermute | solution.py:53
  165.4 1.3 collective-permute-start.24
  167.4 3.6 %collective-permute-start.25 = (f32[1,128]{1,0:T(1,128)S(1)}, f32[1,128]{1,0:T(1,128)S(1)}, u32[]{:S(2)}, u32[]{:S(2)}) collective-permute-start(f32[1,128]{1,0:T(1,128)S(1)} %add.164), channel_id=1, source_target_pairs={{0,2},{1,3},{2,0},{3,1},{4,6},{5,7},{6,4},{7,5},{8,10},{9,11},{10,... | collective-permute-start | bytes 1544 | tf_op jit(solution)/shard_map/ppermute | solution.py:53
  171.0 3.6 %collective-permute-start.26 = (f32[1,128]{1,0:T(1,128)S(1)}, f32[1,128]{1,0:T(1,128)S(1)}, u32[]{:S(2)}, u32[]{:S(2)}) collective-permute-start(f32[1,128]{1,0:T(1,128)S(1)} %add.165), channel_id=1, source_target_pairs={{0,4},{4,0},{8,12},{12,8},{16,20},{20,16},{24,28},{28,24},{1,5},{5... | collective-permute-start | bytes 1544 | tf_op jit(solution)/shard_map/ppermute | solution.py:53
  174.5 3.6 %collective-permute-start.27 = (f32[1,128]{1,0:T(1,128)S(1)}, f32[1,128]{1,0:T(1,128)S(1)}, u32[]{:S(2)}, u32[]{:S(2)}) collective-permute-start(f32[1,128]{1,0:T(1,128)S(1)} %add.166), channel_id=1, source_target_pairs={{0,8},{4,12},{8,0},{12,4},{16,24},{20,28},{24,16},{28,20},{1,9},{5... | collective-permute-start | bytes 1544 | tf_op jit(solution)/shard_map/ppermute | solution.py:53
  178.1 4.5 %collective-permute-start.28 = (f32[1,128]{1,0:T(1,128)S(1)}, f32[1,128]{1,0:T(1,128)S(1)}, u32[]{:S(2)}, u32[]{:S(2)}) collective-permute-start(f32[1,128]{1,0:T(1,128)S(1)} %add.167), channel_id=1, source_target_pairs={{0,16},{4,20},{8,24},{12,28},{16,0},{20,4},{24,8},{28,12},{1,17},{... | collective-permute-start | bytes 1544 | tf_op jit(solution)/shard_map/ppermute | solution.py:53

commit v8 on v6

--- a/solution.py
+++ b/solution.py
@@ -306,11 +306,25 @@
     stacked = jnp.concatenate(
         [probes, observed[None], kappa_sq[None], variance_weight[None]], axis=0
     )
-    ext = extended(stacked, (("rows", 1), ("cols", 2)), HALO)
+    count = lax.axis_size("rows")
+    sent = -(-HALO // 8) * 8
+    assert sent <= rows
+    planes = stacked.shape[0]
+    below = lax.ppermute(
+        stacked[:, rows - sent :].reshape(planes * sent, cols), "rows",
+        [(i, i + 1) for i in range(count - 1)],
+    ).reshape(planes, sent, cols)[:, sent - HALO :]
+    above = lax.ppermute(
+        stacked[:, :sent].reshape(planes * sent, cols), "rows",
+        [(i + 1, i) for i in range(count - 1)],
+    ).reshape(planes, sent, cols)[:, :HALO]
+    ext = jnp.concatenate(
+        [jnp.transpose(piece, (1, 2, 0)) for piece in (below, stacked, above)], axis=0
+    )
+    ext = extended(ext, (("cols", 1),), HALO)
     ext = jnp.pad(
-        ext, ((0, lanes - ext.shape[0]), (0, 0), (0, half + sublanes - ext.shape[2]))
-    )
-    ext = jnp.transpose(ext, (1, 2, 0))
+        ext, ((0, 0), (0, half + sublanes - ext.shape[1]), (0, lanes - ext.shape[2]))
+    )
 
     row_at = lax.axis_index("rows") * rows - HALO + lax.iota(jnp.int32, slab_rows)
     row_in = ((row_at >= 0) & (row_at < rows * lax.axis_size("rows"))).astype(jnp.float32)

time: 172 us -> 167 us (0.971)
  waiting for transfers between devices: 69.1 us -> 55.2 us
  local copies, waits for them, and re-layouts: 5.92 us -> 11 us
  starting transfers between devices: 43.9 us -> 46.1 us
    ppermute x2 -> x1, waiting for transfers between devices: 14.1 us -> 0.01 us  [extended(): lax.ppermute(tail, axis, [(i, (i + 1) % count) for i in range(ends)])]
    ppermute x0 -> x2, starting transfers between devices: none -> 7.49 us  [the longest x1 6.2 us: on_device(): lax.ppermute(stacked[:, rows - sent:].reshape(planes * sent, cols), 'rows...]
    slice x0 -> x4, local copies, waits for them, and re-layouts: none -> 5.24 us  [the longest x2 3 us: on_device(): stacked[:, rows - sent:].reshape(planes * sent, cols)]
    ppermute x2 -> x1, starting transfers between devices: 6.18 us -> 1.93 us  [extended(): lax.ppermute(tail, axis, [(i, (i + 1) % count) for i in range(ends)])]
    slice x2 -> x1, other arithmetic: 3.75 us -> 0.02 us  [extended(): lax.slice_in_dim(cells, cells.shape[dim] - width, cells.shape[dim], axis=...]
    transpose x0 -> x1, other arithmetic: none -> 3.09 us  [on_device(): jnp.transpose(piece, (1, 2, 0))]
    ppermute x0 -> x2, waiting for transfers between devices: none -> 2.21 us  [the longest x1 2.21 us: on_device(): lax.ppermute(stacked[:, rows - sent:].reshape(planes * sent, cols), 'rows...]
    concatenate x0 -> x1, other arithmetic: none -> 2.1 us  [on_device(): jnp.concatenate([probes, observed[None], kappa_sq[None], variance_weight[...]
  transfers between devices with their start and end apart: 29 -> 29, of which waited for: 27 -> 27; matrix products, arithmetic and copies ran while one was open for 1% -> 5% of each run, Pallas kernels for 0% -> 0%
where the time goes in v8:
time: 167 us; the launch traced here: 166 us
  waiting for transfers between devices  55.2 us (33%)
  starting transfers between devices  46.1 us (28%)
  Pallas kernels  38.1 us (23%)
  other arithmetic  15.1 us (9%)
  local copies, waits for them, and re-layouts  11 us (7%)
    ppermute x25, waiting for transfers between devices, all_sum(): lax.ppermute(terms, axis, [(i, i ^ hop) for i in range(count)])  50.5 us
    pallas_call x6, Pallas kernels, _call(): pl.pallas_call(lambda *refs: kernel(plan, *refs), out_shape=out_shapes, i...  38.1 us
    ppermute x25, starting transfers between devices, all_sum(): lax.ppermute(terms, axis, [(i, i ^ hop) for i in range(count)])  35.4 us
    ppermute x1, starting transfers between devices, on_device(): lax.ppermute(stacked[:, rows - sent:].reshape(planes * sent, cols), 'rows...  6.2 us
    add x25, other arithmetic, all_sum(): terms + lax.ppermute(terms, axis, [(i, i ^ hop) for i in range(count)])  6.05 us
  transfers between devices with their start and end apart: 29, of which 27 were waited for; matrix products, arithmetic and copies ran while one was open for 5% of the time, Pallas kernels for 0%

profile of v8, /device:TPU:0, one launch (start us, length us, event | category | flops | bytes accessed | tf_op | source)
XLA Modules:
  0.0 166.3 jit_solution(14102681460278236635)
XLA Ops:
  4.9 2.1 %pad_maximum_fusion = f32[67,16,128]{0,2,1:T(8,128)S(1)} fusion(f32[1,16,128]{0,2,1:T(8,128)S(1)} %copy.10, f32[1,16,128]{0,2,1:T(8,128)S(1)} %copy.9, f32[1,16,128]{0,2,1:T(8,128)} %copy.8, f32[64,16,128]{0,2,1:T(8,128)S(1)} %copy.7), kind=kLoop, calls=%fused_computation.13 | loop fusion | flops 411648 | bytes 1097728 | tf_op jit(solution)/shard_map/concatenate | solution.py:306
  12.5 6.2 %collective-permute-start = (f32[536,128]{1,0:T(8,128)}, f32[536,128]{1,0:T(8,128)}, u32[]{:S(2)}, u32[]{:S(2)}) collective-permute-start(f32[536,128]{1,0:T(8,128)} %bitcast.17), channel_id=1, source_target_pairs={{0,4},{4,8},{8,12},{12,16},{16,20},{20,24},{24,28},{1,5},{5,9},{9,... | collective-permute-start | bytes 823304 | tf_op jit(solution)/shard_map/ppermute | solution.py:313
  18.7 3.1 %fusion.12 = f32[16,128,67]{2,1,0:T(8,128)} fusion(f32[1,16,128]{0,2,1:T(8,128)S(1)} %copy.10, f32[1,16,128]{0,2,1:T(8,128)S(1)} %copy.9, f32[1,16,128]{0,2,1:T(8,128)} %copy.8, f32[64,16,128]{0,2,1:T(8,128)S(1)} %copy.7), kind=kLoop, calls=%fused_computation.28 | loop fusion | flops 411648 | bytes 1097728 | tf_op jit(solution)/shard_map/transpose | solution.py:322
  24.6 2.2 %collective-permute-done = f32[536,128]{1,0:T(8,128)} collective-permute-done((f32[536,128]{1,0:T(8,128)}, f32[536,128]{1,0:T(8,128)}, u32[]{:S(2)}, u32[]{:S(2)}) %collective-permute-start) | collective-permute-done | bytes 274464 | tf_op jit(solution)/shard_map/ppermute | solution.py:313
  31.8 2.5 %collective-permute-done.3 = f32[28,6,67]{2,1,0:T(8,128)S(1)} collective-permute-done((f32[28,6,67]{2,1,0:T(8,128)S(1)}, f32[28,6,67]{2,1,0:T(8,128)S(1)}, u32[]{:S(2)}, u32[]{:S(2)}) %collective-permute-start.3) | collective-permute-done | bytes 45056 | tf_op jit(solution)/shard_map/ppermute | solution.py:22
  36.2 11.3 %shard_map.59 = (f32[28,80,128]{2,1,0:T(8,128)}, f32[28,80,128]{2,1,0:T(8,128)}, f32[28,80,128]{2,1,0:T(8,128)}, f32[28,80,128]{2,1,0:T(8,128)}, f32[28,80,128]{...) custom-call(f32[28,144,128]{2,1,0:T(8,128)} %select_maximum_fusion.refs_0_, ...), custom_call_target="tpu_custom_call" | custom-call | flops 11468800 | bytes 13762560 | tf_op jit(solution)/shard_map/pallas_call | solution.py:284
  47.5 3.4 %collective-permute-start.4 = (f32[2,128]{1,0:T(2,128)}, f32[2,128]{1,0:T(2,128)S(1)}, u32[]{:S(2)}, u32[]{:S(2)}) collective-permute-start(f32[2,128]{1,0:T(2,128)} %get-tuple-element.20), channel_id=1, source_target_pairs={{0,1},{1,0},{2,3},{3,2},{4,5},{5,4},{6,7},{7,6},{8,9},{9,8},{10,11... | collective-permute-start | bytes 3080 | tf_op jit(solution)/shard_map/ppermute | solution.py:56
  52.7 3.5 %collective-permute-done.5 = f32[2,128]{1,0:T(2,128)S(1)} collective-permute-done((f32[2,128]{1,0:T(2,128)S(1)}, f32[2,128]{1,0:T(2,128)S(1)}, u32[]{:S(2)}, u32[]{:S(2)}) %collective-permute-start.5) | collective-permute-done | bytes 1056 | tf_op jit(solution)/shard_map/ppermute | solution.py:56
  56.2 2.5 %collective-permute-start.6 = (f32[2,128]{1,0:T(2,128)S(1)}, f32[2,128]{1,0:T(2,128)S(1)}, u32[]{:S(2)}, u32[]{:S(2)}) collective-permute-start(f32[2,128]{1,0:T(2,128)S(1)} %add.145), channel_id=1, source_target_pairs={{0,4},{4,0},{8,12},{12,8},{16,20},{20,16},{24,28},{28,24},{1,5},{5... | collective-permute-start | bytes 3080 | tf_op jit(solution)/shard_map/ppermute | solution.py:56
  61.8 2.0 %collective-permute-done.7 = f32[2,128]{1,0:T(2,128)S(1)} collective-permute-done((f32[2,128]{1,0:T(2,128)S(1)}, f32[2,128]{1,0:T(2,128)S(1)}, u32[]{:S(2)}, u32[]{:S(2)}) %collective-permute-start.7) | collective-permute-done | bytes 1056 | tf_op jit(solution)/shard_map/ppermute | solution.py:56
  63.8 2.6 %collective-permute-start.8 = (f32[2,128]{1,0:T(2,128)S(1)}, f32[2,128]{1,0:T(2,128)S(1)}, u32[]{:S(2)}, u32[]{:S(2)}) collective-permute-start(f32[2,128]{1,0:T(2,128)S(1)} %add.147), channel_id=1, source_target_pairs={{0,16},{4,20},{8,24},{12,28},{16,0},{20,4},{24,8},{28,12},{1,17},{... | collective-permute-start | bytes 3080 | tf_op jit(solution)/shard_map/ppermute | solution.py:56
  68.9 3.9 %shard_map.60 = (f32[28,80,128]{2,1,0:T(8,128)}, f32[28,80,128]{2,1,0:T(8,128)}, f32[1,128]{1,0:T(1,128)}) custom-call(f32[2,128]{1,0:T(2,128)} %add.148.refs_0_.refs_1_, f32[28,80,128]{2,1,0:T(8,128)} %get-tuple-element.21.refs_1_.refs_3_.refs_4_, f32[28,80,128]{2,1,0:T(8,128)} %get-tuple-element.22.refs_2_, f32[80,128]{1,0:T(8,128)} %add_convert_fusion.1.refs_3_.refs_8_.refs_6_), custom_call_target="tpu_custom_call" | custom-call | flops 11468800 | bytes 8028160 | tf_op jit(solution)/shard_map/pallas_call | solution.py:284
  74.8 3.4 %collective-permute-done.10 = f32[1,128]{1,0:T(1,128)S(1)} collective-permute-done((f32[1,128]{1,0:T(1,128)S(1)}, f32[1,128]{1,0:T(1,128)S(1)}, u32[]{:S(2)}, u32[]{:S(2)}) %collective-permute-start.10) | collective-permute-done | bytes 544 | tf_op jit(solution)/shard_map/ppermute | solution.py:56
  78.3 2.0 %collective-permute-start.11 = (f32[1,128]{1,0:T(1,128)S(1)}, f32[1,128]{1,0:T(1,128)S(1)}, u32[]{:S(2)}, u32[]{:S(2)}) collective-permute-start(f32[1,128]{1,0:T(1,128)S(1)} %add.150), channel_id=1, source_target_pairs={{0,4},{4,0},{8,12},{12,8},{16,20},{20,16},{24,28},{28,24},{1,5},{5... | collective-permute-start | bytes 1544 | tf_op jit(solution)/shard_map/ppermute | solution.py:56
  83.4 2.0 %collective-permute-done.12 = f32[1,128]{1,0:T(1,128)S(1)} collective-permute-done((f32[1,128]{1,0:T(1,128)S(1)}, f32[1,128]{1,0:T(1,128)S(1)}, u32[]{:S(2)}, u32[]{:S(2)}) %collective-permute-start.12) | collective-permute-done | bytes 544 | tf_op jit(solution)/shard_map/ppermute | solution.py:56
  85.4 2.6 %collective-permute-start.13 = (f32[1,128]{1,0:T(1,128)S(1)}, f32[1,128]{1,0:T(1,128)S(1)}, u32[]{:S(2)}, u32[]{:S(2)}) collective-permute-start(f32[1,128]{1,0:T(1,128)S(1)} %add.152), channel_id=1, source_target_pairs={{0,16},{4,20},{8,24},{12,28},{16,0},{20,4},{24,8},{28,12},{1,17},{... | collective-permute-start | bytes 1544 | tf_op jit(solution)/shard_map/ppermute | solution.py:56
  90.4 6.2 %shard_map.61 = (f32[28,80,128]{2,1,0:T(8,128)}, f32[28,80,128]{2,1,0:T(8,128)}, f32[1,128]{1,0:T(1,128)}) custom-call(f32[1,128]{1,0:T(1,128)} %add.153.refs_0_.refs_1_, f32[2,128]{1,0:T(2,128)} %add.148.refs_0_.refs_1_, f32[28,80,128]{2,1,0:T(8,128)} %get-tuple-element.24.refs_2_.refs_4_, f32[28,80,128]{2,1,0:T(8,128)} %get-tuple-element.21.refs_1_.refs_3_.refs_4_, ...), custom_call_target="tpu_custom_call" | custom-call | flops 11468800 | bytes 13762560 | tf_op jit(solution)/shard_map/pallas_call | solution.py:284
  98.7 3.4 %collective-permute-done.15 = f32[1,128]{1,0:T(1,128)S(1)} collective-permute-done((f32[1,128]{1,0:T(1,128)S(1)}, f32[1,128]{1,0:T(1,128)S(1)}, u32[]{:S(2)}, u32[]{:S(2)}) %collective-permute-start.15) | collective-permute-done | bytes 544 | tf_op jit(solution)/shard_map/ppermute | solution.py:56
  102.1 2.0 %collective-permute-start.16 = (f32[1,128]{1,0:T(1,128)S(1)}, f32[1,128]{1,0:T(1,128)S(1)}, u32[]{:S(2)}, u32[]{:S(2)}) collective-permute-start(f32[1,128]{1,0:T(1,128)S(1)} %add.155), channel_id=1, source_target_pairs={{0,4},{4,0},{8,12},{12,8},{16,20},{20,16},{24,28},{28,24},{1,5},{5... | collective-permute-start | bytes 1544 | tf_op jit(solution)/shard_map/ppermute | solution.py:56
  107.3 2.0 %collective-permute-done.17 = f32[1,128]{1,0:T(1,128)S(1)} collective-permute-done((f32[1,128]{1,0:T(1,128)S(1)}, f32[1,128]{1,0:T(1,128)S(1)}, u32[]{:S(2)}, u32[]{:S(2)}) %collective-permute-start.17) | collective-permute-done | bytes 544 | tf_op jit(solution)/shard_map/ppermute | solution.py:56
  109.2 2.6 %collective-permute-start.18 = (f32[1,128]{1,0:T(1,128)S(1)}, f32[1,128]{1,0:T(1,128)S(1)}, u32[]{:S(2)}, u32[]{:S(2)}) collective-permute-start(f32[1,128]{1,0:T(1,128)S(1)} %add.157), channel_id=1, source_target_pairs={{0,16},{4,20},{8,24},{12,28},{16,0},{20,4},{24,8},{28,12},{1,17},{... | collective-permute-start | bytes 1544 | tf_op jit(solution)/shard_map/ppermute | solution.py:56
  114.2 4.6 %shard_map.62 = (f32[28,80,128]{2,1,0:T(8,128)}, f32[28,80,128]{2,1,0:T(8,128)}, f32[1,128]{1,0:T(1,128)}) custom-call(f32[1,128]{1,0:T(1,128)} %add.153.refs_0_.refs_1_, f32[1,128]{1,0:T(1,128)} %add.158.refs_1_, f32[28,80,128]{2,1,0:T(8,128)} %get-tuple-element.28.refs_2_, f32[28,80,128]{2,1,0:T(8,128)} %get-tuple-element.29.refs_3_, ...), custom_call_target="tpu_custom_call" | custom-call | flops 11468800 | bytes 11468800 | tf_op jit(solution)/shard_map/pallas_call | solution.py:284
  120.9 3.4 %collective-permute-done.20 = f32[1,128]{1,0:T(1,128)S(1)} collective-permute-done((f32[1,128]{1,0:T(1,128)S(1)}, f32[1,128]{1,0:T(1,128)S(1)}, u32[]{:S(2)}, u32[]{:S(2)}) %collective-permute-start.20) | collective-permute-done | bytes 544 | tf_op jit(solution)/shard_map/ppermute | solution.py:56
  124.3 2.0 %collective-permute-start.21 = (f32[1,128]{1,0:T(1,128)S(1)}, f32[1,128]{1,0:T(1,128)S(1)}, u32[]{:S(2)}, u32[]{:S(2)}) collective-permute-start(f32[1,128]{1,0:T(1,128)S(1)} %add.160), channel_id=1, source_target_pairs={{0,4},{4,0},{8,12},{12,8},{16,20},{20,16},{24,28},{28,24},{1,5},{5... | collective-permute-start | bytes 1544 | tf_op jit(solution)/shard_map/ppermute | solution.py:56
  129.5 2.0 %collective-permute-done.22 = f32[1,128]{1,0:T(1,128)S(1)} collective-permute-done((f32[1,128]{1,0:T(1,128)S(1)}, f32[1,128]{1,0:T(1,128)S(1)}, u32[]{:S(2)}, u32[]{:S(2)}) %collective-permute-start.22) | collective-permute-done | bytes 544 | tf_op jit(solution)/shard_map/ppermute | solution.py:56
  131.5 2.6 %collective-permute-start.23 = (f32[1,128]{1,0:T(1,128)S(1)}, f32[1,128]{1,0:T(1,128)S(1)}, u32[]{:S(2)}, u32[]{:S(2)}) collective-permute-start(f32[1,128]{1,0:T(1,128)S(1)} %add.162), channel_id=1, source_target_pairs={{0,16},{4,20},{8,24},{12,28},{16,0},{20,4},{24,8},{28,12},{1,17},{... | collective-permute-start | bytes 1544 | tf_op jit(solution)/shard_map/ppermute | solution.py:56
  136.5 6.2 %shard_map.63 = (f32[28,80,128]{2,1,0:T(8,128)}, f32[28,80,128]{2,1,0:T(8,128)}, f32[1,128]{1,0:T(1,128)}) custom-call(f32[1,128]{1,0:T(1,128)} %add.163.refs_0_, f32[1,128]{1,0:T(1,128)} %add.153.refs_0_.refs_1_, f32[28,80,128]{2,1,0:T(8,128)} %get-tuple-element.32.refs_2_, f32[28,80,128]{2,1,0:T(8,128)} %get-tuple-element.29.refs_3_, ...), custom_call_target="tpu_custom_call" | custom-call | flops 11468800 | bytes 13762560 | tf_op jit(solution)/shard_map/pallas_call | solution.py:284
  144.8 3.4 %collective-permute-done.25 = f32[1,128]{1,0:T(1,128)S(1)} collective-permute-done((f32[1,128]{1,0:T(1,128)S(1)}, f32[1,128]{1,0:T(1,128)S(1)}, u32[]{:S(2)}, u32[]{:S(2)}) %collective-permute-start.25) | collective-permute-done | bytes 544 | tf_op jit(solution)/shard_map/ppermute | solution.py:56
  148.3 2.0 %collective-permute-start.26 = (f32[1,128]{1,0:T(1,128)S(1)}, f32[1,128]{1,0:T(1,128)S(1)}, u32[]{:S(2)}, u32[]{:S(2)}) collective-permute-start(f32[1,128]{1,0:T(1,128)S(1)} %add.165), channel_id=1, source_target_pairs={{0,4},{4,0},{8,12},{12,8},{16,20},{20,16},{24,28},{28,24},{1,5},{5... | collective-permute-start | bytes 1544 | tf_op jit(solution)/shard_map/ppermute | solution.py:56
  153.4 2.0 %collective-permute-done.27 = f32[1,128]{1,0:T(1,128)S(1)} collective-permute-done((f32[1,128]{1,0:T(1,128)S(1)}, f32[1,128]{1,0:T(1,128)S(1)}, u32[]{:S(2)}, u32[]{:S(2)}) %collective-permute-start.27) | collective-permute-done | bytes 544 | tf_op jit(solution)/shard_map/ppermute | solution.py:56
  155.4 2.6 %collective-permute-start.28 = (f32[1,128]{1,0:T(1,128)S(1)}, f32[1,128]{1,0:T(1,128)S(1)}, u32[]{:S(2)}, u32[]{:S(2)}) collective-permute-start(f32[1,128]{1,0:T(1,128)S(1)} %add.167), channel_id=1, source_target_pairs={{0,16},{4,20},{8,24},{12,28},{16,0},{20,4},{24,8},{28,12},{1,17},{... | collective-permute-start | bytes 1544 | tf_op jit(solution)/shard_map/ppermute | solution.py:56
  160.4 5.9 %shard_map.64 = (f32[16,128]{1,0:T(8,128)}, f32[16,128]{1,0:T(8,128)}) custom-call(f32[1,128]{1,0:T(1,128)} %add.163.refs_0_, f32[1,128]{1,0:T(1,128)} %add.168.refs_1_, f32[28,80,128]{2,1,0:T(8,128)} %get-tuple-element.34.refs_2_, f32[28,80,128]{2,1,0:T(8,128)} %get-tuple-element.35.refs_3_, f32[28,80,128]{2,1,0:T(8,128)} %get-tuple-element.21.refs_1_.refs_3_.refs_4_, ...), custom_call_target="tpu_custom_call" | custom-call | flops 11468800 | bytes 14909440 | tf_op jit(solution)/shard_map/pallas_call | solution.py:284
  (87 shorter events, 57.2 us)
Async XLA Ops:
  0.6 2.5 %copy-start.1 = (f32[16,128]{1,0:T(8,128)S(1)}, f32[16,128]{1,0:T(8,128)}, u32[]{:S(2)}) copy-start(f32[16,128]{1,0:T(8,128)} %refs_9_.1) | copy-start | bytes 24580
  0.6 2.9 %copy-start.2 = (f32[16,128]{1,0:T(8,128)S(1)}, f32[16,128]{1,0:T(8,128)}, u32[]{:S(2)}) copy-start(f32[16,128]{1,0:T(8,128)} %refs_8_.1) | copy-start | bytes 24580
  9.3 14.2 %collective-permute-start.1 = (f32[536,128]{1,0:T(8,128)S(1)}, f32[536,128]{1,0:T(8,128)}, u32[]{:S(2)}, u32[]{:S(2)}) collective-permute-start(f32[536,128]{1,0:T(8,128)S(1)} %bitcast.16), channel_id=1, source_target_pairs={{4,0},{8,4},{12,8},{16,12},{20,16},{24,20},{28,24},{5,1},{9,5},{13... | collective-permute-start | bytes 823304 | tf_op jit(solution)/shard_map/ppermute | solution.py:317
  12.5 14.3 %collective-permute-start = (f32[536,128]{1,0:T(8,128)}, f32[536,128]{1,0:T(8,128)}, u32[]{:S(2)}, u32[]{:S(2)}) collective-permute-start(f32[536,128]{1,0:T(8,128)} %bitcast.17), channel_id=1, source_target_pairs={{0,4},{4,8},{8,12},{12,16},{16,20},{20,24},{24,28},{1,5},{5,9},{9,... | collective-permute-start | bytes 823304 | tf_op jit(solution)/shard_map/ppermute | solution.py:313
  21.8 6.2 %copy-start = (f32[16,128,67]{2,1,0:T(8,128)S(1)}, f32[16,128,67]{2,1,0:T(8,128)}, u32[]{:S(2)}) copy-start(f32[16,128,67]{2,1,0:T(8,128)} %fusion.12) | copy-start | bytes 1646596
  28.1 3.8 %collective-permute-start.2 = (f32[28,6,67]{2,1,0:T(8,128)S(1)}, f32[28,6,67]{2,1,0:T(8,128)S(1)}, u32[]{:S(2)}, u32[]{:S(2)}) collective-permute-start(f32[28,6,67]{2,1,0:T(8,128)S(1)} %get-tuple-element.38), channel_id=1, source_target_pairs={{0,1},{1,2},{2,3},{4,5},{5,6},{6,7},{8,9},{9,10},{10,11},{12,13},{... | collective-permute-start | bytes 135080 | tf_op jit(solution)/shard_map/ppermute | solution.py:20
  30.0 4.3 %collective-permute-start.3 = (f32[28,6,67]{2,1,0:T(8,128)S(1)}, f32[28,6,67]{2,1,0:T(8,128)S(1)}, u32[]{:S(2)}, u32[]{:S(2)}) collective-permute-start(f32[28,6,67]{2,1,0:T(8,128)S(1)} %get-tuple-element.39), channel_id=1, source_target_pairs={{1,0},{2,1},{3,2},{5,4},{6,5},{7,6},{9,8},{10,9},{11,10},{13,12},{... | collective-permute-start | bytes 135080 | tf_op jit(solution)/shard_map/ppermute | solution.py:22
  47.5 4.4 %collective-permute-start.4 = (f32[2,128]{1,0:T(2,128)}, f32[2,128]{1,0:T(2,128)S(1)}, u32[]{:S(2)}, u32[]{:S(2)}) collective-permute-start(f32[2,128]{1,0:T(2,128)} %get-tuple-element.20), channel_id=1, source_target_pairs={{0,1},{1,0},{2,3},{3,2},{4,5},{5,4},{6,7},{7,6},{8,9},{9,8},{10,11... | collective-permute-start | bytes 3080 | tf_op jit(solution)/shard_map/ppermute | solution.py:56
  52.6 3.6 %collective-permute-start.5 = (f32[2,128]{1,0:T(2,128)S(1)}, f32[2,128]{1,0:T(2,128)S(1)}, u32[]{:S(2)}, u32[]{:S(2)}) collective-permute-start(f32[2,128]{1,0:T(2,128)S(1)} %add.144), channel_id=1, source_target_pairs={{0,2},{1,3},{2,0},{3,1},{4,6},{5,7},{6,4},{7,5},{8,10},{9,11},{10,... | collective-permute-start | bytes 3080 | tf_op jit(solution)/shard_map/ppermute | solution.py:56
  56.2 4.0 %collective-permute-start.6 = (f32[2,128]{1,0:T(2,128)S(1)}, f32[2,128]{1,0:T(2,128)S(1)}, u32[]{:S(2)}, u32[]{:S(2)}) collective-permute-start(f32[2,128]{1,0:T(2,128)S(1)} %add.145), channel_id=1, source_target_pairs={{0,4},{4,0},{8,12},{12,8},{16,20},{20,16},{24,28},{28,24},{1,5},{5... | collective-permute-start | bytes 3080 | tf_op jit(solution)/shard_map/ppermute | solution.py:56
  60.2 3.6 %collective-permute-start.7 = (f32[2,128]{1,0:T(2,128)S(1)}, f32[2,128]{1,0:T(2,128)S(1)}, u32[]{:S(2)}, u32[]{:S(2)}) collective-permute-start(f32[2,128]{1,0:T(2,128)S(1)} %add.146), channel_id=1, source_target_pairs={{0,8},{4,12},{8,0},{12,4},{16,24},{20,28},{24,16},{28,20},{1,9},{5... | collective-permute-start | bytes 3080 | tf_op jit(solution)/shard_map/ppermute | solution.py:56
  63.8 4.5 %collective-permute-start.8 = (f32[2,128]{1,0:T(2,128)S(1)}, f32[2,128]{1,0:T(2,128)S(1)}, u32[]{:S(2)}, u32[]{:S(2)}) collective-permute-start(f32[2,128]{1,0:T(2,128)S(1)} %add.147), channel_id=1, source_target_pairs={{0,16},{4,20},{8,24},{12,28},{16,0},{20,4},{24,8},{28,12},{1,17},{... | collective-permute-start | bytes 3080 | tf_op jit(solution)/shard_map/ppermute | solution.py:56
  72.7 1.4 collective-permute-start.9
  74.7 3.6 %collective-permute-start.10 = (f32[1,128]{1,0:T(1,128)S(1)}, f32[1,128]{1,0:T(1,128)S(1)}, u32[]{:S(2)}, u32[]{:S(2)}) collective-permute-start(f32[1,128]{1,0:T(1,128)S(1)} %add.149), channel_id=1, source_target_pairs={{0,2},{1,3},{2,0},{3,1},{4,6},{5,7},{6,4},{7,5},{8,10},{9,11},{10,... | collective-permute-start | bytes 1544 | tf_op jit(solution)/shard_map/ppermute | solution.py:56
  78.3 3.6 %collective-permute-start.11 = (f32[1,128]{1,0:T(1,128)S(1)}, f32[1,128]{1,0:T(1,128)S(1)}, u32[]{:S(2)}, u32[]{:S(2)}) collective-permute-start(f32[1,128]{1,0:T(1,128)S(1)} %add.150), channel_id=1, source_target_pairs={{0,4},{4,0},{8,12},{12,8},{16,20},{20,16},{24,28},{28,24},{1,5},{5... | collective-permute-start | bytes 1544 | tf_op jit(solution)/shard_map/ppermute | solution.py:56
  81.8 3.6 %collective-permute-start.12 = (f32[1,128]{1,0:T(1,128)S(1)}, f32[1,128]{1,0:T(1,128)S(1)}, u32[]{:S(2)}, u32[]{:S(2)}) collective-permute-start(f32[1,128]{1,0:T(1,128)S(1)} %add.151), channel_id=1, source_target_pairs={{0,8},{4,12},{8,0},{12,4},{16,24},{20,28},{24,16},{28,20},{1,9},{5... | collective-permute-start | bytes 1544 | tf_op jit(solution)/shard_map/ppermute | solution.py:56
  85.4 4.5 %collective-permute-start.13 = (f32[1,128]{1,0:T(1,128)S(1)}, f32[1,128]{1,0:T(1,128)S(1)}, u32[]{:S(2)}, u32[]{:S(2)}) collective-permute-start(f32[1,128]{1,0:T(1,128)S(1)} %add.152), channel_id=1, source_target_pairs={{0,16},{4,20},{8,24},{12,28},{16,0},{20,4},{24,8},{28,12},{1,17},{... | collective-permute-start | bytes 1544 | tf_op jit(solution)/shard_map/ppermute | solution.py:56
  96.6 1.2 collective-permute-start.14
  98.5 3.6 %collective-permute-start.15 = (f32[1,128]{1,0:T(1,128)S(1)}, f32[1,128]{1,0:T(1,128)S(1)}, u32[]{:S(2)}, u32[]{:S(2)}) collective-permute-start(f32[1,128]{1,0:T(1,128)S(1)} %add.154), channel_id=1, source_target_pairs={{0,2},{1,3},{2,0},{3,1},{4,6},{5,7},{6,4},{7,5},{8,10},{9,11},{10,... | collective-permute-start | bytes 1544 | tf_op jit(solution)/shard_map/ppermute | solution.py:56
  102.1 3.6 %collective-permute-start.16 = (f32[1,128]{1,0:T(1,128)S(1)}, f32[1,128]{1,0:T(1,128)S(1)}, u32[]{:S(2)}, u32[]{:S(2)}) collective-permute-start(f32[1,128]{1,0:T(1,128)S(1)} %add.155), channel_id=1, source_target_pairs={{0,4},{4,0},{8,12},{12,8},{16,20},{20,16},{24,28},{28,24},{1,5},{5... | collective-permute-start | bytes 1544 | tf_op jit(solution)/shard_map/ppermute | solution.py:56
  105.7 3.6 %collective-permute-start.17 = (f32[1,128]{1,0:T(1,128)S(1)}, f32[1,128]{1,0:T(1,128)S(1)}, u32[]{:S(2)}, u32[]{:S(2)}) collective-permute-start(f32[1,128]{1,0:T(1,128)S(1)} %add.156), channel_id=1, source_target_pairs={{0,8},{4,12},{8,0},{12,4},{16,24},{20,28},{24,16},{28,20},{1,9},{5... | collective-permute-start | bytes 1544 | tf_op jit(solution)/shard_map/ppermute | solution.py:56
  109.2 4.5 %collective-permute-start.18 = (f32[1,128]{1,0:T(1,128)S(1)}, f32[1,128]{1,0:T(1,128)S(1)}, u32[]{:S(2)}, u32[]{:S(2)}) collective-permute-start(f32[1,128]{1,0:T(1,128)S(1)} %add.157), channel_id=1, source_target_pairs={{0,16},{4,20},{8,24},{12,28},{16,0},{20,4},{24,8},{28,12},{1,17},{... | collective-permute-start | bytes 1544 | tf_op jit(solution)/shard_map/ppermute | solution.py:56
  118.9 1.2 collective-permute-start.19
  120.7 3.6 %collective-permute-start.20 = (f32[1,128]{1,0:T(1,128)S(1)}, f32[1,128]{1,0:T(1,128)S(1)}, u32[]{:S(2)}, u32[]{:S(2)}) collective-permute-start(f32[1,128]{1,0:T(1,128)S(1)} %add.159), channel_id=1, source_target_pairs={{0,2},{1,3},{2,0},{3,1},{4,6},{5,7},{6,4},{7,5},{8,10},{9,11},{10,... | collective-permute-start | bytes 1544 | tf_op jit(solution)/shard_map/ppermute | solution.py:56
  124.3 3.6 %collective-permute-start.21 = (f32[1,128]{1,0:T(1,128)S(1)}, f32[1,128]{1,0:T(1,128)S(1)}, u32[]{:S(2)}, u32[]{:S(2)}) collective-permute-start(f32[1,128]{1,0:T(1,128)S(1)} %add.160), channel_id=1, source_target_pairs={{0,4},{4,0},{8,12},{12,8},{16,20},{20,16},{24,28},{28,24},{1,5},{5... | collective-permute-start | bytes 1544 | tf_op jit(solution)/shard_map/ppermute | solution.py:56
  127.9 3.6 %collective-permute-start.22 = (f32[1,128]{1,0:T(1,128)S(1)}, f32[1,128]{1,0:T(1,128)S(1)}, u32[]{:S(2)}, u32[]{:S(2)}) collective-permute-start(f32[1,128]{1,0:T(1,128)S(1)} %add.161), channel_id=1, source_target_pairs={{0,8},{4,12},{8,0},{12,4},{16,24},{20,28},{24,16},{28,20},{1,9},{5... | collective-permute-start | bytes 1544 | tf_op jit(solution)/shard_map/ppermute | solution.py:56
  131.5 4.5 %collective-permute-start.23 = (f32[1,128]{1,0:T(1,128)S(1)}, f32[1,128]{1,0:T(1,128)S(1)}, u32[]{:S(2)}, u32[]{:S(2)}) collective-permute-start(f32[1,128]{1,0:T(1,128)S(1)} %add.162), channel_id=1, source_target_pairs={{0,16},{4,20},{8,24},{12,28},{16,0},{20,4},{24,8},{28,12},{1,17},{... | collective-permute-start | bytes 1544 | tf_op jit(solution)/shard_map/ppermute | solution.py:56
  142.8 1.3 collective-permute-start.24
  144.7 3.6 %collective-permute-start.25 = (f32[1,128]{1,0:T(1,128)S(1)}, f32[1,128]{1,0:T(1,128)S(1)}, u32[]{:S(2)}, u32[]{:S(2)}) collective-permute-start(f32[1,128]{1,0:T(1,128)S(1)} %add.164), channel_id=1, source_target_pairs={{0,2},{1,3},{2,0},{3,1},{4,6},{5,7},{6,4},{7,5},{8,10},{9,11},{10,... | collective-permute-start | bytes 1544 | tf_op jit(solution)/shard_map/ppermute | solution.py:56
  148.3 3.6 %collective-permute-start.26 = (f32[1,128]{1,0:T(1,128)S(1)}, f32[1,128]{1,0:T(1,128)S(1)}, u32[]{:S(2)}, u32[]{:S(2)}) collective-permute-start(f32[1,128]{1,0:T(1,128)S(1)} %add.165), channel_id=1, source_target_pairs={{0,4},{4,0},{8,12},{12,8},{16,20},{20,16},{24,28},{28,24},{1,5},{5... | collective-permute-start | bytes 1544 | tf_op jit(solution)/shard_map/ppermute | solution.py:56
  151.9 3.6 %collective-permute-start.27 = (f32[1,128]{1,0:T(1,128)S(1)}, f32[1,128]{1,0:T(1,128)S(1)}, u32[]{:S(2)}, u32[]{:S(2)}) collective-permute-start(f32[1,128]{1,0:T(1,128)S(1)} %add.166), channel_id=1, source_target_pairs={{0,8},{4,12},{8,0},{12,4},{16,24},{20,28},{24,16},{28,20},{1,9},{5... | collective-permute-start | bytes 1544 | tf_op jit(solution)/shard_map/ppermute | solution.py:56
  155.4 4.5 %collective-permute-start.28 = (f32[1,128]{1,0:T(1,128)S(1)}, f32[1,128]{1,0:T(1,128)S(1)}, u32[]{:S(2)}, u32[]{:S(2)}) collective-permute-start(f32[1,128]{1,0:T(1,128)S(1)} %add.167), channel_id=1, source_target_pairs={{0,16},{4,20},{8,24},{12,28},{16,0},{20,4},{24,8},{28,12},{1,17},{... | collective-permute-start | bytes 1544 | tf_op jit(solution)/shard_map/ppermute | solution.py:56

commit v9 on v8

--- a/solution.py
+++ b/solution.py
@@ -185,13 +185,11 @@
     lax.fori_loop(0, plan.inner_rows, observed_pass, 0)
 
 
-def _start_kernel(plan, first_ref, z_ref, applied_ref, inner_ref, solution_out, residual_out, rr_out):
+def _start_kernel(plan, first_ref, z_ref, applied_ref, inner_ref, residual_out, rr_out):
     step = _ratio(first_ref, 0, first_ref, 1)
 
     def body(r, totals):
-        z = z_ref[r]
-        residual = z - step * applied_ref[r]
-        solution_out[r] = step * z
+        residual = z_ref[r] - step * applied_ref[r]
         residual_out[r] = residual
         inner = (inner_ref[...] > 0.5) & plan.inner_row(r)
         return totals + _row_sum(residual * residual, inner)
@@ -199,13 +197,12 @@
     rr_out[...] = lax.fori_loop(0, plan.slab_rows, body, jnp.zeros((1, z_ref.shape[2]), jnp.float32))
 
 
-def _update_kernel(plan, norm_ref, curvature_ref, solution_ref, direction_ref, residual_ref,
-                   applied_ref, inner_ref, solution_out, residual_out, rr_out):
+def _update_kernel(plan, norm_ref, curvature_ref, residual_ref, applied_ref, inner_ref,
+                   residual_out, rr_out):
     step = _ratio(norm_ref, 0, curvature_ref, 0)
 
     def body(r, totals):
         residual = residual_ref[r] - step * applied_ref[r]
-        solution_out[r] = solution_ref[r] + step * direction_ref[r]
         residual_out[r] = residual
         inner = (inner_ref[...] > 0.5) & plan.inner_row(r)
         return totals + _row_sum(residual * residual, inner)
@@ -228,15 +225,24 @@
                            scratch, applied_out, direction_out)
 
 
-def _final_kernel(plan, norm_ref, curvature_ref, solution_ref, direction_ref, z_ref, stiff_ref,
-                  gain_ref, stiff_obs_ref, observed_ref, weight_ref, diagonal_ref,
-                  grad_kappa_out, grad_weight_out, scratch):
-    step = _ratio(norm_ref, 0, curvature_ref, 0)
+def _final_kernel(plan, *refs):
+    steps = ITERS
+    ratio_refs = refs[: 2 * steps]
+    direction_refs = refs[2 * steps : 3 * steps]
+    (z_ref, stiff_ref, gain_ref, stiff_obs_ref, observed_ref, weight_ref, diagonal_ref,
+     grad_kappa_out, grad_weight_out, scratch) = refs[3 * steps :]
     lanes = z_ref.shape[2]
     probes = lanes // 2
+    step_lens = []
+    for k in range(steps):
+        num_ref, den_ref = ratio_refs[2 * k], ratio_refs[2 * k + 1]
+        step_lens.append(_ratio(num_ref, 0, den_ref, 1 if k == 0 else 0))
 
     def new_solution(r, carry):
-        scratch[r] = solution_ref[r] + step * direction_ref[r]
+        solution = step_lens[0] * direction_refs[0][r]
+        for k in range(1, steps):
+            solution = solution + step_lens[k] * direction_refs[k][r]
+        scratch[r] = solution
         return carry
 
     lax.fori_loop(0, plan.slab_rows, new_solution, 0)
@@ -357,9 +363,9 @@
         scratch=2, smem=(2,),
     )
     first = all_sum(first)
-    solution, residual, rr = _call(
-        _start_kernel, plan, (first, z, applied, inner), (field, field, lane_row)
-    )
+    residual, rr = _call(_start_kernel, plan, (first, z, applied, inner), (field, lane_row))
+    directions = [z]
+    ratios = [first, first]
     direction = z
     norm_now = first
     for iteration in range(1, ITERS):
@@ -371,17 +377,17 @@
         )
         norm_now = norm_next
         curvature = all_sum(pa)
+        directions.append(direction)
+        ratios += [norm_now, curvature]
         if iteration + 1 < ITERS:
-            solution, residual, rr = _call(
-                _update_kernel, plan,
-                (norm_now, curvature, solution, direction, residual, applied, inner),
-                (field, field, lane_row),
+            residual, rr = _call(
+                _update_kernel, plan, (norm_now, curvature, residual, applied, inner),
+                (field, lane_row),
             )
 
     grad_kappa, grad_weight = _call(
         _final_kernel, plan,
-        (norm_now, curvature, solution, direction, z, stiff_probe, gain, stiff_obs, observed,
-         variance_weight, diagonal),
+        (*ratios, *directions, z, stiff_probe, gain, stiff_obs, observed, variance_weight, diagonal),
         (out_plane, out_plane), scratch=1, field=field,
     )
     return (grad_kappa, grad_weight)

time: 167 us -> 166 us (level)
  no operation moved by 1% of the time
where the time goes in v9:
time: 166 us; the launch traced here: 165 us
  waiting for transfers between devices  55.3 us (33%)
  starting transfers between devices  46.1 us (28%)
  Pallas kernels  36.9 us (22%)
  other arithmetic  15.1 us (9%)
  local copies, waits for them, and re-layouts  11 us (7%)
    ppermute x25, waiting for transfers between devices, all_sum(): lax.ppermute(terms, axis, [(i, i ^ hop) for i in range(count)])  50.5 us
    pallas_call x6, Pallas kernels, _call(): pl.pallas_call(lambda *refs: kernel(plan, *refs), out_shape=out_shapes, i...  36.9 us
    ppermute x25, starting transfers between devices, all_sum(): lax.ppermute(terms, axis, [(i, i ^ hop) for i in range(count)])  35.4 us
    ppermute x1, starting transfers between devices, on_device(): lax.ppermute(stacked[:, rows - sent:].reshape(planes * sent, cols), 'rows...  6.2 us
    add x25, other arithmetic, all_sum(): terms + lax.ppermute(terms, axis, [(i, i ^ hop) for i in range(count)])  6.1 us
  transfers between devices with their start and end apart: 29, of which 27 were waited for; matrix products, arithmetic and copies ran while one was open for 5% of the time, Pallas kernels for 0%

profile of v9, /device:TPU:0, one launch (start us, length us, event | category | flops | bytes accessed | tf_op | source)
XLA Modules:
  0.0 165.2 jit_solution(1641256678171867316)
XLA Ops:
  4.9 2.1 %pad_maximum_fusion = f32[67,16,128]{0,2,1:T(8,128)S(1)} fusion(f32[1,16,128]{0,2,1:T(8,128)S(1)} %copy.10, f32[1,16,128]{0,2,1:T(8,128)S(1)} %copy.9, f32[1,16,128]{0,2,1:T(8,128)} %copy.8, f32[64,16,128]{0,2,1:T(8,128)S(1)} %copy.7), kind=kLoop, calls=%fused_computation.13 | loop fusion | flops 411648 | bytes 1097728 | tf_op jit(solution)/shard_map/concatenate | solution.py:312
  12.5 6.2 %collective-permute-start = (f32[536,128]{1,0:T(8,128)}, f32[536,128]{1,0:T(8,128)}, u32[]{:S(2)}, u32[]{:S(2)}) collective-permute-start(f32[536,128]{1,0:T(8,128)} %bitcast.17), channel_id=1, source_target_pairs={{0,4},{4,8},{8,12},{12,16},{16,20},{20,24},{24,28},{1,5},{5,9},{9,... | collective-permute-start | bytes 823304 | tf_op jit(solution)/shard_map/ppermute | solution.py:319
  18.7 3.1 %fusion.12 = f32[16,128,67]{2,1,0:T(8,128)} fusion(f32[1,16,128]{0,2,1:T(8,128)S(1)} %copy.10, f32[1,16,128]{0,2,1:T(8,128)S(1)} %copy.9, f32[1,16,128]{0,2,1:T(8,128)} %copy.8, f32[64,16,128]{0,2,1:T(8,128)S(1)} %copy.7), kind=kLoop, calls=%fused_computation.28 | loop fusion | flops 411648 | bytes 1097728 | tf_op jit(solution)/shard_map/transpose | solution.py:328
  24.6 2.2 %collective-permute-done = f32[536,128]{1,0:T(8,128)} collective-permute-done((f32[536,128]{1,0:T(8,128)}, f32[536,128]{1,0:T(8,128)}, u32[]{:S(2)}, u32[]{:S(2)}) %collective-permute-start) | collective-permute-done | bytes 274464 | tf_op jit(solution)/shard_map/ppermute | solution.py:319
  31.8 2.5 %collective-permute-done.3 = f32[28,6,67]{2,1,0:T(8,128)S(1)} collective-permute-done((f32[28,6,67]{2,1,0:T(8,128)S(1)}, f32[28,6,67]{2,1,0:T(8,128)S(1)}, u32[]{:S(2)}, u32[]{:S(2)}) %collective-permute-start.3) | collective-permute-done | bytes 45056 | tf_op jit(solution)/shard_map/ppermute | solution.py:22
  36.2 11.2 %shard_map.59 = (f32[28,80,128]{2,1,0:T(8,128)}, f32[28,80,128]{2,1,0:T(8,128)}, f32[28,80,128]{2,1,0:T(8,128)}, f32[28,80,128]{2,1,0:T(8,128)}, f32[28,80,128]{...) custom-call(f32[28,144,128]{2,1,0:T(8,128)} %select_maximum_fusion.refs_0_, ...), custom_call_target="tpu_custom_call" | custom-call | flops 11468800 | bytes 13762560 | tf_op jit(solution)/shard_map/pallas_call | solution.py:290
  47.5 3.4 %collective-permute-start.4 = (f32[2,128]{1,0:T(2,128)}, f32[2,128]{1,0:T(2,128)S(1)}, u32[]{:S(2)}, u32[]{:S(2)}) collective-permute-start(f32[2,128]{1,0:T(2,128)} %get-tuple-element.18), channel_id=1, source_target_pairs={{0,1},{1,0},{2,3},{3,2},{4,5},{5,4},{6,7},{7,6},{8,9},{9,8},{10,11... | collective-permute-start | bytes 3080 | tf_op jit(solution)/shard_map/ppermute | solution.py:56
  52.7 3.5 %collective-permute-done.5 = f32[2,128]{1,0:T(2,128)S(1)} collective-permute-done((f32[2,128]{1,0:T(2,128)S(1)}, f32[2,128]{1,0:T(2,128)S(1)}, u32[]{:S(2)}, u32[]{:S(2)}) %collective-permute-start.5) | collective-permute-done | bytes 1056 | tf_op jit(solution)/shard_map/ppermute | solution.py:56
  56.1 2.5 %collective-permute-start.6 = (f32[2,128]{1,0:T(2,128)S(1)}, f32[2,128]{1,0:T(2,128)S(1)}, u32[]{:S(2)}, u32[]{:S(2)}) collective-permute-start(f32[2,128]{1,0:T(2,128)S(1)} %add.145), channel_id=1, source_target_pairs={{0,4},{4,0},{8,12},{12,8},{16,20},{20,16},{24,28},{28,24},{1,5},{5... | collective-permute-start | bytes 3080 | tf_op jit(solution)/shard_map/ppermute | solution.py:56
  61.8 2.0 %collective-permute-done.7 = f32[2,128]{1,0:T(2,128)S(1)} collective-permute-done((f32[2,128]{1,0:T(2,128)S(1)}, f32[2,128]{1,0:T(2,128)S(1)}, u32[]{:S(2)}, u32[]{:S(2)}) %collective-permute-start.7) | collective-permute-done | bytes 1056 | tf_op jit(solution)/shard_map/ppermute | solution.py:56
  63.8 2.6 %collective-permute-start.8 = (f32[2,128]{1,0:T(2,128)S(1)}, f32[2,128]{1,0:T(2,128)S(1)}, u32[]{:S(2)}, u32[]{:S(2)}) collective-permute-start(f32[2,128]{1,0:T(2,128)S(1)} %add.147), channel_id=1, source_target_pairs={{0,16},{4,20},{8,24},{12,28},{16,0},{20,4},{24,8},{28,12},{1,17},{... | collective-permute-start | bytes 3080 | tf_op jit(solution)/shard_map/ppermute | solution.py:56
  68.8 3.4 %shard_map.60 = (f32[28,80,128]{2,1,0:T(8,128)}, f32[1,128]{1,0:T(1,128)}) custom-call(f32[2,128]{1,0:T(2,128)} %add.148.refs_0_.refs_1_, f32[28,80,128]{2,1,0:T(8,128)} %get-tuple-element.19.refs_1_.refs_3_.refs_6_.refs_9_, f32[28,80,128]{2,1,0:T(8,128)} %get-tuple-element.20.refs_2_, f32[80,128]{1,0:T(8,128)} %add_convert_fusion.1.refs_3_.refs_8_.refs_4_), custom_call_target="tpu_custom_call" | custom-call | flops 11468800 | bytes 6881280 | tf_op jit(solution)/shard_map/pallas_call | solution.py:290
  74.3 3.4 %collective-permute-done.10 = f32[1,128]{1,0:T(1,128)S(1)} collective-permute-done((f32[1,128]{1,0:T(1,128)S(1)}, f32[1,128]{1,0:T(1,128)S(1)}, u32[]{:S(2)}, u32[]{:S(2)}) %collective-permute-start.10) | collective-permute-done | bytes 544 | tf_op jit(solution)/shard_map/ppermute | solution.py:56
  77.7 2.0 %collective-permute-start.11 = (f32[1,128]{1,0:T(1,128)S(1)}, f32[1,128]{1,0:T(1,128)S(1)}, u32[]{:S(2)}, u32[]{:S(2)}) collective-permute-start(f32[1,128]{1,0:T(1,128)S(1)} %add.150), channel_id=1, source_target_pairs={{0,4},{4,0},{8,12},{12,8},{16,20},{20,16},{24,28},{28,24},{1,5},{5... | collective-permute-start | bytes 1544 | tf_op jit(solution)/shard_map/ppermute | solution.py:56
  82.9 2.0 %collective-permute-done.12 = f32[1,128]{1,0:T(1,128)S(1)} collective-permute-done((f32[1,128]{1,0:T(1,128)S(1)}, f32[1,128]{1,0:T(1,128)S(1)}, u32[]{:S(2)}, u32[]{:S(2)}) %collective-permute-start.12) | collective-permute-done | bytes 544 | tf_op jit(solution)/shard_map/ppermute | solution.py:56
  84.9 2.6 %collective-permute-start.13 = (f32[1,128]{1,0:T(1,128)S(1)}, f32[1,128]{1,0:T(1,128)S(1)}, u32[]{:S(2)}, u32[]{:S(2)}) collective-permute-start(f32[1,128]{1,0:T(1,128)S(1)} %add.152), channel_id=1, source_target_pairs={{0,16},{4,20},{8,24},{12,28},{16,0},{20,4},{24,8},{28,12},{1,17},{... | collective-permute-start | bytes 1544 | tf_op jit(solution)/shard_map/ppermute | solution.py:56
  89.9 6.2 %shard_map.61 = (f32[28,80,128]{2,1,0:T(8,128)}, f32[28,80,128]{2,1,0:T(8,128)}, f32[1,128]{1,0:T(1,128)}) custom-call(f32[1,128]{1,0:T(1,128)} %add.153.refs_0_.refs_1_.refs_2_, f32[2,128]{1,0:T(2,128)} %add.148.refs_0_.refs_1_, f32[28,80,128]{2,1,0:T(8,128)} %get-tuple-element.22.refs_2_, f32[28,80,128]{2,1,0:T(8,128)} %get-tuple-element.19.refs_1_.refs_3_.refs_6_.refs_9_, ...), custom_call_target="tpu_custom_call" | custom-call | flops 11468800 | bytes 13762560 | tf_op jit(solution)/shard_map/pallas_call | solution.py:290
  98.2 3.4 %collective-permute-done.15 = f32[1,128]{1,0:T(1,128)S(1)} collective-permute-done((f32[1,128]{1,0:T(1,128)S(1)}, f32[1,128]{1,0:T(1,128)S(1)}, u32[]{:S(2)}, u32[]{:S(2)}) %collective-permute-start.15) | collective-permute-done | bytes 544 | tf_op jit(solution)/shard_map/ppermute | solution.py:56
  101.7 2.0 %collective-permute-start.16 = (f32[1,128]{1,0:T(1,128)S(1)}, f32[1,128]{1,0:T(1,128)S(1)}, u32[]{:S(2)}, u32[]{:S(2)}) collective-permute-start(f32[1,128]{1,0:T(1,128)S(1)} %add.155), channel_id=1, source_target_pairs={{0,4},{4,0},{8,12},{12,8},{16,20},{20,16},{24,28},{28,24},{1,5},{5... | collective-permute-start | bytes 1544 | tf_op jit(solution)/shard_map/ppermute | solution.py:56
  106.8 2.0 %collective-permute-done.17 = f32[1,128]{1,0:T(1,128)S(1)} collective-permute-done((f32[1,128]{1,0:T(1,128)S(1)}, f32[1,128]{1,0:T(1,128)S(1)}, u32[]{:S(2)}, u32[]{:S(2)}) %collective-permute-start.17) | collective-permute-done | bytes 544 | tf_op jit(solution)/shard_map/ppermute | solution.py:56
  108.8 2.6 %collective-permute-start.18 = (f32[1,128]{1,0:T(1,128)S(1)}, f32[1,128]{1,0:T(1,128)S(1)}, u32[]{:S(2)}, u32[]{:S(2)}) collective-permute-start(f32[1,128]{1,0:T(1,128)S(1)} %add.157), channel_id=1, source_target_pairs={{0,16},{4,20},{8,24},{12,28},{16,0},{20,4},{24,8},{28,12},{1,17},{... | collective-permute-start | bytes 1544 | tf_op jit(solution)/shard_map/ppermute | solution.py:56
  113.8 3.5 %shard_map.62 = (f32[28,80,128]{2,1,0:T(8,128)}, f32[1,128]{1,0:T(1,128)}) custom-call(f32[1,128]{1,0:T(1,128)} %add.153.refs_0_.refs_1_.refs_2_, f32[1,128]{1,0:T(1,128)} %add.158.refs_1_.refs_3_, f32[28,80,128]{2,1,0:T(8,128)} %get-tuple-element.22.refs_2_, f32[28,80,128]{2,1,0:T(8,128)} %get-tuple-element.26.refs_3_, ...), custom_call_target="tpu_custom_call" | custom-call | flops 11468800 | bytes 8028160 | tf_op jit(solution)/shard_map/pallas_call | solution.py:290
  119.4 3.4 %collective-permute-done.20 = f32[1,128]{1,0:T(1,128)S(1)} collective-permute-done((f32[1,128]{1,0:T(1,128)S(1)}, f32[1,128]{1,0:T(1,128)S(1)}, u32[]{:S(2)}, u32[]{:S(2)}) %collective-permute-start.20) | collective-permute-done | bytes 544 | tf_op jit(solution)/shard_map/ppermute | solution.py:56
  122.8 2.0 %collective-permute-start.21 = (f32[1,128]{1,0:T(1,128)S(1)}, f32[1,128]{1,0:T(1,128)S(1)}, u32[]{:S(2)}, u32[]{:S(2)}) collective-permute-start(f32[1,128]{1,0:T(1,128)S(1)} %add.160), channel_id=1, source_target_pairs={{0,4},{4,0},{8,12},{12,8},{16,20},{20,16},{24,28},{28,24},{1,5},{5... | collective-permute-start | bytes 1544 | tf_op jit(solution)/shard_map/ppermute | solution.py:56
  128.0 2.0 %collective-permute-done.22 = f32[1,128]{1,0:T(1,128)S(1)} collective-permute-done((f32[1,128]{1,0:T(1,128)S(1)}, f32[1,128]{1,0:T(1,128)S(1)}, u32[]{:S(2)}, u32[]{:S(2)}) %collective-permute-start.22) | collective-permute-done | bytes 544 | tf_op jit(solution)/shard_map/ppermute | solution.py:56
  130.0 2.6 %collective-permute-start.23 = (f32[1,128]{1,0:T(1,128)S(1)}, f32[1,128]{1,0:T(1,128)S(1)}, u32[]{:S(2)}, u32[]{:S(2)}) collective-permute-start(f32[1,128]{1,0:T(1,128)S(1)} %add.162), channel_id=1, source_target_pairs={{0,16},{4,20},{8,24},{12,28},{16,0},{20,4},{24,8},{28,12},{1,17},{... | collective-permute-start | bytes 1544 | tf_op jit(solution)/shard_map/ppermute | solution.py:56
  135.0 6.2 %shard_map.63 = (f32[28,80,128]{2,1,0:T(8,128)}, f32[28,80,128]{2,1,0:T(8,128)}, f32[1,128]{1,0:T(1,128)}) custom-call(f32[1,128]{1,0:T(1,128)} %add.163.refs_0_.refs_4_, f32[1,128]{1,0:T(1,128)} %add.153.refs_0_.refs_1_.refs_2_, f32[28,80,128]{2,1,0:T(8,128)} %get-tuple-element.28.refs_2_, f32[28,80,128]{2,1,0:T(8,128)} %get-tuple-element.29.refs_3_.refs_7_, ...), custom_call_target="tpu_custom_call" | custom-call | flops 11468800 | bytes 13762560 | tf_op jit(solution)/shard_map/pallas_call | solution.py:290
  143.3 3.4 %collective-permute-done.25 = f32[1,128]{1,0:T(1,128)S(1)} collective-permute-done((f32[1,128]{1,0:T(1,128)S(1)}, f32[1,128]{1,0:T(1,128)S(1)}, u32[]{:S(2)}, u32[]{:S(2)}) %collective-permute-start.25) | collective-permute-done | bytes 544 | tf_op jit(solution)/shard_map/ppermute | solution.py:56
  146.7 2.0 %collective-permute-start.26 = (f32[1,128]{1,0:T(1,128)S(1)}, f32[1,128]{1,0:T(1,128)S(1)}, u32[]{:S(2)}, u32[]{:S(2)}) collective-permute-start(f32[1,128]{1,0:T(1,128)S(1)} %add.165), channel_id=1, source_target_pairs={{0,4},{4,0},{8,12},{12,8},{16,20},{20,16},{24,28},{28,24},{1,5},{5... | collective-permute-start | bytes 1544 | tf_op jit(solution)/shard_map/ppermute | solution.py:56
  151.9 2.0 %collective-permute-done.27 = f32[1,128]{1,0:T(1,128)S(1)} collective-permute-done((f32[1,128]{1,0:T(1,128)S(1)}, f32[1,128]{1,0:T(1,128)S(1)}, u32[]{:S(2)}, u32[]{:S(2)}) %collective-permute-start.27) | collective-permute-done | bytes 544 | tf_op jit(solution)/shard_map/ppermute | solution.py:56
  153.9 2.6 %collective-permute-start.28 = (f32[1,128]{1,0:T(1,128)S(1)}, f32[1,128]{1,0:T(1,128)S(1)}, u32[]{:S(2)}, u32[]{:S(2)}) collective-permute-start(f32[1,128]{1,0:T(1,128)S(1)} %add.167), channel_id=1, source_target_pairs={{0,16},{4,20},{8,24},{12,28},{16,0},{20,4},{24,8},{28,12},{1,17},{... | collective-permute-start | bytes 1544 | tf_op jit(solution)/shard_map/ppermute | solution.py:56
  158.9 6.3 %shard_map.64 = (f32[16,128]{1,0:T(8,128)}, f32[16,128]{1,0:T(8,128)}) custom-call(f32[2,128]{1,0:T(2,128)} %add.148.refs_0_.refs_1_, f32[2,128]{1,0:T(2,128)} %add.148.refs_0_.refs_1_, f32[1,128]{1,0:T(1,128)} %add.153.refs_0_.refs_1_.refs_2_, f32[1,128]{1,0:T(1,128)} %add.158.refs_1_.refs_3_, f32[1,128]{1,0:T(1,128)} %add.163.refs_0_.refs_4_, ...), custom_call_target="tpu_custom_call" | custom-call | flops 11468800 | bytes 20643840 | tf_op jit(solution)/shard_map/pallas_call | solution.py:290
  (87 shorter events, 57.3 us)
Async XLA Ops:
  0.6 2.5 %copy-start.1 = (f32[16,128]{1,0:T(8,128)S(1)}, f32[16,128]{1,0:T(8,128)}, u32[]{:S(2)}) copy-start(f32[16,128]{1,0:T(8,128)} %refs_14_.1) | copy-start | bytes 24580
  0.6 2.9 %copy-start.2 = (f32[16,128]{1,0:T(8,128)S(1)}, f32[16,128]{1,0:T(8,128)}, u32[]{:S(2)}) copy-start(f32[16,128]{1,0:T(8,128)} %refs_13_.1) | copy-start | bytes 24580
  9.3 14.2 %collective-permute-start.1 = (f32[536,128]{1,0:T(8,128)S(1)}, f32[536,128]{1,0:T(8,128)}, u32[]{:S(2)}, u32[]{:S(2)}) collective-permute-start(f32[536,128]{1,0:T(8,128)S(1)} %bitcast.16), channel_id=1, source_target_pairs={{4,0},{8,4},{12,8},{16,12},{20,16},{24,20},{28,24},{5,1},{9,5},{13... | collective-permute-start | bytes 823304 | tf_op jit(solution)/shard_map/ppermute | solution.py:323
  12.5 14.3 %collective-permute-start = (f32[536,128]{1,0:T(8,128)}, f32[536,128]{1,0:T(8,128)}, u32[]{:S(2)}, u32[]{:S(2)}) collective-permute-start(f32[536,128]{1,0:T(8,128)} %bitcast.17), channel_id=1, source_target_pairs={{0,4},{4,8},{8,12},{12,16},{16,20},{20,24},{24,28},{1,5},{5,9},{9,... | collective-permute-start | bytes 823304 | tf_op jit(solution)/shard_map/ppermute | solution.py:319
  21.8 6.2 %copy-start = (f32[16,128,67]{2,1,0:T(8,128)S(1)}, f32[16,128,67]{2,1,0:T(8,128)}, u32[]{:S(2)}) copy-start(f32[16,128,67]{2,1,0:T(8,128)} %fusion.12) | copy-start | bytes 1646596
  28.1 3.8 %collective-permute-start.2 = (f32[28,6,67]{2,1,0:T(8,128)S(1)}, f32[28,6,67]{2,1,0:T(8,128)S(1)}, u32[]{:S(2)}, u32[]{:S(2)}) collective-permute-start(f32[28,6,67]{2,1,0:T(8,128)S(1)} %get-tuple-element.34), channel_id=1, source_target_pairs={{0,1},{1,2},{2,3},{4,5},{5,6},{6,7},{8,9},{9,10},{10,11},{12,13},{... | collective-permute-start | bytes 135080 | tf_op jit(solution)/shard_map/ppermute | solution.py:20
  30.0 4.3 %collective-permute-start.3 = (f32[28,6,67]{2,1,0:T(8,128)S(1)}, f32[28,6,67]{2,1,0:T(8,128)S(1)}, u32[]{:S(2)}, u32[]{:S(2)}) collective-permute-start(f32[28,6,67]{2,1,0:T(8,128)S(1)} %get-tuple-element.35), channel_id=1, source_target_pairs={{1,0},{2,1},{3,2},{5,4},{6,5},{7,6},{9,8},{10,9},{11,10},{13,12},{... | collective-permute-start | bytes 135080 | tf_op jit(solution)/shard_map/ppermute | solution.py:22
  47.5 4.4 %collective-permute-start.4 = (f32[2,128]{1,0:T(2,128)}, f32[2,128]{1,0:T(2,128)S(1)}, u32[]{:S(2)}, u32[]{:S(2)}) collective-permute-start(f32[2,128]{1,0:T(2,128)} %get-tuple-element.18), channel_id=1, source_target_pairs={{0,1},{1,0},{2,3},{3,2},{4,5},{5,4},{6,7},{7,6},{8,9},{9,8},{10,11... | collective-permute-start | bytes 3080 | tf_op jit(solution)/shard_map/ppermute | solution.py:56
  52.6 3.6 %collective-permute-start.5 = (f32[2,128]{1,0:T(2,128)S(1)}, f32[2,128]{1,0:T(2,128)S(1)}, u32[]{:S(2)}, u32[]{:S(2)}) collective-permute-start(f32[2,128]{1,0:T(2,128)S(1)} %add.144), channel_id=1, source_target_pairs={{0,2},{1,3},{2,0},{3,1},{4,6},{5,7},{6,4},{7,5},{8,10},{9,11},{10,... | collective-permute-start | bytes 3080 | tf_op jit(solution)/shard_map/ppermute | solution.py:56
  56.1 4.0 %collective-permute-start.6 = (f32[2,128]{1,0:T(2,128)S(1)}, f32[2,128]{1,0:T(2,128)S(1)}, u32[]{:S(2)}, u32[]{:S(2)}) collective-permute-start(f32[2,128]{1,0:T(2,128)S(1)} %add.145), channel_id=1, source_target_pairs={{0,4},{4,0},{8,12},{12,8},{16,20},{20,16},{24,28},{28,24},{1,5},{5... | collective-permute-start | bytes 3080 | tf_op jit(solution)/shard_map/ppermute | solution.py:56
  60.2 3.6 %collective-permute-start.7 = (f32[2,128]{1,0:T(2,128)S(1)}, f32[2,128]{1,0:T(2,128)S(1)}, u32[]{:S(2)}, u32[]{:S(2)}) collective-permute-start(f32[2,128]{1,0:T(2,128)S(1)} %add.146), channel_id=1, source_target_pairs={{0,8},{4,12},{8,0},{12,4},{16,24},{20,28},{24,16},{28,20},{1,9},{5... | collective-permute-start | bytes 3080 | tf_op jit(solution)/shard_map/ppermute | solution.py:56
  63.8 4.5 %collective-permute-start.8 = (f32[2,128]{1,0:T(2,128)S(1)}, f32[2,128]{1,0:T(2,128)S(1)}, u32[]{:S(2)}, u32[]{:S(2)}) collective-permute-start(f32[2,128]{1,0:T(2,128)S(1)} %add.147), channel_id=1, source_target_pairs={{0,16},{4,20},{8,24},{12,28},{16,0},{20,4},{24,8},{28,12},{1,17},{... | collective-permute-start | bytes 3080 | tf_op jit(solution)/shard_map/ppermute | solution.py:56
  72.2 1.3 collective-permute-start.9
  74.1 3.6 %collective-permute-start.10 = (f32[1,128]{1,0:T(1,128)S(1)}, f32[1,128]{1,0:T(1,128)S(1)}, u32[]{:S(2)}, u32[]{:S(2)}) collective-permute-start(f32[1,128]{1,0:T(1,128)S(1)} %add.149), channel_id=1, source_target_pairs={{0,2},{1,3},{2,0},{3,1},{4,6},{5,7},{6,4},{7,5},{8,10},{9,11},{10,... | collective-permute-start | bytes 1544 | tf_op jit(solution)/shard_map/ppermute | solution.py:56
  77.7 3.6 %collective-permute-start.11 = (f32[1,128]{1,0:T(1,128)S(1)}, f32[1,128]{1,0:T(1,128)S(1)}, u32[]{:S(2)}, u32[]{:S(2)}) collective-permute-start(f32[1,128]{1,0:T(1,128)S(1)} %add.150), channel_id=1, source_target_pairs={{0,4},{4,0},{8,12},{12,8},{16,20},{20,16},{24,28},{28,24},{1,5},{5... | collective-permute-start | bytes 1544 | tf_op jit(solution)/shard_map/ppermute | solution.py:56
  81.3 3.6 %collective-permute-start.12 = (f32[1,128]{1,0:T(1,128)S(1)}, f32[1,128]{1,0:T(1,128)S(1)}, u32[]{:S(2)}, u32[]{:S(2)}) collective-permute-start(f32[1,128]{1,0:T(1,128)S(1)} %add.151), channel_id=1, source_target_pairs={{0,8},{4,12},{8,0},{12,4},{16,24},{20,28},{24,16},{28,20},{1,9},{5... | collective-permute-start | bytes 1544 | tf_op jit(solution)/shard_map/ppermute | solution.py:56
  84.9 4.5 %collective-permute-start.13 = (f32[1,128]{1,0:T(1,128)S(1)}, f32[1,128]{1,0:T(1,128)S(1)}, u32[]{:S(2)}, u32[]{:S(2)}) collective-permute-start(f32[1,128]{1,0:T(1,128)S(1)} %add.152), channel_id=1, source_target_pairs={{0,16},{4,20},{8,24},{12,28},{16,0},{20,4},{24,8},{28,12},{1,17},{... | collective-permute-start | bytes 1544 | tf_op jit(solution)/shard_map/ppermute | solution.py:56
  96.2 1.3 collective-permute-start.14
  98.1 3.6 %collective-permute-start.15 = (f32[1,128]{1,0:T(1,128)S(1)}, f32[1,128]{1,0:T(1,128)S(1)}, u32[]{:S(2)}, u32[]{:S(2)}) collective-permute-start(f32[1,128]{1,0:T(1,128)S(1)} %add.154), channel_id=1, source_target_pairs={{0,2},{1,3},{2,0},{3,1},{4,6},{5,7},{6,4},{7,5},{8,10},{9,11},{10,... | collective-permute-start | bytes 1544 | tf_op jit(solution)/shard_map/ppermute | solution.py:56
  101.7 3.6 %collective-permute-start.16 = (f32[1,128]{1,0:T(1,128)S(1)}, f32[1,128]{1,0:T(1,128)S(1)}, u32[]{:S(2)}, u32[]{:S(2)}) collective-permute-start(f32[1,128]{1,0:T(1,128)S(1)} %add.155), channel_id=1, source_target_pairs={{0,4},{4,0},{8,12},{12,8},{16,20},{20,16},{24,28},{28,24},{1,5},{5... | collective-permute-start | bytes 1544 | tf_op jit(solution)/shard_map/ppermute | solution.py:56
  105.3 3.6 %collective-permute-start.17 = (f32[1,128]{1,0:T(1,128)S(1)}, f32[1,128]{1,0:T(1,128)S(1)}, u32[]{:S(2)}, u32[]{:S(2)}) collective-permute-start(f32[1,128]{1,0:T(1,128)S(1)} %add.156), channel_id=1, source_target_pairs={{0,8},{4,12},{8,0},{12,4},{16,24},{20,28},{24,16},{28,20},{1,9},{5... | collective-permute-start | bytes 1544 | tf_op jit(solution)/shard_map/ppermute | solution.py:56
  108.8 4.5 %collective-permute-start.18 = (f32[1,128]{1,0:T(1,128)S(1)}, f32[1,128]{1,0:T(1,128)S(1)}, u32[]{:S(2)}, u32[]{:S(2)}) collective-permute-start(f32[1,128]{1,0:T(1,128)S(1)} %add.157), channel_id=1, source_target_pairs={{0,16},{4,20},{8,24},{12,28},{16,0},{20,4},{24,8},{28,12},{1,17},{... | collective-permute-start | bytes 1544 | tf_op jit(solution)/shard_map/ppermute | solution.py:56
  117.3 1.3 collective-permute-start.19
  119.3 3.6 %collective-permute-start.20 = (f32[1,128]{1,0:T(1,128)S(1)}, f32[1,128]{1,0:T(1,128)S(1)}, u32[]{:S(2)}, u32[]{:S(2)}) collective-permute-start(f32[1,128]{1,0:T(1,128)S(1)} %add.159), channel_id=1, source_target_pairs={{0,2},{1,3},{2,0},{3,1},{4,6},{5,7},{6,4},{7,5},{8,10},{9,11},{10,... | collective-permute-start | bytes 1544 | tf_op jit(solution)/shard_map/ppermute | solution.py:56
  122.8 3.6 %collective-permute-start.21 = (f32[1,128]{1,0:T(1,128)S(1)}, f32[1,128]{1,0:T(1,128)S(1)}, u32[]{:S(2)}, u32[]{:S(2)}) collective-permute-start(f32[1,128]{1,0:T(1,128)S(1)} %add.160), channel_id=1, source_target_pairs={{0,4},{4,0},{8,12},{12,8},{16,20},{20,16},{24,28},{28,24},{1,5},{5... | collective-permute-start | bytes 1544 | tf_op jit(solution)/shard_map/ppermute | solution.py:56
  126.4 3.6 %collective-permute-start.22 = (f32[1,128]{1,0:T(1,128)S(1)}, f32[1,128]{1,0:T(1,128)S(1)}, u32[]{:S(2)}, u32[]{:S(2)}) collective-permute-start(f32[1,128]{1,0:T(1,128)S(1)} %add.161), channel_id=1, source_target_pairs={{0,8},{4,12},{8,0},{12,4},{16,24},{20,28},{24,16},{28,20},{1,9},{5... | collective-permute-start | bytes 1544 | tf_op jit(solution)/shard_map/ppermute | solution.py:56
  130.0 4.5 %collective-permute-start.23 = (f32[1,128]{1,0:T(1,128)S(1)}, f32[1,128]{1,0:T(1,128)S(1)}, u32[]{:S(2)}, u32[]{:S(2)}) collective-permute-start(f32[1,128]{1,0:T(1,128)S(1)} %add.162), channel_id=1, source_target_pairs={{0,16},{4,20},{8,24},{12,28},{16,0},{20,4},{24,8},{28,12},{1,17},{... | collective-permute-start | bytes 1544 | tf_op jit(solution)/shard_map/ppermute | solution.py:56
  141.2 1.3 collective-permute-start.24
  143.2 3.6 %collective-permute-start.25 = (f32[1,128]{1,0:T(1,128)S(1)}, f32[1,128]{1,0:T(1,128)S(1)}, u32[]{:S(2)}, u32[]{:S(2)}) collective-permute-start(f32[1,128]{1,0:T(1,128)S(1)} %add.164), channel_id=1, source_target_pairs={{0,2},{1,3},{2,0},{3,1},{4,6},{5,7},{6,4},{7,5},{8,10},{9,11},{10,... | collective-permute-start | bytes 1544 | tf_op jit(solution)/shard_map/ppermute | solution.py:56
  146.7 3.6 %collective-permute-start.26 = (f32[1,128]{1,0:T(1,128)S(1)}, f32[1,128]{1,0:T(1,128)S(1)}, u32[]{:S(2)}, u32[]{:S(2)}) collective-permute-start(f32[1,128]{1,0:T(1,128)S(1)} %add.165), channel_id=1, source_target_pairs={{0,4},{4,0},{8,12},{12,8},{16,20},{20,16},{24,28},{28,24},{1,5},{5... | collective-permute-start | bytes 1544 | tf_op jit(solution)/shard_map/ppermute | solution.py:56
  150.3 3.6 %collective-permute-start.27 = (f32[1,128]{1,0:T(1,128)S(1)}, f32[1,128]{1,0:T(1,128)S(1)}, u32[]{:S(2)}, u32[]{:S(2)}) collective-permute-start(f32[1,128]{1,0:T(1,128)S(1)} %add.166), channel_id=1, source_target_pairs={{0,8},{4,12},{8,0},{12,4},{16,24},{20,28},{24,16},{28,20},{1,9},{5... | collective-permute-start | bytes 1544 | tf_op jit(solution)/shard_map/ppermute | solution.py:56
  153.9 4.5 %collective-permute-start.28 = (f32[1,128]{1,0:T(1,128)S(1)}, f32[1,128]{1,0:T(1,128)S(1)}, u32[]{:S(2)}, u32[]{:S(2)}) collective-permute-start(f32[1,128]{1,0:T(1,128)S(1)} %add.167), channel_id=1, source_target_pairs={{0,16},{4,20},{8,24},{12,28},{16,0},{20,4},{24,8},{28,12},{1,17},{... | collective-permute-start | bytes 1544 | tf_op jit(solution)/shard_map/ppermute | solution.py:56

commit v10 on v9

--- a/solution.py
+++ b/solution.py
@@ -316,13 +316,17 @@
     sent = -(-HALO // 8) * 8
     assert sent <= rows
     planes = stacked.shape[0]
+    fields = (probes, observed[None], kappa_sq[None], variance_weight[None])
+
+    def edge_rows(start):
+        rows_of = [lax.slice_in_dim(f, start, start + sent, axis=1) for f in fields]
+        return jnp.concatenate(rows_of, axis=0).reshape(planes * sent, cols)
+
     below = lax.ppermute(
-        stacked[:, rows - sent :].reshape(planes * sent, cols), "rows",
-        [(i, i + 1) for i in range(count - 1)],
+        edge_rows(rows - sent), "rows", [(i, i + 1) for i in range(count - 1)]
     ).reshape(planes, sent, cols)[:, sent - HALO :]
     above = lax.ppermute(
-        stacked[:, :sent].reshape(planes * sent, cols), "rows",
-        [(i + 1, i) for i in range(count - 1)],
+        edge_rows(0), "rows", [(i + 1, i) for i in range(count - 1)]
     ).reshape(planes, sent, cols)[:, :HALO]
     ext = jnp.concatenate(
         [jnp.transpose(piece, (1, 2, 0)) for piece in (below, stacked, above)], axis=0

time: 166 us -> 160 us (0.964)
  waiting for transfers between devices: 55.3 us -> 52 us
  local copies, waits for them, and re-layouts: 11 us -> 8.57 us
  starting transfers between devices: 46.1 us -> 48.2 us
  other arithmetic: 15.1 us -> 13.1 us
    ppermute x25, starting transfers between devices: 35.4 us -> 37.5 us  [all_sum(): lax.ppermute(terms, axis, [(i, i ^ hop) for i in range(count)])]
    concatenate x1 -> x0, other arithmetic: 2.1 us -> none  [on_device(): jnp.concatenate([probes, observed[None], kappa_sq[None], variance_weight[...]
    slice x4, local copies, waits for them, and re-layouts: 5.24 us -> 3.57 us  [the longest x3 2.59 us: edge_rows(): rows_of = [lax.slice_in_dim(f, start, start + sent, axis=1) for f in fields]]
    ppermute x25, waiting for transfers between devices: 50.5 us -> 48.9 us  [all_sum(): lax.ppermute(terms, axis, [(i, i ^ hop) for i in range(count)])]
  transfers between devices with their start and end apart: 29 -> 29, of which waited for: 27 -> 27; matrix products, arithmetic and copies ran while one was open for 5% -> 6% of each run, Pallas kernels for 0% -> 0%
where the time goes in v10:
time: 160 us
  waiting for transfers between devices  52 us (32%)
  starting transfers between devices  48.2 us (30%)
  Pallas kernels  36.9 us (23%)
  other arithmetic  13.1 us (8%)
  local copies, waits for them, and re-layouts  8.57 us (5%)
    ppermute x25, waiting for transfers between devices, all_sum(): lax.ppermute(terms, axis, [(i, i ^ hop) for i in range(count)])  48.9 us
    ppermute x25, starting transfers between devices, all_sum(): lax.ppermute(terms, axis, [(i, i ^ hop) for i in range(count)])  37.5 us
    pallas_call x6, Pallas kernels, _call(): pl.pallas_call(lambda *refs: kernel(plan, *refs), out_shape=out_shapes, i...  36.9 us
    ppermute x1, starting transfers between devices, on_device(): lax.ppermute(edge_rows(rows - sent), 'rows', [(i, i + 1) for i in range(c...  6.2 us
    add x25, other arithmetic, all_sum(): terms + lax.ppermute(terms, axis, [(i, i ^ hop) for i in range(count)])  6.1 us
  transfers between devices with their start and end apart: 29, of which 27 were waited for; matrix products, arithmetic and copies ran while one was open for 6% of the time, Pallas kernels for 0%

profile of v10, /device:TPU:0, one launch (start us, length us, event | category | flops | bytes accessed | tf_op | source)
XLA Modules:
  0.0 159.6 jit_solution(7808583741942655652)
XLA Ops:
  5.3 6.2 %collective-permute-start = (f32[536,128]{1,0:T(8,128)}, f32[536,128]{1,0:T(8,128)}, u32[]{:S(2)}, u32[]{:S(2)}) collective-permute-start(f32[536,128]{1,0:T(8,128)} %maximum_bitcast_fusion.1), channel_id=1, source_target_pairs={{0,4},{4,8},{8,12},{12,16},{16,20},{20,24},{24,28},{1,5},{5,9},{9,... | collective-permute-start | bytes 823304 | tf_op jit(solution)/shard_map/ppermute | solution.py:325
  15.8 2.4 %maximum_bitcast_fusion = f32[16,128,67]{2,1,0:T(8,128)S(1)} fusion(f32[1,16,128]{0,2,1:T(8,128)} %copy.17, f32[1,16,128]{0,2,1:T(8,128)S(1)} %copy.16, f32[1,16,128]{0,2,1:T(8,128)} %copy.15, f32[64,16,128]{0,2,1:T(8,128)S(1)} %copy.14), kind=kLoop, calls=%fused_computation.13 | loop fusion | flops 411648 | bytes 1097728 | tf_op jit(solution)/shard_map/transpose | solution.py:332
  22.1 1.9 %collective-permute-start.2 = (f32[28,6,67]{2,1,0:T(8,128)S(1)}, f32[28,6,67]{2,1,0:T(8,128)S(1)}, u32[]{:S(2)}, u32[]{:S(2)}) collective-permute-start(f32[28,6,67]{2,1,0:T(8,128)S(1)} %get-tuple-element.34), channel_id=1, source_target_pairs={{0,1},{1,2},{2,3},{4,5},{5,6},{6,7},{8,9},{9,10},{10,11},{12,13},{... | collective-permute-start | bytes 135080 | tf_op jit(solution)/shard_map/ppermute | solution.py:20
  25.8 2.5 %collective-permute-done.3 = f32[28,6,67]{2,1,0:T(8,128)S(1)} collective-permute-done((f32[28,6,67]{2,1,0:T(8,128)S(1)}, f32[28,6,67]{2,1,0:T(8,128)S(1)}, u32[]{:S(2)}, u32[]{:S(2)}) %collective-permute-start.3) | collective-permute-done | bytes 45056 | tf_op jit(solution)/shard_map/ppermute | solution.py:22
  28.3 1.9 %select_maximum_fusion.refs_0_ = f32[28,144,128]{2,1,0:T(8,128)} fusion(f32[28,6,67]{2,1,0:T(8,128)S(1)} %collective-permute-done.3, f32[28,6,67]{2,1,0:T(8,128)S(1)} %collective-permute-done.2, f32[6,128,67]{2,1,0:T(8,128)S(1)} %bitcast.15, f32[16,128,67]{2,1,0:T(8,128)S(1)} %maximum_bitcast_fusion, f32[6,128,67]{2,1,0:T(8,128)S(1)} %bitcast.17), kind=kLoop, calls=%fused_computation | loop fusion | flops 8773632 | bytes 3114944 | tf_op jit(solution)/shard_map/concatenate | solution.py:18
  30.2 11.3 %shard_map.59 = (f32[28,80,128]{2,1,0:T(8,128)}, f32[28,80,128]{2,1,0:T(8,128)}, f32[28,80,128]{2,1,0:T(8,128)}, f32[28,80,128]{2,1,0:T(8,128)}, f32[28,80,128]{...) custom-call(f32[28,144,128]{2,1,0:T(8,128)} %select_maximum_fusion.refs_0_, ...), custom_call_target="tpu_custom_call" | custom-call | flops 11468800 | bytes 13762560 | tf_op jit(solution)/shard_map/pallas_call | solution.py:290
  41.5 3.4 %collective-permute-start.4 = (f32[2,128]{1,0:T(2,128)}, f32[2,128]{1,0:T(2,128)S(1)}, u32[]{:S(2)}, u32[]{:S(2)}) collective-permute-start(f32[2,128]{1,0:T(2,128)} %get-tuple-element.18), channel_id=1, source_target_pairs={{0,1},{1,0},{2,3},{3,2},{4,5},{5,4},{6,7},{7,6},{8,9},{9,8},{10,11... | collective-permute-start | bytes 3080 | tf_op jit(solution)/shard_map/ppermute | solution.py:56
  46.7 3.5 %collective-permute-done.5 = f32[2,128]{1,0:T(2,128)S(1)} collective-permute-done((f32[2,128]{1,0:T(2,128)S(1)}, f32[2,128]{1,0:T(2,128)S(1)}, u32[]{:S(2)}, u32[]{:S(2)}) %collective-permute-start.5) | collective-permute-done | bytes 1056 | tf_op jit(solution)/shard_map/ppermute | solution.py:56
  50.2 2.5 %collective-permute-start.6 = (f32[2,128]{1,0:T(2,128)S(1)}, f32[2,128]{1,0:T(2,128)S(1)}, u32[]{:S(2)}, u32[]{:S(2)}) collective-permute-start(f32[2,128]{1,0:T(2,128)S(1)} %add.145), channel_id=1, source_target_pairs={{0,4},{4,0},{8,12},{12,8},{16,20},{20,16},{24,28},{28,24},{1,5},{5... | collective-permute-start | bytes 3080 | tf_op jit(solution)/shard_map/ppermute | solution.py:56
  54.2 2.4 %collective-permute-start.7 = (f32[2,128]{1,0:T(2,128)S(1)}, f32[2,128]{1,0:T(2,128)S(1)}, u32[]{:S(2)}, u32[]{:S(2)}) collective-permute-start(f32[2,128]{1,0:T(2,128)S(1)} %add.146), channel_id=1, source_target_pairs={{0,8},{4,12},{8,0},{12,4},{16,24},{20,28},{24,16},{28,20},{1,9},{5... | collective-permute-start | bytes 3080 | tf_op jit(solution)/shard_map/ppermute | solution.py:56
  58.1 3.0 %collective-permute-start.8 = (f32[2,128]{1,0:T(2,128)S(1)}, f32[2,128]{1,0:T(2,128)S(1)}, u32[]{:S(2)}, u32[]{:S(2)}) collective-permute-start(f32[2,128]{1,0:T(2,128)S(1)} %add.147), channel_id=1, source_target_pairs={{0,16},{4,20},{8,24},{12,28},{16,0},{20,4},{24,8},{28,12},{1,17},{... | collective-permute-start | bytes 3080 | tf_op jit(solution)/shard_map/ppermute | solution.py:56
  63.3 3.4 %shard_map.60 = (f32[28,80,128]{2,1,0:T(8,128)}, f32[1,128]{1,0:T(1,128)}) custom-call(f32[2,128]{1,0:T(2,128)} %add.148.refs_0_.refs_1_, f32[28,80,128]{2,1,0:T(8,128)} %get-tuple-element.19.refs_1_.refs_3_.refs_6_.refs_9_, f32[28,80,128]{2,1,0:T(8,128)} %get-tuple-element.20.refs_2_, f32[80,128]{1,0:T(8,128)} %add_convert_fusion.1.refs_3_.refs_8_.refs_4_), custom_call_target="tpu_custom_call" | custom-call | flops 11468800 | bytes 6881280 | tf_op jit(solution)/shard_map/pallas_call | solution.py:290
  68.7 3.4 %collective-permute-done.10 = f32[1,128]{1,0:T(1,128)S(1)} collective-permute-done((f32[1,128]{1,0:T(1,128)S(1)}, f32[1,128]{1,0:T(1,128)S(1)}, u32[]{:S(2)}, u32[]{:S(2)}) %collective-permute-start.10) | collective-permute-done | bytes 544 | tf_op jit(solution)/shard_map/ppermute | solution.py:56
  73.7 2.0 %collective-permute-done.11 = f32[1,128]{1,0:T(1,128)S(1)} collective-permute-done((f32[1,128]{1,0:T(1,128)S(1)}, f32[1,128]{1,0:T(1,128)S(1)}, u32[]{:S(2)}, u32[]{:S(2)}) %collective-permute-start.11) | collective-permute-done | bytes 544 | tf_op jit(solution)/shard_map/ppermute | solution.py:56
  75.7 1.9 %collective-permute-start.12 = (f32[1,128]{1,0:T(1,128)S(1)}, f32[1,128]{1,0:T(1,128)S(1)}, u32[]{:S(2)}, u32[]{:S(2)}) collective-permute-start(f32[1,128]{1,0:T(1,128)S(1)} %add.151), channel_id=1, source_target_pairs={{0,8},{4,12},{8,0},{12,4},{16,24},{20,28},{24,16},{28,20},{1,9},{5... | collective-permute-start | bytes 1544 | tf_op jit(solution)/shard_map/ppermute | solution.py:56
  79.3 2.9 %collective-permute-start.13 = (f32[1,128]{1,0:T(1,128)S(1)}, f32[1,128]{1,0:T(1,128)S(1)}, u32[]{:S(2)}, u32[]{:S(2)}) collective-permute-start(f32[1,128]{1,0:T(1,128)S(1)} %add.152), channel_id=1, source_target_pairs={{0,16},{4,20},{8,24},{12,28},{16,0},{20,4},{24,8},{28,12},{1,17},{... | collective-permute-start | bytes 1544 | tf_op jit(solution)/shard_map/ppermute | solution.py:56
  84.3 6.2 %shard_map.61 = (f32[28,80,128]{2,1,0:T(8,128)}, f32[28,80,128]{2,1,0:T(8,128)}, f32[1,128]{1,0:T(1,128)}) custom-call(f32[1,128]{1,0:T(1,128)} %add.153.refs_0_.refs_1_.refs_2_, f32[2,128]{1,0:T(2,128)} %add.148.refs_0_.refs_1_, f32[28,80,128]{2,1,0:T(8,128)} %get-tuple-element.22.refs_2_, f32[28,80,128]{2,1,0:T(8,128)} %get-tuple-element.19.refs_1_.refs_3_.refs_6_.refs_9_, ...), custom_call_target="tpu_custom_call" | custom-call | flops 11468800 | bytes 13762560 | tf_op jit(solution)/shard_map/pallas_call | solution.py:290
  92.7 3.4 %collective-permute-done.15 = f32[1,128]{1,0:T(1,128)S(1)} collective-permute-done((f32[1,128]{1,0:T(1,128)S(1)}, f32[1,128]{1,0:T(1,128)S(1)}, u32[]{:S(2)}, u32[]{:S(2)}) %collective-permute-start.15) | collective-permute-done | bytes 544 | tf_op jit(solution)/shard_map/ppermute | solution.py:56
  97.7 2.0 %collective-permute-done.16 = f32[1,128]{1,0:T(1,128)S(1)} collective-permute-done((f32[1,128]{1,0:T(1,128)S(1)}, f32[1,128]{1,0:T(1,128)S(1)}, u32[]{:S(2)}, u32[]{:S(2)}) %collective-permute-start.16) | collective-permute-done | bytes 544 | tf_op jit(solution)/shard_map/ppermute | solution.py:56
  99.7 1.9 %collective-permute-start.17 = (f32[1,128]{1,0:T(1,128)S(1)}, f32[1,128]{1,0:T(1,128)S(1)}, u32[]{:S(2)}, u32[]{:S(2)}) collective-permute-start(f32[1,128]{1,0:T(1,128)S(1)} %add.156), channel_id=1, source_target_pairs={{0,8},{4,12},{8,0},{12,4},{16,24},{20,28},{24,16},{28,20},{1,9},{5... | collective-permute-start | bytes 1544 | tf_op jit(solution)/shard_map/ppermute | solution.py:56
  103.2 2.9 %collective-permute-start.18 = (f32[1,128]{1,0:T(1,128)S(1)}, f32[1,128]{1,0:T(1,128)S(1)}, u32[]{:S(2)}, u32[]{:S(2)}) collective-permute-start(f32[1,128]{1,0:T(1,128)S(1)} %add.157), channel_id=1, source_target_pairs={{0,16},{4,20},{8,24},{12,28},{16,0},{20,4},{24,8},{28,12},{1,17},{... | collective-permute-start | bytes 1544 | tf_op jit(solution)/shard_map/ppermute | solution.py:56
  108.3 3.5 %shard_map.62 = (f32[28,80,128]{2,1,0:T(8,128)}, f32[1,128]{1,0:T(1,128)}) custom-call(f32[1,128]{1,0:T(1,128)} %add.153.refs_0_.refs_1_.refs_2_, f32[1,128]{1,0:T(1,128)} %add.158.refs_1_.refs_3_, f32[28,80,128]{2,1,0:T(8,128)} %get-tuple-element.22.refs_2_, f32[28,80,128]{2,1,0:T(8,128)} %get-tuple-element.26.refs_3_, ...), custom_call_target="tpu_custom_call" | custom-call | flops 11468800 | bytes 8028160 | tf_op jit(solution)/shard_map/pallas_call | solution.py:290
  113.8 3.4 %collective-permute-done.20 = f32[1,128]{1,0:T(1,128)S(1)} collective-permute-done((f32[1,128]{1,0:T(1,128)S(1)}, f32[1,128]{1,0:T(1,128)S(1)}, u32[]{:S(2)}, u32[]{:S(2)}) %collective-permute-start.20) | collective-permute-done | bytes 544 | tf_op jit(solution)/shard_map/ppermute | solution.py:56
  118.8 2.0 %collective-permute-done.21 = f32[1,128]{1,0:T(1,128)S(1)} collective-permute-done((f32[1,128]{1,0:T(1,128)S(1)}, f32[1,128]{1,0:T(1,128)S(1)}, u32[]{:S(2)}, u32[]{:S(2)}) %collective-permute-start.21) | collective-permute-done | bytes 544 | tf_op jit(solution)/shard_map/ppermute | solution.py:56
  120.8 1.9 %collective-permute-start.22 = (f32[1,128]{1,0:T(1,128)S(1)}, f32[1,128]{1,0:T(1,128)S(1)}, u32[]{:S(2)}, u32[]{:S(2)}) collective-permute-start(f32[1,128]{1,0:T(1,128)S(1)} %add.161), channel_id=1, source_target_pairs={{0,8},{4,12},{8,0},{12,4},{16,24},{20,28},{24,16},{28,20},{1,9},{5... | collective-permute-start | bytes 1544 | tf_op jit(solution)/shard_map/ppermute | solution.py:56
  124.4 2.9 %collective-permute-start.23 = (f32[1,128]{1,0:T(1,128)S(1)}, f32[1,128]{1,0:T(1,128)S(1)}, u32[]{:S(2)}, u32[]{:S(2)}) collective-permute-start(f32[1,128]{1,0:T(1,128)S(1)} %add.162), channel_id=1, source_target_pairs={{0,16},{4,20},{8,24},{12,28},{16,0},{20,4},{24,8},{28,12},{1,17},{... | collective-permute-start | bytes 1544 | tf_op jit(solution)/shard_map/ppermute | solution.py:56
  129.4 6.2 %shard_map.63 = (f32[28,80,128]{2,1,0:T(8,128)}, f32[28,80,128]{2,1,0:T(8,128)}, f32[1,128]{1,0:T(1,128)}) custom-call(f32[1,128]{1,0:T(1,128)} %add.163.refs_0_.refs_4_, f32[1,128]{1,0:T(1,128)} %add.153.refs_0_.refs_1_.refs_2_, f32[28,80,128]{2,1,0:T(8,128)} %get-tuple-element.28.refs_2_, f32[28,80,128]{2,1,0:T(8,128)} %get-tuple-element.29.refs_3_.refs_7_, ...), custom_call_target="tpu_custom_call" | custom-call | flops 11468800 | bytes 13762560 | tf_op jit(solution)/shard_map/pallas_call | solution.py:290
  137.7 3.4 %collective-permute-done.25 = f32[1,128]{1,0:T(1,128)S(1)} collective-permute-done((f32[1,128]{1,0:T(1,128)S(1)}, f32[1,128]{1,0:T(1,128)S(1)}, u32[]{:S(2)}, u32[]{:S(2)}) %collective-permute-start.25) | collective-permute-done | bytes 544 | tf_op jit(solution)/shard_map/ppermute | solution.py:56
  142.7 2.0 %collective-permute-done.26 = f32[1,128]{1,0:T(1,128)S(1)} collective-permute-done((f32[1,128]{1,0:T(1,128)S(1)}, f32[1,128]{1,0:T(1,128)S(1)}, u32[]{:S(2)}, u32[]{:S(2)}) %collective-permute-start.26) | collective-permute-done | bytes 544 | tf_op jit(solution)/shard_map/ppermute | solution.py:56
  144.7 1.9 %collective-permute-start.27 = (f32[1,128]{1,0:T(1,128)S(1)}, f32[1,128]{1,0:T(1,128)S(1)}, u32[]{:S(2)}, u32[]{:S(2)}) collective-permute-start(f32[1,128]{1,0:T(1,128)S(1)} %add.166), channel_id=1, source_target_pairs={{0,8},{4,12},{8,0},{12,4},{16,24},{20,28},{24,16},{28,20},{1,9},{5... | collective-permute-start | bytes 1544 | tf_op jit(solution)/shard_map/ppermute | solution.py:56
  148.3 2.9 %collective-permute-start.28 = (f32[1,128]{1,0:T(1,128)S(1)}, f32[1,128]{1,0:T(1,128)S(1)}, u32[]{:S(2)}, u32[]{:S(2)}) collective-permute-start(f32[1,128]{1,0:T(1,128)S(1)} %add.167), channel_id=1, source_target_pairs={{0,16},{4,20},{8,24},{12,28},{16,0},{20,4},{24,8},{28,12},{1,17},{... | collective-permute-start | bytes 1544 | tf_op jit(solution)/shard_map/ppermute | solution.py:56
  153.3 6.3 %shard_map.64 = (f32[16,128]{1,0:T(8,128)}, f32[16,128]{1,0:T(8,128)}) custom-call(f32[2,128]{1,0:T(2,128)} %add.148.refs_0_.refs_1_, f32[2,128]{1,0:T(2,128)} %add.148.refs_0_.refs_1_, f32[1,128]{1,0:T(1,128)} %add.153.refs_0_.refs_1_.refs_2_, f32[1,128]{1,0:T(1,128)} %add.158.refs_1_.refs_3_, f32[1,128]{1,0:T(1,128)} %add.163.refs_0_.refs_4_, ...), custom_call_target="tpu_custom_call" | custom-call | flops 11468800 | bytes 20643840 | tf_op jit(solution)/shard_map/pallas_call | solution.py:290
  (90 shorter events, 51.2 us)
Async XLA Ops:
  0.6 11.3 %copy-start = (f32[64,16,128]{2,1,0:T(8,128)S(1)}, f32[64,16,128]{2,1,0:T(8,128)}, u32[]{:S(2)}) copy-start(f32[64,16,128]{2,1,0:T(8,128)} %param.4) | copy-start | bytes 1572868
  0.6 10.9 %copy-start.3 = (f32[16,128]{1,0:T(8,128)S(1)}, f32[16,128]{1,0:T(8,128)}, u32[]{:S(2)}) copy-start(f32[16,128]{1,0:T(8,128)} %param.6) | copy-start | bytes 24580
  2.5 9.8 %copy-start.2 = (f32[16,128]{1,0:T(8,128)S(1)}, f32[16,128]{1,0:T(8,128)}, u32[]{:S(2)}) copy-start(f32[16,128]{1,0:T(8,128)} %refs_13_.1) | copy-start | bytes 24580
  3.3 15.8 %collective-permute-start.1 = (f32[536,128]{1,0:T(8,128)S(1)}, f32[536,128]{1,0:T(8,128)}, u32[]{:S(2)}, u32[]{:S(2)}) collective-permute-start(f32[536,128]{1,0:T(8,128)S(1)} %maximum_bitcast_fusion.2), channel_id=1, source_target_pairs={{4,0},{8,4},{12,8},{16,12},{20,16},{24,20},{28,24},{5,1},{9,5},{13... | collective-permute-start | bytes 823304 | tf_op jit(solution)/shard_map/ppermute | solution.py:328
  5.3 15.5 %collective-permute-start = (f32[536,128]{1,0:T(8,128)}, f32[536,128]{1,0:T(8,128)}, u32[]{:S(2)}, u32[]{:S(2)}) collective-permute-start(f32[536,128]{1,0:T(8,128)} %maximum_bitcast_fusion.1), channel_id=1, source_target_pairs={{0,4},{4,8},{8,12},{12,16},{16,20},{20,24},{24,28},{1,5},{5,9},{9,... | collective-permute-start | bytes 823304 | tf_op jit(solution)/shard_map/ppermute | solution.py:325
  22.1 3.8 %collective-permute-start.2 = (f32[28,6,67]{2,1,0:T(8,128)S(1)}, f32[28,6,67]{2,1,0:T(8,128)S(1)}, u32[]{:S(2)}, u32[]{:S(2)}) collective-permute-start(f32[28,6,67]{2,1,0:T(8,128)S(1)} %get-tuple-element.34), channel_id=1, source_target_pairs={{0,1},{1,2},{2,3},{4,5},{5,6},{6,7},{8,9},{9,10},{10,11},{12,13},{... | collective-permute-start | bytes 135080 | tf_op jit(solution)/shard_map/ppermute | solution.py:20
  24.0 4.3 %collective-permute-start.3 = (f32[28,6,67]{2,1,0:T(8,128)S(1)}, f32[28,6,67]{2,1,0:T(8,128)S(1)}, u32[]{:S(2)}, u32[]{:S(2)}) collective-permute-start(f32[28,6,67]{2,1,0:T(8,128)S(1)} %get-tuple-element.35), channel_id=1, source_target_pairs={{1,0},{2,1},{3,2},{5,4},{6,5},{7,6},{9,8},{10,9},{11,10},{13,12},{... | collective-permute-start | bytes 135080 | tf_op jit(solution)/shard_map/ppermute | solution.py:22
  41.5 4.4 %collective-permute-start.4 = (f32[2,128]{1,0:T(2,128)}, f32[2,128]{1,0:T(2,128)S(1)}, u32[]{:S(2)}, u32[]{:S(2)}) collective-permute-start(f32[2,128]{1,0:T(2,128)} %get-tuple-element.18), channel_id=1, source_target_pairs={{0,1},{1,0},{2,3},{3,2},{4,5},{5,4},{6,7},{7,6},{8,9},{9,8},{10,11... | collective-permute-start | bytes 3080 | tf_op jit(solution)/shard_map/ppermute | solution.py:56
  46.6 3.6 %collective-permute-start.5 = (f32[2,128]{1,0:T(2,128)S(1)}, f32[2,128]{1,0:T(2,128)S(1)}, u32[]{:S(2)}, u32[]{:S(2)}) collective-permute-start(f32[2,128]{1,0:T(2,128)S(1)} %add.144), channel_id=1, source_target_pairs={{0,2},{1,3},{2,0},{3,1},{4,6},{5,7},{6,4},{7,5},{8,10},{9,11},{10,... | collective-permute-start | bytes 3080 | tf_op jit(solution)/shard_map/ppermute | solution.py:56
  50.2 4.0 %collective-permute-start.6 = (f32[2,128]{1,0:T(2,128)S(1)}, f32[2,128]{1,0:T(2,128)S(1)}, u32[]{:S(2)}, u32[]{:S(2)}) collective-permute-start(f32[2,128]{1,0:T(2,128)S(1)} %add.145), channel_id=1, source_target_pairs={{0,4},{4,0},{8,12},{12,8},{16,20},{20,16},{24,28},{28,24},{1,5},{5... | collective-permute-start | bytes 3080 | tf_op jit(solution)/shard_map/ppermute | solution.py:56
  54.2 3.9 %collective-permute-start.7 = (f32[2,128]{1,0:T(2,128)S(1)}, f32[2,128]{1,0:T(2,128)S(1)}, u32[]{:S(2)}, u32[]{:S(2)}) collective-permute-start(f32[2,128]{1,0:T(2,128)S(1)} %add.146), channel_id=1, source_target_pairs={{0,8},{4,12},{8,0},{12,4},{16,24},{20,28},{24,16},{28,20},{1,9},{5... | collective-permute-start | bytes 3080 | tf_op jit(solution)/shard_map/ppermute | solution.py:56
  58.1 4.6 %collective-permute-start.8 = (f32[2,128]{1,0:T(2,128)S(1)}, f32[2,128]{1,0:T(2,128)S(1)}, u32[]{:S(2)}, u32[]{:S(2)}) collective-permute-start(f32[2,128]{1,0:T(2,128)S(1)} %add.147), channel_id=1, source_target_pairs={{0,16},{4,20},{8,24},{12,28},{16,0},{20,4},{24,8},{28,12},{1,17},{... | collective-permute-start | bytes 3080 | tf_op jit(solution)/shard_map/ppermute | solution.py:56
  66.6 1.3 collective-permute-start.9
  68.6 3.6 %collective-permute-start.10 = (f32[1,128]{1,0:T(1,128)S(1)}, f32[1,128]{1,0:T(1,128)S(1)}, u32[]{:S(2)}, u32[]{:S(2)}) collective-permute-start(f32[1,128]{1,0:T(1,128)S(1)} %add.149), channel_id=1, source_target_pairs={{0,2},{1,3},{2,0},{3,1},{4,6},{5,7},{6,4},{7,5},{8,10},{9,11},{10,... | collective-permute-start | bytes 1544 | tf_op jit(solution)/shard_map/ppermute | solution.py:56
  72.2 3.6 %collective-permute-start.11 = (f32[1,128]{1,0:T(1,128)S(1)}, f32[1,128]{1,0:T(1,128)S(1)}, u32[]{:S(2)}, u32[]{:S(2)}) collective-permute-start(f32[1,128]{1,0:T(1,128)S(1)} %add.150), channel_id=1, source_target_pairs={{0,4},{4,0},{8,12},{12,8},{16,20},{20,16},{24,28},{28,24},{1,5},{5... | collective-permute-start | bytes 1544 | tf_op jit(solution)/shard_map/ppermute | solution.py:56
  75.7 3.6 %collective-permute-start.12 = (f32[1,128]{1,0:T(1,128)S(1)}, f32[1,128]{1,0:T(1,128)S(1)}, u32[]{:S(2)}, u32[]{:S(2)}) collective-permute-start(f32[1,128]{1,0:T(1,128)S(1)} %add.151), channel_id=1, source_target_pairs={{0,8},{4,12},{8,0},{12,4},{16,24},{20,28},{24,16},{28,20},{1,9},{5... | collective-permute-start | bytes 1544 | tf_op jit(solution)/shard_map/ppermute | solution.py:56
  79.3 4.5 %collective-permute-start.13 = (f32[1,128]{1,0:T(1,128)S(1)}, f32[1,128]{1,0:T(1,128)S(1)}, u32[]{:S(2)}, u32[]{:S(2)}) collective-permute-start(f32[1,128]{1,0:T(1,128)S(1)} %add.152), channel_id=1, source_target_pairs={{0,16},{4,20},{8,24},{12,28},{16,0},{20,4},{24,8},{28,12},{1,17},{... | collective-permute-start | bytes 1544 | tf_op jit(solution)/shard_map/ppermute | solution.py:56
  90.6 1.3 collective-permute-start.14
  92.5 3.6 %collective-permute-start.15 = (f32[1,128]{1,0:T(1,128)S(1)}, f32[1,128]{1,0:T(1,128)S(1)}, u32[]{:S(2)}, u32[]{:S(2)}) collective-permute-start(f32[1,128]{1,0:T(1,128)S(1)} %add.154), channel_id=1, source_target_pairs={{0,2},{1,3},{2,0},{3,1},{4,6},{5,7},{6,4},{7,5},{8,10},{9,11},{10,... | collective-permute-start | bytes 1544 | tf_op jit(solution)/shard_map/ppermute | solution.py:56
  96.1 3.6 %collective-permute-start.16 = (f32[1,128]{1,0:T(1,128)S(1)}, f32[1,128]{1,0:T(1,128)S(1)}, u32[]{:S(2)}, u32[]{:S(2)}) collective-permute-start(f32[1,128]{1,0:T(1,128)S(1)} %add.155), channel_id=1, source_target_pairs={{0,4},{4,0},{8,12},{12,8},{16,20},{20,16},{24,28},{28,24},{1,5},{5... | collective-permute-start | bytes 1544 | tf_op jit(solution)/shard_map/ppermute | solution.py:56
  99.7 3.6 %collective-permute-start.17 = (f32[1,128]{1,0:T(1,128)S(1)}, f32[1,128]{1,0:T(1,128)S(1)}, u32[]{:S(2)}, u32[]{:S(2)}) collective-permute-start(f32[1,128]{1,0:T(1,128)S(1)} %add.156), channel_id=1, source_target_pairs={{0,8},{4,12},{8,0},{12,4},{16,24},{20,28},{24,16},{28,20},{1,9},{5... | collective-permute-start | bytes 1544 | tf_op jit(solution)/shard_map/ppermute | solution.py:56
  103.2 4.5 %collective-permute-start.18 = (f32[1,128]{1,0:T(1,128)S(1)}, f32[1,128]{1,0:T(1,128)S(1)}, u32[]{:S(2)}, u32[]{:S(2)}) collective-permute-start(f32[1,128]{1,0:T(1,128)S(1)} %add.157), channel_id=1, source_target_pairs={{0,16},{4,20},{8,24},{12,28},{16,0},{20,4},{24,8},{28,12},{1,17},{... | collective-permute-start | bytes 1544 | tf_op jit(solution)/shard_map/ppermute | solution.py:56
  111.7 1.3 collective-permute-start.19
  113.7 3.6 %collective-permute-start.20 = (f32[1,128]{1,0:T(1,128)S(1)}, f32[1,128]{1,0:T(1,128)S(1)}, u32[]{:S(2)}, u32[]{:S(2)}) collective-permute-start(f32[1,128]{1,0:T(1,128)S(1)} %add.159), channel_id=1, source_target_pairs={{0,2},{1,3},{2,0},{3,1},{4,6},{5,7},{6,4},{7,5},{8,10},{9,11},{10,... | collective-permute-start | bytes 1544 | tf_op jit(solution)/shard_map/ppermute | solution.py:56
  117.3 3.6 %collective-permute-start.21 = (f32[1,128]{1,0:T(1,128)S(1)}, f32[1,128]{1,0:T(1,128)S(1)}, u32[]{:S(2)}, u32[]{:S(2)}) collective-permute-start(f32[1,128]{1,0:T(1,128)S(1)} %add.160), channel_id=1, source_target_pairs={{0,4},{4,0},{8,12},{12,8},{16,20},{20,16},{24,28},{28,24},{1,5},{5... | collective-permute-start | bytes 1544 | tf_op jit(solution)/shard_map/ppermute | solution.py:56
  120.8 3.6 %collective-permute-start.22 = (f32[1,128]{1,0:T(1,128)S(1)}, f32[1,128]{1,0:T(1,128)S(1)}, u32[]{:S(2)}, u32[]{:S(2)}) collective-permute-start(f32[1,128]{1,0:T(1,128)S(1)} %add.161), channel_id=1, source_target_pairs={{0,8},{4,12},{8,0},{12,4},{16,24},{20,28},{24,16},{28,20},{1,9},{5... | collective-permute-start | bytes 1544 | tf_op jit(solution)/shard_map/ppermute | solution.py:56
  124.4 4.5 %collective-permute-start.23 = (f32[1,128]{1,0:T(1,128)S(1)}, f32[1,128]{1,0:T(1,128)S(1)}, u32[]{:S(2)}, u32[]{:S(2)}) collective-permute-start(f32[1,128]{1,0:T(1,128)S(1)} %add.162), channel_id=1, source_target_pairs={{0,16},{4,20},{8,24},{12,28},{16,0},{20,4},{24,8},{28,12},{1,17},{... | collective-permute-start | bytes 1544 | tf_op jit(solution)/shard_map/ppermute | solution.py:56
  135.6 1.3 collective-permute-start.24
  137.5 3.6 %collective-permute-start.25 = (f32[1,128]{1,0:T(1,128)S(1)}, f32[1,128]{1,0:T(1,128)S(1)}, u32[]{:S(2)}, u32[]{:S(2)}) collective-permute-start(f32[1,128]{1,0:T(1,128)S(1)} %add.164), channel_id=1, source_target_pairs={{0,2},{1,3},{2,0},{3,1},{4,6},{5,7},{6,4},{7,5},{8,10},{9,11},{10,... | collective-permute-start | bytes 1544 | tf_op jit(solution)/shard_map/ppermute | solution.py:56
  141.1 3.6 %collective-permute-start.26 = (f32[1,128]{1,0:T(1,128)S(1)}, f32[1,128]{1,0:T(1,128)S(1)}, u32[]{:S(2)}, u32[]{:S(2)}) collective-permute-start(f32[1,128]{1,0:T(1,128)S(1)} %add.165), channel_id=1, source_target_pairs={{0,4},{4,0},{8,12},{12,8},{16,20},{20,16},{24,28},{28,24},{1,5},{5... | collective-permute-start | bytes 1544 | tf_op jit(solution)/shard_map/ppermute | solution.py:56
  144.7 3.6 %collective-permute-start.27 = (f32[1,128]{1,0:T(1,128)S(1)}, f32[1,128]{1,0:T(1,128)S(1)}, u32[]{:S(2)}, u32[]{:S(2)}) collective-permute-start(f32[1,128]{1,0:T(1,128)S(1)} %add.166), channel_id=1, source_target_pairs={{0,8},{4,12},{8,0},{12,4},{16,24},{20,28},{24,16},{28,20},{1,9},{5... | collective-permute-start | bytes 1544 | tf_op jit(solution)/shard_map/ppermute | solution.py:56
  148.3 4.5 %collective-permute-start.28 = (f32[1,128]{1,0:T(1,128)S(1)}, f32[1,128]{1,0:T(1,128)S(1)}, u32[]{:S(2)}, u32[]{:S(2)}) collective-permute-start(f32[1,128]{1,0:T(1,128)S(1)} %add.167), channel_id=1, source_target_pairs={{0,16},{4,20},{8,24},{12,28},{16,0},{20,4},{24,8},{28,12},{1,17},{... | collective-permute-start | bytes 1544 | tf_op jit(solution)/shard_map/ppermute | solution.py:56
  (1 other events, 9.1 us)

commit v11 on v10

--- a/solution.py
+++ b/solution.py
@@ -45,16 +45,33 @@
     return stencil(jnp.pad(field, pads), kappa_sq)
 
 
+def _span_sum(terms, basis, partner):
+    if not basis:
+        return partner(0)
+    *rest, top = basis
+    return _span_sum(terms, rest, partner) + _span_sum(terms, rest, lambda m: partner(m ^ top))
+
+
 def all_sum(terms):
-    for axis in ("cols", "rows"):
-        count = lax.axis_size(axis)
-        if count & (count - 1):
+    axes = ("rows", "cols")
+    count = lax.axis_size("rows") * lax.axis_size("cols")
+    if count & (count - 1):
+        for axis in axes:
             terms = lax.psum(terms, axis)
-            continue
-        hop = 1
-        while hop < count:
-            terms = terms + lax.ppermute(terms, axis, [(i, i ^ hop) for i in range(count)])
-            hop *= 2
+        return terms
+    bits = [1 << k for k in range(count.bit_length() - 1)]
+    groups = [bits[:1]] + [bits[k : k + 2] for k in range(1, len(bits), 2)]
+    for basis in groups:
+        received = {}
+
+        def partner(mask, terms=terms, received=received):
+            if mask == 0:
+                return terms
+            if mask not in received:
+                received[mask] = lax.ppermute(terms, axes, [(i, i ^ mask) for i in range(count)])
+            return received[mask]
+
+        terms = _span_sum(terms, basis, partner)
     return terms
 
 

time: 160 us -> 148 us (0.925)
  waiting for transfers between devices: 52 us -> 33.9 us
  starting transfers between devices: 48.2 us -> 54.1 us
    ppermute x25 -> x35, waiting for transfers between devices: 48.9 us -> 30.8 us  [partner(): lax.ppermute(terms, axes, [(i, i ^ mask) for i in range(count)])]
    ppermute x25 -> x35, starting transfers between devices: 37.5 us -> 43.4 us  [partner(): lax.ppermute(terms, axes, [(i, i ^ mask) for i in range(count)])]
    add x25 -> x15, other arithmetic: 6.1 us -> 6.15 us  [_span_sum(): _span_sum(terms, rest, partner)]
  transfers between devices with their start and end apart: 29 -> 39, of which waited for: 27 -> 30; matrix products, arithmetic and copies ran while one was open for 6% -> 7% of each run, Pallas kernels for 0% -> 0%
where the time goes in v11:
time: 148 us; the launch traced here: 147 us
  starting transfers between devices  54.1 us (37%)
  Pallas kernels  36.8 us (25%)
  waiting for transfers between devices  33.9 us (23%)
  other arithmetic  13.2 us (9%)
  local copies, waits for them, and re-layouts  8.58 us (6%)
    ppermute x35, starting transfers between devices, partner(): lax.ppermute(terms, axes, [(i, i ^ mask) for i in range(count)])  43.4 us
    pallas_call x6, Pallas kernels, _call(): pl.pallas_call(lambda *refs: kernel(plan, *refs), out_shape=out_shapes, i...  36.8 us
    ppermute x35, waiting for transfers between devices, partner(): lax.ppermute(terms, axes, [(i, i ^ mask) for i in range(count)])  30.8 us
    ppermute x1, starting transfers between devices, on_device(): lax.ppermute(edge_rows(rows - sent), 'rows', [(i, i + 1) for i in range(c...  6.21 us
    add x15, other arithmetic, _span_sum(): _span_sum(terms, rest, partner)  6.15 us
    broadcast_in_dim x3, local copies, waits for them, and re-layouts, on_device(): fields = (probes, observed[None], kappa_sq[None], variance_weight[None])  3.09 us
  transfers between devices with their start and end apart: 39, of which 30 were waited for; matrix products, arithmetic and copies ran while one was open for 7% of the time, Pallas kernels for 0%

profile of v11, /device:TPU:0, one launch (start us, length us, event | category | flops | bytes accessed | tf_op | source)
XLA Modules:
  0.0 147.5 jit_solution(18182861279742564254)
XLA Ops:
  5.3 6.2 %collective-permute-start = (f32[536,128]{1,0:T(8,128)}, f32[536,128]{1,0:T(8,128)}, u32[]{:S(2)}, u32[]{:S(2)}) collective-permute-start(f32[536,128]{1,0:T(8,128)} %maximum_bitcast_fusion.1), channel_id=1, source_target_pairs={{0,4},{4,8},{8,12},{12,16},{16,20},{20,24},{24,28},{1,5},{5,9},{9,... | collective-permute-start | bytes 823304 | tf_op jit(solution)/shard_map/ppermute | solution.py:342
  15.8 2.4 %maximum_bitcast_fusion = f32[16,128,67]{2,1,0:T(8,128)S(1)} fusion(f32[1,16,128]{0,2,1:T(8,128)} %copy.17, f32[1,16,128]{0,2,1:T(8,128)S(1)} %copy.16, f32[1,16,128]{0,2,1:T(8,128)} %copy.15, f32[64,16,128]{0,2,1:T(8,128)S(1)} %copy.14), kind=kLoop, calls=%fused_computation.13 | loop fusion | flops 411648 | bytes 1097728 | tf_op jit(solution)/shard_map/transpose | solution.py:349
  22.1 1.9 %collective-permute-start.2 = (f32[28,6,67]{2,1,0:T(8,128)S(1)}, f32[28,6,67]{2,1,0:T(8,128)S(1)}, u32[]{:S(2)}, u32[]{:S(2)}) collective-permute-start(f32[28,6,67]{2,1,0:T(8,128)S(1)} %get-tuple-element.34), channel_id=1, source_target_pairs={{0,1},{1,2},{2,3},{4,5},{5,6},{6,7},{8,9},{9,10},{10,11},{12,13},{... | collective-permute-start | bytes 135080 | tf_op jit(solution)/shard_map/ppermute | solution.py:20
  25.8 2.5 %collective-permute-done.3 = f32[28,6,67]{2,1,0:T(8,128)S(1)} collective-permute-done((f32[28,6,67]{2,1,0:T(8,128)S(1)}, f32[28,6,67]{2,1,0:T(8,128)S(1)}, u32[]{:S(2)}, u32[]{:S(2)}) %collective-permute-start.3) | collective-permute-done | bytes 45056 | tf_op jit(solution)/shard_map/ppermute | solution.py:22
  28.3 1.9 %select_maximum_fusion.refs_0_ = f32[28,144,128]{2,1,0:T(8,128)} fusion(f32[28,6,67]{2,1,0:T(8,128)S(1)} %collective-permute-done.3, f32[28,6,67]{2,1,0:T(8,128)S(1)} %collective-permute-done.2, f32[6,128,67]{2,1,0:T(8,128)S(1)} %bitcast.15, f32[16,128,67]{2,1,0:T(8,128)S(1)} %maximum_bitcast_fusion, f32[6,128,67]{2,1,0:T(8,128)S(1)} %bitcast.17), kind=kLoop, calls=%fused_computation | loop fusion | flops 8773632 | bytes 3114944 | tf_op jit(solution)/shard_map/concatenate | solution.py:18
  30.3 11.2 %shard_map.59 = (f32[28,80,128]{2,1,0:T(8,128)}, f32[28,80,128]{2,1,0:T(8,128)}, f32[28,80,128]{2,1,0:T(8,128)}, f32[28,80,128]{2,1,0:T(8,128)}, f32[28,80,128]{...) custom-call(f32[28,144,128]{2,1,0:T(8,128)} %select_maximum_fusion.refs_0_, ...), custom_call_target="tpu_custom_call" | custom-call | flops 11468800 | bytes 13762560 | tf_op jit(solution)/shard_map/pallas_call | solution.py:307
  41.5 3.4 %collective-permute-start.4 = (f32[2,128]{1,0:T(2,128)}, f32[2,128]{1,0:T(2,128)S(1)}, u32[]{:S(2)}, u32[]{:S(2)}) collective-permute-start(f32[2,128]{1,0:T(2,128)} %get-tuple-element.18), channel_id=1, source_target_pairs={{0,1},{1,0},{2,3},{3,2},{4,5},{5,4},{6,7},{7,6},{8,9},{9,8},{10,11... | collective-permute-start | bytes 3080 | tf_op jit(solution)/shard_map/ppermute | solution.py:71
  46.6 2.0 %collective-permute-start.7 = (f32[2,128]{1,0:T(2,128)S(1)}, f32[2,128]{1,0:T(2,128)S(1)}, u32[]{:S(2)}, u32[]{:S(2)}) collective-permute-start(f32[2,128]{1,0:T(2,128)S(1)} %add.174), channel_id=1, source_target_pairs={{0,6},{1,7},{2,4},{3,5},{4,2},{5,3},{6,0},{7,1},{8,14},{9,15},{10,... | collective-permute-start | bytes 3080 | tf_op jit(solution)/shard_map/ppermute | solution.py:71
  49.1 1.5 collective-permute-start.5
  52.7 3.9 %collective-permute-start.10 = (f32[2,128]{1,0:T(2,128)S(1)}, f32[2,128]{1,0:T(2,128)S(1)}, u32[]{:S(2)}, u32[]{:S(2)}) collective-permute-start(f32[2,128]{1,0:T(2,128)S(1)} %add_add_fusion.1), channel_id=1, source_target_pairs={{0,24},{1,25},{2,26},{3,27},{4,28},{5,29},{6,30},{7,31},{8,16},{9,... | collective-permute-start | bytes 3080 | tf_op jit(solution)/shard_map/ppermute | solution.py:71
  58.2 2.9 %collective-permute-done.9 = f32[2,128]{1,0:T(2,128)S(1)} collective-permute-done((f32[2,128]{1,0:T(2,128)S(1)}, f32[2,128]{1,0:T(2,128)S(1)}, u32[]{:S(2)}, u32[]{:S(2)}) %collective-permute-start.9) | collective-permute-done | bytes 1056 | tf_op jit(solution)/shard_map/ppermute | solution.py:71
  61.7 3.3 %shard_map.60 = (f32[28,80,128]{2,1,0:T(8,128)}, f32[1,128]{1,0:T(1,128)}) custom-call(f32[2,128]{1,0:T(2,128)} %add_add_fusion.refs_0_.refs_1_, f32[28,80,128]{2,1,0:T(8,128)} %get-tuple-element.19.refs_1_.refs_3_.refs_6_.refs_9_, f32[28,80,128]{2,1,0:T(8,128)} %get-tuple-element.20.refs_2_, f32[80,128]{1,0:T(8,128)} %add_convert_fusion.1.refs_3_.refs_8_.refs_4_), custom_call_target="tpu_custom_call" | custom-call | flops 11468800 | bytes 6881280 | tf_op jit(solution)/shard_map/pallas_call | solution.py:307
  67.0 1.4 collective-permute-start.14
  68.4 2.0 %collective-permute-start.13 = (f32[1,128]{1,0:T(1,128)S(1)}, f32[1,128]{1,0:T(1,128)S(1)}, u32[]{:S(2)}, u32[]{:S(2)}) collective-permute-start(f32[1,128]{1,0:T(1,128)S(1)} %add.181), channel_id=1, source_target_pairs={{0,4},{1,5},{2,6},{3,7},{4,0},{5,1},{6,2},{7,3},{8,12},{9,13},{10,... | collective-permute-start | bytes 1544 | tf_op jit(solution)/shard_map/ppermute | solution.py:71
  72.0 2.0 %collective-permute-done.12 = f32[1,128]{1,0:T(1,128)S(1)} collective-permute-done((f32[1,128]{1,0:T(1,128)S(1)}, f32[1,128]{1,0:T(1,128)S(1)}, u32[]{:S(2)}, u32[]{:S(2)}) %collective-permute-start.12) | collective-permute-done | bytes 544 | tf_op jit(solution)/shard_map/ppermute | solution.py:71
  73.9 1.5 collective-permute-start.17
  76.0 2.3 %collective-permute-start.15 = (f32[1,128]{1,0:T(1,128)S(1)}, f32[1,128]{1,0:T(1,128)S(1)}, u32[]{:S(2)}, u32[]{:S(2)}) collective-permute-start(f32[1,128]{1,0:T(1,128)S(1)} %add_add_fusion.9), channel_id=1, source_target_pairs={{0,8},{1,9},{2,10},{3,11},{4,12},{5,13},{6,14},{7,15},{8,0},{9,1},... | collective-permute-start | bytes 1544 | tf_op jit(solution)/shard_map/ppermute | solution.py:71
  80.4 6.2 %shard_map.61 = (f32[28,80,128]{2,1,0:T(8,128)}, f32[28,80,128]{2,1,0:T(8,128)}, f32[1,128]{1,0:T(1,128)}) custom-call(f32[1,128]{1,0:T(1,128)} %add_add_fusion.8.refs_0_.refs_1_.refs_2_, f32[2,128]{1,0:T(2,128)} %add_add_fusion.refs_0_.refs_1_, f32[28,80,128]{2,1,0:T(8,128)} %get-tuple-element.22.refs_2_, ...), custom_call_target="tpu_custom_call" | custom-call | flops 11468800 | bytes 13762560 | tf_op jit(solution)/shard_map/pallas_call | solution.py:307
  90.2 1.9 %collective-permute-start.19 = (f32[1,128]{1,0:T(1,128)S(1)}, f32[1,128]{1,0:T(1,128)S(1)}, u32[]{:S(2)}, u32[]{:S(2)}) collective-permute-start(f32[1,128]{1,0:T(1,128)S(1)} %add.188), channel_id=1, source_target_pairs={{0,2},{1,3},{2,0},{3,1},{4,6},{5,7},{6,4},{7,5},{8,10},{9,11},{10,... | collective-permute-start | bytes 1544 | tf_op jit(solution)/shard_map/ppermute | solution.py:71
  93.8 2.6 %collective-permute-start.24 = (f32[1,128]{1,0:T(1,128)S(1)}, f32[1,128]{1,0:T(1,128)S(1)}, u32[]{:S(2)}, u32[]{:S(2)}) collective-permute-start(f32[1,128]{1,0:T(1,128)S(1)} %add_add_fusion.7), channel_id=1, source_target_pairs={{0,24},{1,25},{2,26},{3,27},{4,28},{5,29},{6,30},{7,31},{8,16},{9,... | collective-permute-start | bytes 1544 | tf_op jit(solution)/shard_map/ppermute | solution.py:71
  99.2 1.7 %collective-permute-done.23 = f32[1,128]{1,0:T(1,128)S(1)} collective-permute-done((f32[1,128]{1,0:T(1,128)S(1)}, f32[1,128]{1,0:T(1,128)S(1)}, u32[]{:S(2)}, u32[]{:S(2)}) %collective-permute-start.23) | collective-permute-done | bytes 544 | tf_op jit(solution)/shard_map/ppermute | solution.py:71
  101.4 3.5 %shard_map.62 = (f32[28,80,128]{2,1,0:T(8,128)}, f32[1,128]{1,0:T(1,128)}) custom-call(f32[1,128]{1,0:T(1,128)} %add_add_fusion.8.refs_0_.refs_1_.refs_2_, f32[1,128]{1,0:T(1,128)} %add_add_fusion.6.refs_1_.refs_3_, f32[28,80,128]{2,1,0:T(8,128)} %get-tuple-element.22.refs_2_, f32[28,80,128]{2,1,0:T(8,128)} %get-tuple-element.26.refs_3_, ...), custom_call_target="tpu_custom_call" | custom-call | flops 11468800 | bytes 8028160 | tf_op jit(solution)/shard_map/pallas_call | solution.py:307
  106.8 1.4 collective-permute-start.28
  108.2 2.0 %collective-permute-start.27 = (f32[1,128]{1,0:T(1,128)S(1)}, f32[1,128]{1,0:T(1,128)S(1)}, u32[]{:S(2)}, u32[]{:S(2)}) collective-permute-start(f32[1,128]{1,0:T(1,128)S(1)} %add.195), channel_id=1, source_target_pairs={{0,4},{1,5},{2,6},{3,7},{4,0},{5,1},{6,2},{7,3},{8,12},{9,13},{10,... | collective-permute-start | bytes 1544 | tf_op jit(solution)/shard_map/ppermute | solution.py:71
  111.8 2.0 %collective-permute-done.26 = f32[1,128]{1,0:T(1,128)S(1)} collective-permute-done((f32[1,128]{1,0:T(1,128)S(1)}, f32[1,128]{1,0:T(1,128)S(1)}, u32[]{:S(2)}, u32[]{:S(2)}) %collective-permute-start.26) | collective-permute-done | bytes 544 | tf_op jit(solution)/shard_map/ppermute | solution.py:71
  113.7 1.5 collective-permute-start.31
  116.1 2.0 %collective-permute-start.29 = (f32[1,128]{1,0:T(1,128)S(1)}, f32[1,128]{1,0:T(1,128)S(1)}, u32[]{:S(2)}, u32[]{:S(2)}) collective-permute-start(f32[1,128]{1,0:T(1,128)S(1)} %add_add_fusion.5), channel_id=1, source_target_pairs={{0,8},{1,9},{2,10},{3,11},{4,12},{5,13},{6,14},{7,15},{8,0},{9,1},... | collective-permute-start | bytes 1544 | tf_op jit(solution)/shard_map/ppermute | solution.py:71
  120.3 6.2 %shard_map.63 = (f32[28,80,128]{2,1,0:T(8,128)}, f32[28,80,128]{2,1,0:T(8,128)}, f32[1,128]{1,0:T(1,128)}) custom-call(f32[1,128]{1,0:T(1,128)} %add_add_fusion.4.refs_0_.refs_4_, f32[1,128]{1,0:T(1,128)} %add_add_fusion.8.refs_0_.refs_1_.refs_2_, f32[28,80,128]{2,1,0:T(8,128)} %get-tuple-element.28.refs_2_, ...), custom_call_target="tpu_custom_call" | custom-call | flops 11468800 | bytes 13762560 | tf_op jit(solution)/shard_map/pallas_call | solution.py:307
  130.0 1.9 %collective-permute-start.33 = (f32[1,128]{1,0:T(1,128)S(1)}, f32[1,128]{1,0:T(1,128)S(1)}, u32[]{:S(2)}, u32[]{:S(2)}) collective-permute-start(f32[1,128]{1,0:T(1,128)S(1)} %add.202), channel_id=1, source_target_pairs={{0,2},{1,3},{2,0},{3,1},{4,6},{5,7},{6,4},{7,5},{8,10},{9,11},{10,... | collective-permute-start | bytes 1544 | tf_op jit(solution)/shard_map/ppermute | solution.py:71
  133.6 2.6 %collective-permute-start.38 = (f32[1,128]{1,0:T(1,128)S(1)}, f32[1,128]{1,0:T(1,128)S(1)}, u32[]{:S(2)}, u32[]{:S(2)}) collective-permute-start(f32[1,128]{1,0:T(1,128)S(1)} %add_add_fusion.3), channel_id=1, source_target_pairs={{0,24},{1,25},{2,26},{3,27},{4,28},{5,29},{6,30},{7,31},{8,16},{9,... | collective-permute-start | bytes 1544 | tf_op jit(solution)/shard_map/ppermute | solution.py:71
  138.9 1.7 %collective-permute-done.37 = f32[1,128]{1,0:T(1,128)S(1)} collective-permute-done((f32[1,128]{1,0:T(1,128)S(1)}, f32[1,128]{1,0:T(1,128)S(1)}, u32[]{:S(2)}, u32[]{:S(2)}) %collective-permute-start.37) | collective-permute-done | bytes 544 | tf_op jit(solution)/shard_map/ppermute | solution.py:71
  141.2 6.3 %shard_map.64 = (f32[16,128]{1,0:T(8,128)}, f32[16,128]{1,0:T(8,128)}) custom-call(f32[2,128]{1,0:T(2,128)} %add_add_fusion.refs_0_.refs_1_, f32[2,128]{1,0:T(2,128)} %add_add_fusion.refs_0_.refs_1_, f32[1,128]{1,0:T(1,128)} %add_add_fusion.8.refs_0_.refs_1_.refs_2_, f32[1,128]{1,0:T(1,128)} %add_add_fusion.6.refs_1_.refs_3_, ...), custom_call_target="tpu_custom_call" | custom-call | flops 11468800 | bytes 20643840 | tf_op jit(solution)/shard_map/pallas_call | solution.py:307
  (100 shorter events, 50.9 us)
Async XLA Ops:
  3.3 15.8 %collective-permute-start.1 = (f32[536,128]{1,0:T(8,128)S(1)}, f32[536,128]{1,0:T(8,128)}, u32[]{:S(2)}, u32[]{:S(2)}) collective-permute-start(f32[536,128]{1,0:T(8,128)S(1)} %maximum_bitcast_fusion.2), channel_id=1, source_target_pairs={{4,0},{8,4},{12,8},{16,12},{20,16},{24,20},{28,24},{5,1},{9,5},{13... | collective-permute-start | bytes 823304 | tf_op jit(solution)/shard_map/ppermute | solution.py:345
  5.3 15.5 %collective-permute-start = (f32[536,128]{1,0:T(8,128)}, f32[536,128]{1,0:T(8,128)}, u32[]{:S(2)}, u32[]{:S(2)}) collective-permute-start(f32[536,128]{1,0:T(8,128)} %maximum_bitcast_fusion.1), channel_id=1, source_target_pairs={{0,4},{4,8},{8,12},{12,16},{16,20},{20,24},{24,28},{1,5},{5,9},{9,... | collective-permute-start | bytes 823304 | tf_op jit(solution)/shard_map/ppermute | solution.py:342
  22.1 3.8 %collective-permute-start.2 = (f32[28,6,67]{2,1,0:T(8,128)S(1)}, f32[28,6,67]{2,1,0:T(8,128)S(1)}, u32[]{:S(2)}, u32[]{:S(2)}) collective-permute-start(f32[28,6,67]{2,1,0:T(8,128)S(1)} %get-tuple-element.34), channel_id=1, source_target_pairs={{0,1},{1,2},{2,3},{4,5},{5,6},{6,7},{8,9},{9,10},{10,11},{12,13},{... | collective-permute-start | bytes 135080 | tf_op jit(solution)/shard_map/ppermute | solution.py:20
  24.0 4.3 %collective-permute-start.3 = (f32[28,6,67]{2,1,0:T(8,128)S(1)}, f32[28,6,67]{2,1,0:T(8,128)S(1)}, u32[]{:S(2)}, u32[]{:S(2)}) collective-permute-start(f32[28,6,67]{2,1,0:T(8,128)S(1)} %get-tuple-element.35), channel_id=1, source_target_pairs={{1,0},{2,1},{3,2},{5,4},{6,5},{7,6},{9,8},{10,9},{11,10},{13,12},{... | collective-permute-start | bytes 135080 | tf_op jit(solution)/shard_map/ppermute | solution.py:22
  41.5 4.4 %collective-permute-start.4 = (f32[2,128]{1,0:T(2,128)}, f32[2,128]{1,0:T(2,128)S(1)}, u32[]{:S(2)}, u32[]{:S(2)}) collective-permute-start(f32[2,128]{1,0:T(2,128)} %get-tuple-element.18), channel_id=1, source_target_pairs={{0,1},{1,0},{2,3},{3,2},{4,5},{5,4},{6,7},{7,6},{8,9},{9,8},{10,11... | collective-permute-start | bytes 3080 | tf_op jit(solution)/shard_map/ppermute | solution.py:71
  46.6 4.5 %collective-permute-start.7 = (f32[2,128]{1,0:T(2,128)S(1)}, f32[2,128]{1,0:T(2,128)S(1)}, u32[]{:S(2)}, u32[]{:S(2)}) collective-permute-start(f32[2,128]{1,0:T(2,128)S(1)} %add.174), channel_id=1, source_target_pairs={{0,6},{1,7},{2,4},{3,5},{4,2},{5,3},{6,0},{7,1},{8,14},{9,15},{10,... | collective-permute-start | bytes 3080 | tf_op jit(solution)/shard_map/ppermute | solution.py:71
  48.7 3.6 %collective-permute-start.6 = (f32[2,128]{1,0:T(2,128)S(1)}, f32[2,128]{1,0:T(2,128)S(1)}, u32[]{:S(2)}, u32[]{:S(2)}) collective-permute-start(f32[2,128]{1,0:T(2,128)S(1)} %add.174), channel_id=1, source_target_pairs={{0,4},{1,5},{2,6},{3,7},{4,0},{5,1},{6,2},{7,3},{8,12},{9,13},{10,... | collective-permute-start | bytes 3080 | tf_op jit(solution)/shard_map/ppermute | solution.py:71
  49.1 3.6 %collective-permute-start.5 = (f32[2,128]{1,0:T(2,128)S(1)}, f32[2,128]{1,0:T(2,128)S(1)}, u32[]{:S(2)}, u32[]{:S(2)}) collective-permute-start(f32[2,128]{1,0:T(2,128)S(1)} %add.174), channel_id=1, source_target_pairs={{0,2},{1,3},{2,0},{3,1},{4,6},{5,7},{6,4},{7,5},{8,10},{9,11},{10,... | collective-permute-start | bytes 3080 | tf_op jit(solution)/shard_map/ppermute | solution.py:71
  52.7 5.5 %collective-permute-start.10 = (f32[2,128]{1,0:T(2,128)S(1)}, f32[2,128]{1,0:T(2,128)S(1)}, u32[]{:S(2)}, u32[]{:S(2)}) collective-permute-start(f32[2,128]{1,0:T(2,128)S(1)} %add_add_fusion.1), channel_id=1, source_target_pairs={{0,24},{1,25},{2,26},{3,27},{4,28},{5,29},{6,30},{7,31},{8,16},{9,... | collective-permute-start | bytes 3080 | tf_op jit(solution)/shard_map/ppermute | solution.py:71
  56.6 4.5 %collective-permute-start.9 = (f32[2,128]{1,0:T(2,128)S(1)}, f32[2,128]{1,0:T(2,128)S(1)}, u32[]{:S(2)}, u32[]{:S(2)}) collective-permute-start(f32[2,128]{1,0:T(2,128)S(1)} %add_add_fusion.1), channel_id=1, source_target_pairs={{0,16},{1,17},{2,18},{3,19},{4,20},{5,21},{6,22},{7,23},{8,24},{9,... | collective-permute-start | bytes 3080 | tf_op jit(solution)/shard_map/ppermute | solution.py:71
  56.6 4.5 %collective-permute-start.8 = (f32[2,128]{1,0:T(2,128)S(1)}, f32[2,128]{1,0:T(2,128)S(1)}, u32[]{:S(2)}, u32[]{:S(2)}) collective-permute-start(f32[2,128]{1,0:T(2,128)S(1)} %add_add_fusion.1), channel_id=1, source_target_pairs={{0,8},{1,9},{2,10},{3,11},{4,12},{5,13},{6,14},{7,15},{8,0},{9,1},... | collective-permute-start | bytes 3080 | tf_op jit(solution)/shard_map/ppermute | solution.py:71
  67.0 4.5 %collective-permute-start.14 = (f32[1,128]{1,0:T(1,128)S(1)}, f32[1,128]{1,0:T(1,128)S(1)}, u32[]{:S(2)}, u32[]{:S(2)}) collective-permute-start(f32[1,128]{1,0:T(1,128)S(1)} %add.181), channel_id=1, source_target_pairs={{0,6},{1,7},{2,4},{3,5},{4,2},{5,3},{6,0},{7,1},{8,14},{9,15},{10,... | collective-permute-start | bytes 1544 | tf_op jit(solution)/shard_map/ppermute | solution.py:71
  68.4 3.6 %collective-permute-start.13 = (f32[1,128]{1,0:T(1,128)S(1)}, f32[1,128]{1,0:T(1,128)S(1)}, u32[]{:S(2)}, u32[]{:S(2)}) collective-permute-start(f32[1,128]{1,0:T(1,128)S(1)} %add.181), channel_id=1, source_target_pairs={{0,4},{1,5},{2,6},{3,7},{4,0},{5,1},{6,2},{7,3},{8,12},{9,13},{10,... | collective-permute-start | bytes 1544 | tf_op jit(solution)/shard_map/ppermute | solution.py:71
  70.4 3.6 %collective-permute-start.12 = (f32[1,128]{1,0:T(1,128)S(1)}, f32[1,128]{1,0:T(1,128)S(1)}, u32[]{:S(2)}, u32[]{:S(2)}) collective-permute-start(f32[1,128]{1,0:T(1,128)S(1)} %add.181), channel_id=1, source_target_pairs={{0,2},{1,3},{2,0},{3,1},{4,6},{5,7},{6,4},{7,5},{8,10},{9,11},{10,... | collective-permute-start | bytes 1544 | tf_op jit(solution)/shard_map/ppermute | solution.py:71
  73.9 5.4 %collective-permute-start.17 = (f32[1,128]{1,0:T(1,128)S(1)}, f32[1,128]{1,0:T(1,128)S(1)}, u32[]{:S(2)}, u32[]{:S(2)}) collective-permute-start(f32[1,128]{1,0:T(1,128)S(1)} %add_add_fusion.9), channel_id=1, source_target_pairs={{0,24},{1,25},{2,26},{3,27},{4,28},{5,29},{6,30},{7,31},{8,16},{9,... | collective-permute-start | bytes 1544 | tf_op jit(solution)/shard_map/ppermute | solution.py:71
  75.4 4.5 %collective-permute-start.16 = (f32[1,128]{1,0:T(1,128)S(1)}, f32[1,128]{1,0:T(1,128)S(1)}, u32[]{:S(2)}, u32[]{:S(2)}) collective-permute-start(f32[1,128]{1,0:T(1,128)S(1)} %add_add_fusion.9), channel_id=1, source_target_pairs={{0,16},{1,17},{2,18},{3,19},{4,20},{5,21},{6,22},{7,23},{8,24},{9,... | collective-permute-start | bytes 1544 | tf_op jit(solution)/shard_map/ppermute | solution.py:71
  76.0 3.8 %collective-permute-start.15 = (f32[1,128]{1,0:T(1,128)S(1)}, f32[1,128]{1,0:T(1,128)S(1)}, u32[]{:S(2)}, u32[]{:S(2)}) collective-permute-start(f32[1,128]{1,0:T(1,128)S(1)} %add_add_fusion.9), channel_id=1, source_target_pairs={{0,8},{1,9},{2,10},{3,11},{4,12},{5,13},{6,14},{7,15},{8,0},{9,1},... | collective-permute-start | bytes 1544 | tf_op jit(solution)/shard_map/ppermute | solution.py:71
  88.6 4.5 %collective-permute-start.21 = (f32[1,128]{1,0:T(1,128)S(1)}, f32[1,128]{1,0:T(1,128)S(1)}, u32[]{:S(2)}, u32[]{:S(2)}) collective-permute-start(f32[1,128]{1,0:T(1,128)S(1)} %add.188), channel_id=1, source_target_pairs={{0,6},{1,7},{2,4},{3,5},{4,2},{5,3},{6,0},{7,1},{8,14},{9,15},{10,... | collective-permute-start | bytes 1544 | tf_op jit(solution)/shard_map/ppermute | solution.py:71
  89.0 4.1 %collective-permute-start.20 = (f32[1,128]{1,0:T(1,128)S(1)}, f32[1,128]{1,0:T(1,128)S(1)}, u32[]{:S(2)}, u32[]{:S(2)}) collective-permute-start(f32[1,128]{1,0:T(1,128)S(1)} %add.188), channel_id=1, source_target_pairs={{0,4},{1,5},{2,6},{3,7},{4,0},{5,1},{6,2},{7,3},{8,12},{9,13},{10,... | collective-permute-start | bytes 1544 | tf_op jit(solution)/shard_map/ppermute | solution.py:71
  90.2 3.6 %collective-permute-start.19 = (f32[1,128]{1,0:T(1,128)S(1)}, f32[1,128]{1,0:T(1,128)S(1)}, u32[]{:S(2)}, u32[]{:S(2)}) collective-permute-start(f32[1,128]{1,0:T(1,128)S(1)} %add.188), channel_id=1, source_target_pairs={{0,2},{1,3},{2,0},{3,1},{4,6},{5,7},{6,4},{7,5},{8,10},{9,11},{10,... | collective-permute-start | bytes 1544 | tf_op jit(solution)/shard_map/ppermute | solution.py:71
  93.8 5.4 %collective-permute-start.24 = (f32[1,128]{1,0:T(1,128)S(1)}, f32[1,128]{1,0:T(1,128)S(1)}, u32[]{:S(2)}, u32[]{:S(2)}) collective-permute-start(f32[1,128]{1,0:T(1,128)S(1)} %add_add_fusion.7), channel_id=1, source_target_pairs={{0,24},{1,25},{2,26},{3,27},{4,28},{5,29},{6,30},{7,31},{8,16},{9,... | collective-permute-start | bytes 1544 | tf_op jit(solution)/shard_map/ppermute | solution.py:71
  96.4 4.5 %collective-permute-start.23 = (f32[1,128]{1,0:T(1,128)S(1)}, f32[1,128]{1,0:T(1,128)S(1)}, u32[]{:S(2)}, u32[]{:S(2)}) collective-permute-start(f32[1,128]{1,0:T(1,128)S(1)} %add_add_fusion.7), channel_id=1, source_target_pairs={{0,16},{1,17},{2,18},{3,19},{4,20},{5,21},{6,22},{7,23},{8,24},{9,... | collective-permute-start | bytes 1544 | tf_op jit(solution)/shard_map/ppermute | solution.py:71
  97.3 3.6 %collective-permute-start.22 = (f32[1,128]{1,0:T(1,128)S(1)}, f32[1,128]{1,0:T(1,128)S(1)}, u32[]{:S(2)}, u32[]{:S(2)}) collective-permute-start(f32[1,128]{1,0:T(1,128)S(1)} %add_add_fusion.7), channel_id=1, source_target_pairs={{0,8},{1,9},{2,10},{3,11},{4,12},{5,13},{6,14},{7,15},{8,0},{9,1},... | collective-permute-start | bytes 1544 | tf_op jit(solution)/shard_map/ppermute | solution.py:71
  106.8 4.5 %collective-permute-start.28 = (f32[1,128]{1,0:T(1,128)S(1)}, f32[1,128]{1,0:T(1,128)S(1)}, u32[]{:S(2)}, u32[]{:S(2)}) collective-permute-start(f32[1,128]{1,0:T(1,128)S(1)} %add.195), channel_id=1, source_target_pairs={{0,6},{1,7},{2,4},{3,5},{4,2},{5,3},{6,0},{7,1},{8,14},{9,15},{10,... | collective-permute-start | bytes 1544 | tf_op jit(solution)/shard_map/ppermute | solution.py:71
  110.2 3.6 %collective-permute-start.26 = (f32[1,128]{1,0:T(1,128)S(1)}, f32[1,128]{1,0:T(1,128)S(1)}, u32[]{:S(2)}, u32[]{:S(2)}) collective-permute-start(f32[1,128]{1,0:T(1,128)S(1)} %add.195), channel_id=1, source_target_pairs={{0,2},{1,3},{2,0},{3,1},{4,6},{5,7},{6,4},{7,5},{8,10},{9,11},{10,... | collective-permute-start | bytes 1544 | tf_op jit(solution)/shard_map/ppermute | solution.py:71
  113.7 5.4 %collective-permute-start.31 = (f32[1,128]{1,0:T(1,128)S(1)}, f32[1,128]{1,0:T(1,128)S(1)}, u32[]{:S(2)}, u32[]{:S(2)}) collective-permute-start(f32[1,128]{1,0:T(1,128)S(1)} %add_add_fusion.5), channel_id=1, source_target_pairs={{0,24},{1,25},{2,26},{3,27},{4,28},{5,29},{6,30},{7,31},{8,16},{9,... | collective-permute-start | bytes 1544 | tf_op jit(solution)/shard_map/ppermute | solution.py:71
  115.2 4.5 %collective-permute-start.30 = (f32[1,128]{1,0:T(1,128)S(1)}, f32[1,128]{1,0:T(1,128)S(1)}, u32[]{:S(2)}, u32[]{:S(2)}) collective-permute-start(f32[1,128]{1,0:T(1,128)S(1)} %add_add_fusion.5), channel_id=1, source_target_pairs={{0,16},{1,17},{2,18},{3,19},{4,20},{5,21},{6,22},{7,23},{8,24},{9,... | collective-permute-start | bytes 1544 | tf_op jit(solution)/shard_map/ppermute | solution.py:71
  116.1 3.6 %collective-permute-start.29 = (f32[1,128]{1,0:T(1,128)S(1)}, f32[1,128]{1,0:T(1,128)S(1)}, u32[]{:S(2)}, u32[]{:S(2)}) collective-permute-start(f32[1,128]{1,0:T(1,128)S(1)} %add_add_fusion.5), channel_id=1, source_target_pairs={{0,8},{1,9},{2,10},{3,11},{4,12},{5,13},{6,14},{7,15},{8,0},{9,1},... | collective-permute-start | bytes 1544 | tf_op jit(solution)/shard_map/ppermute | solution.py:71
  128.4 4.5 %collective-permute-start.35 = (f32[1,128]{1,0:T(1,128)S(1)}, f32[1,128]{1,0:T(1,128)S(1)}, u32[]{:S(2)}, u32[]{:S(2)}) collective-permute-start(f32[1,128]{1,0:T(1,128)S(1)} %add.202), channel_id=1, source_target_pairs={{0,6},{1,7},{2,4},{3,5},{4,2},{5,3},{6,0},{7,1},{8,14},{9,15},{10,... | collective-permute-start | bytes 1544 | tf_op jit(solution)/shard_map/ppermute | solution.py:71
  128.8 4.1 %collective-permute-start.34 = (f32[1,128]{1,0:T(1,128)S(1)}, f32[1,128]{1,0:T(1,128)S(1)}, u32[]{:S(2)}, u32[]{:S(2)}) collective-permute-start(f32[1,128]{1,0:T(1,128)S(1)} %add.202), channel_id=1, source_target_pairs={{0,4},{1,5},{2,6},{3,7},{4,0},{5,1},{6,2},{7,3},{8,12},{9,13},{10,... | collective-permute-start | bytes 1544 | tf_op jit(solution)/shard_map/ppermute | solution.py:71
  133.6 5.4 %collective-permute-start.38 = (f32[1,128]{1,0:T(1,128)S(1)}, f32[1,128]{1,0:T(1,128)S(1)}, u32[]{:S(2)}, u32[]{:S(2)}) collective-permute-start(f32[1,128]{1,0:T(1,128)S(1)} %add_add_fusion.3), channel_id=1, source_target_pairs={{0,24},{1,25},{2,26},{3,27},{4,28},{5,29},{6,30},{7,31},{8,16},{9,... | collective-permute-start | bytes 1544 | tf_op jit(solution)/shard_map/ppermute | solution.py:71
  136.1 4.5 %collective-permute-start.37 = (f32[1,128]{1,0:T(1,128)S(1)}, f32[1,128]{1,0:T(1,128)S(1)}, u32[]{:S(2)}, u32[]{:S(2)}) collective-permute-start(f32[1,128]{1,0:T(1,128)S(1)} %add_add_fusion.3), channel_id=1, source_target_pairs={{0,16},{1,17},{2,18},{3,19},{4,20},{5,21},{6,22},{7,23},{8,24},{9,... | collective-permute-start | bytes 1544 | tf_op jit(solution)/shard_map/ppermute | solution.py:71
  (11 other events, 57.0 us)

commit v12 on v11

--- a/solution.py
+++ b/solution.py
@@ -202,31 +202,65 @@
     lax.fori_loop(0, plan.inner_rows, observed_pass, 0)
 
 
+def _accumulate(rr_out, totals):
+    @pl.when(pl.program_id(0) == 0)
+    def _():
+        rr_out[...] = jnp.zeros_like(rr_out)
+
+    rr_out[...] = rr_out[...] + totals
+
+
 def _start_kernel(plan, first_ref, z_ref, applied_ref, inner_ref, residual_out, rr_out):
     step = _ratio(first_ref, 0, first_ref, 1)
+    base = pl.program_id(0) * z_ref.shape[0]
 
     def body(r, totals):
         residual = z_ref[r] - step * applied_ref[r]
         residual_out[r] = residual
-        inner = (inner_ref[...] > 0.5) & plan.inner_row(r)
+        inner = (inner_ref[...] > 0.5) & plan.inner_row(base + r)
         return totals + _row_sum(residual * residual, inner)
 
-    rr_out[...] = lax.fori_loop(0, plan.slab_rows, body, jnp.zeros((1, z_ref.shape[2]), jnp.float32))
+    _accumulate(rr_out, lax.fori_loop(0, z_ref.shape[0], body, jnp.zeros((1, z_ref.shape[2]), jnp.float32)))
 
 
 def _update_kernel(plan, norm_ref, curvature_ref, residual_ref, applied_ref, inner_ref,
                    residual_out, rr_out):
     step = _ratio(norm_ref, 0, curvature_ref, 0)
+    base = pl.program_id(0) * residual_ref.shape[0]
 
     def body(r, totals):
         residual = residual_ref[r] - step * applied_ref[r]
         residual_out[r] = residual
-        inner = (inner_ref[...] > 0.5) & plan.inner_row(r)
+        inner = (inner_ref[...] > 0.5) & plan.inner_row(base + r)
         return totals + _row_sum(residual * residual, inner)
 
-    rr_out[...] = lax.fori_loop(
-        0, plan.slab_rows, body, jnp.zeros((1, residual_ref.shape[2]), jnp.float32)
-    )
+    _accumulate(rr_out, lax.fori_loop(
+        0, residual_ref.shape[0], body, jnp.zeros((1, residual_ref.shape[2]), jnp.float32)
+    ))
+
+
+def _row_call(kernel, plan, inputs, fields, out_shapes):
+    field = out_shapes[0]
+    block = max(d for d in range(1, 9) if field.shape[0] % d == 0)
+    nbytes = 4 * field.shape[0] * field.shape[1] * field.shape[2]
+
+    def spec(value, is_field):
+        if is_field:
+            return pl.BlockSpec((block,) + value.shape[1:], lambda g: (g, 0, 0))
+        return pl.BlockSpec(value.shape, lambda g: (0,) * len(value.shape))
+
+    return pl.pallas_call(
+        lambda *refs: kernel(plan, *refs),
+        out_shape=out_shapes,
+        grid=(field.shape[0] // block,),
+        in_specs=[spec(v, i in fields) for i, v in enumerate(inputs)],
+        out_specs=tuple(spec(o, len(o.shape) == 3) for o in out_shapes),
+        compiler_params=pltpu.CompilerParams(dimension_semantics=("arbitrary",)),
+        cost_estimate=pl.CostEstimate(
+            flops=4 * nbytes // 4, transcendentals=0,
+            bytes_accessed=(len(fields) + 1) * nbytes,
+        ),
+    )(*inputs)
 
 
 def _direction_kernel(plan, next_ref, now_ref, residual_ref, direction_ref, gain_ref, weight_ref,
@@ -384,7 +418,7 @@
         scratch=2, smem=(2,),
     )
     first = all_sum(first)
-    residual, rr = _call(_start_kernel, plan, (first, z, applied, inner), (field, lane_row))
+    residual, rr = _row_call(_start_kernel, plan, (first, z, applied, inner), (1, 2), (field, lane_row))
     directions = [z]
     ratios = [first, first]
     direction = z
@@ -401,8 +435,8 @@
         directions.append(direction)
         ratios += [norm_now, curvature]
         if iteration + 1 < ITERS:
-            residual, rr = _call(
-                _update_kernel, plan, (norm_now, curvature, residual, applied, inner),
+            residual, rr = _row_call(
+                _update_kernel, plan, (norm_now, curvature, residual, applied, inner), (2, 3),
                 (field, lane_row),
             )
 

time: 148 us -> 149 us (level)
    pallas_call x0 -> x2, Pallas kernels: none -> 8.16 us  [_row_call(): pl.pallas_call(lambda *refs: kernel(plan, *refs), out_shape=out_shapes, g...]
    pallas_call x6 -> x4, Pallas kernels: 36.8 us -> 30 us  [_call(): pl.pallas_call(lambda *refs: kernel(plan, *refs), out_shape=out_shapes, i...]
where the time goes in v12:
time: 149 us
  starting transfers between devices  54.1 us (36%)
  Pallas kernels  38.1 us (26%)
  waiting for transfers between devices  33.9 us (23%)
  other arithmetic  13.2 us (9%)
  local copies, waits for them, and re-layouts  8.58 us (6%)
    ppermute x35, starting transfers between devices, partner(): lax.ppermute(terms, axes, [(i, i ^ mask) for i in range(count)])  43.4 us
    ppermute x35, waiting for transfers between devices, partner(): lax.ppermute(terms, axes, [(i, i ^ mask) for i in range(count)])  30.8 us
    pallas_call x4, Pallas kernels, _call(): pl.pallas_call(lambda *refs: kernel(plan, *refs), out_shape=out_shapes, i...  30 us
    pallas_call x2, Pallas kernels, _row_call(): pl.pallas_call(lambda *refs: kernel(plan, *refs), out_shape=out_shapes, g...  8.16 us
    ppermute x1, starting transfers between devices, on_device(): lax.ppermute(edge_rows(rows - sent), 'rows', [(i, i + 1) for i in range(c...  6.21 us
    add x15, other arithmetic, _span_sum(): _span_sum(terms, rest, partner)  6.15 us
    broadcast_in_dim x3, local copies, waits for them, and re-layouts, on_device(): fields = (probes, observed[None], kappa_sq[None], variance_weight[None])  3.09 us
  transfers between devices with their start and end apart: 39, of which 30 were waited for; matrix products, arithmetic and copies ran while one was open for 7% of the time, Pallas kernels for 0%

profile of v12, /device:TPU:0, one launch (start us, length us, event | category | flops | bytes accessed | tf_op | source)
XLA Modules:
  0.0 148.8 jit_solution(15107480288283899012)
XLA Ops:
  5.3 6.2 %collective-permute-start = (f32[536,128]{1,0:T(8,128)}, f32[536,128]{1,0:T(8,128)}, u32[]{:S(2)}, u32[]{:S(2)}) collective-permute-start(f32[536,128]{1,0:T(8,128)} %maximum_bitcast_fusion.1), channel_id=1, source_target_pairs={{0,4},{4,8},{8,12},{12,16},{16,20},{20,24},{24,28},{1,5},{5,9},{9,... | collective-permute-start | bytes 823304 | tf_op jit(solution)/shard_map/ppermute | solution.py:376
  15.8 2.4 %maximum_bitcast_fusion = f32[16,128,67]{2,1,0:T(8,128)S(1)} fusion(f32[1,16,128]{0,2,1:T(8,128)} %copy.17, f32[1,16,128]{0,2,1:T(8,128)S(1)} %copy.16, f32[1,16,128]{0,2,1:T(8,128)} %copy.15, f32[64,16,128]{0,2,1:T(8,128)S(1)} %copy.14), kind=kLoop, calls=%fused_computation.13 | loop fusion | flops 411648 | bytes 1097728 | tf_op jit(solution)/shard_map/transpose | solution.py:383
  22.1 1.9 %collective-permute-start.2 = (f32[28,6,67]{2,1,0:T(8,128)S(1)}, f32[28,6,67]{2,1,0:T(8,128)S(1)}, u32[]{:S(2)}, u32[]{:S(2)}) collective-permute-start(f32[28,6,67]{2,1,0:T(8,128)S(1)} %get-tuple-element.34), channel_id=1, source_target_pairs={{0,1},{1,2},{2,3},{4,5},{5,6},{6,7},{8,9},{9,10},{10,11},{12,13},{... | collective-permute-start | bytes 135080 | tf_op jit(solution)/shard_map/ppermute | solution.py:20
  25.8 2.5 %collective-permute-done.3 = f32[28,6,67]{2,1,0:T(8,128)S(1)} collective-permute-done((f32[28,6,67]{2,1,0:T(8,128)S(1)}, f32[28,6,67]{2,1,0:T(8,128)S(1)}, u32[]{:S(2)}, u32[]{:S(2)}) %collective-permute-start.3) | collective-permute-done | bytes 45056 | tf_op jit(solution)/shard_map/ppermute | solution.py:22
  28.3 1.9 %select_maximum_fusion.refs_0_ = f32[28,144,128]{2,1,0:T(8,128)} fusion(f32[28,6,67]{2,1,0:T(8,128)S(1)} %collective-permute-done.3, f32[28,6,67]{2,1,0:T(8,128)S(1)} %collective-permute-done.2, f32[6,128,67]{2,1,0:T(8,128)S(1)} %bitcast.15, f32[16,128,67]{2,1,0:T(8,128)S(1)} %maximum_bitcast_fusion, f32[6,128,67]{2,1,0:T(8,128)S(1)} %bitcast.17), kind=kLoop, calls=%fused_computation | loop fusion | flops 8773632 | bytes 3114944 | tf_op jit(solution)/shard_map/concatenate | solution.py:18
  30.3 11.2 %shard_map.59 = (f32[28,80,128]{2,1,0:T(8,128)}, f32[28,80,128]{2,1,0:T(8,128)}, f32[28,80,128]{2,1,0:T(8,128)}, f32[28,80,128]{2,1,0:T(8,128)}, f32[28,80,128]{...) custom-call(f32[28,144,128]{2,1,0:T(8,128)} %select_maximum_fusion.refs_0_, ...), custom_call_target="tpu_custom_call" | custom-call | flops 11468800 | bytes 13762560 | tf_op jit(solution)/shard_map/pallas_call | solution.py:341
  41.5 3.4 %collective-permute-start.4 = (f32[2,128]{1,0:T(2,128)}, f32[2,128]{1,0:T(2,128)S(1)}, u32[]{:S(2)}, u32[]{:S(2)}) collective-permute-start(f32[2,128]{1,0:T(2,128)} %get-tuple-element.18), channel_id=1, source_target_pairs={{0,1},{1,0},{2,3},{3,2},{4,5},{5,4},{6,7},{7,6},{8,9},{9,8},{10,11... | collective-permute-start | bytes 3080 | tf_op jit(solution)/shard_map/ppermute | solution.py:71
  46.6 2.0 %collective-permute-start.7 = (f32[2,128]{1,0:T(2,128)S(1)}, f32[2,128]{1,0:T(2,128)S(1)}, u32[]{:S(2)}, u32[]{:S(2)}) collective-permute-start(f32[2,128]{1,0:T(2,128)S(1)} %add.174), channel_id=1, source_target_pairs={{0,6},{1,7},{2,4},{3,5},{4,2},{5,3},{6,0},{7,1},{8,14},{9,15},{10,... | collective-permute-start | bytes 3080 | tf_op jit(solution)/shard_map/ppermute | solution.py:71
  49.1 1.5 collective-permute-start.5
  52.7 3.9 %collective-permute-start.10 = (f32[2,128]{1,0:T(2,128)S(1)}, f32[2,128]{1,0:T(2,128)S(1)}, u32[]{:S(2)}, u32[]{:S(2)}) collective-permute-start(f32[2,128]{1,0:T(2,128)S(1)} %add_add_fusion.1), channel_id=1, source_target_pairs={{0,24},{1,25},{2,26},{3,27},{4,28},{5,29},{6,30},{7,31},{8,16},{9,... | collective-permute-start | bytes 3080 | tf_op jit(solution)/shard_map/ppermute | solution.py:71
  58.2 2.9 %collective-permute-done.9 = f32[2,128]{1,0:T(2,128)S(1)} collective-permute-done((f32[2,128]{1,0:T(2,128)S(1)}, f32[2,128]{1,0:T(2,128)S(1)}, u32[]{:S(2)}, u32[]{:S(2)}) %collective-permute-start.9) | collective-permute-done | bytes 1056 | tf_op jit(solution)/shard_map/ppermute | solution.py:71
  61.7 4.1 %shard_map.60 = (f32[28,80,128]{2,1,0:T(8,128)}, f32[1,128]{1,0:T(1,128)}) custom-call(f32[2,128]{1,0:T(2,128)} %add_add_fusion.refs_0_.refs_1_, f32[28,80,128]{2,1,0:T(8,128)} %get-tuple-element.19.refs_1_.refs_3_.refs_6_.refs_9_, f32[28,80,128]{2,1,0:T(8,128)} %get-tuple-element.20.refs_2_, f32[80,128]{1,0:T(8,128)} %add_convert_fusion.1.refs_3_.refs_8_.refs_4_), custom_call_target="tpu_custom_call" | custom-call | flops 1146880 | bytes 3440640 | tf_op jit(solution)/shard_map/pallas_call | solution.py:252
  67.7 1.4 collective-permute-start.14
  69.1 2.0 %collective-permute-start.13 = (f32[1,128]{1,0:T(1,128)S(1)}, f32[1,128]{1,0:T(1,128)S(1)}, u32[]{:S(2)}, u32[]{:S(2)}) collective-permute-start(f32[1,128]{1,0:T(1,128)S(1)} %add.181), channel_id=1, source_target_pairs={{0,4},{1,5},{2,6},{3,7},{4,0},{5,1},{6,2},{7,3},{8,12},{9,13},{10,... | collective-permute-start | bytes 1544 | tf_op jit(solution)/shard_map/ppermute | solution.py:71
  72.7 2.0 %collective-permute-done.12 = f32[1,128]{1,0:T(1,128)S(1)} collective-permute-done((f32[1,128]{1,0:T(1,128)S(1)}, f32[1,128]{1,0:T(1,128)S(1)}, u32[]{:S(2)}, u32[]{:S(2)}) %collective-permute-start.12) | collective-permute-done | bytes 544 | tf_op jit(solution)/shard_map/ppermute | solution.py:71
  74.7 1.5 collective-permute-start.17
  76.8 2.3 %collective-permute-start.15 = (f32[1,128]{1,0:T(1,128)S(1)}, f32[1,128]{1,0:T(1,128)S(1)}, u32[]{:S(2)}, u32[]{:S(2)}) collective-permute-start(f32[1,128]{1,0:T(1,128)S(1)} %add_add_fusion.9), channel_id=1, source_target_pairs={{0,8},{1,9},{2,10},{3,11},{4,12},{5,13},{6,14},{7,15},{8,0},{9,1},... | collective-permute-start | bytes 1544 | tf_op jit(solution)/shard_map/ppermute | solution.py:71
  81.1 6.2 %shard_map.61 = (f32[28,80,128]{2,1,0:T(8,128)}, f32[28,80,128]{2,1,0:T(8,128)}, f32[1,128]{1,0:T(1,128)}) custom-call(f32[1,128]{1,0:T(1,128)} %add_add_fusion.8.refs_0_.refs_1_.refs_2_, f32[2,128]{1,0:T(2,128)} %add_add_fusion.refs_0_.refs_1_, f32[28,80,128]{2,1,0:T(8,128)} %get-tuple-element.22.refs_2_, ...), custom_call_target="tpu_custom_call" | custom-call | flops 11468800 | bytes 13762560 | tf_op jit(solution)/shard_map/pallas_call | solution.py:341
  90.9 1.9 %collective-permute-start.19 = (f32[1,128]{1,0:T(1,128)S(1)}, f32[1,128]{1,0:T(1,128)S(1)}, u32[]{:S(2)}, u32[]{:S(2)}) collective-permute-start(f32[1,128]{1,0:T(1,128)S(1)} %add.188), channel_id=1, source_target_pairs={{0,2},{1,3},{2,0},{3,1},{4,6},{5,7},{6,4},{7,5},{8,10},{9,11},{10,... | collective-permute-start | bytes 1544 | tf_op jit(solution)/shard_map/ppermute | solution.py:71
  94.5 2.6 %collective-permute-start.24 = (f32[1,128]{1,0:T(1,128)S(1)}, f32[1,128]{1,0:T(1,128)S(1)}, u32[]{:S(2)}, u32[]{:S(2)}) collective-permute-start(f32[1,128]{1,0:T(1,128)S(1)} %add_add_fusion.7), channel_id=1, source_target_pairs={{0,24},{1,25},{2,26},{3,27},{4,28},{5,29},{6,30},{7,31},{8,16},{9,... | collective-permute-start | bytes 1544 | tf_op jit(solution)/shard_map/ppermute | solution.py:71
  99.9 1.7 %collective-permute-done.23 = f32[1,128]{1,0:T(1,128)S(1)} collective-permute-done((f32[1,128]{1,0:T(1,128)S(1)}, f32[1,128]{1,0:T(1,128)S(1)}, u32[]{:S(2)}, u32[]{:S(2)}) %collective-permute-start.23) | collective-permute-done | bytes 544 | tf_op jit(solution)/shard_map/ppermute | solution.py:71
  102.1 4.1 %shard_map.62 = (f32[28,80,128]{2,1,0:T(8,128)}, f32[1,128]{1,0:T(1,128)}) custom-call(f32[1,128]{1,0:T(1,128)} %add_add_fusion.8.refs_0_.refs_1_.refs_2_, f32[1,128]{1,0:T(1,128)} %add_add_fusion.6.refs_1_.refs_3_, f32[28,80,128]{2,1,0:T(8,128)} %get-tuple-element.22.refs_2_, f32[28,80,128]{2,1,0:T(8,128)} %get-tuple-element.26.refs_3_, ...), custom_call_target="tpu_custom_call" | custom-call | flops 1146880 | bytes 3440640 | tf_op jit(solution)/shard_map/pallas_call | solution.py:252
  108.1 1.4 collective-permute-start.28
  109.5 2.0 %collective-permute-start.27 = (f32[1,128]{1,0:T(1,128)S(1)}, f32[1,128]{1,0:T(1,128)S(1)}, u32[]{:S(2)}, u32[]{:S(2)}) collective-permute-start(f32[1,128]{1,0:T(1,128)S(1)} %add.195), channel_id=1, source_target_pairs={{0,4},{1,5},{2,6},{3,7},{4,0},{5,1},{6,2},{7,3},{8,12},{9,13},{10,... | collective-permute-start | bytes 1544 | tf_op jit(solution)/shard_map/ppermute | solution.py:71
  113.1 2.0 %collective-permute-done.26 = f32[1,128]{1,0:T(1,128)S(1)} collective-permute-done((f32[1,128]{1,0:T(1,128)S(1)}, f32[1,128]{1,0:T(1,128)S(1)}, u32[]{:S(2)}, u32[]{:S(2)}) %collective-permute-start.26) | collective-permute-done | bytes 544 | tf_op jit(solution)/shard_map/ppermute | solution.py:71
  115.1 1.5 collective-permute-start.31
  117.4 2.0 %collective-permute-start.29 = (f32[1,128]{1,0:T(1,128)S(1)}, f32[1,128]{1,0:T(1,128)S(1)}, u32[]{:S(2)}, u32[]{:S(2)}) collective-permute-start(f32[1,128]{1,0:T(1,128)S(1)} %add_add_fusion.5), channel_id=1, source_target_pairs={{0,8},{1,9},{2,10},{3,11},{4,12},{5,13},{6,14},{7,15},{8,0},{9,1},... | collective-permute-start | bytes 1544 | tf_op jit(solution)/shard_map/ppermute | solution.py:71
  121.6 6.2 %shard_map.63 = (f32[28,80,128]{2,1,0:T(8,128)}, f32[28,80,128]{2,1,0:T(8,128)}, f32[1,128]{1,0:T(1,128)}) custom-call(f32[1,128]{1,0:T(1,128)} %add_add_fusion.4.refs_0_.refs_4_, f32[1,128]{1,0:T(1,128)} %add_add_fusion.8.refs_0_.refs_1_.refs_2_, f32[28,80,128]{2,1,0:T(8,128)} %get-tuple-element.28.refs_2_, ...), custom_call_target="tpu_custom_call" | custom-call | flops 11468800 | bytes 13762560 | tf_op jit(solution)/shard_map/pallas_call | solution.py:341
  131.3 1.9 %collective-permute-start.33 = (f32[1,128]{1,0:T(1,128)S(1)}, f32[1,128]{1,0:T(1,128)S(1)}, u32[]{:S(2)}, u32[]{:S(2)}) collective-permute-start(f32[1,128]{1,0:T(1,128)S(1)} %add.202), channel_id=1, source_target_pairs={{0,2},{1,3},{2,0},{3,1},{4,6},{5,7},{6,4},{7,5},{8,10},{9,11},{10,... | collective-permute-start | bytes 1544 | tf_op jit(solution)/shard_map/ppermute | solution.py:71
  134.9 2.6 %collective-permute-start.38 = (f32[1,128]{1,0:T(1,128)S(1)}, f32[1,128]{1,0:T(1,128)S(1)}, u32[]{:S(2)}, u32[]{:S(2)}) collective-permute-start(f32[1,128]{1,0:T(1,128)S(1)} %add_add_fusion.3), channel_id=1, source_target_pairs={{0,24},{1,25},{2,26},{3,27},{4,28},{5,29},{6,30},{7,31},{8,16},{9,... | collective-permute-start | bytes 1544 | tf_op jit(solution)/shard_map/ppermute | solution.py:71
  140.3 1.7 %collective-permute-done.37 = f32[1,128]{1,0:T(1,128)S(1)} collective-permute-done((f32[1,128]{1,0:T(1,128)S(1)}, f32[1,128]{1,0:T(1,128)S(1)}, u32[]{:S(2)}, u32[]{:S(2)}) %collective-permute-start.37) | collective-permute-done | bytes 544 | tf_op jit(solution)/shard_map/ppermute | solution.py:71
  142.5 6.3 %shard_map.64 = (f32[16,128]{1,0:T(8,128)}, f32[16,128]{1,0:T(8,128)}) custom-call(f32[2,128]{1,0:T(2,128)} %add_add_fusion.refs_0_.refs_1_, f32[2,128]{1,0:T(2,128)} %add_add_fusion.refs_0_.refs_1_, f32[1,128]{1,0:T(1,128)} %add_add_fusion.8.refs_0_.refs_1_.refs_2_, f32[1,128]{1,0:T(1,128)} %add_add_fusion.6.refs_1_.refs_3_, ...), custom_call_target="tpu_custom_call" | custom-call | flops 11468800 | bytes 20643840 | tf_op jit(solution)/shard_map/pallas_call | solution.py:341
  (100 shorter events, 50.9 us)
Async XLA Ops:
  3.3 15.8 %collective-permute-start.1 = (f32[536,128]{1,0:T(8,128)S(1)}, f32[536,128]{1,0:T(8,128)}, u32[]{:S(2)}, u32[]{:S(2)}) collective-permute-start(f32[536,128]{1,0:T(8,128)S(1)} %maximum_bitcast_fusion.2), channel_id=1, source_target_pairs={{4,0},{8,4},{12,8},{16,12},{20,16},{24,20},{28,24},{5,1},{9,5},{13... | collective-permute-start | bytes 823304 | tf_op jit(solution)/shard_map/ppermute | solution.py:379
  5.3 15.5 %collective-permute-start = (f32[536,128]{1,0:T(8,128)}, f32[536,128]{1,0:T(8,128)}, u32[]{:S(2)}, u32[]{:S(2)}) collective-permute-start(f32[536,128]{1,0:T(8,128)} %maximum_bitcast_fusion.1), channel_id=1, source_target_pairs={{0,4},{4,8},{8,12},{12,16},{16,20},{20,24},{24,28},{1,5},{5,9},{9,... | collective-permute-start | bytes 823304 | tf_op jit(solution)/shard_map/ppermute | solution.py:376
  22.1 3.8 %collective-permute-start.2 = (f32[28,6,67]{2,1,0:T(8,128)S(1)}, f32[28,6,67]{2,1,0:T(8,128)S(1)}, u32[]{:S(2)}, u32[]{:S(2)}) collective-permute-start(f32[28,6,67]{2,1,0:T(8,128)S(1)} %get-tuple-element.34), channel_id=1, source_target_pairs={{0,1},{1,2},{2,3},{4,5},{5,6},{6,7},{8,9},{9,10},{10,11},{12,13},{... | collective-permute-start | bytes 135080 | tf_op jit(solution)/shard_map/ppermute | solution.py:20
  24.0 4.3 %collective-permute-start.3 = (f32[28,6,67]{2,1,0:T(8,128)S(1)}, f32[28,6,67]{2,1,0:T(8,128)S(1)}, u32[]{:S(2)}, u32[]{:S(2)}) collective-permute-start(f32[28,6,67]{2,1,0:T(8,128)S(1)} %get-tuple-element.35), channel_id=1, source_target_pairs={{1,0},{2,1},{3,2},{5,4},{6,5},{7,6},{9,8},{10,9},{11,10},{13,12},{... | collective-permute-start | bytes 135080 | tf_op jit(solution)/shard_map/ppermute | solution.py:22
  41.5 4.4 %collective-permute-start.4 = (f32[2,128]{1,0:T(2,128)}, f32[2,128]{1,0:T(2,128)S(1)}, u32[]{:S(2)}, u32[]{:S(2)}) collective-permute-start(f32[2,128]{1,0:T(2,128)} %get-tuple-element.18), channel_id=1, source_target_pairs={{0,1},{1,0},{2,3},{3,2},{4,5},{5,4},{6,7},{7,6},{8,9},{9,8},{10,11... | collective-permute-start | bytes 3080 | tf_op jit(solution)/shard_map/ppermute | solution.py:71
  46.6 4.5 %collective-permute-start.7 = (f32[2,128]{1,0:T(2,128)S(1)}, f32[2,128]{1,0:T(2,128)S(1)}, u32[]{:S(2)}, u32[]{:S(2)}) collective-permute-start(f32[2,128]{1,0:T(2,128)S(1)} %add.174), channel_id=1, source_target_pairs={{0,6},{1,7},{2,4},{3,5},{4,2},{5,3},{6,0},{7,1},{8,14},{9,15},{10,... | collective-permute-start | bytes 3080 | tf_op jit(solution)/shard_map/ppermute | solution.py:71
  48.7 3.6 %collective-permute-start.6 = (f32[2,128]{1,0:T(2,128)S(1)}, f32[2,128]{1,0:T(2,128)S(1)}, u32[]{:S(2)}, u32[]{:S(2)}) collective-permute-start(f32[2,128]{1,0:T(2,128)S(1)} %add.174), channel_id=1, source_target_pairs={{0,4},{1,5},{2,6},{3,7},{4,0},{5,1},{6,2},{7,3},{8,12},{9,13},{10,... | collective-permute-start | bytes 3080 | tf_op jit(solution)/shard_map/ppermute | solution.py:71
  49.1 3.6 %collective-permute-start.5 = (f32[2,128]{1,0:T(2,128)S(1)}, f32[2,128]{1,0:T(2,128)S(1)}, u32[]{:S(2)}, u32[]{:S(2)}) collective-permute-start(f32[2,128]{1,0:T(2,128)S(1)} %add.174), channel_id=1, source_target_pairs={{0,2},{1,3},{2,0},{3,1},{4,6},{5,7},{6,4},{7,5},{8,10},{9,11},{10,... | collective-permute-start | bytes 3080 | tf_op jit(solution)/shard_map/ppermute | solution.py:71
  52.7 5.5 %collective-permute-start.10 = (f32[2,128]{1,0:T(2,128)S(1)}, f32[2,128]{1,0:T(2,128)S(1)}, u32[]{:S(2)}, u32[]{:S(2)}) collective-permute-start(f32[2,128]{1,0:T(2,128)S(1)} %add_add_fusion.1), channel_id=1, source_target_pairs={{0,24},{1,25},{2,26},{3,27},{4,28},{5,29},{6,30},{7,31},{8,16},{9,... | collective-permute-start | bytes 3080 | tf_op jit(solution)/shard_map/ppermute | solution.py:71
  56.6 4.5 %collective-permute-start.9 = (f32[2,128]{1,0:T(2,128)S(1)}, f32[2,128]{1,0:T(2,128)S(1)}, u32[]{:S(2)}, u32[]{:S(2)}) collective-permute-start(f32[2,128]{1,0:T(2,128)S(1)} %add_add_fusion.1), channel_id=1, source_target_pairs={{0,16},{1,17},{2,18},{3,19},{4,20},{5,21},{6,22},{7,23},{8,24},{9,... | collective-permute-start | bytes 3080 | tf_op jit(solution)/shard_map/ppermute | solution.py:71
  56.6 4.5 %collective-permute-start.8 = (f32[2,128]{1,0:T(2,128)S(1)}, f32[2,128]{1,0:T(2,128)S(1)}, u32[]{:S(2)}, u32[]{:S(2)}) collective-permute-start(f32[2,128]{1,0:T(2,128)S(1)} %add_add_fusion.1), channel_id=1, source_target_pairs={{0,8},{1,9},{2,10},{3,11},{4,12},{5,13},{6,14},{7,15},{8,0},{9,1},... | collective-permute-start | bytes 3080 | tf_op jit(solution)/shard_map/ppermute | solution.py:71
  67.7 4.5 %collective-permute-start.14 = (f32[1,128]{1,0:T(1,128)S(1)}, f32[1,128]{1,0:T(1,128)S(1)}, u32[]{:S(2)}, u32[]{:S(2)}) collective-permute-start(f32[1,128]{1,0:T(1,128)S(1)} %add.181), channel_id=1, source_target_pairs={{0,6},{1,7},{2,4},{3,5},{4,2},{5,3},{6,0},{7,1},{8,14},{9,15},{10,... | collective-permute-start | bytes 1544 | tf_op jit(solution)/shard_map/ppermute | solution.py:71
  69.1 3.6 %collective-permute-start.13 = (f32[1,128]{1,0:T(1,128)S(1)}, f32[1,128]{1,0:T(1,128)S(1)}, u32[]{:S(2)}, u32[]{:S(2)}) collective-permute-start(f32[1,128]{1,0:T(1,128)S(1)} %add.181), channel_id=1, source_target_pairs={{0,4},{1,5},{2,6},{3,7},{4,0},{5,1},{6,2},{7,3},{8,12},{9,13},{10,... | collective-permute-start | bytes 1544 | tf_op jit(solution)/shard_map/ppermute | solution.py:71
  71.1 3.6 %collective-permute-start.12 = (f32[1,128]{1,0:T(1,128)S(1)}, f32[1,128]{1,0:T(1,128)S(1)}, u32[]{:S(2)}, u32[]{:S(2)}) collective-permute-start(f32[1,128]{1,0:T(1,128)S(1)} %add.181), channel_id=1, source_target_pairs={{0,2},{1,3},{2,0},{3,1},{4,6},{5,7},{6,4},{7,5},{8,10},{9,11},{10,... | collective-permute-start | bytes 1544 | tf_op jit(solution)/shard_map/ppermute | solution.py:71
  74.7 5.4 %collective-permute-start.17 = (f32[1,128]{1,0:T(1,128)S(1)}, f32[1,128]{1,0:T(1,128)S(1)}, u32[]{:S(2)}, u32[]{:S(2)}) collective-permute-start(f32[1,128]{1,0:T(1,128)S(1)} %add_add_fusion.9), channel_id=1, source_target_pairs={{0,24},{1,25},{2,26},{3,27},{4,28},{5,29},{6,30},{7,31},{8,16},{9,... | collective-permute-start | bytes 1544 | tf_op jit(solution)/shard_map/ppermute | solution.py:71
  76.1 4.5 %collective-permute-start.16 = (f32[1,128]{1,0:T(1,128)S(1)}, f32[1,128]{1,0:T(1,128)S(1)}, u32[]{:S(2)}, u32[]{:S(2)}) collective-permute-start(f32[1,128]{1,0:T(1,128)S(1)} %add_add_fusion.9), channel_id=1, source_target_pairs={{0,16},{1,17},{2,18},{3,19},{4,20},{5,21},{6,22},{7,23},{8,24},{9,... | collective-permute-start | bytes 1544 | tf_op jit(solution)/shard_map/ppermute | solution.py:71
  76.8 3.8 %collective-permute-start.15 = (f32[1,128]{1,0:T(1,128)S(1)}, f32[1,128]{1,0:T(1,128)S(1)}, u32[]{:S(2)}, u32[]{:S(2)}) collective-permute-start(f32[1,128]{1,0:T(1,128)S(1)} %add_add_fusion.9), channel_id=1, source_target_pairs={{0,8},{1,9},{2,10},{3,11},{4,12},{5,13},{6,14},{7,15},{8,0},{9,1},... | collective-permute-start | bytes 1544 | tf_op jit(solution)/shard_map/ppermute | solution.py:71
  89.3 4.5 %collective-permute-start.21 = (f32[1,128]{1,0:T(1,128)S(1)}, f32[1,128]{1,0:T(1,128)S(1)}, u32[]{:S(2)}, u32[]{:S(2)}) collective-permute-start(f32[1,128]{1,0:T(1,128)S(1)} %add.188), channel_id=1, source_target_pairs={{0,6},{1,7},{2,4},{3,5},{4,2},{5,3},{6,0},{7,1},{8,14},{9,15},{10,... | collective-permute-start | bytes 1544 | tf_op jit(solution)/shard_map/ppermute | solution.py:71
  89.7 4.1 %collective-permute-start.20 = (f32[1,128]{1,0:T(1,128)S(1)}, f32[1,128]{1,0:T(1,128)S(1)}, u32[]{:S(2)}, u32[]{:S(2)}) collective-permute-start(f32[1,128]{1,0:T(1,128)S(1)} %add.188), channel_id=1, source_target_pairs={{0,4},{1,5},{2,6},{3,7},{4,0},{5,1},{6,2},{7,3},{8,12},{9,13},{10,... | collective-permute-start | bytes 1544 | tf_op jit(solution)/shard_map/ppermute | solution.py:71
  90.9 3.6 %collective-permute-start.19 = (f32[1,128]{1,0:T(1,128)S(1)}, f32[1,128]{1,0:T(1,128)S(1)}, u32[]{:S(2)}, u32[]{:S(2)}) collective-permute-start(f32[1,128]{1,0:T(1,128)S(1)} %add.188), channel_id=1, source_target_pairs={{0,2},{1,3},{2,0},{3,1},{4,6},{5,7},{6,4},{7,5},{8,10},{9,11},{10,... | collective-permute-start | bytes 1544 | tf_op jit(solution)/shard_map/ppermute | solution.py:71
  94.5 5.4 %collective-permute-start.24 = (f32[1,128]{1,0:T(1,128)S(1)}, f32[1,128]{1,0:T(1,128)S(1)}, u32[]{:S(2)}, u32[]{:S(2)}) collective-permute-start(f32[1,128]{1,0:T(1,128)S(1)} %add_add_fusion.7), channel_id=1, source_target_pairs={{0,24},{1,25},{2,26},{3,27},{4,28},{5,29},{6,30},{7,31},{8,16},{9,... | collective-permute-start | bytes 1544 | tf_op jit(solution)/shard_map/ppermute | solution.py:71
  97.1 4.5 %collective-permute-start.23 = (f32[1,128]{1,0:T(1,128)S(1)}, f32[1,128]{1,0:T(1,128)S(1)}, u32[]{:S(2)}, u32[]{:S(2)}) collective-permute-start(f32[1,128]{1,0:T(1,128)S(1)} %add_add_fusion.7), channel_id=1, source_target_pairs={{0,16},{1,17},{2,18},{3,19},{4,20},{5,21},{6,22},{7,23},{8,24},{9,... | collective-permute-start | bytes 1544 | tf_op jit(solution)/shard_map/ppermute | solution.py:71
  98.0 3.6 %collective-permute-start.22 = (f32[1,128]{1,0:T(1,128)S(1)}, f32[1,128]{1,0:T(1,128)S(1)}, u32[]{:S(2)}, u32[]{:S(2)}) collective-permute-start(f32[1,128]{1,0:T(1,128)S(1)} %add_add_fusion.7), channel_id=1, source_target_pairs={{0,8},{1,9},{2,10},{3,11},{4,12},{5,13},{6,14},{7,15},{8,0},{9,1},... | collective-permute-start | bytes 1544 | tf_op jit(solution)/shard_map/ppermute | solution.py:71
  108.1 4.5 %collective-permute-start.28 = (f32[1,128]{1,0:T(1,128)S(1)}, f32[1,128]{1,0:T(1,128)S(1)}, u32[]{:S(2)}, u32[]{:S(2)}) collective-permute-start(f32[1,128]{1,0:T(1,128)S(1)} %add.195), channel_id=1, source_target_pairs={{0,6},{1,7},{2,4},{3,5},{4,2},{5,3},{6,0},{7,1},{8,14},{9,15},{10,... | collective-permute-start | bytes 1544 | tf_op jit(solution)/shard_map/ppermute | solution.py:71
  111.5 3.6 %collective-permute-start.26 = (f32[1,128]{1,0:T(1,128)S(1)}, f32[1,128]{1,0:T(1,128)S(1)}, u32[]{:S(2)}, u32[]{:S(2)}) collective-permute-start(f32[1,128]{1,0:T(1,128)S(1)} %add.195), channel_id=1, source_target_pairs={{0,2},{1,3},{2,0},{3,1},{4,6},{5,7},{6,4},{7,5},{8,10},{9,11},{10,... | collective-permute-start | bytes 1544 | tf_op jit(solution)/shard_map/ppermute | solution.py:71
  115.1 5.4 %collective-permute-start.31 = (f32[1,128]{1,0:T(1,128)S(1)}, f32[1,128]{1,0:T(1,128)S(1)}, u32[]{:S(2)}, u32[]{:S(2)}) collective-permute-start(f32[1,128]{1,0:T(1,128)S(1)} %add_add_fusion.5), channel_id=1, source_target_pairs={{0,24},{1,25},{2,26},{3,27},{4,28},{5,29},{6,30},{7,31},{8,16},{9,... | collective-permute-start | bytes 1544 | tf_op jit(solution)/shard_map/ppermute | solution.py:71
  116.5 4.5 %collective-permute-start.30 = (f32[1,128]{1,0:T(1,128)S(1)}, f32[1,128]{1,0:T(1,128)S(1)}, u32[]{:S(2)}, u32[]{:S(2)}) collective-permute-start(f32[1,128]{1,0:T(1,128)S(1)} %add_add_fusion.5), channel_id=1, source_target_pairs={{0,16},{1,17},{2,18},{3,19},{4,20},{5,21},{6,22},{7,23},{8,24},{9,... | collective-permute-start | bytes 1544 | tf_op jit(solution)/shard_map/ppermute | solution.py:71
  117.4 3.6 %collective-permute-start.29 = (f32[1,128]{1,0:T(1,128)S(1)}, f32[1,128]{1,0:T(1,128)S(1)}, u32[]{:S(2)}, u32[]{:S(2)}) collective-permute-start(f32[1,128]{1,0:T(1,128)S(1)} %add_add_fusion.5), channel_id=1, source_target_pairs={{0,8},{1,9},{2,10},{3,11},{4,12},{5,13},{6,14},{7,15},{8,0},{9,1},... | collective-permute-start | bytes 1544 | tf_op jit(solution)/shard_map/ppermute | solution.py:71
  129.7 4.5 %collective-permute-start.35 = (f32[1,128]{1,0:T(1,128)S(1)}, f32[1,128]{1,0:T(1,128)S(1)}, u32[]{:S(2)}, u32[]{:S(2)}) collective-permute-start(f32[1,128]{1,0:T(1,128)S(1)} %add.202), channel_id=1, source_target_pairs={{0,6},{1,7},{2,4},{3,5},{4,2},{5,3},{6,0},{7,1},{8,14},{9,15},{10,... | collective-permute-start | bytes 1544 | tf_op jit(solution)/shard_map/ppermute | solution.py:71
  130.1 4.1 %collective-permute-start.34 = (f32[1,128]{1,0:T(1,128)S(1)}, f32[1,128]{1,0:T(1,128)S(1)}, u32[]{:S(2)}, u32[]{:S(2)}) collective-permute-start(f32[1,128]{1,0:T(1,128)S(1)} %add.202), channel_id=1, source_target_pairs={{0,4},{1,5},{2,6},{3,7},{4,0},{5,1},{6,2},{7,3},{8,12},{9,13},{10,... | collective-permute-start | bytes 1544 | tf_op jit(solution)/shard_map/ppermute | solution.py:71
  134.9 5.4 %collective-permute-start.38 = (f32[1,128]{1,0:T(1,128)S(1)}, f32[1,128]{1,0:T(1,128)S(1)}, u32[]{:S(2)}, u32[]{:S(2)}) collective-permute-start(f32[1,128]{1,0:T(1,128)S(1)} %add_add_fusion.3), channel_id=1, source_target_pairs={{0,24},{1,25},{2,26},{3,27},{4,28},{5,29},{6,30},{7,31},{8,16},{9,... | collective-permute-start | bytes 1544 | tf_op jit(solution)/shard_map/ppermute | solution.py:71
  137.5 4.5 %collective-permute-start.37 = (f32[1,128]{1,0:T(1,128)S(1)}, f32[1,128]{1,0:T(1,128)S(1)}, u32[]{:S(2)}, u32[]{:S(2)}) collective-permute-start(f32[1,128]{1,0:T(1,128)S(1)} %add_add_fusion.3), channel_id=1, source_target_pairs={{0,16},{1,17},{2,18},{3,19},{4,20},{5,21},{6,22},{7,23},{8,24},{9,... | collective-permute-start | bytes 1544 | tf_op jit(solution)/shard_map/ppermute | solution.py:71
  (11 other events, 57.0 us)

commit v13 on v11

--- a/solution.py
+++ b/solution.py
@@ -104,6 +104,9 @@
         self.first_inner = first_inner
         self.inner_rows = inner_rows
 
+    def span(self, halo):
+        return self.first_inner - halo, self.first_inner + self.inner_rows + halo
+
     def inner_row(self, r):
         return (r >= self.first_inner) & (r < self.first_inner + self.inner_rows)
 
@@ -113,17 +116,14 @@
     ref[ref.shape[0] - 1] = jnp.zeros(ref.shape[1:], ref.dtype)
 
 
-def _apply_q(plan, source, gain_ref, weight_ref, inside_ref, row_ref, inner_ref, stiff_ref,
+def _apply_q(plan, reach, source, gain_ref, weight_ref, inside_ref, row_ref, inner_ref, stiff_ref,
              applied_ref, dot_source):
-    last = plan.slab_rows - 1
-    _zero_edges(stiff_ref)
-    _zero_edges(applied_ref)
 
     def first_pass(r, carry):
         stiff_ref[r] = weight_ref[r] * _stiffen_row(source, r, gain_ref[r])
         return carry
 
-    lax.fori_loop(1, last, first_pass, 0)
+    lax.fori_loop(*plan.span(reach + 1), first_pass, 0)
 
     def second_pass(r, totals):
         applied = _stiffen_row(stiff_ref, r, gain_ref[r])
@@ -133,7 +133,7 @@
         inner = (inner_ref[...] > 0.5) & plan.inner_row(r)
         return totals + _row_sum(dot_source[r] * applied, inner)
 
-    return lax.fori_loop(1, last, second_pass, jnp.zeros((1, source.shape[2]), jnp.float32))
+    return lax.fori_loop(*plan.span(reach), second_pass, jnp.zeros((1, source.shape[2]), jnp.float32))
 
 
 def _spread(value, lane):
@@ -147,7 +147,6 @@
 def _first_kernel(plan, ext_ref, inside_ref, row_ref, inner_ref, diagonal_ref,
                   z_out, gain_out, weight_out, stiff_out, applied_out, dots_out, stiff_obs_out,
                   observed_scr, scratch):
-    last = plan.slab_rows - 1
     sublanes = z_out.shape[1]
     lanes = z_out.shape[2]
     probes = lanes // 2
@@ -164,22 +163,17 @@
         return carry
 
     lax.fori_loop(0, plan.slab_rows, relayout, 0)
-    _zero_edges(stiff_out)
+    reach = 2 * (ITERS - 1)
 
     def probe_pass(r, totals):
-        stiff_out[r] = _stiffen_row(z_out, r, gain_out[r])
+        stiffness = _stiffen_row(z_out, r, gain_out[r])
+        stiff_out[r] = stiffness
+        scratch[r] = weight_out[r] * stiffness
         z = z_out[r]
         inner = (inner_ref[...] > 0.5) & plan.inner_row(r)
         return totals + _row_sum(z * z, inner)
 
-    zz = lax.fori_loop(1, last, probe_pass, jnp.zeros((1, lanes), jnp.float32))
-    _zero_edges(scratch)
-
-    def weigh(r, carry):
-        scratch[r] = weight_out[r] * stiff_out[r]
-        return carry
-
-    lax.fori_loop(1, last, weigh, 0)
+    zz = lax.fori_loop(*plan.span(reach + 1), probe_pass, jnp.zeros((1, lanes), jnp.float32))
 
     def second_pass(r, totals):
         applied = _stiffen_row(scratch, r, gain_out[r])
@@ -189,8 +183,7 @@
         inner = (inner_ref[...] > 0.5) & plan.inner_row(r)
         return totals + _row_sum(z_out[r] * applied, inner)
 
-    _zero_edges(applied_out)
-    za = lax.fori_loop(1, last, second_pass, jnp.zeros((1, lanes), jnp.float32))
+    za = lax.fori_loop(*plan.span(reach), second_pass, jnp.zeros((1, lanes), jnp.float32))
     dots_out[0:1, :] = zz
     dots_out[1:2, :] = za
 
@@ -211,10 +204,12 @@
         inner = (inner_ref[...] > 0.5) & plan.inner_row(r)
         return totals + _row_sum(residual * residual, inner)
 
-    rr_out[...] = lax.fori_loop(0, plan.slab_rows, body, jnp.zeros((1, z_ref.shape[2]), jnp.float32))
-
-
-def _update_kernel(plan, norm_ref, curvature_ref, residual_ref, applied_ref, inner_ref,
+    rr_out[...] = lax.fori_loop(
+        *plan.span(2 * (ITERS - 1)), body, jnp.zeros((1, z_ref.shape[2]), jnp.float32)
+    )
+
+
+def _update_kernel(plan, reach, norm_ref, curvature_ref, residual_ref, applied_ref, inner_ref,
                    residual_out, rr_out):
     step = _ratio(norm_ref, 0, curvature_ref, 0)
 
@@ -225,20 +220,21 @@
         return totals + _row_sum(residual * residual, inner)
 
     rr_out[...] = lax.fori_loop(
-        0, plan.slab_rows, body, jnp.zeros((1, residual_ref.shape[2]), jnp.float32)
-    )
-
-
-def _direction_kernel(plan, next_ref, now_ref, residual_ref, direction_ref, gain_ref, weight_ref,
-                      inside_ref, row_ref, inner_ref, direction_out, applied_out, pa_out, scratch):
+        *plan.span(reach), body, jnp.zeros((1, residual_ref.shape[2]), jnp.float32)
+    )
+
+
+def _direction_kernel(plan, reach, next_ref, now_ref, residual_ref, direction_ref, gain_ref,
+                      weight_ref, inside_ref, row_ref, inner_ref, direction_out, applied_out, pa_out,
+                      scratch):
     beta = _ratio(next_ref, 0, now_ref, 0)
 
     def new_direction(r, carry):
         direction_out[r] = residual_ref[r] + beta * direction_ref[r]
         return carry
 
-    lax.fori_loop(0, plan.slab_rows, new_direction, 0)
-    pa_out[...] = _apply_q(plan, direction_out, gain_ref, weight_ref, inside_ref, row_ref, inner_ref,
+    lax.fori_loop(*plan.span(reach + 2), new_direction, 0)
+    pa_out[...] = _apply_q(plan, reach, direction_out, gain_ref, weight_ref, inside_ref, row_ref, inner_ref,
                            scratch, applied_out, direction_out)
 
 
@@ -262,7 +258,7 @@
         scratch[r] = solution
         return carry
 
-    lax.fori_loop(0, plan.slab_rows, new_solution, 0)
+    lax.fori_loop(*plan.span(1), new_solution, 0)
 
     def probe_sum(value, low):
         first = jnp.sum(jnp.where(low, value, 0.0), axis=1, keepdims=True)
@@ -391,8 +387,9 @@
     norm_now = first
     for iteration in range(1, ITERS):
         norm_next = all_sum(rr)
+        reach = 2 * (ITERS - 1 - iteration)
         direction, applied, pa = _call(
-            _direction_kernel, plan,
+            lambda plan, *refs, reach=reach: _direction_kernel(plan, reach, *refs), plan,
             (norm_next, norm_now, residual, direction, gain, weight, inside, row_in, inner),
             (field, field, lane_row), scratch=1, smem=(7,),
         )
@@ -402,7 +399,7 @@
         ratios += [norm_now, curvature]
         if iteration + 1 < ITERS:
             residual, rr = _call(
-                _update_kernel, plan, (norm_now, curvature, residual, applied, inner),
+                lambda plan, *refs, reach=reach: _update_kernel(plan, reach, *refs), plan, (norm_now, curvature, residual, applied, inner),
                 (field, lane_row),
             )
 

time: 148 us -> 146 us (0.986)
  Pallas kernels: 36.8 us -> 34.8 us
    pallas_call x6, Pallas kernels: 36.8 us -> 34.8 us  [_call(): pl.pallas_call(lambda *refs: kernel(plan, *refs), out_shape=out_shapes, i...]
where the time goes in v13:
time: 146 us
  starting transfers between devices  54.1 us (37%)
  Pallas kernels  34.8 us (24%)
  waiting for transfers between devices  33.9 us (23%)
  other arithmetic  13.2 us (9%)
  local copies, waits for them, and re-layouts  8.58 us (6%)
    ppermute x35, starting transfers between devices, partner(): lax.ppermute(terms, axes, [(i, i ^ mask) for i in range(count)])  43.4 us
    pallas_call x6, Pallas kernels, _call(): pl.pallas_call(lambda *refs: kernel(plan, *refs), out_shape=out_shapes, i...  34.8 us
    ppermute x35, waiting for transfers between devices, partner(): lax.ppermute(terms, axes, [(i, i ^ mask) for i in range(count)])  30.8 us
    ppermute x1, starting transfers between devices, on_device(): lax.ppermute(edge_rows(rows - sent), 'rows', [(i, i + 1) for i in range(c...  6.21 us
    add x15, other arithmetic, _span_sum(): _span_sum(terms, rest, partner)  6.15 us
    broadcast_in_dim x3, local copies, waits for them, and re-layouts, on_device(): fields = (probes, observed[None], kappa_sq[None], variance_weight[None])  3.09 us
  transfers between devices with their start and end apart: 39, of which 30 were waited for; matrix products, arithmetic and copies ran while one was open for 7% of the time, Pallas kernels for 0%

profile of v13, /device:TPU:0, one launch (start us, length us, event | category | flops | bytes accessed | tf_op | source)
XLA Modules:
  0.0 145.5 jit_solution(2255331581530823642)
XLA Ops:
  5.3 6.2 %collective-permute-start = (f32[536,128]{1,0:T(8,128)}, f32[536,128]{1,0:T(8,128)}, u32[]{:S(2)}, u32[]{:S(2)}) collective-permute-start(f32[536,128]{1,0:T(8,128)} %maximum_bitcast_fusion.1), channel_id=1, source_target_pairs={{0,4},{4,8},{8,12},{12,16},{16,20},{20,24},{24,28},{1,5},{5,9},{9,... | collective-permute-start | bytes 823304 | tf_op jit(solution)/shard_map/ppermute | solution.py:338
  15.8 2.4 %maximum_bitcast_fusion = f32[16,128,67]{2,1,0:T(8,128)S(1)} fusion(f32[1,16,128]{0,2,1:T(8,128)} %copy.17, f32[1,16,128]{0,2,1:T(8,128)S(1)} %copy.16, f32[1,16,128]{0,2,1:T(8,128)} %copy.15, f32[64,16,128]{0,2,1:T(8,128)S(1)} %copy.14), kind=kLoop, calls=%fused_computation.13 | loop fusion | flops 411648 | bytes 1097728 | tf_op jit(solution)/shard_map/transpose | solution.py:345
  22.1 1.9 %collective-permute-start.2 = (f32[28,6,67]{2,1,0:T(8,128)S(1)}, f32[28,6,67]{2,1,0:T(8,128)S(1)}, u32[]{:S(2)}, u32[]{:S(2)}) collective-permute-start(f32[28,6,67]{2,1,0:T(8,128)S(1)} %get-tuple-element.34), channel_id=1, source_target_pairs={{0,1},{1,2},{2,3},{4,5},{5,6},{6,7},{8,9},{9,10},{10,11},{12,13},{... | collective-permute-start | bytes 135080 | tf_op jit(solution)/shard_map/ppermute | solution.py:20
  25.8 2.5 %collective-permute-done.3 = f32[28,6,67]{2,1,0:T(8,128)S(1)} collective-permute-done((f32[28,6,67]{2,1,0:T(8,128)S(1)}, f32[28,6,67]{2,1,0:T(8,128)S(1)}, u32[]{:S(2)}, u32[]{:S(2)}) %collective-permute-start.3) | collective-permute-done | bytes 45056 | tf_op jit(solution)/shard_map/ppermute | solution.py:22
  28.3 1.9 %select_maximum_fusion.refs_0_ = f32[28,144,128]{2,1,0:T(8,128)} fusion(f32[28,6,67]{2,1,0:T(8,128)S(1)} %collective-permute-done.3, f32[28,6,67]{2,1,0:T(8,128)S(1)} %collective-permute-done.2, f32[6,128,67]{2,1,0:T(8,128)S(1)} %bitcast.15, f32[16,128,67]{2,1,0:T(8,128)S(1)} %maximum_bitcast_fusion, f32[6,128,67]{2,1,0:T(8,128)S(1)} %bitcast.17), kind=kLoop, calls=%fused_computation | loop fusion | flops 8773632 | bytes 3114944 | tf_op jit(solution)/shard_map/concatenate | solution.py:18
  30.3 11.0 %shard_map.59 = (f32[28,80,128]{2,1,0:T(8,128)}, f32[28,80,128]{2,1,0:T(8,128)}, f32[28,80,128]{2,1,0:T(8,128)}, f32[28,80,128]{2,1,0:T(8,128)}, f32[28,80,128]{...) custom-call(f32[28,144,128]{2,1,0:T(8,128)} %select_maximum_fusion.refs_0_, ...), custom_call_target="tpu_custom_call" | custom-call | flops 11468800 | bytes 13762560 | tf_op jit(solution)/shard_map/pallas_call | solution.py:303
  41.3 3.4 %collective-permute-start.4 = (f32[2,128]{1,0:T(2,128)}, f32[2,128]{1,0:T(2,128)S(1)}, u32[]{:S(2)}, u32[]{:S(2)}) collective-permute-start(f32[2,128]{1,0:T(2,128)} %get-tuple-element.18), channel_id=1, source_target_pairs={{0,1},{1,0},{2,3},{3,2},{4,5},{5,4},{6,7},{7,6},{8,9},{9,8},{10,11... | collective-permute-start | bytes 3080 | tf_op jit(solution)/shard_map/ppermute | solution.py:71
  46.4 2.0 %collective-permute-start.7 = (f32[2,128]{1,0:T(2,128)S(1)}, f32[2,128]{1,0:T(2,128)S(1)}, u32[]{:S(2)}, u32[]{:S(2)}) collective-permute-start(f32[2,128]{1,0:T(2,128)S(1)} %add.174), channel_id=1, source_target_pairs={{0,6},{1,7},{2,4},{3,5},{4,2},{5,3},{6,0},{7,1},{8,14},{9,15},{10,... | collective-permute-start | bytes 3080 | tf_op jit(solution)/shard_map/ppermute | solution.py:71
  48.9 1.5 %collective-permute-start.5 = (f32[2,128]{1,0:T(2,128)S(1)}, f32[2,128]{1,0:T(2,128)S(1)}, u32[]{:S(2)}, u32[]{:S(2)}) collective-permute-start(f32[2,128]{1,0:T(2,128)S(1)} %add.174), channel_id=1, source_target_pairs={{0,2},{1,3},{2,0},{3,1},{4,6},{5,7},{6,4},{7,5},{8,10},{9,11},{10,... | collective-permute-start | bytes 3080 | tf_op jit(solution)/shard_map/ppermute | solution.py:71
  52.4 3.9 %collective-permute-start.10 = (f32[2,128]{1,0:T(2,128)S(1)}, f32[2,128]{1,0:T(2,128)S(1)}, u32[]{:S(2)}, u32[]{:S(2)}) collective-permute-start(f32[2,128]{1,0:T(2,128)S(1)} %add_add_fusion.1), channel_id=1, source_target_pairs={{0,24},{1,25},{2,26},{3,27},{4,28},{5,29},{6,30},{7,31},{8,16},{9,... | collective-permute-start | bytes 3080 | tf_op jit(solution)/shard_map/ppermute | solution.py:71
  57.9 2.9 %collective-permute-done.9 = f32[2,128]{1,0:T(2,128)S(1)} collective-permute-done((f32[2,128]{1,0:T(2,128)S(1)}, f32[2,128]{1,0:T(2,128)S(1)}, u32[]{:S(2)}, u32[]{:S(2)}) %collective-permute-start.9) | collective-permute-done | bytes 1056 | tf_op jit(solution)/shard_map/ppermute | solution.py:71
  61.5 3.3 %shard_map.60 = (f32[28,80,128]{2,1,0:T(8,128)}, f32[1,128]{1,0:T(1,128)}) custom-call(f32[2,128]{1,0:T(2,128)} %add_add_fusion.refs_0_.refs_1_, f32[28,80,128]{2,1,0:T(8,128)} %get-tuple-element.19.refs_1_.refs_3_.refs_6_.refs_9_, f32[28,80,128]{2,1,0:T(8,128)} %get-tuple-element.20.refs_2_, f32[80,128]{1,0:T(8,128)} %add_convert_fusion.1.refs_3_.refs_8_.refs_4_), custom_call_target="tpu_custom_call" | custom-call | flops 11468800 | bytes 6881280 | tf_op jit(solution)/shard_map/pallas_call | solution.py:303
  66.7 1.4 collective-permute-start.14
  68.1 2.0 %collective-permute-start.13 = (f32[1,128]{1,0:T(1,128)S(1)}, f32[1,128]{1,0:T(1,128)S(1)}, u32[]{:S(2)}, u32[]{:S(2)}) collective-permute-start(f32[1,128]{1,0:T(1,128)S(1)} %add.181), channel_id=1, source_target_pairs={{0,4},{1,5},{2,6},{3,7},{4,0},{5,1},{6,2},{7,3},{8,12},{9,13},{10,... | collective-permute-start | bytes 1544 | tf_op jit(solution)/shard_map/ppermute | solution.py:71
  71.6 2.0 %collective-permute-done.12 = f32[1,128]{1,0:T(1,128)S(1)} collective-permute-done((f32[1,128]{1,0:T(1,128)S(1)}, f32[1,128]{1,0:T(1,128)S(1)}, u32[]{:S(2)}, u32[]{:S(2)}) %collective-permute-start.12) | collective-permute-done | bytes 544 | tf_op jit(solution)/shard_map/ppermute | solution.py:71
  73.6 1.5 %collective-permute-start.17 = (f32[1,128]{1,0:T(1,128)S(1)}, f32[1,128]{1,0:T(1,128)S(1)}, u32[]{:S(2)}, u32[]{:S(2)}) collective-permute-start(f32[1,128]{1,0:T(1,128)S(1)} %add_add_fusion.9), channel_id=1, source_target_pairs={{0,24},{1,25},{2,26},{3,27},{4,28},{5,29},{6,30},{7,31},{8,16},{9,... | collective-permute-start | bytes 1544 | tf_op jit(solution)/shard_map/ppermute | solution.py:71
  75.7 2.3 %collective-permute-start.15 = (f32[1,128]{1,0:T(1,128)S(1)}, f32[1,128]{1,0:T(1,128)S(1)}, u32[]{:S(2)}, u32[]{:S(2)}) collective-permute-start(f32[1,128]{1,0:T(1,128)S(1)} %add_add_fusion.9), channel_id=1, source_target_pairs={{0,8},{1,9},{2,10},{3,11},{4,12},{5,13},{6,14},{7,15},{8,0},{9,1},... | collective-permute-start | bytes 1544 | tf_op jit(solution)/shard_map/ppermute | solution.py:71
  80.1 5.8 %shard_map.61 = (f32[28,80,128]{2,1,0:T(8,128)}, f32[28,80,128]{2,1,0:T(8,128)}, f32[1,128]{1,0:T(1,128)}) custom-call(f32[1,128]{1,0:T(1,128)} %add_add_fusion.8.refs_0_.refs_1_.refs_2_, f32[2,128]{1,0:T(2,128)} %add_add_fusion.refs_0_.refs_1_, f32[28,80,128]{2,1,0:T(8,128)} %get-tuple-element.22.refs_2_, ...), custom_call_target="tpu_custom_call" | custom-call | flops 11468800 | bytes 13762560 | tf_op jit(solution)/shard_map/pallas_call | solution.py:303
  89.4 1.9 %collective-permute-start.19 = (f32[1,128]{1,0:T(1,128)S(1)}, f32[1,128]{1,0:T(1,128)S(1)}, u32[]{:S(2)}, u32[]{:S(2)}) collective-permute-start(f32[1,128]{1,0:T(1,128)S(1)} %add.188), channel_id=1, source_target_pairs={{0,2},{1,3},{2,0},{3,1},{4,6},{5,7},{6,4},{7,5},{8,10},{9,11},{10,... | collective-permute-start | bytes 1544 | tf_op jit(solution)/shard_map/ppermute | solution.py:71
  93.0 2.6 %collective-permute-start.24 = (f32[1,128]{1,0:T(1,128)S(1)}, f32[1,128]{1,0:T(1,128)S(1)}, u32[]{:S(2)}, u32[]{:S(2)}) collective-permute-start(f32[1,128]{1,0:T(1,128)S(1)} %add_add_fusion.7), channel_id=1, source_target_pairs={{0,24},{1,25},{2,26},{3,27},{4,28},{5,29},{6,30},{7,31},{8,16},{9,... | collective-permute-start | bytes 1544 | tf_op jit(solution)/shard_map/ppermute | solution.py:71
  98.3 1.7 %collective-permute-done.23 = f32[1,128]{1,0:T(1,128)S(1)} collective-permute-done((f32[1,128]{1,0:T(1,128)S(1)}, f32[1,128]{1,0:T(1,128)S(1)}, u32[]{:S(2)}, u32[]{:S(2)}) %collective-permute-start.23) | collective-permute-done | bytes 544 | tf_op jit(solution)/shard_map/ppermute | solution.py:71
  100.6 3.3 %shard_map.62 = (f32[28,80,128]{2,1,0:T(8,128)}, f32[1,128]{1,0:T(1,128)}) custom-call(f32[1,128]{1,0:T(1,128)} %add_add_fusion.8.refs_0_.refs_1_.refs_2_, f32[1,128]{1,0:T(1,128)} %add_add_fusion.6.refs_1_.refs_3_, f32[28,80,128]{2,1,0:T(8,128)} %get-tuple-element.22.refs_2_, f32[28,80,128]{2,1,0:T(8,128)} %get-tuple-element.26.refs_3_, ...), custom_call_target="tpu_custom_call" | custom-call | flops 11468800 | bytes 8028160 | tf_op jit(solution)/shard_map/pallas_call | solution.py:303
  105.8 1.4 collective-permute-start.28
  107.2 2.0 %collective-permute-start.27 = (f32[1,128]{1,0:T(1,128)S(1)}, f32[1,128]{1,0:T(1,128)S(1)}, u32[]{:S(2)}, u32[]{:S(2)}) collective-permute-start(f32[1,128]{1,0:T(1,128)S(1)} %add.195), channel_id=1, source_target_pairs={{0,4},{1,5},{2,6},{3,7},{4,0},{5,1},{6,2},{7,3},{8,12},{9,13},{10,... | collective-permute-start | bytes 1544 | tf_op jit(solution)/shard_map/ppermute | solution.py:71
  110.8 2.0 %collective-permute-done.26 = f32[1,128]{1,0:T(1,128)S(1)} collective-permute-done((f32[1,128]{1,0:T(1,128)S(1)}, f32[1,128]{1,0:T(1,128)S(1)}, u32[]{:S(2)}, u32[]{:S(2)}) %collective-permute-start.26) | collective-permute-done | bytes 544 | tf_op jit(solution)/shard_map/ppermute | solution.py:71
  112.7 1.5 %collective-permute-start.31 = (f32[1,128]{1,0:T(1,128)S(1)}, f32[1,128]{1,0:T(1,128)S(1)}, u32[]{:S(2)}, u32[]{:S(2)}) collective-permute-start(f32[1,128]{1,0:T(1,128)S(1)} %add_add_fusion.5), channel_id=1, source_target_pairs={{0,24},{1,25},{2,26},{3,27},{4,28},{5,29},{6,30},{7,31},{8,16},{9,... | collective-permute-start | bytes 1544 | tf_op jit(solution)/shard_map/ppermute | solution.py:71
  115.1 2.0 %collective-permute-start.29 = (f32[1,128]{1,0:T(1,128)S(1)}, f32[1,128]{1,0:T(1,128)S(1)}, u32[]{:S(2)}, u32[]{:S(2)}) collective-permute-start(f32[1,128]{1,0:T(1,128)S(1)} %add_add_fusion.5), channel_id=1, source_target_pairs={{0,8},{1,9},{2,10},{3,11},{4,12},{5,13},{6,14},{7,15},{8,0},{9,1},... | collective-permute-start | bytes 1544 | tf_op jit(solution)/shard_map/ppermute | solution.py:71
  119.3 5.3 %shard_map.63 = (f32[28,80,128]{2,1,0:T(8,128)}, f32[28,80,128]{2,1,0:T(8,128)}, f32[1,128]{1,0:T(1,128)}) custom-call(f32[1,128]{1,0:T(1,128)} %add_add_fusion.4.refs_0_.refs_4_, f32[1,128]{1,0:T(1,128)} %add_add_fusion.8.refs_0_.refs_1_.refs_2_, f32[28,80,128]{2,1,0:T(8,128)} %get-tuple-element.28.refs_2_, ...), custom_call_target="tpu_custom_call" | custom-call | flops 11468800 | bytes 13762560 | tf_op jit(solution)/shard_map/pallas_call | solution.py:303
  128.1 1.9 %collective-permute-start.33 = (f32[1,128]{1,0:T(1,128)S(1)}, f32[1,128]{1,0:T(1,128)S(1)}, u32[]{:S(2)}, u32[]{:S(2)}) collective-permute-start(f32[1,128]{1,0:T(1,128)S(1)} %add.202), channel_id=1, source_target_pairs={{0,2},{1,3},{2,0},{3,1},{4,6},{5,7},{6,4},{7,5},{8,10},{9,11},{10,... | collective-permute-start | bytes 1544 | tf_op jit(solution)/shard_map/ppermute | solution.py:71
  131.7 2.6 %collective-permute-start.38 = (f32[1,128]{1,0:T(1,128)S(1)}, f32[1,128]{1,0:T(1,128)S(1)}, u32[]{:S(2)}, u32[]{:S(2)}) collective-permute-start(f32[1,128]{1,0:T(1,128)S(1)} %add_add_fusion.3), channel_id=1, source_target_pairs={{0,24},{1,25},{2,26},{3,27},{4,28},{5,29},{6,30},{7,31},{8,16},{9,... | collective-permute-start | bytes 1544 | tf_op jit(solution)/shard_map/ppermute | solution.py:71
  137.1 1.7 %collective-permute-done.37 = f32[1,128]{1,0:T(1,128)S(1)} collective-permute-done((f32[1,128]{1,0:T(1,128)S(1)}, f32[1,128]{1,0:T(1,128)S(1)}, u32[]{:S(2)}, u32[]{:S(2)}) %collective-permute-start.37) | collective-permute-done | bytes 544 | tf_op jit(solution)/shard_map/ppermute | solution.py:71
  139.3 6.2 %shard_map.64 = (f32[16,128]{1,0:T(8,128)}, f32[16,128]{1,0:T(8,128)}) custom-call(f32[2,128]{1,0:T(2,128)} %add_add_fusion.refs_0_.refs_1_, f32[2,128]{1,0:T(2,128)} %add_add_fusion.refs_0_.refs_1_, f32[1,128]{1,0:T(1,128)} %add_add_fusion.8.refs_0_.refs_1_.refs_2_, f32[1,128]{1,0:T(1,128)} %add_add_fusion.6.refs_1_.refs_3_, ...), custom_call_target="tpu_custom_call" | custom-call | flops 11468800 | bytes 20643840 | tf_op jit(solution)/shard_map/pallas_call | solution.py:303
  (100 shorter events, 50.9 us)
Async XLA Ops:
  3.3 15.8 %collective-permute-start.1 = (f32[536,128]{1,0:T(8,128)S(1)}, f32[536,128]{1,0:T(8,128)}, u32[]{:S(2)}, u32[]{:S(2)}) collective-permute-start(f32[536,128]{1,0:T(8,128)S(1)} %maximum_bitcast_fusion.2), channel_id=1, source_target_pairs={{4,0},{8,4},{12,8},{16,12},{20,16},{24,20},{28,24},{5,1},{9,5},{13... | collective-permute-start | bytes 823304 | tf_op jit(solution)/shard_map/ppermute | solution.py:341
  5.3 15.5 %collective-permute-start = (f32[536,128]{1,0:T(8,128)}, f32[536,128]{1,0:T(8,128)}, u32[]{:S(2)}, u32[]{:S(2)}) collective-permute-start(f32[536,128]{1,0:T(8,128)} %maximum_bitcast_fusion.1), channel_id=1, source_target_pairs={{0,4},{4,8},{8,12},{12,16},{16,20},{20,24},{24,28},{1,5},{5,9},{9,... | collective-permute-start | bytes 823304 | tf_op jit(solution)/shard_map/ppermute | solution.py:338
  22.1 3.8 %collective-permute-start.2 = (f32[28,6,67]{2,1,0:T(8,128)S(1)}, f32[28,6,67]{2,1,0:T(8,128)S(1)}, u32[]{:S(2)}, u32[]{:S(2)}) collective-permute-start(f32[28,6,67]{2,1,0:T(8,128)S(1)} %get-tuple-element.34), channel_id=1, source_target_pairs={{0,1},{1,2},{2,3},{4,5},{5,6},{6,7},{8,9},{9,10},{10,11},{12,13},{... | collective-permute-start | bytes 135080 | tf_op jit(solution)/shard_map/ppermute | solution.py:20
  24.0 4.3 %collective-permute-start.3 = (f32[28,6,67]{2,1,0:T(8,128)S(1)}, f32[28,6,67]{2,1,0:T(8,128)S(1)}, u32[]{:S(2)}, u32[]{:S(2)}) collective-permute-start(f32[28,6,67]{2,1,0:T(8,128)S(1)} %get-tuple-element.35), channel_id=1, source_target_pairs={{1,0},{2,1},{3,2},{5,4},{6,5},{7,6},{9,8},{10,9},{11,10},{13,12},{... | collective-permute-start | bytes 135080 | tf_op jit(solution)/shard_map/ppermute | solution.py:22
  41.3 4.4 %collective-permute-start.4 = (f32[2,128]{1,0:T(2,128)}, f32[2,128]{1,0:T(2,128)S(1)}, u32[]{:S(2)}, u32[]{:S(2)}) collective-permute-start(f32[2,128]{1,0:T(2,128)} %get-tuple-element.18), channel_id=1, source_target_pairs={{0,1},{1,0},{2,3},{3,2},{4,5},{5,4},{6,7},{7,6},{8,9},{9,8},{10,11... | collective-permute-start | bytes 3080 | tf_op jit(solution)/shard_map/ppermute | solution.py:71
  46.4 4.5 %collective-permute-start.7 = (f32[2,128]{1,0:T(2,128)S(1)}, f32[2,128]{1,0:T(2,128)S(1)}, u32[]{:S(2)}, u32[]{:S(2)}) collective-permute-start(f32[2,128]{1,0:T(2,128)S(1)} %add.174), channel_id=1, source_target_pairs={{0,6},{1,7},{2,4},{3,5},{4,2},{5,3},{6,0},{7,1},{8,14},{9,15},{10,... | collective-permute-start | bytes 3080 | tf_op jit(solution)/shard_map/ppermute | solution.py:71
  48.4 3.6 %collective-permute-start.6 = (f32[2,128]{1,0:T(2,128)S(1)}, f32[2,128]{1,0:T(2,128)S(1)}, u32[]{:S(2)}, u32[]{:S(2)}) collective-permute-start(f32[2,128]{1,0:T(2,128)S(1)} %add.174), channel_id=1, source_target_pairs={{0,4},{1,5},{2,6},{3,7},{4,0},{5,1},{6,2},{7,3},{8,12},{9,13},{10,... | collective-permute-start | bytes 3080 | tf_op jit(solution)/shard_map/ppermute | solution.py:71
  48.9 3.6 %collective-permute-start.5 = (f32[2,128]{1,0:T(2,128)S(1)}, f32[2,128]{1,0:T(2,128)S(1)}, u32[]{:S(2)}, u32[]{:S(2)}) collective-permute-start(f32[2,128]{1,0:T(2,128)S(1)} %add.174), channel_id=1, source_target_pairs={{0,2},{1,3},{2,0},{3,1},{4,6},{5,7},{6,4},{7,5},{8,10},{9,11},{10,... | collective-permute-start | bytes 3080 | tf_op jit(solution)/shard_map/ppermute | solution.py:71
  52.4 5.5 %collective-permute-start.10 = (f32[2,128]{1,0:T(2,128)S(1)}, f32[2,128]{1,0:T(2,128)S(1)}, u32[]{:S(2)}, u32[]{:S(2)}) collective-permute-start(f32[2,128]{1,0:T(2,128)S(1)} %add_add_fusion.1), channel_id=1, source_target_pairs={{0,24},{1,25},{2,26},{3,27},{4,28},{5,29},{6,30},{7,31},{8,16},{9,... | collective-permute-start | bytes 3080 | tf_op jit(solution)/shard_map/ppermute | solution.py:71
  56.4 4.5 %collective-permute-start.9 = (f32[2,128]{1,0:T(2,128)S(1)}, f32[2,128]{1,0:T(2,128)S(1)}, u32[]{:S(2)}, u32[]{:S(2)}) collective-permute-start(f32[2,128]{1,0:T(2,128)S(1)} %add_add_fusion.1), channel_id=1, source_target_pairs={{0,16},{1,17},{2,18},{3,19},{4,20},{5,21},{6,22},{7,23},{8,24},{9,... | collective-permute-start | bytes 3080 | tf_op jit(solution)/shard_map/ppermute | solution.py:71
  56.4 4.5 %collective-permute-start.8 = (f32[2,128]{1,0:T(2,128)S(1)}, f32[2,128]{1,0:T(2,128)S(1)}, u32[]{:S(2)}, u32[]{:S(2)}) collective-permute-start(f32[2,128]{1,0:T(2,128)S(1)} %add_add_fusion.1), channel_id=1, source_target_pairs={{0,8},{1,9},{2,10},{3,11},{4,12},{5,13},{6,14},{7,15},{8,0},{9,1},... | collective-permute-start | bytes 3080 | tf_op jit(solution)/shard_map/ppermute | solution.py:71
  66.7 4.5 %collective-permute-start.14 = (f32[1,128]{1,0:T(1,128)S(1)}, f32[1,128]{1,0:T(1,128)S(1)}, u32[]{:S(2)}, u32[]{:S(2)}) collective-permute-start(f32[1,128]{1,0:T(1,128)S(1)} %add.181), channel_id=1, source_target_pairs={{0,6},{1,7},{2,4},{3,5},{4,2},{5,3},{6,0},{7,1},{8,14},{9,15},{10,... | collective-permute-start | bytes 1544 | tf_op jit(solution)/shard_map/ppermute | solution.py:71
  68.1 3.6 %collective-permute-start.13 = (f32[1,128]{1,0:T(1,128)S(1)}, f32[1,128]{1,0:T(1,128)S(1)}, u32[]{:S(2)}, u32[]{:S(2)}) collective-permute-start(f32[1,128]{1,0:T(1,128)S(1)} %add.181), channel_id=1, source_target_pairs={{0,4},{1,5},{2,6},{3,7},{4,0},{5,1},{6,2},{7,3},{8,12},{9,13},{10,... | collective-permute-start | bytes 1544 | tf_op jit(solution)/shard_map/ppermute | solution.py:71
  70.0 3.6 %collective-permute-start.12 = (f32[1,128]{1,0:T(1,128)S(1)}, f32[1,128]{1,0:T(1,128)S(1)}, u32[]{:S(2)}, u32[]{:S(2)}) collective-permute-start(f32[1,128]{1,0:T(1,128)S(1)} %add.181), channel_id=1, source_target_pairs={{0,2},{1,3},{2,0},{3,1},{4,6},{5,7},{6,4},{7,5},{8,10},{9,11},{10,... | collective-permute-start | bytes 1544 | tf_op jit(solution)/shard_map/ppermute | solution.py:71
  73.6 5.4 %collective-permute-start.17 = (f32[1,128]{1,0:T(1,128)S(1)}, f32[1,128]{1,0:T(1,128)S(1)}, u32[]{:S(2)}, u32[]{:S(2)}) collective-permute-start(f32[1,128]{1,0:T(1,128)S(1)} %add_add_fusion.9), channel_id=1, source_target_pairs={{0,24},{1,25},{2,26},{3,27},{4,28},{5,29},{6,30},{7,31},{8,16},{9,... | collective-permute-start | bytes 1544 | tf_op jit(solution)/shard_map/ppermute | solution.py:71
  75.1 4.5 %collective-permute-start.16 = (f32[1,128]{1,0:T(1,128)S(1)}, f32[1,128]{1,0:T(1,128)S(1)}, u32[]{:S(2)}, u32[]{:S(2)}) collective-permute-start(f32[1,128]{1,0:T(1,128)S(1)} %add_add_fusion.9), channel_id=1, source_target_pairs={{0,16},{1,17},{2,18},{3,19},{4,20},{5,21},{6,22},{7,23},{8,24},{9,... | collective-permute-start | bytes 1544 | tf_op jit(solution)/shard_map/ppermute | solution.py:71
  75.7 3.8 %collective-permute-start.15 = (f32[1,128]{1,0:T(1,128)S(1)}, f32[1,128]{1,0:T(1,128)S(1)}, u32[]{:S(2)}, u32[]{:S(2)}) collective-permute-start(f32[1,128]{1,0:T(1,128)S(1)} %add_add_fusion.9), channel_id=1, source_target_pairs={{0,8},{1,9},{2,10},{3,11},{4,12},{5,13},{6,14},{7,15},{8,0},{9,1},... | collective-permute-start | bytes 1544 | tf_op jit(solution)/shard_map/ppermute | solution.py:71
  87.8 4.5 %collective-permute-start.21 = (f32[1,128]{1,0:T(1,128)S(1)}, f32[1,128]{1,0:T(1,128)S(1)}, u32[]{:S(2)}, u32[]{:S(2)}) collective-permute-start(f32[1,128]{1,0:T(1,128)S(1)} %add.188), channel_id=1, source_target_pairs={{0,6},{1,7},{2,4},{3,5},{4,2},{5,3},{6,0},{7,1},{8,14},{9,15},{10,... | collective-permute-start | bytes 1544 | tf_op jit(solution)/shard_map/ppermute | solution.py:71
  88.2 4.1 %collective-permute-start.20 = (f32[1,128]{1,0:T(1,128)S(1)}, f32[1,128]{1,0:T(1,128)S(1)}, u32[]{:S(2)}, u32[]{:S(2)}) collective-permute-start(f32[1,128]{1,0:T(1,128)S(1)} %add.188), channel_id=1, source_target_pairs={{0,4},{1,5},{2,6},{3,7},{4,0},{5,1},{6,2},{7,3},{8,12},{9,13},{10,... | collective-permute-start | bytes 1544 | tf_op jit(solution)/shard_map/ppermute | solution.py:71
  93.0 5.4 %collective-permute-start.24 = (f32[1,128]{1,0:T(1,128)S(1)}, f32[1,128]{1,0:T(1,128)S(1)}, u32[]{:S(2)}, u32[]{:S(2)}) collective-permute-start(f32[1,128]{1,0:T(1,128)S(1)} %add_add_fusion.7), channel_id=1, source_target_pairs={{0,24},{1,25},{2,26},{3,27},{4,28},{5,29},{6,30},{7,31},{8,16},{9,... | collective-permute-start | bytes 1544 | tf_op jit(solution)/shard_map/ppermute | solution.py:71
  95.6 4.5 %collective-permute-start.23 = (f32[1,128]{1,0:T(1,128)S(1)}, f32[1,128]{1,0:T(1,128)S(1)}, u32[]{:S(2)}, u32[]{:S(2)}) collective-permute-start(f32[1,128]{1,0:T(1,128)S(1)} %add_add_fusion.7), channel_id=1, source_target_pairs={{0,16},{1,17},{2,18},{3,19},{4,20},{5,21},{6,22},{7,23},{8,24},{9,... | collective-permute-start | bytes 1544 | tf_op jit(solution)/shard_map/ppermute | solution.py:71
  96.5 3.6 %collective-permute-start.22 = (f32[1,128]{1,0:T(1,128)S(1)}, f32[1,128]{1,0:T(1,128)S(1)}, u32[]{:S(2)}, u32[]{:S(2)}) collective-permute-start(f32[1,128]{1,0:T(1,128)S(1)} %add_add_fusion.7), channel_id=1, source_target_pairs={{0,8},{1,9},{2,10},{3,11},{4,12},{5,13},{6,14},{7,15},{8,0},{9,1},... | collective-permute-start | bytes 1544 | tf_op jit(solution)/shard_map/ppermute | solution.py:71
  105.8 4.5 %collective-permute-start.28 = (f32[1,128]{1,0:T(1,128)S(1)}, f32[1,128]{1,0:T(1,128)S(1)}, u32[]{:S(2)}, u32[]{:S(2)}) collective-permute-start(f32[1,128]{1,0:T(1,128)S(1)} %add.195), channel_id=1, source_target_pairs={{0,6},{1,7},{2,4},{3,5},{4,2},{5,3},{6,0},{7,1},{8,14},{9,15},{10,... | collective-permute-start | bytes 1544 | tf_op jit(solution)/shard_map/ppermute | solution.py:71
  107.2 3.6 %collective-permute-start.27 = (f32[1,128]{1,0:T(1,128)S(1)}, f32[1,128]{1,0:T(1,128)S(1)}, u32[]{:S(2)}, u32[]{:S(2)}) collective-permute-start(f32[1,128]{1,0:T(1,128)S(1)} %add.195), channel_id=1, source_target_pairs={{0,4},{1,5},{2,6},{3,7},{4,0},{5,1},{6,2},{7,3},{8,12},{9,13},{10,... | collective-permute-start | bytes 1544 | tf_op jit(solution)/shard_map/ppermute | solution.py:71
  112.7 5.4 %collective-permute-start.31 = (f32[1,128]{1,0:T(1,128)S(1)}, f32[1,128]{1,0:T(1,128)S(1)}, u32[]{:S(2)}, u32[]{:S(2)}) collective-permute-start(f32[1,128]{1,0:T(1,128)S(1)} %add_add_fusion.5), channel_id=1, source_target_pairs={{0,24},{1,25},{2,26},{3,27},{4,28},{5,29},{6,30},{7,31},{8,16},{9,... | collective-permute-start | bytes 1544 | tf_op jit(solution)/shard_map/ppermute | solution.py:71
  114.2 4.5 %collective-permute-start.30 = (f32[1,128]{1,0:T(1,128)S(1)}, f32[1,128]{1,0:T(1,128)S(1)}, u32[]{:S(2)}, u32[]{:S(2)}) collective-permute-start(f32[1,128]{1,0:T(1,128)S(1)} %add_add_fusion.5), channel_id=1, source_target_pairs={{0,16},{1,17},{2,18},{3,19},{4,20},{5,21},{6,22},{7,23},{8,24},{9,... | collective-permute-start | bytes 1544 | tf_op jit(solution)/shard_map/ppermute | solution.py:71
  115.1 3.6 %collective-permute-start.29 = (f32[1,128]{1,0:T(1,128)S(1)}, f32[1,128]{1,0:T(1,128)S(1)}, u32[]{:S(2)}, u32[]{:S(2)}) collective-permute-start(f32[1,128]{1,0:T(1,128)S(1)} %add_add_fusion.5), channel_id=1, source_target_pairs={{0,8},{1,9},{2,10},{3,11},{4,12},{5,13},{6,14},{7,15},{8,0},{9,1},... | collective-permute-start | bytes 1544 | tf_op jit(solution)/shard_map/ppermute | solution.py:71
  126.5 4.5 %collective-permute-start.35 = (f32[1,128]{1,0:T(1,128)S(1)}, f32[1,128]{1,0:T(1,128)S(1)}, u32[]{:S(2)}, u32[]{:S(2)}) collective-permute-start(f32[1,128]{1,0:T(1,128)S(1)} %add.202), channel_id=1, source_target_pairs={{0,6},{1,7},{2,4},{3,5},{4,2},{5,3},{6,0},{7,1},{8,14},{9,15},{10,... | collective-permute-start | bytes 1544 | tf_op jit(solution)/shard_map/ppermute | solution.py:71
  126.9 4.1 %collective-permute-start.34 = (f32[1,128]{1,0:T(1,128)S(1)}, f32[1,128]{1,0:T(1,128)S(1)}, u32[]{:S(2)}, u32[]{:S(2)}) collective-permute-start(f32[1,128]{1,0:T(1,128)S(1)} %add.202), channel_id=1, source_target_pairs={{0,4},{1,5},{2,6},{3,7},{4,0},{5,1},{6,2},{7,3},{8,12},{9,13},{10,... | collective-permute-start | bytes 1544 | tf_op jit(solution)/shard_map/ppermute | solution.py:71
  131.7 5.4 %collective-permute-start.38 = (f32[1,128]{1,0:T(1,128)S(1)}, f32[1,128]{1,0:T(1,128)S(1)}, u32[]{:S(2)}, u32[]{:S(2)}) collective-permute-start(f32[1,128]{1,0:T(1,128)S(1)} %add_add_fusion.3), channel_id=1, source_target_pairs={{0,24},{1,25},{2,26},{3,27},{4,28},{5,29},{6,30},{7,31},{8,16},{9,... | collective-permute-start | bytes 1544 | tf_op jit(solution)/shard_map/ppermute | solution.py:71
  134.3 4.5 %collective-permute-start.37 = (f32[1,128]{1,0:T(1,128)S(1)}, f32[1,128]{1,0:T(1,128)S(1)}, u32[]{:S(2)}, u32[]{:S(2)}) collective-permute-start(f32[1,128]{1,0:T(1,128)S(1)} %add_add_fusion.3), channel_id=1, source_target_pairs={{0,16},{1,17},{2,18},{3,19},{4,20},{5,21},{6,22},{7,23},{8,24},{9,... | collective-permute-start | bytes 1544 | tf_op jit(solution)/shard_map/ppermute | solution.py:71
  135.2 3.6 %collective-permute-start.36 = (f32[1,128]{1,0:T(1,128)S(1)}, f32[1,128]{1,0:T(1,128)S(1)}, u32[]{:S(2)}, u32[]{:S(2)}) collective-permute-start(f32[1,128]{1,0:T(1,128)S(1)} %add_add_fusion.3), channel_id=1, source_target_pairs={{0,8},{1,9},{2,10},{3,11},{4,12},{5,13},{6,14},{7,15},{8,0},{9,1},... | collective-permute-start | bytes 1544 | tf_op jit(solution)/shard_map/ppermute | solution.py:71
  (11 other events, 57.0 us)

commit v14 on v13

--- a/solution.py
+++ b/solution.py
@@ -4,6 +4,7 @@
 from jax.experimental import pallas as pl
 from jax.experimental.pallas import tpu as pltpu
 from jax.sharding import PartitionSpec as P
+
 
 ITERS = 3
 HALO = 2 * ITERS
@@ -26,25 +27,6 @@
     return cells
 
 
-def stencil(padded, kappa_sq):
-    centre = padded[..., 1:-1, 1:-1]
-    edge_sum = (
-        padded[..., :-2, 1:-1]
-        + padded[..., 2:, 1:-1]
-        + padded[..., 1:-1, :-2]
-        + padded[..., 1:-1, 2:]
-    )
-    corners = (
-        padded[..., :-2, :-2] + padded[..., :-2, 2:] + padded[..., 2:, :-2] + padded[..., 2:, 2:]
-    )
-    return (kappa_sq + 20.0 / 6.0) * centre - (4.0 * edge_sum + corners) / 6.0
-
-
-def stiffen(field, kappa_sq):
-    pads = ((0, 0),) * (field.ndim - 2) + ((1, 1), (1, 1))
-    return stencil(jnp.pad(field, pads), kappa_sq)
-
-
 def _span_sum(terms, basis, partner):
     if not basis:
         return partner(0)
@@ -111,11 +93,6 @@
         return (r >= self.first_inner) & (r < self.first_inner + self.inner_rows)
 
 
-def _zero_edges(ref):
-    ref[0] = jnp.zeros(ref.shape[1:], ref.dtype)
-    ref[ref.shape[0] - 1] = jnp.zeros(ref.shape[1:], ref.dtype)
-
-
 def _apply_q(plan, reach, source, gain_ref, weight_ref, inside_ref, row_ref, inner_ref, stiff_ref,
              applied_ref, dot_source):
 
@@ -145,8 +122,8 @@
 
 
 def _first_kernel(plan, ext_ref, inside_ref, row_ref, inner_ref, diagonal_ref,
-                  z_out, gain_out, weight_out, stiff_out, applied_out, dots_out, stiff_obs_out,
-                  observed_scr, scratch):
+                  z_out, gain_out, weight_out, stiff_out, applied_out, dots_out, observed_scr,
+                  scratch):
     sublanes = z_out.shape[1]
     lanes = z_out.shape[2]
     probes = lanes // 2
@@ -187,8 +164,11 @@
     dots_out[0:1, :] = zz
     dots_out[1:2, :] = za
 
+
+def _observed_kernel(plan, observed_ref, gain_ref, diagonal_ref, stiff_obs_out):
     def observed_pass(r, carry):
-        stiff_obs = _stiffen_row(observed_scr, plan.first_inner + r, gain_out[plan.first_inner + r])
+        row = plan.first_inner + r
+        stiff_obs = _stiffen_row(observed_ref, row, gain_ref[row])
         stiff_obs_out[pl.ds(r, 1), :] = _plane_row(stiff_obs, diagonal_ref[...] > 0.5)
         return carry
 
@@ -374,10 +354,13 @@
     lane_row = jax.ShapeDtypeStruct((1, lanes), jnp.float32)
     out_plane = jax.ShapeDtypeStruct((rows, cols), jnp.float32)
 
-    z, gain, weight, stiff_probe, applied, first, stiff_obs = _call(
+    z, gain, weight, stiff_probe, applied, first, observed_lanes = _call(
         _first_kernel, plan, (ext, inside, row_in, inner, diagonal),
-        (field, field, field, field, field, jax.ShapeDtypeStruct((2, lanes), jnp.float32), out_plane),
-        scratch=2, smem=(2,),
+        (field, field, field, field, field, jax.ShapeDtypeStruct((2, lanes), jnp.float32), field),
+        scratch=1, smem=(2,),
+    )
+    (stiff_obs,) = _call(
+        _observed_kernel, plan, (observed_lanes, gain, diagonal), (out_plane,), field=field
     )
     first = all_sum(first)
     residual, rr = _call(_start_kernel, plan, (first, z, applied, inner), (field, lane_row))

time: 146 us -> 146 us (level)
  waiting for transfers between devices: 33.9 us -> 31.2 us
  Pallas kernels: 34.8 us -> 37.4 us
    ppermute x35, waiting for transfers between devices: 30.8 us -> 28.1 us  [partner(): lax.ppermute(terms, axes, [(i, i ^ mask) for i in range(count)])]
    pallas_call x6 -> x7, Pallas kernels: 34.8 us -> 37.4 us  [_call(): pl.pallas_call(lambda *refs: kernel(plan, *refs), out_shape=out_shapes, i...]
  transfers between devices with their start and end apart: 39 -> 39, of which waited for: 30 -> 28; matrix products, arithmetic and copies ran while one was open for 7% -> 7% of each run, Pallas kernels for 0% -> 2%
where the time goes in v14:
time: 146 us; the launch traced here: 145 us
  starting transfers between devices  54.1 us (37%)
  Pallas kernels  37.4 us (26%)
  waiting for transfers between devices  31.2 us (21%)
  other arithmetic  13.2 us (9%)
  local copies, waits for them, and re-layouts  8.58 us (6%)
    ppermute x35, starting transfers between devices, partner(): lax.ppermute(terms, axes, [(i, i ^ mask) for i in range(count)])  43.4 us
    pallas_call x7, Pallas kernels, _call(): pl.pallas_call(lambda *refs: kernel(plan, *refs), out_shape=out_shapes, i...  37.4 us
    ppermute x35, waiting for transfers between devices, partner(): lax.ppermute(terms, axes, [(i, i ^ mask) for i in range(count)])  28.1 us
    ppermute x1, starting transfers between devices, on_device(): lax.ppermute(edge_rows(rows - sent), 'rows', [(i, i + 1) for i in range(c...  6.21 us
    add x15, other arithmetic, _span_sum(): _span_sum(terms, rest, partner)  6.12 us
    broadcast_in_dim x3, local copies, waits for them, and re-layouts, on_device(): fields = (probes, observed[None], kappa_sq[None], variance_weight[None])  3.09 us
  transfers between devices with their start and end apart: 39, of which 28 were waited for; matrix products, arithmetic and copies ran while one was open for 7% of the time, Pallas kernels for 2%

profile of v14, /device:TPU:0, one launch (start us, length us, event | category | flops | bytes accessed | tf_op | source)
XLA Modules:
  0.0 145.4 jit_solution(16844951485890833390)
XLA Ops:
  5.3 6.2 %collective-permute-start = (f32[536,128]{1,0:T(8,128)}, f32[536,128]{1,0:T(8,128)}, u32[]{:S(2)}, u32[]{:S(2)}) collective-permute-start(f32[536,128]{1,0:T(8,128)} %maximum_bitcast_fusion.1), channel_id=1, source_target_pairs={{0,4},{4,8},{8,12},{12,16},{16,20},{20,24},{24,28},{1,5},{5,9},{9,... | collective-permute-start | bytes 823304 | tf_op jit(solution)/shard_map/ppermute | solution.py:318
  15.8 2.4 %maximum_bitcast_fusion = f32[16,128,67]{2,1,0:T(8,128)S(1)} fusion(f32[1,16,128]{0,2,1:T(8,128)} %copy.17, f32[1,16,128]{0,2,1:T(8,128)S(1)} %copy.16, f32[1,16,128]{0,2,1:T(8,128)} %copy.15, f32[64,16,128]{0,2,1:T(8,128)S(1)} %copy.14), kind=kLoop, calls=%fused_computation.13 | loop fusion | flops 411648 | bytes 1097728 | tf_op jit(solution)/shard_map/transpose | solution.py:325
  22.1 1.9 %collective-permute-start.2 = (f32[28,6,67]{2,1,0:T(8,128)S(1)}, f32[28,6,67]{2,1,0:T(8,128)S(1)}, u32[]{:S(2)}, u32[]{:S(2)}) collective-permute-start(f32[28,6,67]{2,1,0:T(8,128)S(1)} %get-tuple-element.34), channel_id=1, source_target_pairs={{0,1},{1,2},{2,3},{4,5},{5,6},{6,7},{8,9},{9,10},{10,11},{12,13},{... | collective-permute-start | bytes 135080 | tf_op jit(solution)/shard_map/ppermute | solution.py:21
  25.8 2.5 %collective-permute-done.3 = f32[28,6,67]{2,1,0:T(8,128)S(1)} collective-permute-done((f32[28,6,67]{2,1,0:T(8,128)S(1)}, f32[28,6,67]{2,1,0:T(8,128)S(1)}, u32[]{:S(2)}, u32[]{:S(2)}) %collective-permute-start.3) | collective-permute-done | bytes 45056 | tf_op jit(solution)/shard_map/ppermute | solution.py:23
  28.3 1.9 %select_maximum_fusion.refs_0_ = f32[28,144,128]{2,1,0:T(8,128)} fusion(f32[28,6,67]{2,1,0:T(8,128)S(1)} %collective-permute-done.3, f32[28,6,67]{2,1,0:T(8,128)S(1)} %collective-permute-done.2, f32[6,128,67]{2,1,0:T(8,128)S(1)} %bitcast.15, f32[16,128,67]{2,1,0:T(8,128)S(1)} %maximum_bitcast_fusion, f32[6,128,67]{2,1,0:T(8,128)S(1)} %bitcast.17), kind=kLoop, calls=%fused_computation | loop fusion | flops 8773632 | bytes 3114944 | tf_op jit(solution)/shard_map/concatenate | solution.py:19
  30.3 10.7 %shard_map.59 = (f32[28,80,128]{2,1,0:T(8,128)}, f32[28,80,128]{2,1,0:T(8,128)}, f32[28,80,128]{2,1,0:T(8,128)}, f32[28,80,128]{2,1,0:T(8,128)}, f32[28,80,128]{...) custom-call(f32[28,144,128]{2,1,0:T(8,128)} %select_maximum_fusion.refs_0_, ...), custom_call_target="tpu_custom_call" | custom-call | flops 11468800 | bytes 13762560 | tf_op jit(solution)/shard_map/pallas_call | solution.py:283
  41.0 3.4 %collective-permute-start.4 = (f32[2,128]{1,0:T(2,128)}, f32[2,128]{1,0:T(2,128)S(1)}, u32[]{:S(2)}, u32[]{:S(2)}) collective-permute-start(f32[2,128]{1,0:T(2,128)} %get-tuple-element.18), channel_id=1, source_target_pairs={{0,1},{1,0},{2,3},{3,2},{4,5},{5,4},{6,7},{7,6},{8,9},{9,8},{10,11... | collective-permute-start | bytes 3080 | tf_op jit(solution)/shard_map/ppermute | solution.py:53
  46.1 2.0 %collective-permute-start.7 = (f32[2,128]{1,0:T(2,128)S(1)}, f32[2,128]{1,0:T(2,128)S(1)}, u32[]{:S(2)}, u32[]{:S(2)}) collective-permute-start(f32[2,128]{1,0:T(2,128)S(1)} %add.178), channel_id=1, source_target_pairs={{0,6},{1,7},{2,4},{3,5},{4,2},{5,3},{6,0},{7,1},{8,14},{9,15},{10,... | collective-permute-start | bytes 3080 | tf_op jit(solution)/shard_map/ppermute | solution.py:53
  48.6 1.5 %collective-permute-start.5 = (f32[2,128]{1,0:T(2,128)S(1)}, f32[2,128]{1,0:T(2,128)S(1)}, u32[]{:S(2)}, u32[]{:S(2)}) collective-permute-start(f32[2,128]{1,0:T(2,128)S(1)} %add.178), channel_id=1, source_target_pairs={{0,2},{1,3},{2,0},{3,1},{4,6},{5,7},{6,4},{7,5},{8,10},{9,11},{10,... | collective-permute-start | bytes 3080 | tf_op jit(solution)/shard_map/ppermute | solution.py:53
  52.1 3.9 %collective-permute-start.10 = (f32[2,128]{1,0:T(2,128)S(1)}, f32[2,128]{1,0:T(2,128)S(1)}, u32[]{:S(2)}, u32[]{:S(2)}) collective-permute-start(f32[2,128]{1,0:T(2,128)S(1)} %add_add_fusion.1), channel_id=1, source_target_pairs={{0,24},{1,25},{2,26},{3,27},{4,28},{5,29},{6,30},{7,31},{8,16},{9,... | collective-permute-start | bytes 3080 | tf_op jit(solution)/shard_map/ppermute | solution.py:53
  57.6 2.9 %collective-permute-done.9 = f32[2,128]{1,0:T(2,128)S(1)} collective-permute-done((f32[2,128]{1,0:T(2,128)S(1)}, f32[2,128]{1,0:T(2,128)S(1)}, u32[]{:S(2)}, u32[]{:S(2)}) %collective-permute-start.9) | collective-permute-done | bytes 1056 | tf_op jit(solution)/shard_map/ppermute | solution.py:53
  61.1 3.4 %shard_map.60 = (f32[28,80,128]{2,1,0:T(8,128)}, f32[1,128]{1,0:T(1,128)}) custom-call(f32[2,128]{1,0:T(2,128)} %add_add_fusion.refs_0_.refs_1_, f32[28,80,128]{2,1,0:T(8,128)} %get-tuple-element.19.refs_1_.refs_3_.refs_6_.refs_9_, f32[28,80,128]{2,1,0:T(8,128)} %get-tuple-element.20.refs_2_, f32[80,128]{1,0:T(8,128)} %add_convert_fusion.1.refs_3_.refs_8_.refs_4_), custom_call_target="tpu_custom_call" | custom-call | flops 11468800 | bytes 6881280 | tf_op jit(solution)/shard_map/pallas_call | solution.py:283
  66.5 1.4 collective-permute-start.14
  67.9 2.0 %collective-permute-start.13 = (f32[1,128]{1,0:T(1,128)S(1)}, f32[1,128]{1,0:T(1,128)S(1)}, u32[]{:S(2)}, u32[]{:S(2)}) collective-permute-start(f32[1,128]{1,0:T(1,128)S(1)} %add.185), channel_id=1, source_target_pairs={{0,4},{1,5},{2,6},{3,7},{4,0},{5,1},{6,2},{7,3},{8,12},{9,13},{10,... | collective-permute-start | bytes 1544 | tf_op jit(solution)/shard_map/ppermute | solution.py:53
  71.5 2.0 %collective-permute-done.12 = f32[1,128]{1,0:T(1,128)S(1)} collective-permute-done((f32[1,128]{1,0:T(1,128)S(1)}, f32[1,128]{1,0:T(1,128)S(1)}, u32[]{:S(2)}, u32[]{:S(2)}) %collective-permute-start.12) | collective-permute-done | bytes 544 | tf_op jit(solution)/shard_map/ppermute | solution.py:53
  73.4 1.5 %collective-permute-start.17 = (f32[1,128]{1,0:T(1,128)S(1)}, f32[1,128]{1,0:T(1,128)S(1)}, u32[]{:S(2)}, u32[]{:S(2)}) collective-permute-start(f32[1,128]{1,0:T(1,128)S(1)} %add_add_fusion.9), channel_id=1, source_target_pairs={{0,24},{1,25},{2,26},{3,27},{4,28},{5,29},{6,30},{7,31},{8,16},{9,... | collective-permute-start | bytes 1544 | tf_op jit(solution)/shard_map/ppermute | solution.py:53
  75.5 2.3 %collective-permute-start.15 = (f32[1,128]{1,0:T(1,128)S(1)}, f32[1,128]{1,0:T(1,128)S(1)}, u32[]{:S(2)}, u32[]{:S(2)}) collective-permute-start(f32[1,128]{1,0:T(1,128)S(1)} %add_add_fusion.9), channel_id=1, source_target_pairs={{0,8},{1,9},{2,10},{3,11},{4,12},{5,13},{6,14},{7,15},{8,0},{9,1},... | collective-permute-start | bytes 1544 | tf_op jit(solution)/shard_map/ppermute | solution.py:53
  79.9 5.8 %shard_map.61 = (f32[28,80,128]{2,1,0:T(8,128)}, f32[28,80,128]{2,1,0:T(8,128)}, f32[1,128]{1,0:T(1,128)}) custom-call(f32[1,128]{1,0:T(1,128)} %add_add_fusion.8.refs_0_.refs_1_.refs_2_, f32[2,128]{1,0:T(2,128)} %add_add_fusion.refs_0_.refs_1_, f32[28,80,128]{2,1,0:T(8,128)} %get-tuple-element.22.refs_2_, ...), custom_call_target="tpu_custom_call" | custom-call | flops 11468800 | bytes 13762560 | tf_op jit(solution)/shard_map/pallas_call | solution.py:283
  89.2 1.9 %collective-permute-start.19 = (f32[1,128]{1,0:T(1,128)S(1)}, f32[1,128]{1,0:T(1,128)S(1)}, u32[]{:S(2)}, u32[]{:S(2)}) collective-permute-start(f32[1,128]{1,0:T(1,128)S(1)} %add.192), channel_id=1, source_target_pairs={{0,2},{1,3},{2,0},{3,1},{4,6},{5,7},{6,4},{7,5},{8,10},{9,11},{10,... | collective-permute-start | bytes 1544 | tf_op jit(solution)/shard_map/ppermute | solution.py:53
  92.8 2.6 %collective-permute-start.24 = (f32[1,128]{1,0:T(1,128)S(1)}, f32[1,128]{1,0:T(1,128)S(1)}, u32[]{:S(2)}, u32[]{:S(2)}) collective-permute-start(f32[1,128]{1,0:T(1,128)S(1)} %add_add_fusion.7), channel_id=1, source_target_pairs={{0,24},{1,25},{2,26},{3,27},{4,28},{5,29},{6,30},{7,31},{8,16},{9,... | collective-permute-start | bytes 1544 | tf_op jit(solution)/shard_map/ppermute | solution.py:53
  98.1 1.7 %collective-permute-done.23 = f32[1,128]{1,0:T(1,128)S(1)} collective-permute-done((f32[1,128]{1,0:T(1,128)S(1)}, f32[1,128]{1,0:T(1,128)S(1)}, u32[]{:S(2)}, u32[]{:S(2)}) %collective-permute-start.23) | collective-permute-done | bytes 544 | tf_op jit(solution)/shard_map/ppermute | solution.py:53
  100.4 3.2 %shard_map.62 = (f32[28,80,128]{2,1,0:T(8,128)}, f32[1,128]{1,0:T(1,128)}) custom-call(f32[1,128]{1,0:T(1,128)} %add_add_fusion.8.refs_0_.refs_1_.refs_2_, f32[1,128]{1,0:T(1,128)} %add_add_fusion.6.refs_1_.refs_3_, f32[28,80,128]{2,1,0:T(8,128)} %get-tuple-element.22.refs_2_, f32[28,80,128]{2,1,0:T(8,128)} %get-tuple-element.26.refs_3_, ...), custom_call_target="tpu_custom_call" | custom-call | flops 11468800 | bytes 8028160 | tf_op jit(solution)/shard_map/pallas_call | solution.py:283
  105.5 1.4 collective-permute-start.28
  106.9 2.0 %collective-permute-start.27 = (f32[1,128]{1,0:T(1,128)S(1)}, f32[1,128]{1,0:T(1,128)S(1)}, u32[]{:S(2)}, u32[]{:S(2)}) collective-permute-start(f32[1,128]{1,0:T(1,128)S(1)} %add.199), channel_id=1, source_target_pairs={{0,4},{1,5},{2,6},{3,7},{4,0},{5,1},{6,2},{7,3},{8,12},{9,13},{10,... | collective-permute-start | bytes 1544 | tf_op jit(solution)/shard_map/ppermute | solution.py:53
  110.5 2.0 %collective-permute-done.26 = f32[1,128]{1,0:T(1,128)S(1)} collective-permute-done((f32[1,128]{1,0:T(1,128)S(1)}, f32[1,128]{1,0:T(1,128)S(1)}, u32[]{:S(2)}, u32[]{:S(2)}) %collective-permute-start.26) | collective-permute-done | bytes 544 | tf_op jit(solution)/shard_map/ppermute | solution.py:53
  112.5 1.5 %collective-permute-start.31 = (f32[1,128]{1,0:T(1,128)S(1)}, f32[1,128]{1,0:T(1,128)S(1)}, u32[]{:S(2)}, u32[]{:S(2)}) collective-permute-start(f32[1,128]{1,0:T(1,128)S(1)} %add_add_fusion.5), channel_id=1, source_target_pairs={{0,24},{1,25},{2,26},{3,27},{4,28},{5,29},{6,30},{7,31},{8,16},{9,... | collective-permute-start | bytes 1544 | tf_op jit(solution)/shard_map/ppermute | solution.py:53
  114.8 2.0 %collective-permute-start.29 = (f32[1,128]{1,0:T(1,128)S(1)}, f32[1,128]{1,0:T(1,128)S(1)}, u32[]{:S(2)}, u32[]{:S(2)}) collective-permute-start(f32[1,128]{1,0:T(1,128)S(1)} %add_add_fusion.5), channel_id=1, source_target_pairs={{0,8},{1,9},{2,10},{3,11},{4,12},{5,13},{6,14},{7,15},{8,0},{9,1},... | collective-permute-start | bytes 1544 | tf_op jit(solution)/shard_map/ppermute | solution.py:53
  118.9 5.4 %shard_map.63 = (f32[28,80,128]{2,1,0:T(8,128)}, f32[28,80,128]{2,1,0:T(8,128)}, f32[1,128]{1,0:T(1,128)}) custom-call(f32[1,128]{1,0:T(1,128)} %add_add_fusion.4.refs_0_.refs_4_, f32[1,128]{1,0:T(1,128)} %add_add_fusion.8.refs_0_.refs_1_.refs_2_, f32[28,80,128]{2,1,0:T(8,128)} %get-tuple-element.28.refs_2_, ...), custom_call_target="tpu_custom_call" | custom-call | flops 11468800 | bytes 13762560 | tf_op jit(solution)/shard_map/pallas_call | solution.py:283
  127.8 1.9 %collective-permute-start.33 = (f32[1,128]{1,0:T(1,128)S(1)}, f32[1,128]{1,0:T(1,128)S(1)}, u32[]{:S(2)}, u32[]{:S(2)}) collective-permute-start(f32[1,128]{1,0:T(1,128)S(1)} %add.206), channel_id=1, source_target_pairs={{0,2},{1,3},{2,0},{3,1},{4,6},{5,7},{6,4},{7,5},{8,10},{9,11},{10,... | collective-permute-start | bytes 1544 | tf_op jit(solution)/shard_map/ppermute | solution.py:53
  131.4 2.6 %collective-permute-start.38 = (f32[1,128]{1,0:T(1,128)S(1)}, f32[1,128]{1,0:T(1,128)S(1)}, u32[]{:S(2)}, u32[]{:S(2)}) collective-permute-start(f32[1,128]{1,0:T(1,128)S(1)} %add_add_fusion.3), channel_id=1, source_target_pairs={{0,24},{1,25},{2,26},{3,27},{4,28},{5,29},{6,30},{7,31},{8,16},{9,... | collective-permute-start | bytes 1544 | tf_op jit(solution)/shard_map/ppermute | solution.py:53
  135.8 2.8 %shard_map.64.refs_12_ = f32[16,128]{1,0:T(8,128)} custom-call(f32[28,80,128]{2,1,0:T(8,128)} %get-tuple-element.33.refs_0_, f32[28,80,128]{2,1,0:T(8,128)} %get-tuple-element.23.refs_4_.refs_1_.refs_11_, f32[80,128]{1,0:T(8,128)} %get-tuple-element.46.refs_4_.refs_2_.refs_15_), custom_call_target="tpu_custom_call" | custom-call | flops 11468800 | bytes 4587520 | tf_op jit(solution)/shard_map/pallas_call | solution.py:283
  139.2 6.2 %shard_map.65 = (f32[16,128]{1,0:T(8,128)}, f32[16,128]{1,0:T(8,128)}) custom-call(f32[2,128]{1,0:T(2,128)} %add_add_fusion.refs_0_.refs_1_, f32[2,128]{1,0:T(2,128)} %add_add_fusion.refs_0_.refs_1_, f32[1,128]{1,0:T(1,128)} %add_add_fusion.8.refs_0_.refs_1_.refs_2_, f32[1,128]{1,0:T(1,128)} %add_add_fusion.6.refs_1_.refs_3_, ...), custom_call_target="tpu_custom_call" | custom-call | flops 11468800 | bytes 20643840 | tf_op jit(solution)/shard_map/pallas_call | solution.py:283
  (101 shorter events, 49.9 us)
Async XLA Ops:
  3.3 15.8 %collective-permute-start.1 = (f32[536,128]{1,0:T(8,128)S(1)}, f32[536,128]{1,0:T(8,128)}, u32[]{:S(2)}, u32[]{:S(2)}) collective-permute-start(f32[536,128]{1,0:T(8,128)S(1)} %maximum_bitcast_fusion.2), channel_id=1, source_target_pairs={{4,0},{8,4},{12,8},{16,12},{20,16},{24,20},{28,24},{5,1},{9,5},{13... | collective-permute-start | bytes 823304 | tf_op jit(solution)/shard_map/ppermute | solution.py:321
  5.3 15.5 %collective-permute-start = (f32[536,128]{1,0:T(8,128)}, f32[536,128]{1,0:T(8,128)}, u32[]{:S(2)}, u32[]{:S(2)}) collective-permute-start(f32[536,128]{1,0:T(8,128)} %maximum_bitcast_fusion.1), channel_id=1, source_target_pairs={{0,4},{4,8},{8,12},{12,16},{16,20},{20,24},{24,28},{1,5},{5,9},{9,... | collective-permute-start | bytes 823304 | tf_op jit(solution)/shard_map/ppermute | solution.py:318
  22.1 3.8 %collective-permute-start.2 = (f32[28,6,67]{2,1,0:T(8,128)S(1)}, f32[28,6,67]{2,1,0:T(8,128)S(1)}, u32[]{:S(2)}, u32[]{:S(2)}) collective-permute-start(f32[28,6,67]{2,1,0:T(8,128)S(1)} %get-tuple-element.34), channel_id=1, source_target_pairs={{0,1},{1,2},{2,3},{4,5},{5,6},{6,7},{8,9},{9,10},{10,11},{12,13},{... | collective-permute-start | bytes 135080 | tf_op jit(solution)/shard_map/ppermute | solution.py:21
  24.0 4.3 %collective-permute-start.3 = (f32[28,6,67]{2,1,0:T(8,128)S(1)}, f32[28,6,67]{2,1,0:T(8,128)S(1)}, u32[]{:S(2)}, u32[]{:S(2)}) collective-permute-start(f32[28,6,67]{2,1,0:T(8,128)S(1)} %get-tuple-element.35), channel_id=1, source_target_pairs={{1,0},{2,1},{3,2},{5,4},{6,5},{7,6},{9,8},{10,9},{11,10},{13,12},{... | collective-permute-start | bytes 135080 | tf_op jit(solution)/shard_map/ppermute | solution.py:23
  41.0 4.4 %collective-permute-start.4 = (f32[2,128]{1,0:T(2,128)}, f32[2,128]{1,0:T(2,128)S(1)}, u32[]{:S(2)}, u32[]{:S(2)}) collective-permute-start(f32[2,128]{1,0:T(2,128)} %get-tuple-element.18), channel_id=1, source_target_pairs={{0,1},{1,0},{2,3},{3,2},{4,5},{5,4},{6,7},{7,6},{8,9},{9,8},{10,11... | collective-permute-start | bytes 3080 | tf_op jit(solution)/shard_map/ppermute | solution.py:53
  46.1 4.5 %collective-permute-start.7 = (f32[2,128]{1,0:T(2,128)S(1)}, f32[2,128]{1,0:T(2,128)S(1)}, u32[]{:S(2)}, u32[]{:S(2)}) collective-permute-start(f32[2,128]{1,0:T(2,128)S(1)} %add.178), channel_id=1, source_target_pairs={{0,6},{1,7},{2,4},{3,5},{4,2},{5,3},{6,0},{7,1},{8,14},{9,15},{10,... | collective-permute-start | bytes 3080 | tf_op jit(solution)/shard_map/ppermute | solution.py:53
  48.1 3.6 %collective-permute-start.6 = (f32[2,128]{1,0:T(2,128)S(1)}, f32[2,128]{1,0:T(2,128)S(1)}, u32[]{:S(2)}, u32[]{:S(2)}) collective-permute-start(f32[2,128]{1,0:T(2,128)S(1)} %add.178), channel_id=1, source_target_pairs={{0,4},{1,5},{2,6},{3,7},{4,0},{5,1},{6,2},{7,3},{8,12},{9,13},{10,... | collective-permute-start | bytes 3080 | tf_op jit(solution)/shard_map/ppermute | solution.py:53
  48.6 3.6 %collective-permute-start.5 = (f32[2,128]{1,0:T(2,128)S(1)}, f32[2,128]{1,0:T(2,128)S(1)}, u32[]{:S(2)}, u32[]{:S(2)}) collective-permute-start(f32[2,128]{1,0:T(2,128)S(1)} %add.178), channel_id=1, source_target_pairs={{0,2},{1,3},{2,0},{3,1},{4,6},{5,7},{6,4},{7,5},{8,10},{9,11},{10,... | collective-permute-start | bytes 3080 | tf_op jit(solution)/shard_map/ppermute | solution.py:53
  52.1 5.5 %collective-permute-start.10 = (f32[2,128]{1,0:T(2,128)S(1)}, f32[2,128]{1,0:T(2,128)S(1)}, u32[]{:S(2)}, u32[]{:S(2)}) collective-permute-start(f32[2,128]{1,0:T(2,128)S(1)} %add_add_fusion.1), channel_id=1, source_target_pairs={{0,24},{1,25},{2,26},{3,27},{4,28},{5,29},{6,30},{7,31},{8,16},{9,... | collective-permute-start | bytes 3080 | tf_op jit(solution)/shard_map/ppermute | solution.py:53
  56.1 4.5 %collective-permute-start.9 = (f32[2,128]{1,0:T(2,128)S(1)}, f32[2,128]{1,0:T(2,128)S(1)}, u32[]{:S(2)}, u32[]{:S(2)}) collective-permute-start(f32[2,128]{1,0:T(2,128)S(1)} %add_add_fusion.1), channel_id=1, source_target_pairs={{0,16},{1,17},{2,18},{3,19},{4,20},{5,21},{6,22},{7,23},{8,24},{9,... | collective-permute-start | bytes 3080 | tf_op jit(solution)/shard_map/ppermute | solution.py:53
  56.1 4.5 %collective-permute-start.8 = (f32[2,128]{1,0:T(2,128)S(1)}, f32[2,128]{1,0:T(2,128)S(1)}, u32[]{:S(2)}, u32[]{:S(2)}) collective-permute-start(f32[2,128]{1,0:T(2,128)S(1)} %add_add_fusion.1), channel_id=1, source_target_pairs={{0,8},{1,9},{2,10},{3,11},{4,12},{5,13},{6,14},{7,15},{8,0},{9,1},... | collective-permute-start | bytes 3080 | tf_op jit(solution)/shard_map/ppermute | solution.py:53
  66.5 4.5 %collective-permute-start.14 = (f32[1,128]{1,0:T(1,128)S(1)}, f32[1,128]{1,0:T(1,128)S(1)}, u32[]{:S(2)}, u32[]{:S(2)}) collective-permute-start(f32[1,128]{1,0:T(1,128)S(1)} %add.185), channel_id=1, source_target_pairs={{0,6},{1,7},{2,4},{3,5},{4,2},{5,3},{6,0},{7,1},{8,14},{9,15},{10,... | collective-permute-start | bytes 1544 | tf_op jit(solution)/shard_map/ppermute | solution.py:53
  67.9 3.6 %collective-permute-start.13 = (f32[1,128]{1,0:T(1,128)S(1)}, f32[1,128]{1,0:T(1,128)S(1)}, u32[]{:S(2)}, u32[]{:S(2)}) collective-permute-start(f32[1,128]{1,0:T(1,128)S(1)} %add.185), channel_id=1, source_target_pairs={{0,4},{1,5},{2,6},{3,7},{4,0},{5,1},{6,2},{7,3},{8,12},{9,13},{10,... | collective-permute-start | bytes 1544 | tf_op jit(solution)/shard_map/ppermute | solution.py:53
  69.9 3.6 %collective-permute-start.12 = (f32[1,128]{1,0:T(1,128)S(1)}, f32[1,128]{1,0:T(1,128)S(1)}, u32[]{:S(2)}, u32[]{:S(2)}) collective-permute-start(f32[1,128]{1,0:T(1,128)S(1)} %add.185), channel_id=1, source_target_pairs={{0,2},{1,3},{2,0},{3,1},{4,6},{5,7},{6,4},{7,5},{8,10},{9,11},{10,... | collective-permute-start | bytes 1544 | tf_op jit(solution)/shard_map/ppermute | solution.py:53
  73.4 5.4 %collective-permute-start.17 = (f32[1,128]{1,0:T(1,128)S(1)}, f32[1,128]{1,0:T(1,128)S(1)}, u32[]{:S(2)}, u32[]{:S(2)}) collective-permute-start(f32[1,128]{1,0:T(1,128)S(1)} %add_add_fusion.9), channel_id=1, source_target_pairs={{0,24},{1,25},{2,26},{3,27},{4,28},{5,29},{6,30},{7,31},{8,16},{9,... | collective-permute-start | bytes 1544 | tf_op jit(solution)/shard_map/ppermute | solution.py:53
  74.9 4.5 %collective-permute-start.16 = (f32[1,128]{1,0:T(1,128)S(1)}, f32[1,128]{1,0:T(1,128)S(1)}, u32[]{:S(2)}, u32[]{:S(2)}) collective-permute-start(f32[1,128]{1,0:T(1,128)S(1)} %add_add_fusion.9), channel_id=1, source_target_pairs={{0,16},{1,17},{2,18},{3,19},{4,20},{5,21},{6,22},{7,23},{8,24},{9,... | collective-permute-start | bytes 1544 | tf_op jit(solution)/shard_map/ppermute | solution.py:53
  75.5 3.8 %collective-permute-start.15 = (f32[1,128]{1,0:T(1,128)S(1)}, f32[1,128]{1,0:T(1,128)S(1)}, u32[]{:S(2)}, u32[]{:S(2)}) collective-permute-start(f32[1,128]{1,0:T(1,128)S(1)} %add_add_fusion.9), channel_id=1, source_target_pairs={{0,8},{1,9},{2,10},{3,11},{4,12},{5,13},{6,14},{7,15},{8,0},{9,1},... | collective-permute-start | bytes 1544 | tf_op jit(solution)/shard_map/ppermute | solution.py:53
  87.6 4.5 %collective-permute-start.21 = (f32[1,128]{1,0:T(1,128)S(1)}, f32[1,128]{1,0:T(1,128)S(1)}, u32[]{:S(2)}, u32[]{:S(2)}) collective-permute-start(f32[1,128]{1,0:T(1,128)S(1)} %add.192), channel_id=1, source_target_pairs={{0,6},{1,7},{2,4},{3,5},{4,2},{5,3},{6,0},{7,1},{8,14},{9,15},{10,... | collective-permute-start | bytes 1544 | tf_op jit(solution)/shard_map/ppermute | solution.py:53
  88.0 4.1 %collective-permute-start.20 = (f32[1,128]{1,0:T(1,128)S(1)}, f32[1,128]{1,0:T(1,128)S(1)}, u32[]{:S(2)}, u32[]{:S(2)}) collective-permute-start(f32[1,128]{1,0:T(1,128)S(1)} %add.192), channel_id=1, source_target_pairs={{0,4},{1,5},{2,6},{3,7},{4,0},{5,1},{6,2},{7,3},{8,12},{9,13},{10,... | collective-permute-start | bytes 1544 | tf_op jit(solution)/shard_map/ppermute | solution.py:53
  89.2 3.6 %collective-permute-start.19 = (f32[1,128]{1,0:T(1,128)S(1)}, f32[1,128]{1,0:T(1,128)S(1)}, u32[]{:S(2)}, u32[]{:S(2)}) collective-permute-start(f32[1,128]{1,0:T(1,128)S(1)} %add.192), channel_id=1, source_target_pairs={{0,2},{1,3},{2,0},{3,1},{4,6},{5,7},{6,4},{7,5},{8,10},{9,11},{10,... | collective-permute-start | bytes 1544 | tf_op jit(solution)/shard_map/ppermute | solution.py:53
  92.8 5.4 %collective-permute-start.24 = (f32[1,128]{1,0:T(1,128)S(1)}, f32[1,128]{1,0:T(1,128)S(1)}, u32[]{:S(2)}, u32[]{:S(2)}) collective-permute-start(f32[1,128]{1,0:T(1,128)S(1)} %add_add_fusion.7), channel_id=1, source_target_pairs={{0,24},{1,25},{2,26},{3,27},{4,28},{5,29},{6,30},{7,31},{8,16},{9,... | collective-permute-start | bytes 1544 | tf_op jit(solution)/shard_map/ppermute | solution.py:53
  95.3 4.5 %collective-permute-start.23 = (f32[1,128]{1,0:T(1,128)S(1)}, f32[1,128]{1,0:T(1,128)S(1)}, u32[]{:S(2)}, u32[]{:S(2)}) collective-permute-start(f32[1,128]{1,0:T(1,128)S(1)} %add_add_fusion.7), channel_id=1, source_target_pairs={{0,16},{1,17},{2,18},{3,19},{4,20},{5,21},{6,22},{7,23},{8,24},{9,... | collective-permute-start | bytes 1544 | tf_op jit(solution)/shard_map/ppermute | solution.py:53
  96.3 3.6 %collective-permute-start.22 = (f32[1,128]{1,0:T(1,128)S(1)}, f32[1,128]{1,0:T(1,128)S(1)}, u32[]{:S(2)}, u32[]{:S(2)}) collective-permute-start(f32[1,128]{1,0:T(1,128)S(1)} %add_add_fusion.7), channel_id=1, source_target_pairs={{0,8},{1,9},{2,10},{3,11},{4,12},{5,13},{6,14},{7,15},{8,0},{9,1},... | collective-permute-start | bytes 1544 | tf_op jit(solution)/shard_map/ppermute | solution.py:53
  105.5 4.5 %collective-permute-start.28 = (f32[1,128]{1,0:T(1,128)S(1)}, f32[1,128]{1,0:T(1,128)S(1)}, u32[]{:S(2)}, u32[]{:S(2)}) collective-permute-start(f32[1,128]{1,0:T(1,128)S(1)} %add.199), channel_id=1, source_target_pairs={{0,6},{1,7},{2,4},{3,5},{4,2},{5,3},{6,0},{7,1},{8,14},{9,15},{10,... | collective-permute-start | bytes 1544 | tf_op jit(solution)/shard_map/ppermute | solution.py:53
  112.5 5.4 %collective-permute-start.31 = (f32[1,128]{1,0:T(1,128)S(1)}, f32[1,128]{1,0:T(1,128)S(1)}, u32[]{:S(2)}, u32[]{:S(2)}) collective-permute-start(f32[1,128]{1,0:T(1,128)S(1)} %add_add_fusion.5), channel_id=1, source_target_pairs={{0,24},{1,25},{2,26},{3,27},{4,28},{5,29},{6,30},{7,31},{8,16},{9,... | collective-permute-start | bytes 1544 | tf_op jit(solution)/shard_map/ppermute | solution.py:53
  113.9 4.5 %collective-permute-start.30 = (f32[1,128]{1,0:T(1,128)S(1)}, f32[1,128]{1,0:T(1,128)S(1)}, u32[]{:S(2)}, u32[]{:S(2)}) collective-permute-start(f32[1,128]{1,0:T(1,128)S(1)} %add_add_fusion.5), channel_id=1, source_target_pairs={{0,16},{1,17},{2,18},{3,19},{4,20},{5,21},{6,22},{7,23},{8,24},{9,... | collective-permute-start | bytes 1544 | tf_op jit(solution)/shard_map/ppermute | solution.py:53
  114.8 3.6 %collective-permute-start.29 = (f32[1,128]{1,0:T(1,128)S(1)}, f32[1,128]{1,0:T(1,128)S(1)}, u32[]{:S(2)}, u32[]{:S(2)}) collective-permute-start(f32[1,128]{1,0:T(1,128)S(1)} %add_add_fusion.5), channel_id=1, source_target_pairs={{0,8},{1,9},{2,10},{3,11},{4,12},{5,13},{6,14},{7,15},{8,0},{9,1},... | collective-permute-start | bytes 1544 | tf_op jit(solution)/shard_map/ppermute | solution.py:53
  126.2 4.5 %collective-permute-start.35 = (f32[1,128]{1,0:T(1,128)S(1)}, f32[1,128]{1,0:T(1,128)S(1)}, u32[]{:S(2)}, u32[]{:S(2)}) collective-permute-start(f32[1,128]{1,0:T(1,128)S(1)} %add.206), channel_id=1, source_target_pairs={{0,6},{1,7},{2,4},{3,5},{4,2},{5,3},{6,0},{7,1},{8,14},{9,15},{10,... | collective-permute-start | bytes 1544 | tf_op jit(solution)/shard_map/ppermute | solution.py:53
  126.6 4.1 %collective-permute-start.34 = (f32[1,128]{1,0:T(1,128)S(1)}, f32[1,128]{1,0:T(1,128)S(1)}, u32[]{:S(2)}, u32[]{:S(2)}) collective-permute-start(f32[1,128]{1,0:T(1,128)S(1)} %add.206), channel_id=1, source_target_pairs={{0,4},{1,5},{2,6},{3,7},{4,0},{5,1},{6,2},{7,3},{8,12},{9,13},{10,... | collective-permute-start | bytes 1544 | tf_op jit(solution)/shard_map/ppermute | solution.py:53
  131.4 7.2 %collective-permute-start.38 = (f32[1,128]{1,0:T(1,128)S(1)}, f32[1,128]{1,0:T(1,128)S(1)}, u32[]{:S(2)}, u32[]{:S(2)}) collective-permute-start(f32[1,128]{1,0:T(1,128)S(1)} %add_add_fusion.3), channel_id=1, source_target_pairs={{0,24},{1,25},{2,26},{3,27},{4,28},{5,29},{6,30},{7,31},{8,16},{9,... | collective-permute-start | bytes 1544 | tf_op jit(solution)/shard_map/ppermute | solution.py:53
  134.0 4.6 %collective-permute-start.37 = (f32[1,128]{1,0:T(1,128)S(1)}, f32[1,128]{1,0:T(1,128)S(1)}, u32[]{:S(2)}, u32[]{:S(2)}) collective-permute-start(f32[1,128]{1,0:T(1,128)S(1)} %add_add_fusion.3), channel_id=1, source_target_pairs={{0,16},{1,17},{2,18},{3,19},{4,20},{5,21},{6,22},{7,23},{8,24},{9,... | collective-permute-start | bytes 1544 | tf_op jit(solution)/shard_map/ppermute | solution.py:53
  134.9 3.7 %collective-permute-start.36 = (f32[1,128]{1,0:T(1,128)S(1)}, f32[1,128]{1,0:T(1,128)S(1)}, u32[]{:S(2)}, u32[]{:S(2)}) collective-permute-start(f32[1,128]{1,0:T(1,128)S(1)} %add_add_fusion.3), channel_id=1, source_target_pairs={{0,8},{1,9},{2,10},{3,11},{4,12},{5,13},{6,14},{7,15},{8,0},{9,1},... | collective-permute-start | bytes 1544 | tf_op jit(solution)/shard_map/ppermute | solution.py:53
  (11 other events, 57.0 us)

commit v15 on v13

--- a/solution.py
+++ b/solution.py
@@ -151,19 +151,34 @@
     lanes = z_out.shape[2]
     probes = lanes // 2
 
-    def relayout(r, carry):
+    reach = 2 * (ITERS - 1)
+
+    def halves(r):
         cells = ext_ref[r]
-        left = cells[0:sublanes]
-        right = cells[plan.half : plan.half + sublanes]
         low = lax.broadcasted_iota(jnp.int32, (sublanes, lanes), 1) < probes
+        return cells[0:sublanes], cells[plan.half : plan.half + sublanes], low
+
+    def probe_rows(r, carry):
+        left, right, low = halves(r)
         z_out[r] = jnp.where(low, left, pltpu.roll(right, probes, 1))
-        observed_scr[r] = jnp.where(low, _spread(left, probes), _spread(right, probes))
+        return carry
+
+    lax.fori_loop(0, plan.slab_rows, probe_rows, 0)
+
+    def parameter_rows(r, carry):
+        left, right, low = halves(r)
         gain_out[r] = jnp.where(low, _spread(left, probes + 1), _spread(right, probes + 1)) + 20.0 / 6.0
         weight_out[r] = jnp.where(low, _spread(left, probes + 2), _spread(right, probes + 2))
         return carry
 
-    lax.fori_loop(0, plan.slab_rows, relayout, 0)
-    reach = 2 * (ITERS - 1)
+    lax.fori_loop(*plan.span(reach + 1), parameter_rows, 0)
+
+    def observed_rows(r, carry):
+        left, right, low = halves(r)
+        observed_scr[r] = jnp.where(low, _spread(left, probes), _spread(right, probes))
+        return carry
+
+    lax.fori_loop(*plan.span(1), observed_rows, 0)
 
     def probe_pass(r, totals):
         stiffness = _stiffen_row(z_out, r, gain_out[r])

time: 146 us -> 149 us (1.021)
  Pallas kernels: 34.8 us -> 37.5 us
    pallas_call x6, Pallas kernels: 34.8 us -> 37.5 us  [_call(): pl.pallas_call(lambda *refs: kernel(plan, *refs), out_shape=out_shapes, i...]
where the time goes in v15:
time: 149 us; the launch traced here: 148 us
  starting transfers between devices  54.1 us (36%)
  Pallas kernels  37.5 us (25%)
  waiting for transfers between devices  33.9 us (23%)
  other arithmetic  13.2 us (9%)
  local copies, waits for them, and re-layouts  8.58 us (6%)
    ppermute x35, starting transfers between devices, partner(): lax.ppermute(terms, axes, [(i, i ^ mask) for i in range(count)])  43.4 us
    pallas_call x6, Pallas kernels, _call(): pl.pallas_call(lambda *refs: kernel(plan, *refs), out_shape=out_shapes, i...  37.5 us
    ppermute x35, waiting for transfers between devices, partner(): lax.ppermute(terms, axes, [(i, i ^ mask) for i in range(count)])  30.8 us
    ppermute x1, starting transfers between devices, on_device(): lax.ppermute(edge_rows(rows - sent), 'rows', [(i, i + 1) for i in range(c...  6.21 us
    add x15, other arithmetic, _span_sum(): _span_sum(terms, rest, partner)  6.15 us
    broadcast_in_dim x3, local copies, waits for them, and re-layouts, on_device(): fields = (probes, observed[None], kappa_sq[None], variance_weight[None])  3.09 us
  transfers between devices with their start and end apart: 39, of which 30 were waited for; matrix products, arithmetic and copies ran while one was open for 7% of the time, Pallas kernels for 0%

profile of v15, /device:TPU:0, one launch (start us, length us, event | category | flops | bytes accessed | tf_op | source)
XLA Modules:
  0.0 148.2 jit_solution(1857030146870390518)
XLA Ops:
  5.3 6.2 %collective-permute-start = (f32[536,128]{1,0:T(8,128)}, f32[536,128]{1,0:T(8,128)}, u32[]{:S(2)}, u32[]{:S(2)}) collective-permute-start(f32[536,128]{1,0:T(8,128)} %maximum_bitcast_fusion.1), channel_id=1, source_target_pairs={{0,4},{4,8},{8,12},{12,16},{16,20},{20,24},{24,28},{1,5},{5,9},{9,... | collective-permute-start | bytes 823304 | tf_op jit(solution)/shard_map/ppermute | solution.py:353
  15.8 2.4 %maximum_bitcast_fusion = f32[16,128,67]{2,1,0:T(8,128)S(1)} fusion(f32[1,16,128]{0,2,1:T(8,128)} %copy.17, f32[1,16,128]{0,2,1:T(8,128)S(1)} %copy.16, f32[1,16,128]{0,2,1:T(8,128)} %copy.15, f32[64,16,128]{0,2,1:T(8,128)S(1)} %copy.14), kind=kLoop, calls=%fused_computation.13 | loop fusion | flops 411648 | bytes 1097728 | tf_op jit(solution)/shard_map/transpose | solution.py:360
  22.1 1.9 %collective-permute-start.2 = (f32[28,6,67]{2,1,0:T(8,128)S(1)}, f32[28,6,67]{2,1,0:T(8,128)S(1)}, u32[]{:S(2)}, u32[]{:S(2)}) collective-permute-start(f32[28,6,67]{2,1,0:T(8,128)S(1)} %get-tuple-element.34), channel_id=1, source_target_pairs={{0,1},{1,2},{2,3},{4,5},{5,6},{6,7},{8,9},{9,10},{10,11},{12,13},{... | collective-permute-start | bytes 135080 | tf_op jit(solution)/shard_map/ppermute | solution.py:20
  25.8 2.5 %collective-permute-done.3 = f32[28,6,67]{2,1,0:T(8,128)S(1)} collective-permute-done((f32[28,6,67]{2,1,0:T(8,128)S(1)}, f32[28,6,67]{2,1,0:T(8,128)S(1)}, u32[]{:S(2)}, u32[]{:S(2)}) %collective-permute-start.3) | collective-permute-done | bytes 45056 | tf_op jit(solution)/shard_map/ppermute | solution.py:22
  28.3 1.9 %select_maximum_fusion.refs_0_ = f32[28,144,128]{2,1,0:T(8,128)} fusion(f32[28,6,67]{2,1,0:T(8,128)S(1)} %collective-permute-done.3, f32[28,6,67]{2,1,0:T(8,128)S(1)} %collective-permute-done.2, f32[6,128,67]{2,1,0:T(8,128)S(1)} %bitcast.15, f32[16,128,67]{2,1,0:T(8,128)S(1)} %maximum_bitcast_fusion, f32[6,128,67]{2,1,0:T(8,128)S(1)} %bitcast.17), kind=kLoop, calls=%fused_computation | loop fusion | flops 8773632 | bytes 3114944 | tf_op jit(solution)/shard_map/concatenate | solution.py:18
  30.3 13.6 %shard_map.59 = (f32[28,80,128]{2,1,0:T(8,128)}, f32[28,80,128]{2,1,0:T(8,128)}, f32[28,80,128]{2,1,0:T(8,128)}, f32[28,80,128]{2,1,0:T(8,128)}, f32[28,80,128]{...) custom-call(f32[28,144,128]{2,1,0:T(8,128)} %select_maximum_fusion.refs_0_, ...), custom_call_target="tpu_custom_call" | custom-call | flops 11468800 | bytes 13762560 | tf_op jit(solution)/shard_map/pallas_call | solution.py:318
  43.9 3.4 %collective-permute-start.4 = (f32[2,128]{1,0:T(2,128)}, f32[2,128]{1,0:T(2,128)S(1)}, u32[]{:S(2)}, u32[]{:S(2)}) collective-permute-start(f32[2,128]{1,0:T(2,128)} %get-tuple-element.18), channel_id=1, source_target_pairs={{0,1},{1,0},{2,3},{3,2},{4,5},{5,4},{6,7},{7,6},{8,9},{9,8},{10,11... | collective-permute-start | bytes 3080 | tf_op jit(solution)/shard_map/ppermute | solution.py:71
  49.0 2.0 %collective-permute-start.7 = (f32[2,128]{1,0:T(2,128)S(1)}, f32[2,128]{1,0:T(2,128)S(1)}, u32[]{:S(2)}, u32[]{:S(2)}) collective-permute-start(f32[2,128]{1,0:T(2,128)S(1)} %add.174), channel_id=1, source_target_pairs={{0,6},{1,7},{2,4},{3,5},{4,2},{5,3},{6,0},{7,1},{8,14},{9,15},{10,... | collective-permute-start | bytes 3080 | tf_op jit(solution)/shard_map/ppermute | solution.py:71
  51.5 1.5 collective-permute-start.5
  55.1 3.9 %collective-permute-start.10 = (f32[2,128]{1,0:T(2,128)S(1)}, f32[2,128]{1,0:T(2,128)S(1)}, u32[]{:S(2)}, u32[]{:S(2)}) collective-permute-start(f32[2,128]{1,0:T(2,128)S(1)} %add_add_fusion.1), channel_id=1, source_target_pairs={{0,24},{1,25},{2,26},{3,27},{4,28},{5,29},{6,30},{7,31},{8,16},{9,... | collective-permute-start | bytes 3080 | tf_op jit(solution)/shard_map/ppermute | solution.py:71
  60.6 2.9 %collective-permute-done.9 = f32[2,128]{1,0:T(2,128)S(1)} collective-permute-done((f32[2,128]{1,0:T(2,128)S(1)}, f32[2,128]{1,0:T(2,128)S(1)}, u32[]{:S(2)}, u32[]{:S(2)}) %collective-permute-start.9) | collective-permute-done | bytes 1056 | tf_op jit(solution)/shard_map/ppermute | solution.py:71
  64.1 3.3 %shard_map.60 = (f32[28,80,128]{2,1,0:T(8,128)}, f32[1,128]{1,0:T(1,128)}) custom-call(f32[2,128]{1,0:T(2,128)} %add_add_fusion.refs_0_.refs_1_, f32[28,80,128]{2,1,0:T(8,128)} %get-tuple-element.19.refs_1_.refs_3_.refs_6_.refs_9_, f32[28,80,128]{2,1,0:T(8,128)} %get-tuple-element.20.refs_2_, f32[80,128]{1,0:T(8,128)} %add_convert_fusion.1.refs_3_.refs_8_.refs_4_), custom_call_target="tpu_custom_call" | custom-call | flops 11468800 | bytes 6881280 | tf_op jit(solution)/shard_map/pallas_call | solution.py:318
  69.3 1.4 collective-permute-start.14
  70.7 2.0 %collective-permute-start.13 = (f32[1,128]{1,0:T(1,128)S(1)}, f32[1,128]{1,0:T(1,128)S(1)}, u32[]{:S(2)}, u32[]{:S(2)}) collective-permute-start(f32[1,128]{1,0:T(1,128)S(1)} %add.181), channel_id=1, source_target_pairs={{0,4},{1,5},{2,6},{3,7},{4,0},{5,1},{6,2},{7,3},{8,12},{9,13},{10,... | collective-permute-start | bytes 1544 | tf_op jit(solution)/shard_map/ppermute | solution.py:71
  74.3 2.0 %collective-permute-done.12 = f32[1,128]{1,0:T(1,128)S(1)} collective-permute-done((f32[1,128]{1,0:T(1,128)S(1)}, f32[1,128]{1,0:T(1,128)S(1)}, u32[]{:S(2)}, u32[]{:S(2)}) %collective-permute-start.12) | collective-permute-done | bytes 544 | tf_op jit(solution)/shard_map/ppermute | solution.py:71
  76.3 1.5 collective-permute-start.17
  78.4 2.3 %collective-permute-start.15 = (f32[1,128]{1,0:T(1,128)S(1)}, f32[1,128]{1,0:T(1,128)S(1)}, u32[]{:S(2)}, u32[]{:S(2)}) collective-permute-start(f32[1,128]{1,0:T(1,128)S(1)} %add_add_fusion.9), channel_id=1, source_target_pairs={{0,8},{1,9},{2,10},{3,11},{4,12},{5,13},{6,14},{7,15},{8,0},{9,1},... | collective-permute-start | bytes 1544 | tf_op jit(solution)/shard_map/ppermute | solution.py:71
  82.7 5.8 %shard_map.61 = (f32[28,80,128]{2,1,0:T(8,128)}, f32[28,80,128]{2,1,0:T(8,128)}, f32[1,128]{1,0:T(1,128)}) custom-call(f32[1,128]{1,0:T(1,128)} %add_add_fusion.8.refs_0_.refs_1_.refs_2_, f32[2,128]{1,0:T(2,128)} %add_add_fusion.refs_0_.refs_1_, f32[28,80,128]{2,1,0:T(8,128)} %get-tuple-element.22.refs_2_, ...), custom_call_target="tpu_custom_call" | custom-call | flops 11468800 | bytes 13762560 | tf_op jit(solution)/shard_map/pallas_call | solution.py:318
  92.0 1.9 %collective-permute-start.19 = (f32[1,128]{1,0:T(1,128)S(1)}, f32[1,128]{1,0:T(1,128)S(1)}, u32[]{:S(2)}, u32[]{:S(2)}) collective-permute-start(f32[1,128]{1,0:T(1,128)S(1)} %add.188), channel_id=1, source_target_pairs={{0,2},{1,3},{2,0},{3,1},{4,6},{5,7},{6,4},{7,5},{8,10},{9,11},{10,... | collective-permute-start | bytes 1544 | tf_op jit(solution)/shard_map/ppermute | solution.py:71
  95.6 2.6 %collective-permute-start.24 = (f32[1,128]{1,0:T(1,128)S(1)}, f32[1,128]{1,0:T(1,128)S(1)}, u32[]{:S(2)}, u32[]{:S(2)}) collective-permute-start(f32[1,128]{1,0:T(1,128)S(1)} %add_add_fusion.7), channel_id=1, source_target_pairs={{0,24},{1,25},{2,26},{3,27},{4,28},{5,29},{6,30},{7,31},{8,16},{9,... | collective-permute-start | bytes 1544 | tf_op jit(solution)/shard_map/ppermute | solution.py:71
  101.0 1.7 %collective-permute-done.23 = f32[1,128]{1,0:T(1,128)S(1)} collective-permute-done((f32[1,128]{1,0:T(1,128)S(1)}, f32[1,128]{1,0:T(1,128)S(1)}, u32[]{:S(2)}, u32[]{:S(2)}) %collective-permute-start.23) | collective-permute-done | bytes 544 | tf_op jit(solution)/shard_map/ppermute | solution.py:71
  103.2 3.3 %shard_map.62 = (f32[28,80,128]{2,1,0:T(8,128)}, f32[1,128]{1,0:T(1,128)}) custom-call(f32[1,128]{1,0:T(1,128)} %add_add_fusion.8.refs_0_.refs_1_.refs_2_, f32[1,128]{1,0:T(1,128)} %add_add_fusion.6.refs_1_.refs_3_, f32[28,80,128]{2,1,0:T(8,128)} %get-tuple-element.22.refs_2_, f32[28,80,128]{2,1,0:T(8,128)} %get-tuple-element.26.refs_3_, ...), custom_call_target="tpu_custom_call" | custom-call | flops 11468800 | bytes 8028160 | tf_op jit(solution)/shard_map/pallas_call | solution.py:318
  108.4 1.4 collective-permute-start.28
  109.8 2.0 %collective-permute-start.27 = (f32[1,128]{1,0:T(1,128)S(1)}, f32[1,128]{1,0:T(1,128)S(1)}, u32[]{:S(2)}, u32[]{:S(2)}) collective-permute-start(f32[1,128]{1,0:T(1,128)S(1)} %add.195), channel_id=1, source_target_pairs={{0,4},{1,5},{2,6},{3,7},{4,0},{5,1},{6,2},{7,3},{8,12},{9,13},{10,... | collective-permute-start | bytes 1544 | tf_op jit(solution)/shard_map/ppermute | solution.py:71
  113.4 2.0 %collective-permute-done.26 = f32[1,128]{1,0:T(1,128)S(1)} collective-permute-done((f32[1,128]{1,0:T(1,128)S(1)}, f32[1,128]{1,0:T(1,128)S(1)}, u32[]{:S(2)}, u32[]{:S(2)}) %collective-permute-start.26) | collective-permute-done | bytes 544 | tf_op jit(solution)/shard_map/ppermute | solution.py:71
  115.4 1.5 collective-permute-start.31
  117.7 2.0 %collective-permute-start.29 = (f32[1,128]{1,0:T(1,128)S(1)}, f32[1,128]{1,0:T(1,128)S(1)}, u32[]{:S(2)}, u32[]{:S(2)}) collective-permute-start(f32[1,128]{1,0:T(1,128)S(1)} %add_add_fusion.5), channel_id=1, source_target_pairs={{0,8},{1,9},{2,10},{3,11},{4,12},{5,13},{6,14},{7,15},{8,0},{9,1},... | collective-permute-start | bytes 1544 | tf_op jit(solution)/shard_map/ppermute | solution.py:71
  121.9 5.3 %shard_map.63 = (f32[28,80,128]{2,1,0:T(8,128)}, f32[28,80,128]{2,1,0:T(8,128)}, f32[1,128]{1,0:T(1,128)}) custom-call(f32[1,128]{1,0:T(1,128)} %add_add_fusion.4.refs_0_.refs_4_, f32[1,128]{1,0:T(1,128)} %add_add_fusion.8.refs_0_.refs_1_.refs_2_, f32[28,80,128]{2,1,0:T(8,128)} %get-tuple-element.28.refs_2_, ...), custom_call_target="tpu_custom_call" | custom-call | flops 11468800 | bytes 13762560 | tf_op jit(solution)/shard_map/pallas_call | solution.py:318
  130.8 1.9 %collective-permute-start.33 = (f32[1,128]{1,0:T(1,128)S(1)}, f32[1,128]{1,0:T(1,128)S(1)}, u32[]{:S(2)}, u32[]{:S(2)}) collective-permute-start(f32[1,128]{1,0:T(1,128)S(1)} %add.202), channel_id=1, source_target_pairs={{0,2},{1,3},{2,0},{3,1},{4,6},{5,7},{6,4},{7,5},{8,10},{9,11},{10,... | collective-permute-start | bytes 1544 | tf_op jit(solution)/shard_map/ppermute | solution.py:71
  134.3 2.6 %collective-permute-start.38 = (f32[1,128]{1,0:T(1,128)S(1)}, f32[1,128]{1,0:T(1,128)S(1)}, u32[]{:S(2)}, u32[]{:S(2)}) collective-permute-start(f32[1,128]{1,0:T(1,128)S(1)} %add_add_fusion.3), channel_id=1, source_target_pairs={{0,24},{1,25},{2,26},{3,27},{4,28},{5,29},{6,30},{7,31},{8,16},{9,... | collective-permute-start | bytes 1544 | tf_op jit(solution)/shard_map/ppermute | solution.py:71
  139.7 1.7 %collective-permute-done.37 = f32[1,128]{1,0:T(1,128)S(1)} collective-permute-done((f32[1,128]{1,0:T(1,128)S(1)}, f32[1,128]{1,0:T(1,128)S(1)}, u32[]{:S(2)}, u32[]{:S(2)}) %collective-permute-start.37) | collective-permute-done | bytes 544 | tf_op jit(solution)/shard_map/ppermute | solution.py:71
  141.9 6.2 %shard_map.64 = (f32[16,128]{1,0:T(8,128)}, f32[16,128]{1,0:T(8,128)}) custom-call(f32[2,128]{1,0:T(2,128)} %add_add_fusion.refs_0_.refs_1_, f32[2,128]{1,0:T(2,128)} %add_add_fusion.refs_0_.refs_1_, f32[1,128]{1,0:T(1,128)} %add_add_fusion.8.refs_0_.refs_1_.refs_2_, f32[1,128]{1,0:T(1,128)} %add_add_fusion.6.refs_1_.refs_3_, ...), custom_call_target="tpu_custom_call" | custom-call | flops 11468800 | bytes 20643840 | tf_op jit(solution)/shard_map/pallas_call | solution.py:318
  (100 shorter events, 50.9 us)
Async XLA Ops:
  3.3 15.8 %collective-permute-start.1 = (f32[536,128]{1,0:T(8,128)S(1)}, f32[536,128]{1,0:T(8,128)}, u32[]{:S(2)}, u32[]{:S(2)}) collective-permute-start(f32[536,128]{1,0:T(8,128)S(1)} %maximum_bitcast_fusion.2), channel_id=1, source_target_pairs={{4,0},{8,4},{12,8},{16,12},{20,16},{24,20},{28,24},{5,1},{9,5},{13... | collective-permute-start | bytes 823304 | tf_op jit(solution)/shard_map/ppermute | solution.py:356
  5.3 15.5 %collective-permute-start = (f32[536,128]{1,0:T(8,128)}, f32[536,128]{1,0:T(8,128)}, u32[]{:S(2)}, u32[]{:S(2)}) collective-permute-start(f32[536,128]{1,0:T(8,128)} %maximum_bitcast_fusion.1), channel_id=1, source_target_pairs={{0,4},{4,8},{8,12},{12,16},{16,20},{20,24},{24,28},{1,5},{5,9},{9,... | collective-permute-start | bytes 823304 | tf_op jit(solution)/shard_map/ppermute | solution.py:353
  22.1 3.8 %collective-permute-start.2 = (f32[28,6,67]{2,1,0:T(8,128)S(1)}, f32[28,6,67]{2,1,0:T(8,128)S(1)}, u32[]{:S(2)}, u32[]{:S(2)}) collective-permute-start(f32[28,6,67]{2,1,0:T(8,128)S(1)} %get-tuple-element.34), channel_id=1, source_target_pairs={{0,1},{1,2},{2,3},{4,5},{5,6},{6,7},{8,9},{9,10},{10,11},{12,13},{... | collective-permute-start | bytes 135080 | tf_op jit(solution)/shard_map/ppermute | solution.py:20
  24.0 4.3 %collective-permute-start.3 = (f32[28,6,67]{2,1,0:T(8,128)S(1)}, f32[28,6,67]{2,1,0:T(8,128)S(1)}, u32[]{:S(2)}, u32[]{:S(2)}) collective-permute-start(f32[28,6,67]{2,1,0:T(8,128)S(1)} %get-tuple-element.35), channel_id=1, source_target_pairs={{1,0},{2,1},{3,2},{5,4},{6,5},{7,6},{9,8},{10,9},{11,10},{13,12},{... | collective-permute-start | bytes 135080 | tf_op jit(solution)/shard_map/ppermute | solution.py:22
  43.9 4.4 %collective-permute-start.4 = (f32[2,128]{1,0:T(2,128)}, f32[2,128]{1,0:T(2,128)S(1)}, u32[]{:S(2)}, u32[]{:S(2)}) collective-permute-start(f32[2,128]{1,0:T(2,128)} %get-tuple-element.18), channel_id=1, source_target_pairs={{0,1},{1,0},{2,3},{3,2},{4,5},{5,4},{6,7},{7,6},{8,9},{9,8},{10,11... | collective-permute-start | bytes 3080 | tf_op jit(solution)/shard_map/ppermute | solution.py:71
  49.0 4.5 %collective-permute-start.7 = (f32[2,128]{1,0:T(2,128)S(1)}, f32[2,128]{1,0:T(2,128)S(1)}, u32[]{:S(2)}, u32[]{:S(2)}) collective-permute-start(f32[2,128]{1,0:T(2,128)S(1)} %add.174), channel_id=1, source_target_pairs={{0,6},{1,7},{2,4},{3,5},{4,2},{5,3},{6,0},{7,1},{8,14},{9,15},{10,... | collective-permute-start | bytes 3080 | tf_op jit(solution)/shard_map/ppermute | solution.py:71
  51.1 3.6 %collective-permute-start.6 = (f32[2,128]{1,0:T(2,128)S(1)}, f32[2,128]{1,0:T(2,128)S(1)}, u32[]{:S(2)}, u32[]{:S(2)}) collective-permute-start(f32[2,128]{1,0:T(2,128)S(1)} %add.174), channel_id=1, source_target_pairs={{0,4},{1,5},{2,6},{3,7},{4,0},{5,1},{6,2},{7,3},{8,12},{9,13},{10,... | collective-permute-start | bytes 3080 | tf_op jit(solution)/shard_map/ppermute | solution.py:71
  51.5 3.6 %collective-permute-start.5 = (f32[2,128]{1,0:T(2,128)S(1)}, f32[2,128]{1,0:T(2,128)S(1)}, u32[]{:S(2)}, u32[]{:S(2)}) collective-permute-start(f32[2,128]{1,0:T(2,128)S(1)} %add.174), channel_id=1, source_target_pairs={{0,2},{1,3},{2,0},{3,1},{4,6},{5,7},{6,4},{7,5},{8,10},{9,11},{10,... | collective-permute-start | bytes 3080 | tf_op jit(solution)/shard_map/ppermute | solution.py:71
  55.1 5.5 %collective-permute-start.10 = (f32[2,128]{1,0:T(2,128)S(1)}, f32[2,128]{1,0:T(2,128)S(1)}, u32[]{:S(2)}, u32[]{:S(2)}) collective-permute-start(f32[2,128]{1,0:T(2,128)S(1)} %add_add_fusion.1), channel_id=1, source_target_pairs={{0,24},{1,25},{2,26},{3,27},{4,28},{5,29},{6,30},{7,31},{8,16},{9,... | collective-permute-start | bytes 3080 | tf_op jit(solution)/shard_map/ppermute | solution.py:71
  59.0 4.5 %collective-permute-start.9 = (f32[2,128]{1,0:T(2,128)S(1)}, f32[2,128]{1,0:T(2,128)S(1)}, u32[]{:S(2)}, u32[]{:S(2)}) collective-permute-start(f32[2,128]{1,0:T(2,128)S(1)} %add_add_fusion.1), channel_id=1, source_target_pairs={{0,16},{1,17},{2,18},{3,19},{4,20},{5,21},{6,22},{7,23},{8,24},{9,... | collective-permute-start | bytes 3080 | tf_op jit(solution)/shard_map/ppermute | solution.py:71
  59.0 4.5 %collective-permute-start.8 = (f32[2,128]{1,0:T(2,128)S(1)}, f32[2,128]{1,0:T(2,128)S(1)}, u32[]{:S(2)}, u32[]{:S(2)}) collective-permute-start(f32[2,128]{1,0:T(2,128)S(1)} %add_add_fusion.1), channel_id=1, source_target_pairs={{0,8},{1,9},{2,10},{3,11},{4,12},{5,13},{6,14},{7,15},{8,0},{9,1},... | collective-permute-start | bytes 3080 | tf_op jit(solution)/shard_map/ppermute | solution.py:71
  69.3 4.5 %collective-permute-start.14 = (f32[1,128]{1,0:T(1,128)S(1)}, f32[1,128]{1,0:T(1,128)S(1)}, u32[]{:S(2)}, u32[]{:S(2)}) collective-permute-start(f32[1,128]{1,0:T(1,128)S(1)} %add.181), channel_id=1, source_target_pairs={{0,6},{1,7},{2,4},{3,5},{4,2},{5,3},{6,0},{7,1},{8,14},{9,15},{10,... | collective-permute-start | bytes 1544 | tf_op jit(solution)/shard_map/ppermute | solution.py:71
  70.7 3.6 %collective-permute-start.13 = (f32[1,128]{1,0:T(1,128)S(1)}, f32[1,128]{1,0:T(1,128)S(1)}, u32[]{:S(2)}, u32[]{:S(2)}) collective-permute-start(f32[1,128]{1,0:T(1,128)S(1)} %add.181), channel_id=1, source_target_pairs={{0,4},{1,5},{2,6},{3,7},{4,0},{5,1},{6,2},{7,3},{8,12},{9,13},{10,... | collective-permute-start | bytes 1544 | tf_op jit(solution)/shard_map/ppermute | solution.py:71
  72.7 3.6 %collective-permute-start.12 = (f32[1,128]{1,0:T(1,128)S(1)}, f32[1,128]{1,0:T(1,128)S(1)}, u32[]{:S(2)}, u32[]{:S(2)}) collective-permute-start(f32[1,128]{1,0:T(1,128)S(1)} %add.181), channel_id=1, source_target_pairs={{0,2},{1,3},{2,0},{3,1},{4,6},{5,7},{6,4},{7,5},{8,10},{9,11},{10,... | collective-permute-start | bytes 1544 | tf_op jit(solution)/shard_map/ppermute | solution.py:71
  76.3 5.4 %collective-permute-start.17 = (f32[1,128]{1,0:T(1,128)S(1)}, f32[1,128]{1,0:T(1,128)S(1)}, u32[]{:S(2)}, u32[]{:S(2)}) collective-permute-start(f32[1,128]{1,0:T(1,128)S(1)} %add_add_fusion.9), channel_id=1, source_target_pairs={{0,24},{1,25},{2,26},{3,27},{4,28},{5,29},{6,30},{7,31},{8,16},{9,... | collective-permute-start | bytes 1544 | tf_op jit(solution)/shard_map/ppermute | solution.py:71
  77.7 4.5 %collective-permute-start.16 = (f32[1,128]{1,0:T(1,128)S(1)}, f32[1,128]{1,0:T(1,128)S(1)}, u32[]{:S(2)}, u32[]{:S(2)}) collective-permute-start(f32[1,128]{1,0:T(1,128)S(1)} %add_add_fusion.9), channel_id=1, source_target_pairs={{0,16},{1,17},{2,18},{3,19},{4,20},{5,21},{6,22},{7,23},{8,24},{9,... | collective-permute-start | bytes 1544 | tf_op jit(solution)/shard_map/ppermute | solution.py:71
  78.4 3.8 %collective-permute-start.15 = (f32[1,128]{1,0:T(1,128)S(1)}, f32[1,128]{1,0:T(1,128)S(1)}, u32[]{:S(2)}, u32[]{:S(2)}) collective-permute-start(f32[1,128]{1,0:T(1,128)S(1)} %add_add_fusion.9), channel_id=1, source_target_pairs={{0,8},{1,9},{2,10},{3,11},{4,12},{5,13},{6,14},{7,15},{8,0},{9,1},... | collective-permute-start | bytes 1544 | tf_op jit(solution)/shard_map/ppermute | solution.py:71
  90.5 4.5 %collective-permute-start.21 = (f32[1,128]{1,0:T(1,128)S(1)}, f32[1,128]{1,0:T(1,128)S(1)}, u32[]{:S(2)}, u32[]{:S(2)}) collective-permute-start(f32[1,128]{1,0:T(1,128)S(1)} %add.188), channel_id=1, source_target_pairs={{0,6},{1,7},{2,4},{3,5},{4,2},{5,3},{6,0},{7,1},{8,14},{9,15},{10,... | collective-permute-start | bytes 1544 | tf_op jit(solution)/shard_map/ppermute | solution.py:71
  90.8 4.1 %collective-permute-start.20 = (f32[1,128]{1,0:T(1,128)S(1)}, f32[1,128]{1,0:T(1,128)S(1)}, u32[]{:S(2)}, u32[]{:S(2)}) collective-permute-start(f32[1,128]{1,0:T(1,128)S(1)} %add.188), channel_id=1, source_target_pairs={{0,4},{1,5},{2,6},{3,7},{4,0},{5,1},{6,2},{7,3},{8,12},{9,13},{10,... | collective-permute-start | bytes 1544 | tf_op jit(solution)/shard_map/ppermute | solution.py:71
  95.6 5.4 %collective-permute-start.24 = (f32[1,128]{1,0:T(1,128)S(1)}, f32[1,128]{1,0:T(1,128)S(1)}, u32[]{:S(2)}, u32[]{:S(2)}) collective-permute-start(f32[1,128]{1,0:T(1,128)S(1)} %add_add_fusion.7), channel_id=1, source_target_pairs={{0,24},{1,25},{2,26},{3,27},{4,28},{5,29},{6,30},{7,31},{8,16},{9,... | collective-permute-start | bytes 1544 | tf_op jit(solution)/shard_map/ppermute | solution.py:71
  98.2 4.5 %collective-permute-start.23 = (f32[1,128]{1,0:T(1,128)S(1)}, f32[1,128]{1,0:T(1,128)S(1)}, u32[]{:S(2)}, u32[]{:S(2)}) collective-permute-start(f32[1,128]{1,0:T(1,128)S(1)} %add_add_fusion.7), channel_id=1, source_target_pairs={{0,16},{1,17},{2,18},{3,19},{4,20},{5,21},{6,22},{7,23},{8,24},{9,... | collective-permute-start | bytes 1544 | tf_op jit(solution)/shard_map/ppermute | solution.py:71
  99.1 3.6 %collective-permute-start.22 = (f32[1,128]{1,0:T(1,128)S(1)}, f32[1,128]{1,0:T(1,128)S(1)}, u32[]{:S(2)}, u32[]{:S(2)}) collective-permute-start(f32[1,128]{1,0:T(1,128)S(1)} %add_add_fusion.7), channel_id=1, source_target_pairs={{0,8},{1,9},{2,10},{3,11},{4,12},{5,13},{6,14},{7,15},{8,0},{9,1},... | collective-permute-start | bytes 1544 | tf_op jit(solution)/shard_map/ppermute | solution.py:71
  108.4 4.5 %collective-permute-start.28 = (f32[1,128]{1,0:T(1,128)S(1)}, f32[1,128]{1,0:T(1,128)S(1)}, u32[]{:S(2)}, u32[]{:S(2)}) collective-permute-start(f32[1,128]{1,0:T(1,128)S(1)} %add.195), channel_id=1, source_target_pairs={{0,6},{1,7},{2,4},{3,5},{4,2},{5,3},{6,0},{7,1},{8,14},{9,15},{10,... | collective-permute-start | bytes 1544 | tf_op jit(solution)/shard_map/ppermute | solution.py:71
  115.4 5.4 %collective-permute-start.31 = (f32[1,128]{1,0:T(1,128)S(1)}, f32[1,128]{1,0:T(1,128)S(1)}, u32[]{:S(2)}, u32[]{:S(2)}) collective-permute-start(f32[1,128]{1,0:T(1,128)S(1)} %add_add_fusion.5), channel_id=1, source_target_pairs={{0,24},{1,25},{2,26},{3,27},{4,28},{5,29},{6,30},{7,31},{8,16},{9,... | collective-permute-start | bytes 1544 | tf_op jit(solution)/shard_map/ppermute | solution.py:71
  116.8 4.5 %collective-permute-start.30 = (f32[1,128]{1,0:T(1,128)S(1)}, f32[1,128]{1,0:T(1,128)S(1)}, u32[]{:S(2)}, u32[]{:S(2)}) collective-permute-start(f32[1,128]{1,0:T(1,128)S(1)} %add_add_fusion.5), channel_id=1, source_target_pairs={{0,16},{1,17},{2,18},{3,19},{4,20},{5,21},{6,22},{7,23},{8,24},{9,... | collective-permute-start | bytes 1544 | tf_op jit(solution)/shard_map/ppermute | solution.py:71
  117.7 3.6 %collective-permute-start.29 = (f32[1,128]{1,0:T(1,128)S(1)}, f32[1,128]{1,0:T(1,128)S(1)}, u32[]{:S(2)}, u32[]{:S(2)}) collective-permute-start(f32[1,128]{1,0:T(1,128)S(1)} %add_add_fusion.5), channel_id=1, source_target_pairs={{0,8},{1,9},{2,10},{3,11},{4,12},{5,13},{6,14},{7,15},{8,0},{9,1},... | collective-permute-start | bytes 1544 | tf_op jit(solution)/shard_map/ppermute | solution.py:71
  129.2 4.5 %collective-permute-start.35 = (f32[1,128]{1,0:T(1,128)S(1)}, f32[1,128]{1,0:T(1,128)S(1)}, u32[]{:S(2)}, u32[]{:S(2)}) collective-permute-start(f32[1,128]{1,0:T(1,128)S(1)} %add.202), channel_id=1, source_target_pairs={{0,6},{1,7},{2,4},{3,5},{4,2},{5,3},{6,0},{7,1},{8,14},{9,15},{10,... | collective-permute-start | bytes 1544 | tf_op jit(solution)/shard_map/ppermute | solution.py:71
  129.5 4.1 %collective-permute-start.34 = (f32[1,128]{1,0:T(1,128)S(1)}, f32[1,128]{1,0:T(1,128)S(1)}, u32[]{:S(2)}, u32[]{:S(2)}) collective-permute-start(f32[1,128]{1,0:T(1,128)S(1)} %add.202), channel_id=1, source_target_pairs={{0,4},{1,5},{2,6},{3,7},{4,0},{5,1},{6,2},{7,3},{8,12},{9,13},{10,... | collective-permute-start | bytes 1544 | tf_op jit(solution)/shard_map/ppermute | solution.py:71
  130.8 3.6 %collective-permute-start.33 = (f32[1,128]{1,0:T(1,128)S(1)}, f32[1,128]{1,0:T(1,128)S(1)}, u32[]{:S(2)}, u32[]{:S(2)}) collective-permute-start(f32[1,128]{1,0:T(1,128)S(1)} %add.202), channel_id=1, source_target_pairs={{0,2},{1,3},{2,0},{3,1},{4,6},{5,7},{6,4},{7,5},{8,10},{9,11},{10,... | collective-permute-start | bytes 1544 | tf_op jit(solution)/shard_map/ppermute | solution.py:71
  134.3 5.4 %collective-permute-start.38 = (f32[1,128]{1,0:T(1,128)S(1)}, f32[1,128]{1,0:T(1,128)S(1)}, u32[]{:S(2)}, u32[]{:S(2)}) collective-permute-start(f32[1,128]{1,0:T(1,128)S(1)} %add_add_fusion.3), channel_id=1, source_target_pairs={{0,24},{1,25},{2,26},{3,27},{4,28},{5,29},{6,30},{7,31},{8,16},{9,... | collective-permute-start | bytes 1544 | tf_op jit(solution)/shard_map/ppermute | solution.py:71
  136.9 4.5 %collective-permute-start.37 = (f32[1,128]{1,0:T(1,128)S(1)}, f32[1,128]{1,0:T(1,128)S(1)}, u32[]{:S(2)}, u32[]{:S(2)}) collective-permute-start(f32[1,128]{1,0:T(1,128)S(1)} %add_add_fusion.3), channel_id=1, source_target_pairs={{0,16},{1,17},{2,18},{3,19},{4,20},{5,21},{6,22},{7,23},{8,24},{9,... | collective-permute-start | bytes 1544 | tf_op jit(solution)/shard_map/ppermute | solution.py:71
  137.8 3.6 %collective-permute-start.36 = (f32[1,128]{1,0:T(1,128)S(1)}, f32[1,128]{1,0:T(1,128)S(1)}, u32[]{:S(2)}, u32[]{:S(2)}) collective-permute-start(f32[1,128]{1,0:T(1,128)S(1)} %add_add_fusion.3), channel_id=1, source_target_pairs={{0,8},{1,9},{2,10},{3,11},{4,12},{5,13},{6,14},{7,15},{8,0},{9,1},... | collective-permute-start | bytes 1544 | tf_op jit(solution)/shard_map/ppermute | solution.py:71
  (11 other events, 57.0 us)

commit v16 on v13

--- a/solution.py
+++ b/solution.py
@@ -162,10 +162,13 @@
         weight_out[r] = jnp.where(low, _spread(left, probes + 2), _spread(right, probes + 2))
         return carry
 
-    lax.fori_loop(0, plan.slab_rows, relayout, 0)
     reach = 2 * (ITERS - 1)
+    start, stop = plan.span(reach + 1)
+    assert start >= 1 and stop == plan.slab_rows - 1
+    lax.fori_loop(0, start + 1, relayout, 0)
 
     def probe_pass(r, totals):
+        relayout(r + 1, 0)
         stiffness = _stiffen_row(z_out, r, gain_out[r])
         stiff_out[r] = stiffness
         scratch[r] = weight_out[r] * stiffness

time: 146 us -> 145 us (level)
  no operation moved by 1% of the time
where the time goes in v16:
time: 145 us; the launch traced here: 144 us
  starting transfers between devices  54.1 us (37%)
  waiting for transfers between devices  33.9 us (23%)
  Pallas kernels  33.8 us (23%)
  other arithmetic  13.2 us (9%)
  local copies, waits for them, and re-layouts  8.58 us (6%)
    ppermute x35, starting transfers between devices, partner(): lax.ppermute(terms, axes, [(i, i ^ mask) for i in range(count)])  43.4 us
    pallas_call x6, Pallas kernels, _call(): pl.pallas_call(lambda *refs: kernel(plan, *refs), out_shape=out_shapes, i...  33.8 us
    ppermute x35, waiting for transfers between devices, partner(): lax.ppermute(terms, axes, [(i, i ^ mask) for i in range(count)])  30.8 us
    ppermute x1, starting transfers between devices, on_device(): lax.ppermute(edge_rows(rows - sent), 'rows', [(i, i + 1) for i in range(c...  6.21 us
    add x15, other arithmetic, _span_sum(): _span_sum(terms, rest, partner)  6.15 us
    broadcast_in_dim x3, local copies, waits for them, and re-layouts, on_device(): fields = (probes, observed[None], kappa_sq[None], variance_weight[None])  3.09 us
  transfers between devices with their start and end apart: 39, of which 30 were waited for; matrix products, arithmetic and copies ran while one was open for 7% of the time, Pallas kernels for 0%

profile of v16, /device:TPU:0, one launch (start us, length us, event | category | flops | bytes accessed | tf_op | source)
XLA Modules:
  0.0 144.5 jit_solution(3631575755105316810)
XLA Ops:
  5.3 6.2 %collective-permute-start = (f32[536,128]{1,0:T(8,128)}, f32[536,128]{1,0:T(8,128)}, u32[]{:S(2)}, u32[]{:S(2)}) collective-permute-start(f32[536,128]{1,0:T(8,128)} %maximum_bitcast_fusion.1), channel_id=1, source_target_pairs={{0,4},{4,8},{8,12},{12,16},{16,20},{20,24},{24,28},{1,5},{5,9},{9,... | collective-permute-start | bytes 823304 | tf_op jit(solution)/shard_map/ppermute | solution.py:341
  15.8 2.4 %maximum_bitcast_fusion = f32[16,128,67]{2,1,0:T(8,128)S(1)} fusion(f32[1,16,128]{0,2,1:T(8,128)} %copy.17, f32[1,16,128]{0,2,1:T(8,128)S(1)} %copy.16, f32[1,16,128]{0,2,1:T(8,128)} %copy.15, f32[64,16,128]{0,2,1:T(8,128)S(1)} %copy.14), kind=kLoop, calls=%fused_computation.13 | loop fusion | flops 411648 | bytes 1097728 | tf_op jit(solution)/shard_map/transpose | solution.py:348
  22.1 1.9 %collective-permute-start.2 = (f32[28,6,67]{2,1,0:T(8,128)S(1)}, f32[28,6,67]{2,1,0:T(8,128)S(1)}, u32[]{:S(2)}, u32[]{:S(2)}) collective-permute-start(f32[28,6,67]{2,1,0:T(8,128)S(1)} %get-tuple-element.34), channel_id=1, source_target_pairs={{0,1},{1,2},{2,3},{4,5},{5,6},{6,7},{8,9},{9,10},{10,11},{12,13},{... | collective-permute-start | bytes 135080 | tf_op jit(solution)/shard_map/ppermute | solution.py:20
  25.8 2.5 %collective-permute-done.3 = f32[28,6,67]{2,1,0:T(8,128)S(1)} collective-permute-done((f32[28,6,67]{2,1,0:T(8,128)S(1)}, f32[28,6,67]{2,1,0:T(8,128)S(1)}, u32[]{:S(2)}, u32[]{:S(2)}) %collective-permute-start.3) | collective-permute-done | bytes 45056 | tf_op jit(solution)/shard_map/ppermute | solution.py:22
  28.3 1.9 %select_maximum_fusion.refs_0_ = f32[28,144,128]{2,1,0:T(8,128)} fusion(f32[28,6,67]{2,1,0:T(8,128)S(1)} %collective-permute-done.3, f32[28,6,67]{2,1,0:T(8,128)S(1)} %collective-permute-done.2, f32[6,128,67]{2,1,0:T(8,128)S(1)} %bitcast.15, f32[16,128,67]{2,1,0:T(8,128)S(1)} %maximum_bitcast_fusion, f32[6,128,67]{2,1,0:T(8,128)S(1)} %bitcast.17), kind=kLoop, calls=%fused_computation | loop fusion | flops 8773632 | bytes 3114944 | tf_op jit(solution)/shard_map/concatenate | solution.py:18
  30.3 10.0 %shard_map.59 = (f32[28,80,128]{2,1,0:T(8,128)}, f32[28,80,128]{2,1,0:T(8,128)}, f32[28,80,128]{2,1,0:T(8,128)}, f32[28,80,128]{2,1,0:T(8,128)}, f32[28,80,128]{...) custom-call(f32[28,144,128]{2,1,0:T(8,128)} %select_maximum_fusion.refs_0_, ...), custom_call_target="tpu_custom_call" | custom-call | flops 11468800 | bytes 13762560 | tf_op jit(solution)/shard_map/pallas_call | solution.py:306
  40.2 3.4 %collective-permute-start.4 = (f32[2,128]{1,0:T(2,128)}, f32[2,128]{1,0:T(2,128)S(1)}, u32[]{:S(2)}, u32[]{:S(2)}) collective-permute-start(f32[2,128]{1,0:T(2,128)} %get-tuple-element.18), channel_id=1, source_target_pairs={{0,1},{1,0},{2,3},{3,2},{4,5},{5,4},{6,7},{7,6},{8,9},{9,8},{10,11... | collective-permute-start | bytes 3080 | tf_op jit(solution)/shard_map/ppermute | solution.py:71
  45.4 2.0 %collective-permute-start.7 = (f32[2,128]{1,0:T(2,128)S(1)}, f32[2,128]{1,0:T(2,128)S(1)}, u32[]{:S(2)}, u32[]{:S(2)}) collective-permute-start(f32[2,128]{1,0:T(2,128)S(1)} %add.174), channel_id=1, source_target_pairs={{0,6},{1,7},{2,4},{3,5},{4,2},{5,3},{6,0},{7,1},{8,14},{9,15},{10,... | collective-permute-start | bytes 3080 | tf_op jit(solution)/shard_map/ppermute | solution.py:71
  47.8 1.5 %collective-permute-start.5 = (f32[2,128]{1,0:T(2,128)S(1)}, f32[2,128]{1,0:T(2,128)S(1)}, u32[]{:S(2)}, u32[]{:S(2)}) collective-permute-start(f32[2,128]{1,0:T(2,128)S(1)} %add.174), channel_id=1, source_target_pairs={{0,2},{1,3},{2,0},{3,1},{4,6},{5,7},{6,4},{7,5},{8,10},{9,11},{10,... | collective-permute-start | bytes 3080 | tf_op jit(solution)/shard_map/ppermute | solution.py:71
  51.4 3.9 %collective-permute-start.10 = (f32[2,128]{1,0:T(2,128)S(1)}, f32[2,128]{1,0:T(2,128)S(1)}, u32[]{:S(2)}, u32[]{:S(2)}) collective-permute-start(f32[2,128]{1,0:T(2,128)S(1)} %add_add_fusion.1), channel_id=1, source_target_pairs={{0,24},{1,25},{2,26},{3,27},{4,28},{5,29},{6,30},{7,31},{8,16},{9,... | collective-permute-start | bytes 3080 | tf_op jit(solution)/shard_map/ppermute | solution.py:71
  56.9 2.9 %collective-permute-done.9 = f32[2,128]{1,0:T(2,128)S(1)} collective-permute-done((f32[2,128]{1,0:T(2,128)S(1)}, f32[2,128]{1,0:T(2,128)S(1)}, u32[]{:S(2)}, u32[]{:S(2)}) %collective-permute-start.9) | collective-permute-done | bytes 1056 | tf_op jit(solution)/shard_map/ppermute | solution.py:71
  60.4 3.3 %shard_map.60 = (f32[28,80,128]{2,1,0:T(8,128)}, f32[1,128]{1,0:T(1,128)}) custom-call(f32[2,128]{1,0:T(2,128)} %add_add_fusion.refs_0_.refs_1_, f32[28,80,128]{2,1,0:T(8,128)} %get-tuple-element.19.refs_1_.refs_3_.refs_6_.refs_9_, f32[28,80,128]{2,1,0:T(8,128)} %get-tuple-element.20.refs_2_, f32[80,128]{1,0:T(8,128)} %add_convert_fusion.1.refs_3_.refs_8_.refs_4_), custom_call_target="tpu_custom_call" | custom-call | flops 11468800 | bytes 6881280 | tf_op jit(solution)/shard_map/pallas_call | solution.py:306
  65.6 1.4 collective-permute-start.14
  67.0 2.0 %collective-permute-start.13 = (f32[1,128]{1,0:T(1,128)S(1)}, f32[1,128]{1,0:T(1,128)S(1)}, u32[]{:S(2)}, u32[]{:S(2)}) collective-permute-start(f32[1,128]{1,0:T(1,128)S(1)} %add.181), channel_id=1, source_target_pairs={{0,4},{1,5},{2,6},{3,7},{4,0},{5,1},{6,2},{7,3},{8,12},{9,13},{10,... | collective-permute-start | bytes 1544 | tf_op jit(solution)/shard_map/ppermute | solution.py:71
  70.6 2.0 %collective-permute-done.12 = f32[1,128]{1,0:T(1,128)S(1)} collective-permute-done((f32[1,128]{1,0:T(1,128)S(1)}, f32[1,128]{1,0:T(1,128)S(1)}, u32[]{:S(2)}, u32[]{:S(2)}) %collective-permute-start.12) | collective-permute-done | bytes 544 | tf_op jit(solution)/shard_map/ppermute | solution.py:71
  72.6 1.5 %collective-permute-start.17 = (f32[1,128]{1,0:T(1,128)S(1)}, f32[1,128]{1,0:T(1,128)S(1)}, u32[]{:S(2)}, u32[]{:S(2)}) collective-permute-start(f32[1,128]{1,0:T(1,128)S(1)} %add_add_fusion.9), channel_id=1, source_target_pairs={{0,24},{1,25},{2,26},{3,27},{4,28},{5,29},{6,30},{7,31},{8,16},{9,... | collective-permute-start | bytes 1544 | tf_op jit(solution)/shard_map/ppermute | solution.py:71
  74.7 2.3 %collective-permute-start.15 = (f32[1,128]{1,0:T(1,128)S(1)}, f32[1,128]{1,0:T(1,128)S(1)}, u32[]{:S(2)}, u32[]{:S(2)}) collective-permute-start(f32[1,128]{1,0:T(1,128)S(1)} %add_add_fusion.9), channel_id=1, source_target_pairs={{0,8},{1,9},{2,10},{3,11},{4,12},{5,13},{6,14},{7,15},{8,0},{9,1},... | collective-permute-start | bytes 1544 | tf_op jit(solution)/shard_map/ppermute | solution.py:71
  79.1 5.8 %shard_map.61 = (f32[28,80,128]{2,1,0:T(8,128)}, f32[28,80,128]{2,1,0:T(8,128)}, f32[1,128]{1,0:T(1,128)}) custom-call(f32[1,128]{1,0:T(1,128)} %add_add_fusion.8.refs_0_.refs_1_.refs_2_, f32[2,128]{1,0:T(2,128)} %add_add_fusion.refs_0_.refs_1_, f32[28,80,128]{2,1,0:T(8,128)} %get-tuple-element.22.refs_2_, ...), custom_call_target="tpu_custom_call" | custom-call | flops 11468800 | bytes 13762560 | tf_op jit(solution)/shard_map/pallas_call | solution.py:306
  88.4 1.9 %collective-permute-start.19 = (f32[1,128]{1,0:T(1,128)S(1)}, f32[1,128]{1,0:T(1,128)S(1)}, u32[]{:S(2)}, u32[]{:S(2)}) collective-permute-start(f32[1,128]{1,0:T(1,128)S(1)} %add.188), channel_id=1, source_target_pairs={{0,2},{1,3},{2,0},{3,1},{4,6},{5,7},{6,4},{7,5},{8,10},{9,11},{10,... | collective-permute-start | bytes 1544 | tf_op jit(solution)/shard_map/ppermute | solution.py:71
  91.9 2.6 %collective-permute-start.24 = (f32[1,128]{1,0:T(1,128)S(1)}, f32[1,128]{1,0:T(1,128)S(1)}, u32[]{:S(2)}, u32[]{:S(2)}) collective-permute-start(f32[1,128]{1,0:T(1,128)S(1)} %add_add_fusion.7), channel_id=1, source_target_pairs={{0,24},{1,25},{2,26},{3,27},{4,28},{5,29},{6,30},{7,31},{8,16},{9,... | collective-permute-start | bytes 1544 | tf_op jit(solution)/shard_map/ppermute | solution.py:71
  97.3 1.7 %collective-permute-done.23 = f32[1,128]{1,0:T(1,128)S(1)} collective-permute-done((f32[1,128]{1,0:T(1,128)S(1)}, f32[1,128]{1,0:T(1,128)S(1)}, u32[]{:S(2)}, u32[]{:S(2)}) %collective-permute-start.23) | collective-permute-done | bytes 544 | tf_op jit(solution)/shard_map/ppermute | solution.py:71
  99.5 3.3 %shard_map.62 = (f32[28,80,128]{2,1,0:T(8,128)}, f32[1,128]{1,0:T(1,128)}) custom-call(f32[1,128]{1,0:T(1,128)} %add_add_fusion.8.refs_0_.refs_1_.refs_2_, f32[1,128]{1,0:T(1,128)} %add_add_fusion.6.refs_1_.refs_3_, f32[28,80,128]{2,1,0:T(8,128)} %get-tuple-element.22.refs_2_, f32[28,80,128]{2,1,0:T(8,128)} %get-tuple-element.26.refs_3_, ...), custom_call_target="tpu_custom_call" | custom-call | flops 11468800 | bytes 8028160 | tf_op jit(solution)/shard_map/pallas_call | solution.py:306
  104.8 1.4 collective-permute-start.28
  106.2 2.0 %collective-permute-start.27 = (f32[1,128]{1,0:T(1,128)S(1)}, f32[1,128]{1,0:T(1,128)S(1)}, u32[]{:S(2)}, u32[]{:S(2)}) collective-permute-start(f32[1,128]{1,0:T(1,128)S(1)} %add.195), channel_id=1, source_target_pairs={{0,4},{1,5},{2,6},{3,7},{4,0},{5,1},{6,2},{7,3},{8,12},{9,13},{10,... | collective-permute-start | bytes 1544 | tf_op jit(solution)/shard_map/ppermute | solution.py:71
  109.7 2.0 %collective-permute-done.26 = f32[1,128]{1,0:T(1,128)S(1)} collective-permute-done((f32[1,128]{1,0:T(1,128)S(1)}, f32[1,128]{1,0:T(1,128)S(1)}, u32[]{:S(2)}, u32[]{:S(2)}) %collective-permute-start.26) | collective-permute-done | bytes 544 | tf_op jit(solution)/shard_map/ppermute | solution.py:71
  111.7 1.5 %collective-permute-start.31 = (f32[1,128]{1,0:T(1,128)S(1)}, f32[1,128]{1,0:T(1,128)S(1)}, u32[]{:S(2)}, u32[]{:S(2)}) collective-permute-start(f32[1,128]{1,0:T(1,128)S(1)} %add_add_fusion.5), channel_id=1, source_target_pairs={{0,24},{1,25},{2,26},{3,27},{4,28},{5,29},{6,30},{7,31},{8,16},{9,... | collective-permute-start | bytes 1544 | tf_op jit(solution)/shard_map/ppermute | solution.py:71
  114.1 2.0 %collective-permute-start.29 = (f32[1,128]{1,0:T(1,128)S(1)}, f32[1,128]{1,0:T(1,128)S(1)}, u32[]{:S(2)}, u32[]{:S(2)}) collective-permute-start(f32[1,128]{1,0:T(1,128)S(1)} %add_add_fusion.5), channel_id=1, source_target_pairs={{0,8},{1,9},{2,10},{3,11},{4,12},{5,13},{6,14},{7,15},{8,0},{9,1},... | collective-permute-start | bytes 1544 | tf_op jit(solution)/shard_map/ppermute | solution.py:71
  118.2 5.3 %shard_map.63 = (f32[28,80,128]{2,1,0:T(8,128)}, f32[28,80,128]{2,1,0:T(8,128)}, f32[1,128]{1,0:T(1,128)}) custom-call(f32[1,128]{1,0:T(1,128)} %add_add_fusion.4.refs_0_.refs_4_, f32[1,128]{1,0:T(1,128)} %add_add_fusion.8.refs_0_.refs_1_.refs_2_, f32[28,80,128]{2,1,0:T(8,128)} %get-tuple-element.28.refs_2_, ...), custom_call_target="tpu_custom_call" | custom-call | flops 11468800 | bytes 13762560 | tf_op jit(solution)/shard_map/pallas_call | solution.py:306
  127.1 1.9 %collective-permute-start.33 = (f32[1,128]{1,0:T(1,128)S(1)}, f32[1,128]{1,0:T(1,128)S(1)}, u32[]{:S(2)}, u32[]{:S(2)}) collective-permute-start(f32[1,128]{1,0:T(1,128)S(1)} %add.202), channel_id=1, source_target_pairs={{0,2},{1,3},{2,0},{3,1},{4,6},{5,7},{6,4},{7,5},{8,10},{9,11},{10,... | collective-permute-start | bytes 1544 | tf_op jit(solution)/shard_map/ppermute | solution.py:71
  130.7 2.6 %collective-permute-start.38 = (f32[1,128]{1,0:T(1,128)S(1)}, f32[1,128]{1,0:T(1,128)S(1)}, u32[]{:S(2)}, u32[]{:S(2)}) collective-permute-start(f32[1,128]{1,0:T(1,128)S(1)} %add_add_fusion.3), channel_id=1, source_target_pairs={{0,24},{1,25},{2,26},{3,27},{4,28},{5,29},{6,30},{7,31},{8,16},{9,... | collective-permute-start | bytes 1544 | tf_op jit(solution)/shard_map/ppermute | solution.py:71
  136.0 1.7 %collective-permute-done.37 = f32[1,128]{1,0:T(1,128)S(1)} collective-permute-done((f32[1,128]{1,0:T(1,128)S(1)}, f32[1,128]{1,0:T(1,128)S(1)}, u32[]{:S(2)}, u32[]{:S(2)}) %collective-permute-start.37) | collective-permute-done | bytes 544 | tf_op jit(solution)/shard_map/ppermute | solution.py:71
  138.3 6.2 %shard_map.64 = (f32[16,128]{1,0:T(8,128)}, f32[16,128]{1,0:T(8,128)}) custom-call(f32[2,128]{1,0:T(2,128)} %add_add_fusion.refs_0_.refs_1_, f32[2,128]{1,0:T(2,128)} %add_add_fusion.refs_0_.refs_1_, f32[1,128]{1,0:T(1,128)} %add_add_fusion.8.refs_0_.refs_1_.refs_2_, f32[1,128]{1,0:T(1,128)} %add_add_fusion.6.refs_1_.refs_3_, ...), custom_call_target="tpu_custom_call" | custom-call | flops 11468800 | bytes 20643840 | tf_op jit(solution)/shard_map/pallas_call | solution.py:306
  (100 shorter events, 50.9 us)
Async XLA Ops:
  3.3 15.8 %collective-permute-start.1 = (f32[536,128]{1,0:T(8,128)S(1)}, f32[536,128]{1,0:T(8,128)}, u32[]{:S(2)}, u32[]{:S(2)}) collective-permute-start(f32[536,128]{1,0:T(8,128)S(1)} %maximum_bitcast_fusion.2), channel_id=1, source_target_pairs={{4,0},{8,4},{12,8},{16,12},{20,16},{24,20},{28,24},{5,1},{9,5},{13... | collective-permute-start | bytes 823304 | tf_op jit(solution)/shard_map/ppermute | solution.py:344
  5.3 15.5 %collective-permute-start = (f32[536,128]{1,0:T(8,128)}, f32[536,128]{1,0:T(8,128)}, u32[]{:S(2)}, u32[]{:S(2)}) collective-permute-start(f32[536,128]{1,0:T(8,128)} %maximum_bitcast_fusion.1), channel_id=1, source_target_pairs={{0,4},{4,8},{8,12},{12,16},{16,20},{20,24},{24,28},{1,5},{5,9},{9,... | collective-permute-start | bytes 823304 | tf_op jit(solution)/shard_map/ppermute | solution.py:341
  22.1 3.8 %collective-permute-start.2 = (f32[28,6,67]{2,1,0:T(8,128)S(1)}, f32[28,6,67]{2,1,0:T(8,128)S(1)}, u32[]{:S(2)}, u32[]{:S(2)}) collective-permute-start(f32[28,6,67]{2,1,0:T(8,128)S(1)} %get-tuple-element.34), channel_id=1, source_target_pairs={{0,1},{1,2},{2,3},{4,5},{5,6},{6,7},{8,9},{9,10},{10,11},{12,13},{... | collective-permute-start | bytes 135080 | tf_op jit(solution)/shard_map/ppermute | solution.py:20
  24.0 4.3 %collective-permute-start.3 = (f32[28,6,67]{2,1,0:T(8,128)S(1)}, f32[28,6,67]{2,1,0:T(8,128)S(1)}, u32[]{:S(2)}, u32[]{:S(2)}) collective-permute-start(f32[28,6,67]{2,1,0:T(8,128)S(1)} %get-tuple-element.35), channel_id=1, source_target_pairs={{1,0},{2,1},{3,2},{5,4},{6,5},{7,6},{9,8},{10,9},{11,10},{13,12},{... | collective-permute-start | bytes 135080 | tf_op jit(solution)/shard_map/ppermute | solution.py:22
  40.2 4.4 %collective-permute-start.4 = (f32[2,128]{1,0:T(2,128)}, f32[2,128]{1,0:T(2,128)S(1)}, u32[]{:S(2)}, u32[]{:S(2)}) collective-permute-start(f32[2,128]{1,0:T(2,128)} %get-tuple-element.18), channel_id=1, source_target_pairs={{0,1},{1,0},{2,3},{3,2},{4,5},{5,4},{6,7},{7,6},{8,9},{9,8},{10,11... | collective-permute-start | bytes 3080 | tf_op jit(solution)/shard_map/ppermute | solution.py:71
  45.4 4.5 %collective-permute-start.7 = (f32[2,128]{1,0:T(2,128)S(1)}, f32[2,128]{1,0:T(2,128)S(1)}, u32[]{:S(2)}, u32[]{:S(2)}) collective-permute-start(f32[2,128]{1,0:T(2,128)S(1)} %add.174), channel_id=1, source_target_pairs={{0,6},{1,7},{2,4},{3,5},{4,2},{5,3},{6,0},{7,1},{8,14},{9,15},{10,... | collective-permute-start | bytes 3080 | tf_op jit(solution)/shard_map/ppermute | solution.py:71
  47.4 3.6 %collective-permute-start.6 = (f32[2,128]{1,0:T(2,128)S(1)}, f32[2,128]{1,0:T(2,128)S(1)}, u32[]{:S(2)}, u32[]{:S(2)}) collective-permute-start(f32[2,128]{1,0:T(2,128)S(1)} %add.174), channel_id=1, source_target_pairs={{0,4},{1,5},{2,6},{3,7},{4,0},{5,1},{6,2},{7,3},{8,12},{9,13},{10,... | collective-permute-start | bytes 3080 | tf_op jit(solution)/shard_map/ppermute | solution.py:71
  47.8 3.6 %collective-permute-start.5 = (f32[2,128]{1,0:T(2,128)S(1)}, f32[2,128]{1,0:T(2,128)S(1)}, u32[]{:S(2)}, u32[]{:S(2)}) collective-permute-start(f32[2,128]{1,0:T(2,128)S(1)} %add.174), channel_id=1, source_target_pairs={{0,2},{1,3},{2,0},{3,1},{4,6},{5,7},{6,4},{7,5},{8,10},{9,11},{10,... | collective-permute-start | bytes 3080 | tf_op jit(solution)/shard_map/ppermute | solution.py:71
  51.4 5.5 %collective-permute-start.10 = (f32[2,128]{1,0:T(2,128)S(1)}, f32[2,128]{1,0:T(2,128)S(1)}, u32[]{:S(2)}, u32[]{:S(2)}) collective-permute-start(f32[2,128]{1,0:T(2,128)S(1)} %add_add_fusion.1), channel_id=1, source_target_pairs={{0,24},{1,25},{2,26},{3,27},{4,28},{5,29},{6,30},{7,31},{8,16},{9,... | collective-permute-start | bytes 3080 | tf_op jit(solution)/shard_map/ppermute | solution.py:71
  55.4 4.5 %collective-permute-start.9 = (f32[2,128]{1,0:T(2,128)S(1)}, f32[2,128]{1,0:T(2,128)S(1)}, u32[]{:S(2)}, u32[]{:S(2)}) collective-permute-start(f32[2,128]{1,0:T(2,128)S(1)} %add_add_fusion.1), channel_id=1, source_target_pairs={{0,16},{1,17},{2,18},{3,19},{4,20},{5,21},{6,22},{7,23},{8,24},{9,... | collective-permute-start | bytes 3080 | tf_op jit(solution)/shard_map/ppermute | solution.py:71
  55.4 4.5 %collective-permute-start.8 = (f32[2,128]{1,0:T(2,128)S(1)}, f32[2,128]{1,0:T(2,128)S(1)}, u32[]{:S(2)}, u32[]{:S(2)}) collective-permute-start(f32[2,128]{1,0:T(2,128)S(1)} %add_add_fusion.1), channel_id=1, source_target_pairs={{0,8},{1,9},{2,10},{3,11},{4,12},{5,13},{6,14},{7,15},{8,0},{9,1},... | collective-permute-start | bytes 3080 | tf_op jit(solution)/shard_map/ppermute | solution.py:71
  65.6 4.5 %collective-permute-start.14 = (f32[1,128]{1,0:T(1,128)S(1)}, f32[1,128]{1,0:T(1,128)S(1)}, u32[]{:S(2)}, u32[]{:S(2)}) collective-permute-start(f32[1,128]{1,0:T(1,128)S(1)} %add.181), channel_id=1, source_target_pairs={{0,6},{1,7},{2,4},{3,5},{4,2},{5,3},{6,0},{7,1},{8,14},{9,15},{10,... | collective-permute-start | bytes 1544 | tf_op jit(solution)/shard_map/ppermute | solution.py:71
  67.0 3.6 %collective-permute-start.13 = (f32[1,128]{1,0:T(1,128)S(1)}, f32[1,128]{1,0:T(1,128)S(1)}, u32[]{:S(2)}, u32[]{:S(2)}) collective-permute-start(f32[1,128]{1,0:T(1,128)S(1)} %add.181), channel_id=1, source_target_pairs={{0,4},{1,5},{2,6},{3,7},{4,0},{5,1},{6,2},{7,3},{8,12},{9,13},{10,... | collective-permute-start | bytes 1544 | tf_op jit(solution)/shard_map/ppermute | solution.py:71
  69.0 3.6 %collective-permute-start.12 = (f32[1,128]{1,0:T(1,128)S(1)}, f32[1,128]{1,0:T(1,128)S(1)}, u32[]{:S(2)}, u32[]{:S(2)}) collective-permute-start(f32[1,128]{1,0:T(1,128)S(1)} %add.181), channel_id=1, source_target_pairs={{0,2},{1,3},{2,0},{3,1},{4,6},{5,7},{6,4},{7,5},{8,10},{9,11},{10,... | collective-permute-start | bytes 1544 | tf_op jit(solution)/shard_map/ppermute | solution.py:71
  72.6 5.4 %collective-permute-start.17 = (f32[1,128]{1,0:T(1,128)S(1)}, f32[1,128]{1,0:T(1,128)S(1)}, u32[]{:S(2)}, u32[]{:S(2)}) collective-permute-start(f32[1,128]{1,0:T(1,128)S(1)} %add_add_fusion.9), channel_id=1, source_target_pairs={{0,24},{1,25},{2,26},{3,27},{4,28},{5,29},{6,30},{7,31},{8,16},{9,... | collective-permute-start | bytes 1544 | tf_op jit(solution)/shard_map/ppermute | solution.py:71
  74.0 4.5 %collective-permute-start.16 = (f32[1,128]{1,0:T(1,128)S(1)}, f32[1,128]{1,0:T(1,128)S(1)}, u32[]{:S(2)}, u32[]{:S(2)}) collective-permute-start(f32[1,128]{1,0:T(1,128)S(1)} %add_add_fusion.9), channel_id=1, source_target_pairs={{0,16},{1,17},{2,18},{3,19},{4,20},{5,21},{6,22},{7,23},{8,24},{9,... | collective-permute-start | bytes 1544 | tf_op jit(solution)/shard_map/ppermute | solution.py:71
  74.7 3.8 %collective-permute-start.15 = (f32[1,128]{1,0:T(1,128)S(1)}, f32[1,128]{1,0:T(1,128)S(1)}, u32[]{:S(2)}, u32[]{:S(2)}) collective-permute-start(f32[1,128]{1,0:T(1,128)S(1)} %add_add_fusion.9), channel_id=1, source_target_pairs={{0,8},{1,9},{2,10},{3,11},{4,12},{5,13},{6,14},{7,15},{8,0},{9,1},... | collective-permute-start | bytes 1544 | tf_op jit(solution)/shard_map/ppermute | solution.py:71
  86.8 4.5 %collective-permute-start.21 = (f32[1,128]{1,0:T(1,128)S(1)}, f32[1,128]{1,0:T(1,128)S(1)}, u32[]{:S(2)}, u32[]{:S(2)}) collective-permute-start(f32[1,128]{1,0:T(1,128)S(1)} %add.188), channel_id=1, source_target_pairs={{0,6},{1,7},{2,4},{3,5},{4,2},{5,3},{6,0},{7,1},{8,14},{9,15},{10,... | collective-permute-start | bytes 1544 | tf_op jit(solution)/shard_map/ppermute | solution.py:71
  87.1 4.1 %collective-permute-start.20 = (f32[1,128]{1,0:T(1,128)S(1)}, f32[1,128]{1,0:T(1,128)S(1)}, u32[]{:S(2)}, u32[]{:S(2)}) collective-permute-start(f32[1,128]{1,0:T(1,128)S(1)} %add.188), channel_id=1, source_target_pairs={{0,4},{1,5},{2,6},{3,7},{4,0},{5,1},{6,2},{7,3},{8,12},{9,13},{10,... | collective-permute-start | bytes 1544 | tf_op jit(solution)/shard_map/ppermute | solution.py:71
  88.4 3.6 %collective-permute-start.19 = (f32[1,128]{1,0:T(1,128)S(1)}, f32[1,128]{1,0:T(1,128)S(1)}, u32[]{:S(2)}, u32[]{:S(2)}) collective-permute-start(f32[1,128]{1,0:T(1,128)S(1)} %add.188), channel_id=1, source_target_pairs={{0,2},{1,3},{2,0},{3,1},{4,6},{5,7},{6,4},{7,5},{8,10},{9,11},{10,... | collective-permute-start | bytes 1544 | tf_op jit(solution)/shard_map/ppermute | solution.py:71
  91.9 5.4 %collective-permute-start.24 = (f32[1,128]{1,0:T(1,128)S(1)}, f32[1,128]{1,0:T(1,128)S(1)}, u32[]{:S(2)}, u32[]{:S(2)}) collective-permute-start(f32[1,128]{1,0:T(1,128)S(1)} %add_add_fusion.7), channel_id=1, source_target_pairs={{0,24},{1,25},{2,26},{3,27},{4,28},{5,29},{6,30},{7,31},{8,16},{9,... | collective-permute-start | bytes 1544 | tf_op jit(solution)/shard_map/ppermute | solution.py:71
  94.5 4.5 %collective-permute-start.23 = (f32[1,128]{1,0:T(1,128)S(1)}, f32[1,128]{1,0:T(1,128)S(1)}, u32[]{:S(2)}, u32[]{:S(2)}) collective-permute-start(f32[1,128]{1,0:T(1,128)S(1)} %add_add_fusion.7), channel_id=1, source_target_pairs={{0,16},{1,17},{2,18},{3,19},{4,20},{5,21},{6,22},{7,23},{8,24},{9,... | collective-permute-start | bytes 1544 | tf_op jit(solution)/shard_map/ppermute | solution.py:71
  95.4 3.6 %collective-permute-start.22 = (f32[1,128]{1,0:T(1,128)S(1)}, f32[1,128]{1,0:T(1,128)S(1)}, u32[]{:S(2)}, u32[]{:S(2)}) collective-permute-start(f32[1,128]{1,0:T(1,128)S(1)} %add_add_fusion.7), channel_id=1, source_target_pairs={{0,8},{1,9},{2,10},{3,11},{4,12},{5,13},{6,14},{7,15},{8,0},{9,1},... | collective-permute-start | bytes 1544 | tf_op jit(solution)/shard_map/ppermute | solution.py:71
  104.8 4.5 %collective-permute-start.28 = (f32[1,128]{1,0:T(1,128)S(1)}, f32[1,128]{1,0:T(1,128)S(1)}, u32[]{:S(2)}, u32[]{:S(2)}) collective-permute-start(f32[1,128]{1,0:T(1,128)S(1)} %add.195), channel_id=1, source_target_pairs={{0,6},{1,7},{2,4},{3,5},{4,2},{5,3},{6,0},{7,1},{8,14},{9,15},{10,... | collective-permute-start | bytes 1544 | tf_op jit(solution)/shard_map/ppermute | solution.py:71
  108.1 3.6 %collective-permute-start.26 = (f32[1,128]{1,0:T(1,128)S(1)}, f32[1,128]{1,0:T(1,128)S(1)}, u32[]{:S(2)}, u32[]{:S(2)}) collective-permute-start(f32[1,128]{1,0:T(1,128)S(1)} %add.195), channel_id=1, source_target_pairs={{0,2},{1,3},{2,0},{3,1},{4,6},{5,7},{6,4},{7,5},{8,10},{9,11},{10,... | collective-permute-start | bytes 1544 | tf_op jit(solution)/shard_map/ppermute | solution.py:71
  111.7 5.4 %collective-permute-start.31 = (f32[1,128]{1,0:T(1,128)S(1)}, f32[1,128]{1,0:T(1,128)S(1)}, u32[]{:S(2)}, u32[]{:S(2)}) collective-permute-start(f32[1,128]{1,0:T(1,128)S(1)} %add_add_fusion.5), channel_id=1, source_target_pairs={{0,24},{1,25},{2,26},{3,27},{4,28},{5,29},{6,30},{7,31},{8,16},{9,... | collective-permute-start | bytes 1544 | tf_op jit(solution)/shard_map/ppermute | solution.py:71
  113.2 4.5 %collective-permute-start.30 = (f32[1,128]{1,0:T(1,128)S(1)}, f32[1,128]{1,0:T(1,128)S(1)}, u32[]{:S(2)}, u32[]{:S(2)}) collective-permute-start(f32[1,128]{1,0:T(1,128)S(1)} %add_add_fusion.5), channel_id=1, source_target_pairs={{0,16},{1,17},{2,18},{3,19},{4,20},{5,21},{6,22},{7,23},{8,24},{9,... | collective-permute-start | bytes 1544 | tf_op jit(solution)/shard_map/ppermute | solution.py:71
  114.1 3.6 %collective-permute-start.29 = (f32[1,128]{1,0:T(1,128)S(1)}, f32[1,128]{1,0:T(1,128)S(1)}, u32[]{:S(2)}, u32[]{:S(2)}) collective-permute-start(f32[1,128]{1,0:T(1,128)S(1)} %add_add_fusion.5), channel_id=1, source_target_pairs={{0,8},{1,9},{2,10},{3,11},{4,12},{5,13},{6,14},{7,15},{8,0},{9,1},... | collective-permute-start | bytes 1544 | tf_op jit(solution)/shard_map/ppermute | solution.py:71
  125.5 4.5 %collective-permute-start.35 = (f32[1,128]{1,0:T(1,128)S(1)}, f32[1,128]{1,0:T(1,128)S(1)}, u32[]{:S(2)}, u32[]{:S(2)}) collective-permute-start(f32[1,128]{1,0:T(1,128)S(1)} %add.202), channel_id=1, source_target_pairs={{0,6},{1,7},{2,4},{3,5},{4,2},{5,3},{6,0},{7,1},{8,14},{9,15},{10,... | collective-permute-start | bytes 1544 | tf_op jit(solution)/shard_map/ppermute | solution.py:71
  125.9 4.1 %collective-permute-start.34 = (f32[1,128]{1,0:T(1,128)S(1)}, f32[1,128]{1,0:T(1,128)S(1)}, u32[]{:S(2)}, u32[]{:S(2)}) collective-permute-start(f32[1,128]{1,0:T(1,128)S(1)} %add.202), channel_id=1, source_target_pairs={{0,4},{1,5},{2,6},{3,7},{4,0},{5,1},{6,2},{7,3},{8,12},{9,13},{10,... | collective-permute-start | bytes 1544 | tf_op jit(solution)/shard_map/ppermute | solution.py:71
  130.7 5.4 %collective-permute-start.38 = (f32[1,128]{1,0:T(1,128)S(1)}, f32[1,128]{1,0:T(1,128)S(1)}, u32[]{:S(2)}, u32[]{:S(2)}) collective-permute-start(f32[1,128]{1,0:T(1,128)S(1)} %add_add_fusion.3), channel_id=1, source_target_pairs={{0,24},{1,25},{2,26},{3,27},{4,28},{5,29},{6,30},{7,31},{8,16},{9,... | collective-permute-start | bytes 1544 | tf_op jit(solution)/shard_map/ppermute | solution.py:71
  133.3 4.5 %collective-permute-start.37 = (f32[1,128]{1,0:T(1,128)S(1)}, f32[1,128]{1,0:T(1,128)S(1)}, u32[]{:S(2)}, u32[]{:S(2)}) collective-permute-start(f32[1,128]{1,0:T(1,128)S(1)} %add_add_fusion.3), channel_id=1, source_target_pairs={{0,16},{1,17},{2,18},{3,19},{4,20},{5,21},{6,22},{7,23},{8,24},{9,... | collective-permute-start | bytes 1544 | tf_op jit(solution)/shard_map/ppermute | solution.py:71
  (11 other events, 57.0 us)

commit v17 on v16

--- a/solution.py
+++ b/solution.py
@@ -117,9 +117,11 @@
 
 
 def _apply_q(plan, reach, source, gain_ref, weight_ref, inside_ref, row_ref, inner_ref, stiff_ref,
-             applied_ref, dot_source):
+             applied_ref, dot_source, ahead=None):
 
     def first_pass(r, carry):
+        if ahead is not None:
+            ahead(r + 1, 0)
         stiff_ref[r] = weight_ref[r] * _stiffen_row(source, r, gain_ref[r])
         return carry
 
@@ -236,9 +238,10 @@
         direction_out[r] = residual_ref[r] + beta * direction_ref[r]
         return carry
 
-    lax.fori_loop(*plan.span(reach + 2), new_direction, 0)
+    first, _ = plan.span(reach + 2)
+    lax.fori_loop(first, first + 2, new_direction, 0)
     pa_out[...] = _apply_q(plan, reach, direction_out, gain_ref, weight_ref, inside_ref, row_ref, inner_ref,
-                           scratch, applied_out, direction_out)
+                           scratch, applied_out, direction_out, ahead=new_direction)
 
 
 def _final_kernel(plan, *refs):

time: 145 us -> 145 us (level)
  no operation moved by 1% of the time
where the time goes in v17:
time: 145 us; the launch traced here: 144 us
  starting transfers between devices  54.1 us (37%)
  waiting for transfers between devices  33.9 us (23%)
  Pallas kernels  33.5 us (23%)
  other arithmetic  13.2 us (9%)
  local copies, waits for them, and re-layouts  8.58 us (6%)
    ppermute x35, starting transfers between devices, partner(): lax.ppermute(terms, axes, [(i, i ^ mask) for i in range(count)])  43.4 us
    pallas_call x6, Pallas kernels, _call(): pl.pallas_call(lambda *refs: kernel(plan, *refs), out_shape=out_shapes, i...  33.5 us
    ppermute x35, waiting for transfers between devices, partner(): lax.ppermute(terms, axes, [(i, i ^ mask) for i in range(count)])  30.8 us
    ppermute x1, starting transfers between devices, on_device(): lax.ppermute(edge_rows(rows - sent), 'rows', [(i, i + 1) for i in range(c...  6.21 us
    add x15, other arithmetic, _span_sum(): _span_sum(terms, rest, partner)  6.15 us
    broadcast_in_dim x3, local copies, waits for them, and re-layouts, on_device(): fields = (probes, observed[None], kappa_sq[None], variance_weight[None])  3.09 us
  transfers between devices with their start and end apart: 39, of which 30 were waited for; matrix products, arithmetic and copies ran while one was open for 7% of the time, Pallas kernels for 0%

profile of v17, /device:TPU:0, one launch (start us, length us, event | category | flops | bytes accessed | tf_op | source)
XLA Modules:
  0.0 144.2 jit_solution(10538889312884528349)
XLA Ops:
  5.3 6.2 %collective-permute-start = (f32[536,128]{1,0:T(8,128)}, f32[536,128]{1,0:T(8,128)}, u32[]{:S(2)}, u32[]{:S(2)}) collective-permute-start(f32[536,128]{1,0:T(8,128)} %maximum_bitcast_fusion.1), channel_id=1, source_target_pairs={{0,4},{4,8},{8,12},{12,16},{16,20},{20,24},{24,28},{1,5},{5,9},{9,... | collective-permute-start | bytes 823304 | tf_op jit(solution)/shard_map/ppermute | solution.py:344
  15.8 2.4 %maximum_bitcast_fusion = f32[16,128,67]{2,1,0:T(8,128)S(1)} fusion(f32[1,16,128]{0,2,1:T(8,128)} %copy.17, f32[1,16,128]{0,2,1:T(8,128)S(1)} %copy.16, f32[1,16,128]{0,2,1:T(8,128)} %copy.15, f32[64,16,128]{0,2,1:T(8,128)S(1)} %copy.14), kind=kLoop, calls=%fused_computation.13 | loop fusion | flops 411648 | bytes 1097728 | tf_op jit(solution)/shard_map/transpose | solution.py:351
  22.1 1.9 %collective-permute-start.2 = (f32[28,6,67]{2,1,0:T(8,128)S(1)}, f32[28,6,67]{2,1,0:T(8,128)S(1)}, u32[]{:S(2)}, u32[]{:S(2)}) collective-permute-start(f32[28,6,67]{2,1,0:T(8,128)S(1)} %get-tuple-element.34), channel_id=1, source_target_pairs={{0,1},{1,2},{2,3},{4,5},{5,6},{6,7},{8,9},{9,10},{10,11},{12,13},{... | collective-permute-start | bytes 135080 | tf_op jit(solution)/shard_map/ppermute | solution.py:20
  25.8 2.5 %collective-permute-done.3 = f32[28,6,67]{2,1,0:T(8,128)S(1)} collective-permute-done((f32[28,6,67]{2,1,0:T(8,128)S(1)}, f32[28,6,67]{2,1,0:T(8,128)S(1)}, u32[]{:S(2)}, u32[]{:S(2)}) %collective-permute-start.3) | collective-permute-done | bytes 45056 | tf_op jit(solution)/shard_map/ppermute | solution.py:22
  28.3 1.9 %select_maximum_fusion.refs_0_ = f32[28,144,128]{2,1,0:T(8,128)} fusion(f32[28,6,67]{2,1,0:T(8,128)S(1)} %collective-permute-done.3, f32[28,6,67]{2,1,0:T(8,128)S(1)} %collective-permute-done.2, f32[6,128,67]{2,1,0:T(8,128)S(1)} %bitcast.15, f32[16,128,67]{2,1,0:T(8,128)S(1)} %maximum_bitcast_fusion, f32[6,128,67]{2,1,0:T(8,128)S(1)} %bitcast.17), kind=kLoop, calls=%fused_computation | loop fusion | flops 8773632 | bytes 3114944 | tf_op jit(solution)/shard_map/concatenate | solution.py:18
  30.3 10.0 %shard_map.59 = (f32[28,80,128]{2,1,0:T(8,128)}, f32[28,80,128]{2,1,0:T(8,128)}, f32[28,80,128]{2,1,0:T(8,128)}, f32[28,80,128]{2,1,0:T(8,128)}, f32[28,80,128]{...) custom-call(f32[28,144,128]{2,1,0:T(8,128)} %select_maximum_fusion.refs_0_, ...), custom_call_target="tpu_custom_call" | custom-call | flops 11468800 | bytes 13762560 | tf_op jit(solution)/shard_map/pallas_call | solution.py:309
  40.2 3.4 %collective-permute-start.4 = (f32[2,128]{1,0:T(2,128)}, f32[2,128]{1,0:T(2,128)S(1)}, u32[]{:S(2)}, u32[]{:S(2)}) collective-permute-start(f32[2,128]{1,0:T(2,128)} %get-tuple-element.18), channel_id=1, source_target_pairs={{0,1},{1,0},{2,3},{3,2},{4,5},{5,4},{6,7},{7,6},{8,9},{9,8},{10,11... | collective-permute-start | bytes 3080 | tf_op jit(solution)/shard_map/ppermute | solution.py:71
  45.4 2.0 %collective-permute-start.7 = (f32[2,128]{1,0:T(2,128)S(1)}, f32[2,128]{1,0:T(2,128)S(1)}, u32[]{:S(2)}, u32[]{:S(2)}) collective-permute-start(f32[2,128]{1,0:T(2,128)S(1)} %add.174), channel_id=1, source_target_pairs={{0,6},{1,7},{2,4},{3,5},{4,2},{5,3},{6,0},{7,1},{8,14},{9,15},{10,... | collective-permute-start | bytes 3080 | tf_op jit(solution)/shard_map/ppermute | solution.py:71
  47.8 1.5 %collective-permute-start.5 = (f32[2,128]{1,0:T(2,128)S(1)}, f32[2,128]{1,0:T(2,128)S(1)}, u32[]{:S(2)}, u32[]{:S(2)}) collective-permute-start(f32[2,128]{1,0:T(2,128)S(1)} %add.174), channel_id=1, source_target_pairs={{0,2},{1,3},{2,0},{3,1},{4,6},{5,7},{6,4},{7,5},{8,10},{9,11},{10,... | collective-permute-start | bytes 3080 | tf_op jit(solution)/shard_map/ppermute | solution.py:71
  51.4 3.9 %collective-permute-start.10 = (f32[2,128]{1,0:T(2,128)S(1)}, f32[2,128]{1,0:T(2,128)S(1)}, u32[]{:S(2)}, u32[]{:S(2)}) collective-permute-start(f32[2,128]{1,0:T(2,128)S(1)} %add_add_fusion.1), channel_id=1, source_target_pairs={{0,24},{1,25},{2,26},{3,27},{4,28},{5,29},{6,30},{7,31},{8,16},{9,... | collective-permute-start | bytes 3080 | tf_op jit(solution)/shard_map/ppermute | solution.py:71
  56.9 2.9 %collective-permute-done.9 = f32[2,128]{1,0:T(2,128)S(1)} collective-permute-done((f32[2,128]{1,0:T(2,128)S(1)}, f32[2,128]{1,0:T(2,128)S(1)}, u32[]{:S(2)}, u32[]{:S(2)}) %collective-permute-start.9) | collective-permute-done | bytes 1056 | tf_op jit(solution)/shard_map/ppermute | solution.py:71
  60.4 3.3 %shard_map.60 = (f32[28,80,128]{2,1,0:T(8,128)}, f32[1,128]{1,0:T(1,128)}) custom-call(f32[2,128]{1,0:T(2,128)} %add_add_fusion.refs_0_.refs_1_, f32[28,80,128]{2,1,0:T(8,128)} %get-tuple-element.19.refs_1_.refs_3_.refs_6_.refs_9_, f32[28,80,128]{2,1,0:T(8,128)} %get-tuple-element.20.refs_2_, f32[80,128]{1,0:T(8,128)} %add_convert_fusion.1.refs_3_.refs_8_.refs_4_), custom_call_target="tpu_custom_call" | custom-call | flops 11468800 | bytes 6881280 | tf_op jit(solution)/shard_map/pallas_call | solution.py:309
  65.6 1.4 collective-permute-start.14
  67.0 2.0 %collective-permute-start.13 = (f32[1,128]{1,0:T(1,128)S(1)}, f32[1,128]{1,0:T(1,128)S(1)}, u32[]{:S(2)}, u32[]{:S(2)}) collective-permute-start(f32[1,128]{1,0:T(1,128)S(1)} %add.181), channel_id=1, source_target_pairs={{0,4},{1,5},{2,6},{3,7},{4,0},{5,1},{6,2},{7,3},{8,12},{9,13},{10,... | collective-permute-start | bytes 1544 | tf_op jit(solution)/shard_map/ppermute | solution.py:71
  70.6 2.0 %collective-permute-done.12 = f32[1,128]{1,0:T(1,128)S(1)} collective-permute-done((f32[1,128]{1,0:T(1,128)S(1)}, f32[1,128]{1,0:T(1,128)S(1)}, u32[]{:S(2)}, u32[]{:S(2)}) %collective-permute-start.12) | collective-permute-done | bytes 544 | tf_op jit(solution)/shard_map/ppermute | solution.py:71
  72.6 1.5 %collective-permute-start.17 = (f32[1,128]{1,0:T(1,128)S(1)}, f32[1,128]{1,0:T(1,128)S(1)}, u32[]{:S(2)}, u32[]{:S(2)}) collective-permute-start(f32[1,128]{1,0:T(1,128)S(1)} %add_add_fusion.9), channel_id=1, source_target_pairs={{0,24},{1,25},{2,26},{3,27},{4,28},{5,29},{6,30},{7,31},{8,16},{9,... | collective-permute-start | bytes 1544 | tf_op jit(solution)/shard_map/ppermute | solution.py:71
  74.7 2.3 %collective-permute-start.15 = (f32[1,128]{1,0:T(1,128)S(1)}, f32[1,128]{1,0:T(1,128)S(1)}, u32[]{:S(2)}, u32[]{:S(2)}) collective-permute-start(f32[1,128]{1,0:T(1,128)S(1)} %add_add_fusion.9), channel_id=1, source_target_pairs={{0,8},{1,9},{2,10},{3,11},{4,12},{5,13},{6,14},{7,15},{8,0},{9,1},... | collective-permute-start | bytes 1544 | tf_op jit(solution)/shard_map/ppermute | solution.py:71
  79.1 5.6 %shard_map.61 = (f32[28,80,128]{2,1,0:T(8,128)}, f32[28,80,128]{2,1,0:T(8,128)}, f32[1,128]{1,0:T(1,128)}) custom-call(f32[1,128]{1,0:T(1,128)} %add_add_fusion.8.refs_0_.refs_1_.refs_2_, f32[2,128]{1,0:T(2,128)} %add_add_fusion.refs_0_.refs_1_, f32[28,80,128]{2,1,0:T(8,128)} %get-tuple-element.22.refs_2_, ...), custom_call_target="tpu_custom_call" | custom-call | flops 11468800 | bytes 13762560 | tf_op jit(solution)/shard_map/pallas_call | solution.py:309
  88.2 1.9 %collective-permute-start.19 = (f32[1,128]{1,0:T(1,128)S(1)}, f32[1,128]{1,0:T(1,128)S(1)}, u32[]{:S(2)}, u32[]{:S(2)}) collective-permute-start(f32[1,128]{1,0:T(1,128)S(1)} %add.188), channel_id=1, source_target_pairs={{0,2},{1,3},{2,0},{3,1},{4,6},{5,7},{6,4},{7,5},{8,10},{9,11},{10,... | collective-permute-start | bytes 1544 | tf_op jit(solution)/shard_map/ppermute | solution.py:71
  91.8 2.6 %collective-permute-start.24 = (f32[1,128]{1,0:T(1,128)S(1)}, f32[1,128]{1,0:T(1,128)S(1)}, u32[]{:S(2)}, u32[]{:S(2)}) collective-permute-start(f32[1,128]{1,0:T(1,128)S(1)} %add_add_fusion.7), channel_id=1, source_target_pairs={{0,24},{1,25},{2,26},{3,27},{4,28},{5,29},{6,30},{7,31},{8,16},{9,... | collective-permute-start | bytes 1544 | tf_op jit(solution)/shard_map/ppermute | solution.py:71
  97.2 1.7 %collective-permute-done.23 = f32[1,128]{1,0:T(1,128)S(1)} collective-permute-done((f32[1,128]{1,0:T(1,128)S(1)}, f32[1,128]{1,0:T(1,128)S(1)}, u32[]{:S(2)}, u32[]{:S(2)}) %collective-permute-start.23) | collective-permute-done | bytes 544 | tf_op jit(solution)/shard_map/ppermute | solution.py:71
  99.4 3.3 %shard_map.62 = (f32[28,80,128]{2,1,0:T(8,128)}, f32[1,128]{1,0:T(1,128)}) custom-call(f32[1,128]{1,0:T(1,128)} %add_add_fusion.8.refs_0_.refs_1_.refs_2_, f32[1,128]{1,0:T(1,128)} %add_add_fusion.6.refs_1_.refs_3_, f32[28,80,128]{2,1,0:T(8,128)} %get-tuple-element.22.refs_2_, f32[28,80,128]{2,1,0:T(8,128)} %get-tuple-element.26.refs_3_, ...), custom_call_target="tpu_custom_call" | custom-call | flops 11468800 | bytes 8028160 | tf_op jit(solution)/shard_map/pallas_call | solution.py:309
  104.6 1.4 collective-permute-start.28
  106.0 2.0 %collective-permute-start.27 = (f32[1,128]{1,0:T(1,128)S(1)}, f32[1,128]{1,0:T(1,128)S(1)}, u32[]{:S(2)}, u32[]{:S(2)}) collective-permute-start(f32[1,128]{1,0:T(1,128)S(1)} %add.195), channel_id=1, source_target_pairs={{0,4},{1,5},{2,6},{3,7},{4,0},{5,1},{6,2},{7,3},{8,12},{9,13},{10,... | collective-permute-start | bytes 1544 | tf_op jit(solution)/shard_map/ppermute | solution.py:71
  109.6 2.0 %collective-permute-done.26 = f32[1,128]{1,0:T(1,128)S(1)} collective-permute-done((f32[1,128]{1,0:T(1,128)S(1)}, f32[1,128]{1,0:T(1,128)S(1)}, u32[]{:S(2)}, u32[]{:S(2)}) %collective-permute-start.26) | collective-permute-done | bytes 544 | tf_op jit(solution)/shard_map/ppermute | solution.py:71
  111.5 1.5 %collective-permute-start.31 = (f32[1,128]{1,0:T(1,128)S(1)}, f32[1,128]{1,0:T(1,128)S(1)}, u32[]{:S(2)}, u32[]{:S(2)}) collective-permute-start(f32[1,128]{1,0:T(1,128)S(1)} %add_add_fusion.5), channel_id=1, source_target_pairs={{0,24},{1,25},{2,26},{3,27},{4,28},{5,29},{6,30},{7,31},{8,16},{9,... | collective-permute-start | bytes 1544 | tf_op jit(solution)/shard_map/ppermute | solution.py:71
  113.9 2.0 %collective-permute-start.29 = (f32[1,128]{1,0:T(1,128)S(1)}, f32[1,128]{1,0:T(1,128)S(1)}, u32[]{:S(2)}, u32[]{:S(2)}) collective-permute-start(f32[1,128]{1,0:T(1,128)S(1)} %add_add_fusion.5), channel_id=1, source_target_pairs={{0,8},{1,9},{2,10},{3,11},{4,12},{5,13},{6,14},{7,15},{8,0},{9,1},... | collective-permute-start | bytes 1544 | tf_op jit(solution)/shard_map/ppermute | solution.py:71
  118.1 5.2 %shard_map.63 = (f32[28,80,128]{2,1,0:T(8,128)}, f32[28,80,128]{2,1,0:T(8,128)}, f32[1,128]{1,0:T(1,128)}) custom-call(f32[1,128]{1,0:T(1,128)} %add_add_fusion.4.refs_0_.refs_4_, f32[1,128]{1,0:T(1,128)} %add_add_fusion.8.refs_0_.refs_1_.refs_2_, f32[28,80,128]{2,1,0:T(8,128)} %get-tuple-element.28.refs_2_, ...), custom_call_target="tpu_custom_call" | custom-call | flops 11468800 | bytes 13762560 | tf_op jit(solution)/shard_map/pallas_call | solution.py:309
  126.8 1.9 %collective-permute-start.33 = (f32[1,128]{1,0:T(1,128)S(1)}, f32[1,128]{1,0:T(1,128)S(1)}, u32[]{:S(2)}, u32[]{:S(2)}) collective-permute-start(f32[1,128]{1,0:T(1,128)S(1)} %add.202), channel_id=1, source_target_pairs={{0,2},{1,3},{2,0},{3,1},{4,6},{5,7},{6,4},{7,5},{8,10},{9,11},{10,... | collective-permute-start | bytes 1544 | tf_op jit(solution)/shard_map/ppermute | solution.py:71
  130.4 2.6 %collective-permute-start.38 = (f32[1,128]{1,0:T(1,128)S(1)}, f32[1,128]{1,0:T(1,128)S(1)}, u32[]{:S(2)}, u32[]{:S(2)}) collective-permute-start(f32[1,128]{1,0:T(1,128)S(1)} %add_add_fusion.3), channel_id=1, source_target_pairs={{0,24},{1,25},{2,26},{3,27},{4,28},{5,29},{6,30},{7,31},{8,16},{9,... | collective-permute-start | bytes 1544 | tf_op jit(solution)/shard_map/ppermute | solution.py:71
  135.7 1.7 %collective-permute-done.37 = f32[1,128]{1,0:T(1,128)S(1)} collective-permute-done((f32[1,128]{1,0:T(1,128)S(1)}, f32[1,128]{1,0:T(1,128)S(1)}, u32[]{:S(2)}, u32[]{:S(2)}) %collective-permute-start.37) | collective-permute-done | bytes 544 | tf_op jit(solution)/shard_map/ppermute | solution.py:71
  138.0 6.2 %shard_map.64 = (f32[16,128]{1,0:T(8,128)}, f32[16,128]{1,0:T(8,128)}) custom-call(f32[2,128]{1,0:T(2,128)} %add_add_fusion.refs_0_.refs_1_, f32[2,128]{1,0:T(2,128)} %add_add_fusion.refs_0_.refs_1_, f32[1,128]{1,0:T(1,128)} %add_add_fusion.8.refs_0_.refs_1_.refs_2_, f32[1,128]{1,0:T(1,128)} %add_add_fusion.6.refs_1_.refs_3_, ...), custom_call_target="tpu_custom_call" | custom-call | flops 11468800 | bytes 20643840 | tf_op jit(solution)/shard_map/pallas_call | solution.py:309
  (100 shorter events, 50.9 us)
Async XLA Ops:
  3.3 15.8 %collective-permute-start.1 = (f32[536,128]{1,0:T(8,128)S(1)}, f32[536,128]{1,0:T(8,128)}, u32[]{:S(2)}, u32[]{:S(2)}) collective-permute-start(f32[536,128]{1,0:T(8,128)S(1)} %maximum_bitcast_fusion.2), channel_id=1, source_target_pairs={{4,0},{8,4},{12,8},{16,12},{20,16},{24,20},{28,24},{5,1},{9,5},{13... | collective-permute-start | bytes 823304 | tf_op jit(solution)/shard_map/ppermute | solution.py:347
  5.3 15.5 %collective-permute-start = (f32[536,128]{1,0:T(8,128)}, f32[536,128]{1,0:T(8,128)}, u32[]{:S(2)}, u32[]{:S(2)}) collective-permute-start(f32[536,128]{1,0:T(8,128)} %maximum_bitcast_fusion.1), channel_id=1, source_target_pairs={{0,4},{4,8},{8,12},{12,16},{16,20},{20,24},{24,28},{1,5},{5,9},{9,... | collective-permute-start | bytes 823304 | tf_op jit(solution)/shard_map/ppermute | solution.py:344
  22.1 3.8 %collective-permute-start.2 = (f32[28,6,67]{2,1,0:T(8,128)S(1)}, f32[28,6,67]{2,1,0:T(8,128)S(1)}, u32[]{:S(2)}, u32[]{:S(2)}) collective-permute-start(f32[28,6,67]{2,1,0:T(8,128)S(1)} %get-tuple-element.34), channel_id=1, source_target_pairs={{0,1},{1,2},{2,3},{4,5},{5,6},{6,7},{8,9},{9,10},{10,11},{12,13},{... | collective-permute-start | bytes 135080 | tf_op jit(solution)/shard_map/ppermute | solution.py:20
  24.0 4.3 %collective-permute-start.3 = (f32[28,6,67]{2,1,0:T(8,128)S(1)}, f32[28,6,67]{2,1,0:T(8,128)S(1)}, u32[]{:S(2)}, u32[]{:S(2)}) collective-permute-start(f32[28,6,67]{2,1,0:T(8,128)S(1)} %get-tuple-element.35), channel_id=1, source_target_pairs={{1,0},{2,1},{3,2},{5,4},{6,5},{7,6},{9,8},{10,9},{11,10},{13,12},{... | collective-permute-start | bytes 135080 | tf_op jit(solution)/shard_map/ppermute | solution.py:22
  40.2 4.4 %collective-permute-start.4 = (f32[2,128]{1,0:T(2,128)}, f32[2,128]{1,0:T(2,128)S(1)}, u32[]{:S(2)}, u32[]{:S(2)}) collective-permute-start(f32[2,128]{1,0:T(2,128)} %get-tuple-element.18), channel_id=1, source_target_pairs={{0,1},{1,0},{2,3},{3,2},{4,5},{5,4},{6,7},{7,6},{8,9},{9,8},{10,11... | collective-permute-start | bytes 3080 | tf_op jit(solution)/shard_map/ppermute | solution.py:71
  45.4 4.5 %collective-permute-start.7 = (f32[2,128]{1,0:T(2,128)S(1)}, f32[2,128]{1,0:T(2,128)S(1)}, u32[]{:S(2)}, u32[]{:S(2)}) collective-permute-start(f32[2,128]{1,0:T(2,128)S(1)} %add.174), channel_id=1, source_target_pairs={{0,6},{1,7},{2,4},{3,5},{4,2},{5,3},{6,0},{7,1},{8,14},{9,15},{10,... | collective-permute-start | bytes 3080 | tf_op jit(solution)/shard_map/ppermute | solution.py:71
  47.4 3.6 %collective-permute-start.6 = (f32[2,128]{1,0:T(2,128)S(1)}, f32[2,128]{1,0:T(2,128)S(1)}, u32[]{:S(2)}, u32[]{:S(2)}) collective-permute-start(f32[2,128]{1,0:T(2,128)S(1)} %add.174), channel_id=1, source_target_pairs={{0,4},{1,5},{2,6},{3,7},{4,0},{5,1},{6,2},{7,3},{8,12},{9,13},{10,... | collective-permute-start | bytes 3080 | tf_op jit(solution)/shard_map/ppermute | solution.py:71
  47.8 3.6 %collective-permute-start.5 = (f32[2,128]{1,0:T(2,128)S(1)}, f32[2,128]{1,0:T(2,128)S(1)}, u32[]{:S(2)}, u32[]{:S(2)}) collective-permute-start(f32[2,128]{1,0:T(2,128)S(1)} %add.174), channel_id=1, source_target_pairs={{0,2},{1,3},{2,0},{3,1},{4,6},{5,7},{6,4},{7,5},{8,10},{9,11},{10,... | collective-permute-start | bytes 3080 | tf_op jit(solution)/shard_map/ppermute | solution.py:71
  51.4 5.5 %collective-permute-start.10 = (f32[2,128]{1,0:T(2,128)S(1)}, f32[2,128]{1,0:T(2,128)S(1)}, u32[]{:S(2)}, u32[]{:S(2)}) collective-permute-start(f32[2,128]{1,0:T(2,128)S(1)} %add_add_fusion.1), channel_id=1, source_target_pairs={{0,24},{1,25},{2,26},{3,27},{4,28},{5,29},{6,30},{7,31},{8,16},{9,... | collective-permute-start | bytes 3080 | tf_op jit(solution)/shard_map/ppermute | solution.py:71
  55.4 4.5 %collective-permute-start.9 = (f32[2,128]{1,0:T(2,128)S(1)}, f32[2,128]{1,0:T(2,128)S(1)}, u32[]{:S(2)}, u32[]{:S(2)}) collective-permute-start(f32[2,128]{1,0:T(2,128)S(1)} %add_add_fusion.1), channel_id=1, source_target_pairs={{0,16},{1,17},{2,18},{3,19},{4,20},{5,21},{6,22},{7,23},{8,24},{9,... | collective-permute-start | bytes 3080 | tf_op jit(solution)/shard_map/ppermute | solution.py:71
  55.4 4.5 %collective-permute-start.8 = (f32[2,128]{1,0:T(2,128)S(1)}, f32[2,128]{1,0:T(2,128)S(1)}, u32[]{:S(2)}, u32[]{:S(2)}) collective-permute-start(f32[2,128]{1,0:T(2,128)S(1)} %add_add_fusion.1), channel_id=1, source_target_pairs={{0,8},{1,9},{2,10},{3,11},{4,12},{5,13},{6,14},{7,15},{8,0},{9,1},... | collective-permute-start | bytes 3080 | tf_op jit(solution)/shard_map/ppermute | solution.py:71
  65.6 4.5 %collective-permute-start.14 = (f32[1,128]{1,0:T(1,128)S(1)}, f32[1,128]{1,0:T(1,128)S(1)}, u32[]{:S(2)}, u32[]{:S(2)}) collective-permute-start(f32[1,128]{1,0:T(1,128)S(1)} %add.181), channel_id=1, source_target_pairs={{0,6},{1,7},{2,4},{3,5},{4,2},{5,3},{6,0},{7,1},{8,14},{9,15},{10,... | collective-permute-start | bytes 1544 | tf_op jit(solution)/shard_map/ppermute | solution.py:71
  67.0 3.6 %collective-permute-start.13 = (f32[1,128]{1,0:T(1,128)S(1)}, f32[1,128]{1,0:T(1,128)S(1)}, u32[]{:S(2)}, u32[]{:S(2)}) collective-permute-start(f32[1,128]{1,0:T(1,128)S(1)} %add.181), channel_id=1, source_target_pairs={{0,4},{1,5},{2,6},{3,7},{4,0},{5,1},{6,2},{7,3},{8,12},{9,13},{10,... | collective-permute-start | bytes 1544 | tf_op jit(solution)/shard_map/ppermute | solution.py:71
  69.0 3.6 %collective-permute-start.12 = (f32[1,128]{1,0:T(1,128)S(1)}, f32[1,128]{1,0:T(1,128)S(1)}, u32[]{:S(2)}, u32[]{:S(2)}) collective-permute-start(f32[1,128]{1,0:T(1,128)S(1)} %add.181), channel_id=1, source_target_pairs={{0,2},{1,3},{2,0},{3,1},{4,6},{5,7},{6,4},{7,5},{8,10},{9,11},{10,... | collective-permute-start | bytes 1544 | tf_op jit(solution)/shard_map/ppermute | solution.py:71
  72.6 5.4 %collective-permute-start.17 = (f32[1,128]{1,0:T(1,128)S(1)}, f32[1,128]{1,0:T(1,128)S(1)}, u32[]{:S(2)}, u32[]{:S(2)}) collective-permute-start(f32[1,128]{1,0:T(1,128)S(1)} %add_add_fusion.9), channel_id=1, source_target_pairs={{0,24},{1,25},{2,26},{3,27},{4,28},{5,29},{6,30},{7,31},{8,16},{9,... | collective-permute-start | bytes 1544 | tf_op jit(solution)/shard_map/ppermute | solution.py:71
  74.0 4.5 %collective-permute-start.16 = (f32[1,128]{1,0:T(1,128)S(1)}, f32[1,128]{1,0:T(1,128)S(1)}, u32[]{:S(2)}, u32[]{:S(2)}) collective-permute-start(f32[1,128]{1,0:T(1,128)S(1)} %add_add_fusion.9), channel_id=1, source_target_pairs={{0,16},{1,17},{2,18},{3,19},{4,20},{5,21},{6,22},{7,23},{8,24},{9,... | collective-permute-start | bytes 1544 | tf_op jit(solution)/shard_map/ppermute | solution.py:71
  74.7 3.8 %collective-permute-start.15 = (f32[1,128]{1,0:T(1,128)S(1)}, f32[1,128]{1,0:T(1,128)S(1)}, u32[]{:S(2)}, u32[]{:S(2)}) collective-permute-start(f32[1,128]{1,0:T(1,128)S(1)} %add_add_fusion.9), channel_id=1, source_target_pairs={{0,8},{1,9},{2,10},{3,11},{4,12},{5,13},{6,14},{7,15},{8,0},{9,1},... | collective-permute-start | bytes 1544 | tf_op jit(solution)/shard_map/ppermute | solution.py:71
  86.6 4.5 %collective-permute-start.21 = (f32[1,128]{1,0:T(1,128)S(1)}, f32[1,128]{1,0:T(1,128)S(1)}, u32[]{:S(2)}, u32[]{:S(2)}) collective-permute-start(f32[1,128]{1,0:T(1,128)S(1)} %add.188), channel_id=1, source_target_pairs={{0,6},{1,7},{2,4},{3,5},{4,2},{5,3},{6,0},{7,1},{8,14},{9,15},{10,... | collective-permute-start | bytes 1544 | tf_op jit(solution)/shard_map/ppermute | solution.py:71
  87.0 4.1 %collective-permute-start.20 = (f32[1,128]{1,0:T(1,128)S(1)}, f32[1,128]{1,0:T(1,128)S(1)}, u32[]{:S(2)}, u32[]{:S(2)}) collective-permute-start(f32[1,128]{1,0:T(1,128)S(1)} %add.188), channel_id=1, source_target_pairs={{0,4},{1,5},{2,6},{3,7},{4,0},{5,1},{6,2},{7,3},{8,12},{9,13},{10,... | collective-permute-start | bytes 1544 | tf_op jit(solution)/shard_map/ppermute | solution.py:71
  88.2 3.6 %collective-permute-start.19 = (f32[1,128]{1,0:T(1,128)S(1)}, f32[1,128]{1,0:T(1,128)S(1)}, u32[]{:S(2)}, u32[]{:S(2)}) collective-permute-start(f32[1,128]{1,0:T(1,128)S(1)} %add.188), channel_id=1, source_target_pairs={{0,2},{1,3},{2,0},{3,1},{4,6},{5,7},{6,4},{7,5},{8,10},{9,11},{10,... | collective-permute-start | bytes 1544 | tf_op jit(solution)/shard_map/ppermute | solution.py:71
  91.8 5.4 %collective-permute-start.24 = (f32[1,128]{1,0:T(1,128)S(1)}, f32[1,128]{1,0:T(1,128)S(1)}, u32[]{:S(2)}, u32[]{:S(2)}) collective-permute-start(f32[1,128]{1,0:T(1,128)S(1)} %add_add_fusion.7), channel_id=1, source_target_pairs={{0,24},{1,25},{2,26},{3,27},{4,28},{5,29},{6,30},{7,31},{8,16},{9,... | collective-permute-start | bytes 1544 | tf_op jit(solution)/shard_map/ppermute | solution.py:71
  94.4 4.5 %collective-permute-start.23 = (f32[1,128]{1,0:T(1,128)S(1)}, f32[1,128]{1,0:T(1,128)S(1)}, u32[]{:S(2)}, u32[]{:S(2)}) collective-permute-start(f32[1,128]{1,0:T(1,128)S(1)} %add_add_fusion.7), channel_id=1, source_target_pairs={{0,16},{1,17},{2,18},{3,19},{4,20},{5,21},{6,22},{7,23},{8,24},{9,... | collective-permute-start | bytes 1544 | tf_op jit(solution)/shard_map/ppermute | solution.py:71
  95.3 3.6 %collective-permute-start.22 = (f32[1,128]{1,0:T(1,128)S(1)}, f32[1,128]{1,0:T(1,128)S(1)}, u32[]{:S(2)}, u32[]{:S(2)}) collective-permute-start(f32[1,128]{1,0:T(1,128)S(1)} %add_add_fusion.7), channel_id=1, source_target_pairs={{0,8},{1,9},{2,10},{3,11},{4,12},{5,13},{6,14},{7,15},{8,0},{9,1},... | collective-permute-start | bytes 1544 | tf_op jit(solution)/shard_map/ppermute | solution.py:71
  104.6 4.5 %collective-permute-start.28 = (f32[1,128]{1,0:T(1,128)S(1)}, f32[1,128]{1,0:T(1,128)S(1)}, u32[]{:S(2)}, u32[]{:S(2)}) collective-permute-start(f32[1,128]{1,0:T(1,128)S(1)} %add.195), channel_id=1, source_target_pairs={{0,6},{1,7},{2,4},{3,5},{4,2},{5,3},{6,0},{7,1},{8,14},{9,15},{10,... | collective-permute-start | bytes 1544 | tf_op jit(solution)/shard_map/ppermute | solution.py:71
  108.0 3.6 %collective-permute-start.26 = (f32[1,128]{1,0:T(1,128)S(1)}, f32[1,128]{1,0:T(1,128)S(1)}, u32[]{:S(2)}, u32[]{:S(2)}) collective-permute-start(f32[1,128]{1,0:T(1,128)S(1)} %add.195), channel_id=1, source_target_pairs={{0,2},{1,3},{2,0},{3,1},{4,6},{5,7},{6,4},{7,5},{8,10},{9,11},{10,... | collective-permute-start | bytes 1544 | tf_op jit(solution)/shard_map/ppermute | solution.py:71
  111.5 5.4 %collective-permute-start.31 = (f32[1,128]{1,0:T(1,128)S(1)}, f32[1,128]{1,0:T(1,128)S(1)}, u32[]{:S(2)}, u32[]{:S(2)}) collective-permute-start(f32[1,128]{1,0:T(1,128)S(1)} %add_add_fusion.5), channel_id=1, source_target_pairs={{0,24},{1,25},{2,26},{3,27},{4,28},{5,29},{6,30},{7,31},{8,16},{9,... | collective-permute-start | bytes 1544 | tf_op jit(solution)/shard_map/ppermute | solution.py:71
  113.0 4.5 %collective-permute-start.30 = (f32[1,128]{1,0:T(1,128)S(1)}, f32[1,128]{1,0:T(1,128)S(1)}, u32[]{:S(2)}, u32[]{:S(2)}) collective-permute-start(f32[1,128]{1,0:T(1,128)S(1)} %add_add_fusion.5), channel_id=1, source_target_pairs={{0,16},{1,17},{2,18},{3,19},{4,20},{5,21},{6,22},{7,23},{8,24},{9,... | collective-permute-start | bytes 1544 | tf_op jit(solution)/shard_map/ppermute | solution.py:71
  113.9 3.6 %collective-permute-start.29 = (f32[1,128]{1,0:T(1,128)S(1)}, f32[1,128]{1,0:T(1,128)S(1)}, u32[]{:S(2)}, u32[]{:S(2)}) collective-permute-start(f32[1,128]{1,0:T(1,128)S(1)} %add_add_fusion.5), channel_id=1, source_target_pairs={{0,8},{1,9},{2,10},{3,11},{4,12},{5,13},{6,14},{7,15},{8,0},{9,1},... | collective-permute-start | bytes 1544 | tf_op jit(solution)/shard_map/ppermute | solution.py:71
  125.2 4.5 %collective-permute-start.35 = (f32[1,128]{1,0:T(1,128)S(1)}, f32[1,128]{1,0:T(1,128)S(1)}, u32[]{:S(2)}, u32[]{:S(2)}) collective-permute-start(f32[1,128]{1,0:T(1,128)S(1)} %add.202), channel_id=1, source_target_pairs={{0,6},{1,7},{2,4},{3,5},{4,2},{5,3},{6,0},{7,1},{8,14},{9,15},{10,... | collective-permute-start | bytes 1544 | tf_op jit(solution)/shard_map/ppermute | solution.py:71
  125.6 4.1 %collective-permute-start.34 = (f32[1,128]{1,0:T(1,128)S(1)}, f32[1,128]{1,0:T(1,128)S(1)}, u32[]{:S(2)}, u32[]{:S(2)}) collective-permute-start(f32[1,128]{1,0:T(1,128)S(1)} %add.202), channel_id=1, source_target_pairs={{0,4},{1,5},{2,6},{3,7},{4,0},{5,1},{6,2},{7,3},{8,12},{9,13},{10,... | collective-permute-start | bytes 1544 | tf_op jit(solution)/shard_map/ppermute | solution.py:71
  130.4 5.4 %collective-permute-start.38 = (f32[1,128]{1,0:T(1,128)S(1)}, f32[1,128]{1,0:T(1,128)S(1)}, u32[]{:S(2)}, u32[]{:S(2)}) collective-permute-start(f32[1,128]{1,0:T(1,128)S(1)} %add_add_fusion.3), channel_id=1, source_target_pairs={{0,24},{1,25},{2,26},{3,27},{4,28},{5,29},{6,30},{7,31},{8,16},{9,... | collective-permute-start | bytes 1544 | tf_op jit(solution)/shard_map/ppermute | solution.py:71
  133.0 4.5 %collective-permute-start.37 = (f32[1,128]{1,0:T(1,128)S(1)}, f32[1,128]{1,0:T(1,128)S(1)}, u32[]{:S(2)}, u32[]{:S(2)}) collective-permute-start(f32[1,128]{1,0:T(1,128)S(1)} %add_add_fusion.3), channel_id=1, source_target_pairs={{0,16},{1,17},{2,18},{3,19},{4,20},{5,21},{6,22},{7,23},{8,24},{9,... | collective-permute-start | bytes 1544 | tf_op jit(solution)/shard_map/ppermute | solution.py:71
  (11 other events, 57.0 us)
